TPU v7x, 32 devices: a whole 2x2x4 slice. The times are simulated.
32 devices in a mesh: ctx: 16 (over z, x, core), head: 2 (over y).
Axes of the slice: x: 2, y: 2, z: 4, core: 2. Of those that a mesh axis runs over, the one named last changes fastest.
Arguments:
- query_rows: bfloat16 [4096, 1024], P(('ctx', 'head')), may hold values from -6 to 6
- key_rows: bfloat16 [4096, 1024], P(('ctx', 'head')), may hold values from -6 to 6
- value_rows: bfloat16 [4096, 2048], P(('ctx', 'head')), may hold values from -6 to 6
- output_gate: bfloat16 [4096, 2048], P(('ctx', 'head')), may hold values from -6 to 6
- beta_logit: bfloat16 [4096, 16], P(('ctx', 'head')), may hold values from -7 to -3.5
- log_decay: bfloat16 [4096, 16], P(('ctx', 'head')), may hold values from -1 to 0
- norm_gain: bfloat16 [128], replicated, may hold values from 0.5 to 1.5
Outputs:
- layer_out: bfloat16 [4096, 2048], P(('ctx', 'head'))
All inputs are finite; a program needn't handle non-finite values.
Results may differ from a plain program's by a relative error of at most 0.0049.
Values may be sent and summed in bfloat16 or wider, within the bound.
No kernel may reach another device: no remote copies, remote signals or barrier semaphores. Data moves between devices by JAX's collectives and lax.ppermute only.
A program may use at most 128 MiB of HBM per device.

v0:
```python
import jax
import jax.numpy as jnp
from jax import lax
from jax.sharding import PartitionSpec as P

DK = 128
DV = 128
SPAN = 128


FULL_PRECISION = lax.Precision.HIGHEST
LOCAL_PRECISION = lax.Precision.HIGH


def unit_rows(rows):
    return rows * lax.rsqrt(jnp.sum(rows * rows, axis=-1, keepdims=True) + 1e-06)


def compose(earlier, later):
    return (
        jnp.matmul(later[0], earlier[0], precision=FULL_PRECISION),
        jnp.matmul(later[0], earlier[1], precision=FULL_PRECISION) + later[1],
    )


def arrange(key_part, value_part, beta_part, decay_part):
    blocks = key_part.shape[0] // SPAN
    key_heads = key_part.shape[1] // DK
    value_heads = value_part.shape[1] // DV
    key_unit = unit_rows(
        key_part.astype(jnp.float32).reshape(blocks, SPAN, key_heads, DK)
    ).transpose(2, 0, 1, 3)
    value_f = (
        value_part.astype(jnp.float32).reshape(blocks, SPAN, value_heads, DV).transpose(2, 0, 1, 3)
    )
    beta_gate = (
        jax.nn.sigmoid(beta_part.astype(jnp.float32))
        .reshape(blocks, SPAN, value_heads)
        .transpose(2, 0, 1)
    )
    decay_log = decay_part.astype(jnp.float32).reshape(blocks, SPAN, value_heads).transpose(2, 0, 1)
    return (key_unit, value_f, beta_gate, decay_log)


def arrange_query(query_part):
    blocks = query_part.shape[0] // SPAN
    key_heads = query_part.shape[1] // DK
    query_f = query_part.astype(jnp.float32).reshape(blocks, SPAN, key_heads, DK)
    return (unit_rows(query_f) * DK ** (-0.5)).transpose(2, 0, 1, 3)


def unit_lower_inverse(strictly_lower):
    inverse = jnp.eye(SPAN, dtype=jnp.float32) - strictly_lower
    power = jnp.matmul(strictly_lower, strictly_lower, precision=LOCAL_PRECISION)
    covered = 2
    while covered < SPAN:
        if 2 * covered < SPAN:
            both = jnp.matmul(
                jnp.concatenate([inverse, power], axis=-2), power, precision=LOCAL_PRECISION
            )
            inverse = inverse + both[..., :SPAN, :]
            power = both[..., SPAN:, :]
        else:
            inverse = inverse + jnp.matmul(inverse, power, precision=LOCAL_PRECISION)
        covered = covered * 2
    return inverse


def span_pass(key_unit, value_f, beta_gate, decay_log, group_size):
    rowpos = lax.broadcasted_iota(jnp.int32, (SPAN, SPAN), 0)
    colpos = lax.broadcasted_iota(jnp.int32, (SPAN, SPAN), 1)
    cum_log = jnp.cumsum(decay_log, axis=2)
    spread = cum_log[..., :, None] - cum_log[..., None, :]
    strict = jnp.exp(jnp.where(colpos < rowpos, spread, -jnp.inf))
    key_inner = jnp.repeat(
        jnp.einsum("hmik,hmjk->hmij", key_unit, key_unit, precision=LOCAL_PRECISION),
        group_size,
        axis=0,
    )
    inverse = unit_lower_inverse(beta_gate[..., :, None] * strict * key_inner)
    wide_keys = jnp.repeat(key_unit, group_size, axis=0)
    targets = jnp.concatenate(
        [beta_gate[..., None] * value_f, (beta_gate * jnp.exp(cum_log))[..., None] * wide_keys],
        axis=-1,
    )
    solved = jnp.matmul(inverse, targets, precision=LOCAL_PRECISION)
    written = solved[..., :DV]
    weights = solved[..., DV:]
    faded_keys = wide_keys * jnp.exp(cum_log[..., -1:] - cum_log)[..., None]
    tail_decay = jnp.exp(cum_log[..., -1])
    carry_mat = tail_decay[..., None, None] * jnp.eye(DK, dtype=jnp.float32) - jnp.einsum(
        "hmck,hmcj->hmkj", faded_keys, weights, precision=LOCAL_PRECISION
    )
    write_mat = jnp.einsum("hmck,hmcv->hmkv", faded_keys, written, precision=LOCAL_PRECISION)
    return (cum_log, spread, written, weights, carry_mat, write_mat)


def span_prep(query_unit, key_unit, group_size, pieces):
    cum_log, spread, written, weights, carry_mat, write_mat = pieces
    rowpos = lax.broadcasted_iota(jnp.int32, (SPAN, SPAN), 0)
    colpos = lax.broadcasted_iota(jnp.int32, (SPAN, SPAN), 1)
    within = jnp.exp(jnp.where(colpos <= rowpos, spread, -jnp.inf))
    scores = (
        jnp.repeat(
            jnp.einsum("hmik,hmjk->hmij", query_unit, key_unit, precision=LOCAL_PRECISION),
            group_size,
            axis=0,
        )
        * within
    )
    wide_query = jnp.repeat(query_unit, group_size, axis=0)
    inner = jnp.einsum("hmij,hmjv->hmiv", scores, written, precision=LOCAL_PRECISION)
    reach = wide_query * jnp.exp(cum_log)[..., None] - jnp.einsum(
        "hmij,hmjk->hmik", scores, weights, precision=LOCAL_PRECISION
    )
    head_count, blocks = (carry_mat.shape[0], carry_mat.shape[1])
    reach_map = jnp.broadcast_to(jnp.eye(DK, dtype=jnp.float32), (head_count, DK, DK))
    reach_add = jnp.zeros((head_count, DK, DV), jnp.float32)
    fixed, scaled = ([], [])
    for m in range(blocks):
        if m == 0:
            fixed.append(inner[:, m])
            scaled.append(reach[:, m])
        else:
            fixed.append(
                inner[:, m]
                + jnp.matmul(reach[:, m], reach_add, precision=LOCAL_PRECISION)
            )
            scaled.append(jnp.matmul(reach[:, m], reach_map, precision=LOCAL_PRECISION))
        reach_map, reach_add = compose((reach_map, reach_add), (carry_mat[:, m], write_mat[:, m]))
    return (jnp.stack(fixed, axis=1), jnp.stack(scaled, axis=1), reach_map, reach_add)


def span_out(fixed, scaled, state_in):
    return fixed + jnp.einsum("hmck,hkv->hmcv", scaled, state_in, precision=FULL_PRECISION)


def to_rows(core_out):
    head_count, blocks = (core_out.shape[0], core_out.shape[1])
    return core_out.transpose(1, 2, 0, 3).reshape(blocks * SPAN, head_count * DV)


def joined(carry, write):
    return jnp.concatenate([carry, write], axis=-1)


def inclusive_scan(carry, write, size, stride):
    count = size // stride
    shift = 1
    while shift < count:
        pairs = [(i, i + shift * stride) for i in range(size - shift * stride)]
        if 2 * shift < count:
            got = lax.ppermute(joined(carry, write), "ctx", pairs)
            carry, write = compose((got[..., :DK], got[..., DK:]), (carry, write))
        else:
            got = lax.ppermute(write, "ctx", pairs)
            write = jnp.matmul(carry, got, precision=FULL_PRECISION) + write
        shift *= 2
    return write


def chain_states(block_carry, block_write):
    size = lax.axis_size("ctx")
    head_count = block_carry.shape[0]
    if size % 2 or head_count % 2:
        write = inclusive_scan(block_carry, block_write, size, 1)
        return lax.ppermute(write, "ctx", [(i, i + 1) for i in range(size - 1)])
    half = head_count // 2
    odd = lax.axis_index("ctx") % 2 == 1
    both = joined(block_carry, block_write)
    mine = jnp.where(odd, both[half:], both[:half])
    other = jnp.where(odd, both[:half], both[half:])
    swap = [(i, i ^ 1) for i in range(size)]
    got = lax.ppermute(other, "ctx", swap)
    earlier = jnp.where(odd, got, mine)
    later = jnp.where(odd, mine, got)
    pair_carry, pair_write = compose(
        (earlier[..., :DK], earlier[..., DK:]), (later[..., :DK], later[..., DK:])
    )
    pair_write = inclusive_scan(pair_carry, pair_write, size, 2)
    from_odd = lax.ppermute(pair_write, "ctx", [(i, i + 1) for i in range(1, size - 1, 2)])
    from_even = lax.ppermute(pair_write, "ctx", [(i, i + 2) for i in range(0, size - 2, 2)])
    even_state = jnp.concatenate([from_even, from_odd], axis=0)
    odd_state = (
        jnp.matmul(block_carry, even_state, precision=FULL_PRECISION) + block_write
    )
    odd_state = lax.ppermute(odd_state, "ctx", [(i, i + 1) for i in range(0, size, 2)])
    return jnp.where(odd, odd_state, even_state)


def gated_norm(core_rows, output_gate, norm_gain):
    token_count = core_rows.shape[0]
    head_count = core_rows.shape[1] // DV
    core_f = core_rows.astype(jnp.float32).reshape(token_count, head_count, DV)
    inv_rms = lax.rsqrt(jnp.mean(core_f * core_f, axis=-1, keepdims=True) + 1e-06)
    gate_f = output_gate.astype(jnp.float32).reshape(token_count, head_count, DV)
    gated_rows = core_f * inv_rms * norm_gain.astype(jnp.float32) * jax.nn.silu(gate_f)
    return gated_rows.reshape(token_count, head_count * DV).astype(jnp.bfloat16)


def on_device(query_rows, key_rows, value_rows, output_gate, beta_logit, log_decay, norm_gain):
    parts = lax.axis_size("head")
    tokens = query_rows.shape[0]
    pieces_in = [query_rows, key_rows, value_rows, beta_logit, log_decay]
    widths = [part.shape[1] // parts for part in pieces_in]
    packed = jnp.concatenate(
        [part.reshape(tokens, parts, width) for part, width in zip(pieces_in, widths)], axis=-1
    )
    packed = lax.all_to_all(packed, "head", split_axis=1, concat_axis=0, tiled=True)
    packed = packed.reshape(tokens * parts, sum(widths))
    ends = [sum(widths[: i + 1]) for i in range(len(widths))]
    q_head, k_head, v_head, b_head, d_head = (
        packed[:, end - width : end] for end, width in zip(ends, widths)
    )
    key_unit, value_f, beta_gate, decay_log = arrange(k_head, v_head, b_head, d_head)
    group_size = value_f.shape[0] // key_unit.shape[0]
    pieces = span_pass(key_unit, value_f, beta_gate, decay_log, group_size)
    query_unit = arrange_query(q_head)
    fixed, scaled, total_carry, total_write = span_prep(query_unit, key_unit, group_size, pieces)
    state_in = chain_states(total_carry, total_write)
    core_out = span_out(fixed, scaled, state_in)
    core_rows = lax.all_to_all(
        to_rows(core_out).astype(jnp.bfloat16), "head", split_axis=0, concat_axis=1, tiled=True
    )
    return gated_norm(core_rows, output_gate, norm_gain)


def solution(mesh):
    placed = (
        P(("ctx", "head"), None),
        P(("ctx", "head"), None),
        P(("ctx", "head"), None),
        P(("ctx", "head"), None),
        P(("ctx", "head"), None),
        P(("ctx", "head"), None),
        P(),
    )
    return jax.shard_map(
        on_device, mesh=mesh, in_specs=placed, out_specs=P(("ctx", "head"), None), check_vma=False
    )
```

profile of v0, /device:TPU:0, one launch (start us, length us, event | category | flops | bytes accessed | tf_op | source)
XLA Modules:
  0.0 141.1 jit_solution(13257693860238721685)
XLA Ops:
  0.0 1.1 copy.121
  1.9 1.1 copy.122
  3.0 1.3 copy.123
  7.1 4.2 %all-to-all-start = ((bf16[128,2,2064]{0,2,1:T(8,128)(2,1)}), bf16[128,2,2064]{0,2,1:T(8,128)(2,1)S(1)}, u32[]{:S(2)}, u32[]{:S(2)}) async-start(bf16[128,2,2064]{0,2,1:T(8,128)(2,1)} %constant_dynamic-update-slice_fusion), calls=%async_computation | async-start | bytes 2113536 | tf_op jit(solution)/shard_map/all_to_all | solution.py:209
  12.6 13.3 %all-to-all-done = bf16[128,2,2064]{0,2,1:T(8,128)(2,1)S(1)} async-done(((bf16[128,2,2064]{0,2,1:T(8,128)(2,1)}), bf16[128,2,2064]{0,2,1:T(8,128)(2,1)S(1)}, u32[]{:S(2)}, u32[]{:S(2)}) %all-to-all-start) | async-done | bytes 1056800 | tf_op jit(solution)/shard_map/all_to_all | solution.py:209
  33.3 1.1 fusion
  34.4 1.6 %slice_add_fusion.5 = (f32[8,2,128,128]{3,2,1,0:T(8,128)S(1)}, f32[8,2,128,128]{3,2,1,0:T(8,128)S(1)}, f32[8,2,128,128]{3,2,1,0:T(8,128)S(1)}, f32[8,2,128,128]{3,2,1,0:T(8,128)}) fusion(f32[8,2,256,128]{3,2,1,0:T(8,128)S(1)} %fusion, f32[4,2,128,128]{3,2,1,0:T(8,128)S(1)} %fusion.75, f32[8,2,128]{2,1,0:T(2,128)S(1)} %copy.128, ...), kind=kLoop, calls=%fused_computation.61 | loop fusion | flops 2359296 | bytes 8511488 | tf_op jit(solution)/shard_map/add | solution.py:61
  36.0 1.1 fusion.4
  37.4 1.1 fusion.8
  38.7 1.1 fusion.12
  40.1 1.1 fusion.16
  41.1 1.7 %convolution_add_fusion = f32[8,2,128,128]{3,2,1,0:T(8,128)} fusion(f32[8,2,256,128]{3,2,1,0:T(8,128)S(1)} %fusion.16, f32[8,2,128,128]{3,2,1,0:T(8,128)S(1)} %get-tuple-element.5), kind=kOutput, calls=%fused_computation.28 | convolution fusion | flops 201850880 | bytes 4194304 | tf_op jit(solution)/shard_map/dot_general | solution.py:64
  44.2 2.4 %fusion.20 = f32[8,2,128,256]{3,2,1,0:T(8,128)S(1)} fusion(f32[8,2,128,128]{3,2,1,0:T(8,128)S(1)} %copy-done.7, f32[8,2,128,128]{3,2,1,0:T(8,128)S(1)} %get-tuple-element.21, f32[8,2,128,128]{3,2,1,0:T(8,128)} %get-tuple-element.27), kind=kOutput, calls=%fused_computation.20 | convolution fusion | flops 403177472 | bytes 5242880 | tf_op jit(solution)/shard_map/dot_general | solution.py:86
  47.6 1.1 convolution_subtract_fusion
  49.7 1.8 %fusion.49 = f32[8,128,128]{1,2,0:T(8,128)} fusion(f32[8,128,128]{2,1,0:T(8,128)S(1)} %fusion.48, f32[8,2,128,128]{3,2,1,0:T(8,128)S(1)} %convolution_subtract_fusion), kind=kOutput, calls=%fused_computation.94 | convolution fusion | flops 201326592 | bytes 1572864 | tf_op jit(solution)/shard_map/dot_general | solution.py:21
  52.4 2.0 %copy.192 = f32[8,1,128,128]{3,2,0,1:T(8,128)} copy(f32[8,1,128,128]{2,3,1,0:T(8,128)} %slice.170) | data formatting | bytes 1048576
  54.4 1.8 %convolution_add_fusion.5 = f32[8,128,128]{2,1,0:T(8,128)S(1)} fusion(f32[8,1,128,128]{3,2,0,1:T(8,128)} %copy.192, f32[8,2,128,128]{3,2,1,0:T(8,128)} %copy-done), kind=kOutput, calls=%fused_computation.39 | convolution fusion | flops 201457664 | bytes 1572864 | tf_op jit(solution)/shard_map/dot_general | solution.py:22
  56.2 2.5 %convolution_add_fusion.3 = f32[8,128,128]{1,2,0:T(8,128)S(1)} fusion(f32[8,128,128]{2,1,0:T(8,128)S(1)} %convolution_add_fusion.5, f32[8,2,128,128]{2,3,1,0:T(8,128)} %copy-done.6, f32[8,2,128,128]{3,2,1,0:T(8,128)} %copy-done), kind=kOutput, calls=%fused_computation.36 | convolution fusion | flops 201457664 | bytes 2097152 | tf_op jit(solution)/shard_map/dot_general | solution.py:22
  58.9 1.9 %collective-permute-done = f32[4,128,256]{1,2,0:T(8,128)S(1)} collective-permute-done((f32[4,128,256]{1,2,0:T(8,128)S(1)}, f32[4,128,256]{1,2,0:T(8,128)S(1)}, u32[]{:S(2)}, u32[]{:S(2)}) %collective-permute-start) | collective-permute-done | bytes 524320 | tf_op jit(solution)/shard_map/ppermute | solution.py:174
  61.7 3.8 %collective-permute-start.1 = (f32[4,128,256]{1,2,0:T(8,128)S(1)}, f32[4,128,256]{1,2,0:T(8,128)S(1)}, u32[]{:S(2)}, u32[]{:S(2)}) collective-permute-start(f32[4,128,256]{1,2,0:T(8,128)S(1)} %pad_maximum_fusion.2), channel_id=1, source_target_pairs={{0,4},{2,6},{4,8},{6,10},{8,12},{10,14},{12,16},{14,18},{16,20},{1... | collective-permute-start | bytes 1572872 | tf_op jit(solution)/shard_map/ppermute | solution.py:153
  65.5 11.4 %collective-permute-done.1 = f32[4,128,256]{1,2,0:T(8,128)S(1)} collective-permute-done((f32[4,128,256]{1,2,0:T(8,128)S(1)}, f32[4,128,256]{1,2,0:T(8,128)S(1)}, u32[]{:S(2)}, u32[]{:S(2)}) %collective-permute-start.1) | collective-permute-done | bytes 524320 | tf_op jit(solution)/shard_map/ppermute | solution.py:153
  77.7 5.4 %collective-permute-start.2 = (f32[4,128,256]{1,2,0:T(8,128)S(1)}, f32[4,128,256]{1,2,0:T(8,128)S(1)}, u32[]{:S(2)}, u32[]{:S(2)}) collective-permute-start(f32[4,128,256]{1,2,0:T(8,128)S(1)} %pad_maximum_fusion.3), channel_id=1, source_target_pairs={{0,8},{2,10},{4,12},{6,14},{8,16},{10,18},{12,20},{14,22},{16,24},... | collective-permute-start | bytes 1572872 | tf_op jit(solution)/shard_map/ppermute | solution.py:153
  83.5 10.2 %collective-permute-done.2 = f32[4,128,256]{1,2,0:T(8,128)S(1)} collective-permute-done((f32[4,128,256]{1,2,0:T(8,128)S(1)}, f32[4,128,256]{1,2,0:T(8,128)S(1)}, u32[]{:S(2)}, u32[]{:S(2)}) %collective-permute-start.2) | collective-permute-done | bytes 524320 | tf_op jit(solution)/shard_map/ppermute | solution.py:153
  94.1 5.4 %collective-permute-start.3 = (f32[4,128,128]{1,2,0:T(8,128)S(1)}, f32[4,128,128]{1,2,0:T(8,128)S(1)}, u32[]{:S(2)}, u32[]{:S(2)}) collective-permute-start(f32[4,128,128]{1,2,0:T(8,128)S(1)} %convolution_add_fusion.7), channel_id=1, source_target_pairs={{0,16},{2,18},{4,20},{6,22},{8,24},{10,26},{12,28},{14,30},{1,17},... | collective-permute-start | bytes 786440 | tf_op jit(solution)/shard_map/ppermute | solution.py:156
  100.7 2.9 %collective-permute-done.3 = f32[4,128,128]{1,2,0:T(8,128)S(1)} collective-permute-done((f32[4,128,128]{1,2,0:T(8,128)S(1)}, f32[4,128,128]{1,2,0:T(8,128)S(1)}, u32[]{:S(2)}, u32[]{:S(2)}) %collective-permute-start.3) | collective-permute-done | bytes 262176 | tf_op jit(solution)/shard_map/ppermute | solution.py:156
  104.3 2.5 %collective-permute-start.4 = (f32[4,128,128]{1,2,0:T(8,128)S(1)}, f32[4,128,128]{1,2,0:T(8,128)S(1)}, u32[]{:S(2)}, u32[]{:S(2)}) collective-permute-start(f32[4,128,128]{1,2,0:T(8,128)S(1)} %convolution_add_fusion.6), channel_id=1, source_target_pairs={{0,4},{4,8},{8,12},{12,16},{16,20},{20,24},{24,28},{1,5},{5,9},{9,... | collective-permute-start | bytes 786440 | tf_op jit(solution)/shard_map/ppermute | solution.py:182
  108.6 2.1 %collective-permute-done.4 = f32[4,128,128]{1,2,0:T(8,128)S(1)} collective-permute-done((f32[4,128,128]{1,2,0:T(8,128)S(1)}, f32[4,128,128]{1,2,0:T(8,128)S(1)}, u32[]{:S(2)}, u32[]{:S(2)}) %collective-permute-start.4) | collective-permute-done | bytes 262176 | tf_op jit(solution)/shard_map/ppermute | solution.py:182
  111.4 11.3 %collective-permute-start.6 = (f32[8,128,128]{1,2,0:T(8,128)S(1)}, f32[8,128,128]{1,2,0:T(8,128)S(1)}, u32[]{:S(2)}, u32[]{:S(2)}) collective-permute-start(f32[8,128,128]{1,2,0:T(8,128)S(1)} %convolution_add_fusion.2), channel_id=1, source_target_pairs={{0,2},{4,6},{8,10},{12,14},{16,18},{20,22},{24,26},{28,30},{1,3},{... | collective-permute-start | bytes 1572872 | tf_op jit(solution)/shard_map/ppermute | solution.py:187
  124.2 1.9 %fusion.24 = bf16[8,2,128,128]{2,3,0,1:T(8,128)(2,1)} fusion(f32[8,1,128,128]{2,3,0,1:T(8,128)S(1)} %fusion.25, f32[8,1,128,128]{2,3,0,1:T(8,128)S(1)} %slice_bitcast_fusion.5, f32[8,128,128]{1,2,0:T(8,128)S(1)} %collective-permute-done.6, f32[8,128,128]{1,2,0:T(8,128)S(1)} %constant_dynamic-update-slice_fusion.5, pred[]{:T(512)S(6)} %eq.19, ...), kind=kOutput, calls=%fused_computation.34 | convolution fusion | flops 403832832 | bytes 3670017 | tf_op jit(solution)/shard_map/hmck,hkv->hmcv/dot_general | solution.py:135
  126.1 3.5 %all-to-all-start.1 = ((bf16[2,128,1024]{1,2,0:T(8,128)(2,1)}), bf16[2,128,1024]{1,2,0:T(8,128)(2,1)S(1)}, u32[]{:S(2)}, u32[]{:S(2)}) async-start(bf16[2,128,1024]{1,2,0:T(8,128)(2,1)} %bitcast.30), calls=%async_computation.1 | async-start | bytes 1048576 | tf_op jit(solution)/shard_map/all_to_all | solution.py:222
  129.6 8.7 %all-to-all-done.1 = bf16[2,128,1024]{1,2,0:T(8,128)(2,1)S(1)} async-done(((bf16[2,128,1024]{1,2,0:T(8,128)(2,1)}), bf16[2,128,1024]{1,2,0:T(8,128)(2,1)S(1)}, u32[]{:S(2)}, u32[]{:S(2)}) %all-to-all-start.1) | async-done | bytes 524320 | tf_op jit(solution)/shard_map/all_to_all | solution.py:222
  139.7 1.5 %fusion.38 = bf16[128,2048]{1,0:T(8,128)(2,1)} fusion(bf16[128,2048]{1,0:T(8,128)(2,1)S(1)} %copy-done.9, f32[128,2048]{1,0:T(8,128)S(1)} %copy.188, f32[16,8,16,128]{3,2,1,0:T(8,128)S(1)} %bitcast.125, f32[2048]{0:T(1024)S(1)} %broadcast_bitcast_fusion), kind=kLoop, calls=%fused_computation.69 | loop fusion | flops 2359296 | bytes 3153920 | tf_op jit(solution)/shard_map/convert_element_type | solution.py:198
  (110 shorter events, 26.4 us)
Async XLA Ops:
  0.0 5.9 %copy-start.12 = (bf16[128,16]{0,1:T(8,128)(2,1)S(1)}, bf16[128,16]{0,1:T(8,128)(2,1)}, u32[]{:S(2)}) copy-start(bf16[128,16]{0,1:T(8,128)(2,1)} %param.11) | copy-start | bytes 12292
  0.0 6.5 %copy-start.13 = (bf16[128,16]{0,1:T(8,128)(2,1)S(1)}, bf16[128,16]{0,1:T(8,128)(2,1)}, u32[]{:S(2)}) copy-start(bf16[128,16]{0,1:T(8,128)(2,1)} %param.12) | copy-start | bytes 12292
  7.1 18.8 %all-to-all-start = ((bf16[128,2,2064]{0,2,1:T(8,128)(2,1)}), bf16[128,2,2064]{0,2,1:T(8,128)(2,1)S(1)}, u32[]{:S(2)}, u32[]{:S(2)}) async-start(bf16[128,2,2064]{0,2,1:T(8,128)(2,1)} %constant_dynamic-update-slice_fusion), calls=%async_computation | async-start | bytes 2113536 | tf_op jit(solution)/shard_map/all_to_all | solution.py:209
  28.0 3.1 %copy-start.10 = (pred[128,128]{1,0:T(8,128)(4,1)S(1)}, pred[128,128]{1,0:T(8,128)(4,1)}, u32[]{:S(2)}) copy-start(pred[128,128]{1,0:T(8,128)(4,1)} %get-tuple-element.28) | copy-start | bytes 49156
  28.7 3.7 %copy-start.4 = (f32[4,2,128,128]{3,0,2,1:T(4,128)}, f32[4,2,128,128]{3,0,2,1:T(4,128)S(1)}, u32[]{:S(2)}) copy-start(f32[4,2,128,128]{3,0,2,1:T(4,128)S(1)} %get-tuple-element.31) | copy-start | bytes 1572868
  33.3 1.1 copy-start.11
  41.1 1.8 %copy-start.8 = (f32[4,2,128,128]{3,2,1,0:T(8,128)S(1)}, f32[4,2,128,128]{3,2,1,0:T(8,128)}, u32[]{:S(2)}) copy-start(f32[4,2,128,128]{3,2,1,0:T(8,128)} %copy.126) | copy-start | bytes 1572868
  42.9 1.2 copy-start.7
  47.6 4.0 %copy-start.6 = (f32[8,2,128,128]{2,3,1,0:T(8,128)}, f32[8,2,128,128]{2,3,1,0:T(8,128)S(1)}, u32[]{:S(2)}) copy-start(f32[8,2,128,128]{2,3,1,0:T(8,128)S(1)} %fusion.41) | copy-start | bytes 3145732
  48.7 1.0 copy-start
  49.7 1.8 %copy-start.2 = (f32[8,128,128]{2,1,0:T(8,128)}, f32[8,128,128]{2,1,0:T(8,128)S(1)}, u32[]{:S(2)}) copy-start(f32[8,128,128]{2,1,0:T(8,128)S(1)} %fusion.48) | copy-start | bytes 1572868
  54.4 4.3 %copy-start.1 = (f32[8,128,128]{1,2,0:T(8,128)S(1)}, f32[8,128,128]{1,2,0:T(8,128)}, u32[]{:S(2)}) copy-start(f32[8,128,128]{1,2,0:T(8,128)} %fusion.49) | copy-start | bytes 1572868
  58.8 2.0 %collective-permute-start = (f32[4,128,256]{1,2,0:T(8,128)S(1)}, f32[4,128,256]{1,2,0:T(8,128)S(1)}, u32[]{:S(2)}, u32[]{:S(2)}) collective-permute-start(f32[4,128,256]{1,2,0:T(8,128)S(1)} %broadcast_select_fusion.2), channel_id=1, source_target_pairs={{0,2},{2,0},{4,6},{6,4},{8,10},{10,8},{12,14},{14,12},{16,18},{18,... | collective-permute-start | bytes 1572872 | tf_op jit(solution)/shard_map/ppermute | solution.py:174
  61.6 21.5 %copy-start.5 = (f32[4,2,128,128]{3,0,2,1:T(4,128)S(1)}, f32[4,2,128,128]{3,0,2,1:T(4,128)}, u32[]{:S(2)}) copy-start(f32[4,2,128,128]{3,0,2,1:T(4,128)} %copy-done.4) | copy-start | bytes 1572868
  61.7 15.2 %collective-permute-start.1 = (f32[4,128,256]{1,2,0:T(8,128)S(1)}, f32[4,128,256]{1,2,0:T(8,128)S(1)}, u32[]{:S(2)}, u32[]{:S(2)}) collective-permute-start(f32[4,128,256]{1,2,0:T(8,128)S(1)} %pad_maximum_fusion.2), channel_id=1, source_target_pairs={{0,4},{2,6},{4,8},{6,10},{8,12},{10,14},{12,16},{14,18},{16,20},{1... | collective-permute-start | bytes 1572872 | tf_op jit(solution)/shard_map/ppermute | solution.py:153
  77.7 16.0 %collective-permute-start.2 = (f32[4,128,256]{1,2,0:T(8,128)S(1)}, f32[4,128,256]{1,2,0:T(8,128)S(1)}, u32[]{:S(2)}, u32[]{:S(2)}) collective-permute-start(f32[4,128,256]{1,2,0:T(8,128)S(1)} %pad_maximum_fusion.3), channel_id=1, source_target_pairs={{0,8},{2,10},{4,12},{6,14},{8,16},{10,18},{12,20},{14,22},{16,24},... | collective-permute-start | bytes 1572872 | tf_op jit(solution)/shard_map/ppermute | solution.py:153
  94.1 9.6 %collective-permute-start.3 = (f32[4,128,128]{1,2,0:T(8,128)S(1)}, f32[4,128,128]{1,2,0:T(8,128)S(1)}, u32[]{:S(2)}, u32[]{:S(2)}) collective-permute-start(f32[4,128,128]{1,2,0:T(8,128)S(1)} %convolution_add_fusion.7), channel_id=1, source_target_pairs={{0,16},{2,18},{4,20},{6,22},{8,24},{10,26},{12,28},{14,30},{1,17},... | collective-permute-start | bytes 786440 | tf_op jit(solution)/shard_map/ppermute | solution.py:156
  104.3 6.4 %collective-permute-start.4 = (f32[4,128,128]{1,2,0:T(8,128)S(1)}, f32[4,128,128]{1,2,0:T(8,128)S(1)}, u32[]{:S(2)}, u32[]{:S(2)}) collective-permute-start(f32[4,128,128]{1,2,0:T(8,128)S(1)} %convolution_add_fusion.6), channel_id=1, source_target_pairs={{0,4},{4,8},{8,12},{12,16},{16,20},{20,24},{24,28},{1,5},{5,9},{9,... | collective-permute-start | bytes 786440 | tf_op jit(solution)/shard_map/ppermute | solution.py:182
  106.8 3.9 %collective-permute-start.5 = (f32[4,128,128]{1,2,0:T(8,128)S(1)}, f32[4,128,128]{1,2,0:T(8,128)S(1)}, u32[]{:S(2)}, u32[]{:S(2)}) collective-permute-start(f32[4,128,128]{1,2,0:T(8,128)S(1)} %convolution_add_fusion.6), channel_id=1, source_target_pairs={{2,4},{6,8},{10,12},{14,16},{18,20},{22,24},{26,28},{3,5},{7,9},{1... | collective-permute-start | bytes 786440 | tf_op jit(solution)/shard_map/ppermute | solution.py:181
  108.5 14.1 %copy-start.3 = (f32[8,128,128]{2,1,0:T(8,128)S(1)}, f32[8,128,128]{2,1,0:T(8,128)}, u32[]{:S(2)}) copy-start(f32[8,128,128]{2,1,0:T(8,128)} %copy-done.2) | copy-start | bytes 1572868
  111.4 12.8 %collective-permute-start.6 = (f32[8,128,128]{1,2,0:T(8,128)S(1)}, f32[8,128,128]{1,2,0:T(8,128)S(1)}, u32[]{:S(2)}, u32[]{:S(2)}) collective-permute-start(f32[8,128,128]{1,2,0:T(8,128)S(1)} %convolution_add_fusion.2), channel_id=1, source_target_pairs={{0,2},{4,6},{8,10},{12,14},{16,18},{20,22},{24,26},{28,30},{1,3},{... | collective-permute-start | bytes 1572872 | tf_op jit(solution)/shard_map/ppermute | solution.py:187
  123.7 5.9 %copy-start.14 = (bf16[128]{0:T(256)(128)(2,1)S(1)}, bf16[128]{0:T(256)(128)(2,1)}, u32[]{:S(2)}) copy-start(bf16[128]{0:T(256)(128)(2,1)} %param.13) | copy-start | bytes 772
  126.1 12.3 %all-to-all-start.1 = ((bf16[2,128,1024]{1,2,0:T(8,128)(2,1)}), bf16[2,128,1024]{1,2,0:T(8,128)(2,1)S(1)}, u32[]{:S(2)}, u32[]{:S(2)}) async-start(bf16[2,128,1024]{1,2,0:T(8,128)(2,1)} %bitcast.30), calls=%async_computation.1 | async-start | bytes 1048576 | tf_op jit(solution)/shard_map/all_to_all | solution.py:222
  138.6 1.0 copy-start.9
where the time goes:
time: 142 us; the launch traced here: 141 us
  waiting for transfers between devices  51 us (36%)
  starting transfers between devices  36.9 us (26%)
  matrix products  28.4 us (20%)
  local copies, waits for them, and re-layouts  14.8 us (10%)
  other arithmetic  9.36 us (7%)
    ppermute x2, waiting for transfers between devices, inclusive_scan(): got = lax.ppermute(joined(carry, write), 'ctx', pairs)  21.6 us
    all_to_all x1, waiting for transfers between devices, on_device(): lax.all_to_all(packed, 'head', split_axis=1, concat_axis=0, tiled=True)  13.3 us
    ppermute x1, starting transfers between devices, chain_states(): lax.ppermute(odd_state, 'ctx', [(i, i + 1) for i in range(0, size, 2)])  11.3 us
    unnamed x43, local copies, waits for them, and re-layouts  10.2 us
    ppermute x2, starting transfers between devices, inclusive_scan(): got = lax.ppermute(joined(carry, write), 'ctx', pairs)  9.18 us
    all_to_all x1, waiting for transfers between devices, on_device(): lax.all_to_all(to_rows(core_out).astype(jnp.bfloat16), 'head', split_axis...  8.74 us
    ppermute x1, starting transfers between devices, inclusive_scan(): got = lax.ppermute(write, 'ctx', pairs)  5.42 us
    dot_general x5, matrix products, compose(): jnp.matmul(later[0], earlier[1], precision=FULL_PRECISION) + later[1]  5.41 us
  transfers between devices with their start and end apart: 9, of which 8 were waited for; matrix products, arithmetic and copies ran while one was open for 3% of the time, Pallas kernels for 0%

commit v1 on v0

--- a/solution.py
+++ b/solution.py
@@ -198,10 +198,29 @@
     return gated_rows.reshape(token_count, head_count * DV).astype(jnp.bfloat16)
 
 
-def on_device(query_rows, key_rows, value_rows, output_gate, beta_logit, log_decay, norm_gain):
+def head_swap(rows):
+    width = rows.shape[1] // 2
+    first = lax.axis_index("head") == 0
+    own = jnp.where(first, rows[:, :width], rows[:, width:])
+    sent = jnp.where(first, rows[:, width:], rows[:, :width])
+    got = lax.ppermute(sent, "head", [(0, 1), (1, 0)])
+    return jnp.where(first, jnp.concatenate([own, got], 0), jnp.concatenate([got, own], 0))
+
+
+def head_return(rows):
+    tokens = rows.shape[0] // 2
+    first = lax.axis_index("head") == 0
+    own = jnp.where(first, rows[:tokens], rows[tokens:])
+    sent = jnp.where(first, rows[tokens:], rows[:tokens])
+    got = lax.ppermute(sent, "head", [(0, 1), (1, 0)])
+    return jnp.where(first, jnp.concatenate([own, got], 1), jnp.concatenate([got, own], 1))
+
+
+def head_inputs(pieces_in):
     parts = lax.axis_size("head")
-    tokens = query_rows.shape[0]
-    pieces_in = [query_rows, key_rows, value_rows, beta_logit, log_decay]
+    if parts == 2:
+        return [head_swap(part) for part in pieces_in]
+    tokens = pieces_in[0].shape[0]
     widths = [part.shape[1] // parts for part in pieces_in]
     packed = jnp.concatenate(
         [part.reshape(tokens, parts, width) for part, width in zip(pieces_in, widths)], axis=-1
@@ -209,8 +228,18 @@
     packed = lax.all_to_all(packed, "head", split_axis=1, concat_axis=0, tiled=True)
     packed = packed.reshape(tokens * parts, sum(widths))
     ends = [sum(widths[: i + 1]) for i in range(len(widths))]
-    q_head, k_head, v_head, b_head, d_head = (
-        packed[:, end - width : end] for end, width in zip(ends, widths)
+    return [packed[:, end - width : end] for end, width in zip(ends, widths)]
+
+
+def head_outputs(rows):
+    if lax.axis_size("head") == 2:
+        return head_return(rows)
+    return lax.all_to_all(rows, "head", split_axis=0, concat_axis=1, tiled=True)
+
+
+def on_device(query_rows, key_rows, value_rows, output_gate, beta_logit, log_decay, norm_gain):
+    q_head, k_head, v_head, b_head, d_head = head_inputs(
+        [query_rows, key_rows, value_rows, beta_logit, log_decay]
     )
     key_unit, value_f, beta_gate, decay_log = arrange(k_head, v_head, b_head, d_head)
     group_size = value_f.shape[0] // key_unit.shape[0]
@@ -219,9 +248,7 @@
     fixed, scaled, total_carry, total_write = span_prep(query_unit, key_unit, group_size, pieces)
     state_in = chain_states(total_carry, total_write)
     core_out = span_out(fixed, scaled, state_in)
-    core_rows = lax.all_to_all(
-        to_rows(core_out).astype(jnp.bfloat16), "head", split_axis=0, concat_axis=1, tiled=True
-    )
+    core_rows = head_outputs(to_rows(core_out).astype(jnp.bfloat16))
     return gated_norm(core_rows, output_gate, norm_gain)
 
 

time: 142 us -> 118 us (0.83)
  waiting for transfers between devices: 51 us -> 37.1 us
  local copies, waits for them, and re-layouts: 14.8 us -> 5.04 us
  matrix products: 28.4 us -> 25.3 us
  other arithmetic: 9.36 us -> 12 us
    all_to_all x2 -> x0, waiting for transfers between devices: 22 us -> none  [the longest x1 13.3 us: on_device(): lax.all_to_all(packed, 'head', split_axis=1, concat_axis=0, tiled=True)]
    ppermute x0 -> x6, waiting for transfers between devices: none -> 8.07 us  [the longest x1 8.06 us: head_return(): got = lax.ppermute(sent, 'head', [(0, 1), (1, 0)])]
    ppermute x0 -> x6, starting transfers between devices: none -> 7.79 us  [the longest x5 7.21 us: head_swap(): got = lax.ppermute(sent, 'head', [(0, 1), (1, 0)])]
    all_to_all x2 -> x0, starting transfers between devices: 7.72 us -> none  [the longest x1 4.23 us: on_device(): lax.all_to_all(packed, 'head', split_axis=1, concat_axis=0, tiled=True)]
    unnamed x43 -> x22, local copies, waits for them, and re-layouts: 10.2 us -> 3.11 us
    select_n x0 -> x6, other arithmetic: none -> 4.49 us  [the longest x5 4.45 us: head_swap(): own = jnp.where(first, rows[:, :width], rows[:, width:])]
  transfers between devices with their start and end apart: 9 -> 13, of which waited for: 8 -> 7; matrix products, arithmetic and copies ran while one was open for 3% -> 12% of each run, Pallas kernels for 0% -> 0%
where the time goes in v1:
time: 118 us; the launch traced here: 117 us
  waiting for transfers between devices  37.1 us (31%)
  starting transfers between devices  36.7 us (31%)
  matrix products  25.3 us (21%)
  other arithmetic  12 us (10%)
  local copies, waits for them, and re-layouts  5.04 us (4%)
    ppermute x2, waiting for transfers between devices, inclusive_scan(): got = lax.ppermute(joined(carry, write), 'ctx', pairs)  21.6 us
    ppermute x1, starting transfers between devices, chain_states(): lax.ppermute(odd_state, 'ctx', [(i, i + 1) for i in range(0, size, 2)])  11.3 us
    ppermute x2, starting transfers between devices, inclusive_scan(): got = lax.ppermute(joined(carry, write), 'ctx', pairs)  8.99 us
    ppermute x1, waiting for transfers between devices, head_return(): got = lax.ppermute(sent, 'head', [(0, 1), (1, 0)])  8.06 us
    ppermute x5, starting transfers between devices, head_swap(): got = lax.ppermute(sent, 'head', [(0, 1), (1, 0)])  7.21 us
    ppermute x1, starting transfers between devices, inclusive_scan(): got = lax.ppermute(write, 'ctx', pairs)  5.4 us
    dot_general x5, matrix products, unit_lower_inverse(): jnp.matmul(jnp.concatenate([inverse, power], axis=-2), power, precision=L...  5.36 us
    dot_general x5, matrix products, compose(): jnp.matmul(later[0], earlier[1], precision=FULL_PRECISION) + later[1]  5.2 us
  transfers between devices with their start and end apart: 13, of which 7 were waited for; matrix products, arithmetic and copies ran while one was open for 12% of the time, Pallas kernels for 0%

profile of v1, /device:TPU:0, one launch (start us, length us, event | category | flops | bytes accessed | tf_op | source)
XLA Modules:
  0.0 116.8 jit_solution(12343497294714851394)
XLA Ops:
  0.0 1.0 broadcast_select_fusion.10
  1.0 3.0 %collective-permute-start = (bf16[128,512]{1,0:T(8,128)(2,1)S(1)}, bf16[128,512]{1,0:T(8,128)(2,1)S(1)}, u32[]{:S(2)}, u32[]{:S(2)}) collective-permute-start(bf16[128,512]{1,0:T(8,128)(2,1)S(1)} %get-tuple-element.24), channel_id=1, source_target_pairs={{0,1},{1,0},{2,3},{3,2},{4,5},{5,4},{6,7},{7,6},{8,9},{9,8},{10,11... | collective-permute-start | bytes 393224 | tf_op jit(solution)/shard_map/ppermute | solution.py:206
  5.8 2.0 %collective-permute-start.2 = (bf16[128,8]{0,1:T(8,128)(2,1)S(1)}, bf16[128,8]{0,1:T(8,128)(2,1)S(1)}, u32[]{:S(2)}, u32[]{:S(2)}) collective-permute-start(bf16[128,8]{0,1:T(8,128)(2,1)S(1)} %get-tuple-element.35), channel_id=1, source_target_pairs={{0,1},{1,0},{2,3},{3,2},{4,5},{5,4},{6,7},{7,6},{8,9},{9,8},{10,11... | collective-permute-start | bytes 6152 | tf_op jit(solution)/shard_map/ppermute | solution.py:206
  8.5 1.1 broadcast_select_fusion.5
  9.6 2.1 %collective-permute-start.4 = (bf16[128,1024]{1,0:T(8,128)(2,1)S(1)}, bf16[128,1024]{1,0:T(8,128)(2,1)S(1)}, u32[]{:S(2)}, u32[]{:S(2)}) collective-permute-start(bf16[128,1024]{1,0:T(8,128)(2,1)S(1)} %get-tuple-element.20), channel_id=1, source_target_pairs={{0,1},{1,0},{2,3},{3,2},{4,5},{5,4},{6,7},{7,6},{8,9},{9,8},{10,11... | collective-permute-start | bytes 786440 | tf_op jit(solution)/shard_map/ppermute | solution.py:206
  16.6 1.1 fusion
  19.3 1.0 slice_add_fusion.5
  20.3 1.1 fusion.4
  21.7 1.1 fusion.8
  23.0 1.1 fusion.12
  24.4 1.1 fusion.16
  26.2 1.2 %fusion.20 = f32[8,2,128,256]{3,2,1,0:T(8,128)S(1)} fusion(f32[8,2,128,128]{3,2,1,0:T(8,128)S(1)} %convolution_add_fusion, f32[8,2,128,128]{3,2,1,0:T(8,128)S(1)} %get-tuple-element.21, f32[8,2,128,128]{3,2,1,0:T(8,128)S(1)} %get-tuple-element.31), kind=kOutput, calls=%fused_computation.20 | convolution fusion | flops 403177472 | bytes 5242880 | tf_op jit(solution)/shard_map/dot_general | solution.py:86
  27.4 1.0 fusion.42
  28.5 1.1 convolution_subtract_fusion
  30.6 1.8 %fusion.50 = f32[8,128,128]{1,2,0:T(8,128)} fusion(f32[8,128,128]{2,1,0:T(8,128)S(1)} %fusion.49, f32[8,2,128,128]{3,2,1,0:T(8,128)S(1)} %convolution_subtract_fusion), kind=kOutput, calls=%fused_computation.98 | convolution fusion | flops 201326592 | bytes 1572864 | tf_op jit(solution)/shard_map/dot_general | solution.py:21
  33.2 2.0 %copy.126 = f32[8,1,128,128]{3,2,0,1:T(8,128)} copy(f32[8,1,128,128]{2,3,1,0:T(8,128)} %slice.207) | data formatting | bytes 1048576
  35.3 1.8 %convolution_add_fusion.5 = f32[8,128,128]{2,1,0:T(8,128)S(1)} fusion(f32[8,1,128,128]{3,2,0,1:T(8,128)} %copy.126, f32[8,2,128,128]{3,2,1,0:T(8,128)} %copy-done), kind=kOutput, calls=%fused_computation.42 | convolution fusion | flops 201457664 | bytes 1572864 | tf_op jit(solution)/shard_map/dot_general | solution.py:22
  37.1 2.2 %convolution_add_fusion.3 = f32[8,128,128]{1,2,0:T(8,128)S(1)} fusion(f32[8,128,128]{2,1,0:T(8,128)S(1)} %convolution_add_fusion.5, f32[8,2,128,128]{2,3,1,0:T(8,128)} %copy-done.6, f32[8,2,128,128]{3,2,1,0:T(8,128)} %copy-done), kind=kOutput, calls=%fused_computation.39 | convolution fusion | flops 201457664 | bytes 2097152 | tf_op jit(solution)/shard_map/dot_general | solution.py:22
  39.5 1.9 %collective-permute-done.5 = f32[4,128,256]{1,2,0:T(8,128)S(1)} collective-permute-done((f32[4,128,256]{1,2,0:T(8,128)S(1)}, f32[4,128,256]{1,2,0:T(8,128)S(1)}, u32[]{:S(2)}, u32[]{:S(2)}) %collective-permute-start.5) | collective-permute-done | bytes 524320 | tf_op jit(solution)/shard_map/ppermute | solution.py:174
  42.5 3.6 %collective-permute-start.6 = (f32[4,128,256]{1,2,0:T(8,128)S(1)}, f32[4,128,256]{1,2,0:T(8,128)S(1)}, u32[]{:S(2)}, u32[]{:S(2)}) collective-permute-start(f32[4,128,256]{1,2,0:T(8,128)S(1)} %pad_maximum_fusion.2), channel_id=1, source_target_pairs={{0,4},{2,6},{4,8},{6,10},{8,12},{10,14},{12,16},{14,18},{16,20},{1... | collective-permute-start | bytes 1572872 | tf_op jit(solution)/shard_map/ppermute | solution.py:153
  46.1 11.4 %collective-permute-done.6 = f32[4,128,256]{1,2,0:T(8,128)S(1)} collective-permute-done((f32[4,128,256]{1,2,0:T(8,128)S(1)}, f32[4,128,256]{1,2,0:T(8,128)S(1)}, u32[]{:S(2)}, u32[]{:S(2)}) %collective-permute-start.6) | collective-permute-done | bytes 524320 | tf_op jit(solution)/shard_map/ppermute | solution.py:153
  58.4 5.4 %collective-permute-start.7 = (f32[4,128,256]{1,2,0:T(8,128)S(1)}, f32[4,128,256]{1,2,0:T(8,128)S(1)}, u32[]{:S(2)}, u32[]{:S(2)}) collective-permute-start(f32[4,128,256]{1,2,0:T(8,128)S(1)} %pad_maximum_fusion.3), channel_id=1, source_target_pairs={{0,8},{2,10},{4,12},{6,14},{8,16},{10,18},{12,20},{14,22},{16,24},... | collective-permute-start | bytes 1572872 | tf_op jit(solution)/shard_map/ppermute | solution.py:153
  64.2 10.2 %collective-permute-done.7 = f32[4,128,256]{1,2,0:T(8,128)S(1)} collective-permute-done((f32[4,128,256]{1,2,0:T(8,128)S(1)}, f32[4,128,256]{1,2,0:T(8,128)S(1)}, u32[]{:S(2)}, u32[]{:S(2)}) %collective-permute-start.7) | collective-permute-done | bytes 524320 | tf_op jit(solution)/shard_map/ppermute | solution.py:153
  74.8 5.4 %collective-permute-start.8 = (f32[4,128,128]{1,2,0:T(8,128)S(1)}, f32[4,128,128]{1,2,0:T(8,128)S(1)}, u32[]{:S(2)}, u32[]{:S(2)}) collective-permute-start(f32[4,128,128]{1,2,0:T(8,128)S(1)} %convolution_add_fusion.7), channel_id=1, source_target_pairs={{0,16},{2,18},{4,20},{6,22},{8,24},{10,26},{12,28},{14,30},{1,17},... | collective-permute-start | bytes 786440 | tf_op jit(solution)/shard_map/ppermute | solution.py:156
  81.4 2.9 %collective-permute-done.8 = f32[4,128,128]{1,2,0:T(8,128)S(1)} collective-permute-done((f32[4,128,128]{1,2,0:T(8,128)S(1)}, f32[4,128,128]{1,2,0:T(8,128)S(1)}, u32[]{:S(2)}, u32[]{:S(2)}) %collective-permute-start.8) | collective-permute-done | bytes 262176 | tf_op jit(solution)/shard_map/ppermute | solution.py:156
  85.0 2.5 %collective-permute-start.9 = (f32[4,128,128]{1,2,0:T(8,128)S(1)}, f32[4,128,128]{1,2,0:T(8,128)S(1)}, u32[]{:S(2)}, u32[]{:S(2)}) collective-permute-start(f32[4,128,128]{1,2,0:T(8,128)S(1)} %convolution_add_fusion.6), channel_id=1, source_target_pairs={{0,4},{4,8},{8,12},{12,16},{16,20},{20,24},{24,28},{1,5},{5,9},{9,... | collective-permute-start | bytes 786440 | tf_op jit(solution)/shard_map/ppermute | solution.py:182
  88.2 1.0 fusion.44
  89.2 2.1 %collective-permute-done.9 = f32[4,128,128]{1,2,0:T(8,128)S(1)} collective-permute-done((f32[4,128,128]{1,2,0:T(8,128)S(1)}, f32[4,128,128]{1,2,0:T(8,128)S(1)}, u32[]{:S(2)}, u32[]{:S(2)}) %collective-permute-start.9) | collective-permute-done | bytes 262176 | tf_op jit(solution)/shard_map/ppermute | solution.py:182
  92.0 11.3 %collective-permute-start.11 = (f32[8,128,128]{1,2,0:T(8,128)S(1)}, f32[8,128,128]{1,2,0:T(8,128)S(1)}, u32[]{:S(2)}, u32[]{:S(2)}) collective-permute-start(f32[8,128,128]{1,2,0:T(8,128)S(1)} %convolution_add_fusion.2), channel_id=1, source_target_pairs={{0,2},{4,6},{8,10},{12,14},{16,18},{20,22},{24,26},{28,30},{1,3},{... | collective-permute-start | bytes 1572872 | tf_op jit(solution)/shard_map/ppermute | solution.py:187
  104.8 1.1 fusion.25
  106.6 8.1 %collective-permute-done.12 = bf16[128,1024]{0,1:T(8,128)(2,1)S(1)} collective-permute-done((bf16[128,1024]{0,1:T(8,128)(2,1)S(1)}, bf16[128,1024]{0,1:T(8,128)(2,1)S(1)}, u32[]{:S(2)}, u32[]{:S(2)}) %collective-permute-start.12) | collective-permute-done | bytes 262176 | tf_op jit(solution)/shard_map/ppermute | solution.py:215
  115.7 1.1 fusion.39
  (98 shorter events, 21.2 us)
Async XLA Ops:
  1.0 11.7 %collective-permute-start = (bf16[128,512]{1,0:T(8,128)(2,1)S(1)}, bf16[128,512]{1,0:T(8,128)(2,1)S(1)}, u32[]{:S(2)}, u32[]{:S(2)}) collective-permute-start(bf16[128,512]{1,0:T(8,128)(2,1)S(1)} %get-tuple-element.24), channel_id=1, source_target_pairs={{0,1},{1,0},{2,3},{3,2},{4,5},{5,4},{6,7},{7,6},{8,9},{9,8},{10,11... | collective-permute-start | bytes 393224 | tf_op jit(solution)/shard_map/ppermute | solution.py:206
  5.0 8.4 %collective-permute-start.1 = (bf16[128,512]{1,0:T(8,128)(2,1)S(1)}, bf16[128,512]{1,0:T(8,128)(2,1)S(1)}, u32[]{:S(2)}, u32[]{:S(2)}) collective-permute-start(bf16[128,512]{1,0:T(8,128)(2,1)S(1)} %get-tuple-element.26), channel_id=1, source_target_pairs={{0,1},{1,0},{2,3},{3,2},{4,5},{5,4},{6,7},{7,6},{8,9},{9,8},{10,11... | collective-permute-start | bytes 393224 | tf_op jit(solution)/shard_map/ppermute | solution.py:206
  5.8 5.9 %collective-permute-start.2 = (bf16[128,8]{0,1:T(8,128)(2,1)S(1)}, bf16[128,8]{0,1:T(8,128)(2,1)S(1)}, u32[]{:S(2)}, u32[]{:S(2)}) collective-permute-start(bf16[128,8]{0,1:T(8,128)(2,1)S(1)} %get-tuple-element.35), channel_id=1, source_target_pairs={{0,1},{1,0},{2,3},{3,2},{4,5},{5,4},{6,7},{7,6},{8,9},{9,8},{10,11... | collective-permute-start | bytes 6152 | tf_op jit(solution)/shard_map/ppermute | solution.py:206
  8.5 4.0 %collective-permute-start.3 = (bf16[128,8]{0,1:T(8,128)(2,1)S(1)}, bf16[128,8]{0,1:T(8,128)(2,1)S(1)}, u32[]{:S(2)}, u32[]{:S(2)}) collective-permute-start(bf16[128,8]{0,1:T(8,128)(2,1)S(1)} %get-tuple-element.33), channel_id=1, source_target_pairs={{0,1},{1,0},{2,3},{3,2},{4,5},{5,4},{6,7},{7,6},{8,9},{9,8},{10,11... | collective-permute-start | bytes 6152 | tf_op jit(solution)/shard_map/ppermute | solution.py:206
  9.6 9.4 %collective-permute-start.4 = (bf16[128,1024]{1,0:T(8,128)(2,1)S(1)}, bf16[128,1024]{1,0:T(8,128)(2,1)S(1)}, u32[]{:S(2)}, u32[]{:S(2)}) collective-permute-start(bf16[128,1024]{1,0:T(8,128)(2,1)S(1)} %get-tuple-element.20), channel_id=1, source_target_pairs={{0,1},{1,0},{2,3},{3,2},{4,5},{5,4},{6,7},{7,6},{8,9},{9,8},{10,11... | collective-permute-start | bytes 786440 | tf_op jit(solution)/shard_map/ppermute | solution.py:206
  14.6 3.6 %copy-start.4 = (f32[4,2,128,128]{3,0,2,1:T(4,128)}, f32[4,2,128,128]{3,0,2,1:T(4,128)S(1)}, u32[]{:S(2)}) copy-start(f32[4,2,128,128]{3,0,2,1:T(4,128)S(1)} %get-tuple-element.39) | copy-start | bytes 1572868
  28.4 4.0 %copy-start.6 = (f32[8,2,128,128]{2,3,1,0:T(8,128)}, f32[8,2,128,128]{2,3,1,0:T(8,128)S(1)}, u32[]{:S(2)}) copy-start(f32[8,2,128,128]{2,3,1,0:T(8,128)S(1)} %fusion.42) | copy-start | bytes 3145732
  29.6 1.0 copy-start
  30.6 1.8 %copy-start.2 = (f32[8,128,128]{2,1,0:T(8,128)}, f32[8,128,128]{2,1,0:T(8,128)S(1)}, u32[]{:S(2)}) copy-start(f32[8,128,128]{2,1,0:T(8,128)S(1)} %fusion.49) | copy-start | bytes 1572868
  35.3 4.1 %copy-start.1 = (f32[8,128,128]{1,2,0:T(8,128)S(1)}, f32[8,128,128]{1,2,0:T(8,128)}, u32[]{:S(2)}) copy-start(f32[8,128,128]{1,2,0:T(8,128)} %fusion.50) | copy-start | bytes 1572868
  39.4 2.0 %collective-permute-start.5 = (f32[4,128,256]{1,2,0:T(8,128)S(1)}, f32[4,128,256]{1,2,0:T(8,128)S(1)}, u32[]{:S(2)}, u32[]{:S(2)}) collective-permute-start(f32[4,128,256]{1,2,0:T(8,128)S(1)} %broadcast_select_fusion.2), channel_id=1, source_target_pairs={{0,2},{2,0},{4,6},{6,4},{8,10},{10,8},{12,14},{14,12},{16,18},{18,... | collective-permute-start | bytes 1572872 | tf_op jit(solution)/shard_map/ppermute | solution.py:174
  42.5 21.3 %copy-start.5 = (f32[4,2,128,128]{3,0,2,1:T(4,128)S(1)}, f32[4,2,128,128]{3,0,2,1:T(4,128)}, u32[]{:S(2)}) copy-start(f32[4,2,128,128]{3,0,2,1:T(4,128)} %copy-done.4) | copy-start | bytes 1572868
  42.5 15.0 %collective-permute-start.6 = (f32[4,128,256]{1,2,0:T(8,128)S(1)}, f32[4,128,256]{1,2,0:T(8,128)S(1)}, u32[]{:S(2)}, u32[]{:S(2)}) collective-permute-start(f32[4,128,256]{1,2,0:T(8,128)S(1)} %pad_maximum_fusion.2), channel_id=1, source_target_pairs={{0,4},{2,6},{4,8},{6,10},{8,12},{10,14},{12,16},{14,18},{16,20},{1... | collective-permute-start | bytes 1572872 | tf_op jit(solution)/shard_map/ppermute | solution.py:153
  58.4 16.0 %collective-permute-start.7 = (f32[4,128,256]{1,2,0:T(8,128)S(1)}, f32[4,128,256]{1,2,0:T(8,128)S(1)}, u32[]{:S(2)}, u32[]{:S(2)}) collective-permute-start(f32[4,128,256]{1,2,0:T(8,128)S(1)} %pad_maximum_fusion.3), channel_id=1, source_target_pairs={{0,8},{2,10},{4,12},{6,14},{8,16},{10,18},{12,20},{14,22},{16,24},... | collective-permute-start | bytes 1572872 | tf_op jit(solution)/shard_map/ppermute | solution.py:153
  74.8 9.5 %collective-permute-start.8 = (f32[4,128,128]{1,2,0:T(8,128)S(1)}, f32[4,128,128]{1,2,0:T(8,128)S(1)}, u32[]{:S(2)}, u32[]{:S(2)}) collective-permute-start(f32[4,128,128]{1,2,0:T(8,128)S(1)} %convolution_add_fusion.7), channel_id=1, source_target_pairs={{0,16},{2,18},{4,20},{6,22},{8,24},{10,26},{12,28},{14,30},{1,17},... | collective-permute-start | bytes 786440 | tf_op jit(solution)/shard_map/ppermute | solution.py:156
  85.0 6.4 %collective-permute-start.9 = (f32[4,128,128]{1,2,0:T(8,128)S(1)}, f32[4,128,128]{1,2,0:T(8,128)S(1)}, u32[]{:S(2)}, u32[]{:S(2)}) collective-permute-start(f32[4,128,128]{1,2,0:T(8,128)S(1)} %convolution_add_fusion.6), channel_id=1, source_target_pairs={{0,4},{4,8},{8,12},{12,16},{16,20},{20,24},{24,28},{1,5},{5,9},{9,... | collective-permute-start | bytes 786440 | tf_op jit(solution)/shard_map/ppermute | solution.py:182
  87.5 3.9 %collective-permute-start.10 = (f32[4,128,128]{1,2,0:T(8,128)S(1)}, f32[4,128,128]{1,2,0:T(8,128)S(1)}, u32[]{:S(2)}, u32[]{:S(2)}) collective-permute-start(f32[4,128,128]{1,2,0:T(8,128)S(1)} %convolution_add_fusion.6), channel_id=1, source_target_pairs={{2,4},{6,8},{10,12},{14,16},{18,20},{22,24},{26,28},{3,5},{7,9},{1... | collective-permute-start | bytes 786440 | tf_op jit(solution)/shard_map/ppermute | solution.py:181
  89.2 14.1 %copy-start.3 = (f32[8,128,128]{2,1,0:T(8,128)S(1)}, f32[8,128,128]{2,1,0:T(8,128)}, u32[]{:S(2)}) copy-start(f32[8,128,128]{2,1,0:T(8,128)} %copy-done.2) | copy-start | bytes 1572868
  92.0 12.8 %collective-permute-start.11 = (f32[8,128,128]{1,2,0:T(8,128)S(1)}, f32[8,128,128]{1,2,0:T(8,128)S(1)}, u32[]{:S(2)}, u32[]{:S(2)}) collective-permute-start(f32[8,128,128]{1,2,0:T(8,128)S(1)} %convolution_add_fusion.2), channel_id=1, source_target_pairs={{0,2},{4,6},{8,10},{12,14},{16,18},{20,22},{24,26},{28,30},{1,3},{... | collective-permute-start | bytes 1572872 | tf_op jit(solution)/shard_map/ppermute | solution.py:187
  104.4 2.2 %copy-start.8 = (bf16[128]{0:T(256)(128)(2,1)S(1)}, bf16[128]{0:T(256)(128)(2,1)}, u32[]{:S(2)}) copy-start(bf16[128]{0:T(256)(128)(2,1)} %param.13) | copy-start | bytes 772
  106.0 8.7 %collective-permute-start.12 = (bf16[128,1024]{0,1:T(8,128)(2,1)S(1)}, bf16[128,1024]{0,1:T(8,128)(2,1)S(1)}, u32[]{:S(2)}, u32[]{:S(2)}) collective-permute-start(bf16[128,1024]{0,1:T(8,128)(2,1)S(1)} %bitcast.104), channel_id=1, source_target_pairs={{0,1},{1,0},{2,3},{3,2},{4,5},{5,4},{6,7},{7,6},{8,9},{9,8},{10,11... | collective-permute-start | bytes 786440 | tf_op jit(solution)/shard_map/ppermute | solution.py:215
  114.7 1.0 copy-start.7

commit v2 on v1

--- a/solution.py
+++ b/solution.py
@@ -144,48 +144,66 @@
     return jnp.concatenate([carry, write], axis=-1)
 
 
-def inclusive_scan(carry, write, size, stride):
+def split(both):
+    return (both[..., :DK], both[..., DK:])
+
+
+def exclusive_scan(carry, write, size, stride):
     count = size // stride
+    if count == 1:
+        return jnp.zeros_like(write)
+    rounds = 0
+    while 2 ** (rounds + 1) < count:
+        rounds += 1
     shift = 1
-    while shift < count:
+    for _ in range(rounds):
         pairs = [(i, i + shift * stride) for i in range(size - shift * stride)]
-        if 2 * shift < count:
-            got = lax.ppermute(joined(carry, write), "ctx", pairs)
-            carry, write = compose((got[..., :DK], got[..., DK:]), (carry, write))
-        else:
-            got = lax.ppermute(write, "ctx", pairs)
-            write = jnp.matmul(carry, got, precision=FULL_PRECISION) + write
+        got = lax.ppermute(joined(carry, write), "ctx", pairs)
+        carry, write = compose(split(got), (carry, write))
         shift *= 2
-    return write
+    near = [(i, i + stride) for i in range(size - stride)]
+    far = 2**rounds + 1
+    if far >= count:
+        return lax.ppermute(write, "ctx", near)
+    got_carry, got_write = split(lax.ppermute(joined(carry, write), "ctx", near))
+    far_write = lax.ppermute(
+        write, "ctx", [(i, i + far * stride) for i in range(size - far * stride)]
+    )
+    return jnp.matmul(got_carry, far_write, precision=FULL_PRECISION) + got_write
 
 
 def chain_states(block_carry, block_write):
     size = lax.axis_size("ctx")
-    head_count = block_carry.shape[0]
-    if size % 2 or head_count % 2:
-        write = inclusive_scan(block_carry, block_write, size, 1)
-        return lax.ppermute(write, "ctx", [(i, i + 1) for i in range(size - 1)])
-    half = head_count // 2
-    odd = lax.axis_index("ctx") % 2 == 1
-    both = joined(block_carry, block_write)
-    mine = jnp.where(odd, both[half:], both[:half])
-    other = jnp.where(odd, both[:half], both[half:])
-    swap = [(i, i ^ 1) for i in range(size)]
-    got = lax.ppermute(other, "ctx", swap)
-    earlier = jnp.where(odd, got, mine)
-    later = jnp.where(odd, mine, got)
-    pair_carry, pair_write = compose(
-        (earlier[..., :DK], earlier[..., DK:]), (later[..., :DK], later[..., DK:])
-    )
-    pair_write = inclusive_scan(pair_carry, pair_write, size, 2)
-    from_odd = lax.ppermute(pair_write, "ctx", [(i, i + 1) for i in range(1, size - 1, 2)])
-    from_even = lax.ppermute(pair_write, "ctx", [(i, i + 2) for i in range(0, size - 2, 2)])
-    even_state = jnp.concatenate([from_even, from_odd], axis=0)
-    odd_state = (
-        jnp.matmul(block_carry, even_state, precision=FULL_PRECISION) + block_write
-    )
-    odd_state = lax.ppermute(odd_state, "ctx", [(i, i + 1) for i in range(0, size, 2)])
-    return jnp.where(odd, odd_state, even_state)
+    me = lax.axis_index("ctx")
+    levels = 0
+    while size % 2 ** (levels + 1) == 0 and block_carry.shape[0] % 2 ** (levels + 1) == 0:
+        levels += 1
+    current = joined(block_carry, block_write)
+    saved = []
+    for level in range(levels):
+        stride = 2**level
+        upper = (me // stride) % 2 == 1
+        half = current.shape[0] // 2
+        mine = jnp.where(upper, current[half:], current[:half])
+        other = jnp.where(upper, current[:half], current[half:])
+        got = lax.ppermute(other, "ctx", [(i, i ^ stride) for i in range(size)])
+        earlier = jnp.where(upper, got, mine)
+        later = jnp.where(upper, mine, got)
+        saved.append((upper, earlier))
+        current = joined(*compose(split(earlier), split(later)))
+    state = exclusive_scan(*split(current), size, 2**levels)
+    for level in reversed(range(levels)):
+        stride = 2**level
+        upper, earlier = saved[level]
+        earlier_carry, earlier_write = split(earlier)
+        after = jnp.matmul(earlier_carry, state, precision=FULL_PRECISION) + earlier_write
+        mine = jnp.where(upper, after, state)
+        other = jnp.where(upper, state, after)
+        got = lax.ppermute(other, "ctx", [(i, i ^ stride) for i in range(size)])
+        state = jnp.where(
+            upper, jnp.concatenate([got, mine], axis=0), jnp.concatenate([mine, got], axis=0)
+        )
+    return state
 
 
 def gated_norm(core_rows, output_gate, norm_gain):

time: 118 us -> 92.9 us (0.79)
  starting transfers between devices: 36.7 us -> 19.2 us
  waiting for transfers between devices: 37.1 us -> 26.5 us
  other arithmetic: 12 us -> 16.1 us
  matrix products: 25.3 us -> 24.1 us
    ppermute x7, starting transfers between devices: 28.9 us -> 11.4 us  [the longest x6 6.87 us: chain_states(): got = lax.ppermute(other, 'ctx', [(i, i ^ stride) for i in range(size)])]
    ppermute x7, waiting for transfers between devices: 29 us -> 18.7 us  [the longest x6 17.3 us: chain_states(): got = lax.ppermute(other, 'ctx', [(i, i ^ stride) for i in range(size)])]
    select_n x2 -> x6, other arithmetic: 0.37 us -> 4.59 us  [the longest x3 2.93 us: chain_states(): later = jnp.where(upper, mine, got)]
    unnamed x22 -> x33, local copies, waits for them, and re-layouts: 3.11 us -> 3.83 us
    dot_general x5 -> x4, matrix products: 3.74 us -> 3.05 us  [compose(): jnp.matmul(later[0], earlier[0], precision=FULL_PRECISION)]
  transfers between devices with their start and end apart: 13 -> 13, of which waited for: 7 -> 8; matrix products, arithmetic and copies ran while one was open for 12% -> 15% of each run, Pallas kernels for 0% -> 0%
where the time goes in v2:
time: 92.9 us; the launch traced here: 92.5 us
  waiting for transfers between devices  26.5 us (29%)
  matrix products  24.1 us (26%)
  starting transfers between devices  19.2 us (21%)
  other arithmetic  16.1 us (17%)
  local copies, waits for them, and re-layouts  5.74 us (6%)
    ppermute x6, waiting for transfers between devices, chain_states(): got = lax.ppermute(other, 'ctx', [(i, i ^ stride) for i in range(size)])  17.3 us
    ppermute x1, waiting for transfers between devices, head_return(): got = lax.ppermute(sent, 'head', [(0, 1), (1, 0)])  7.84 us
    ppermute x5, starting transfers between devices, head_swap(): got = lax.ppermute(sent, 'head', [(0, 1), (1, 0)])  7.21 us
    ppermute x6, starting transfers between devices, chain_states(): got = lax.ppermute(other, 'ctx', [(i, i ^ stride) for i in range(size)])  6.87 us
    dot_general x5, matrix products, unit_lower_inverse(): jnp.matmul(jnp.concatenate([inverse, power], axis=-2), power, precision=L...  5.37 us
    dot_general x5, matrix products, compose(): jnp.matmul(later[0], earlier[1], precision=FULL_PRECISION) + later[1]  5.05 us
    ppermute x1, starting transfers between devices, exclusive_scan(): return lax.ppermute(write, 'ctx', near)  4.51 us
    select_n x5, other arithmetic, head_swap(): own = jnp.where(first, rows[:, :width], rows[:, width:])  4.45 us
  transfers between devices with their start and end apart: 13, of which 8 were waited for; matrix products, arithmetic and copies ran while one was open for 15% of the time, Pallas kernels for 0%

profile of v2, /device:TPU:0, one launch (start us, length us, event | category | flops | bytes accessed | tf_op | source)
XLA Modules:
  0.0 92.5 jit_solution(5749166084432973853)
XLA Ops:
  1.0 3.0 %collective-permute-start = (bf16[128,512]{1,0:T(8,128)(2,1)S(1)}, bf16[128,512]{1,0:T(8,128)(2,1)S(1)}, u32[]{:S(2)}, u32[]{:S(2)}) collective-permute-start(bf16[128,512]{1,0:T(8,128)(2,1)S(1)} %get-tuple-element.32), channel_id=1, source_target_pairs={{0,1},{1,0},{2,3},{3,2},{4,5},{5,4},{6,7},{7,6},{8,9},{9,8},{10,11... | collective-permute-start | bytes 393224 | tf_op jit(solution)/shard_map/ppermute | solution.py:224
  5.8 2.0 %collective-permute-start.2 = (bf16[128,8]{0,1:T(8,128)(2,1)S(1)}, bf16[128,8]{0,1:T(8,128)(2,1)S(1)}, u32[]{:S(2)}, u32[]{:S(2)}) collective-permute-start(bf16[128,8]{0,1:T(8,128)(2,1)S(1)} %get-tuple-element.45), channel_id=1, source_target_pairs={{0,1},{1,0},{2,3},{3,2},{4,5},{5,4},{6,7},{7,6},{8,9},{9,8},{10,11... | collective-permute-start | bytes 6152 | tf_op jit(solution)/shard_map/ppermute | solution.py:224
  8.5 1.1 %broadcast_select_fusion.5 = (bf16[128,1024]{1,0:T(8,128)(2,1)S(1)}, bf16[128,1024]{1,0:T(8,128)(2,1)S(1)}) fusion(pred[]{:T(512)S(6)} %eq.34, bf16[128,2048]{1,0:T(8,128)(2,1)} %param.9), kind=kLoop, calls=%fused_computation.125 | loop fusion | flops 262144 | bytes 1048577 | tf_op jit(solution)/shard_map/jit(_where)/select_n | solution.py:222
  9.6 2.1 %collective-permute-start.4 = (bf16[128,1024]{1,0:T(8,128)(2,1)S(1)}, bf16[128,1024]{1,0:T(8,128)(2,1)S(1)}, u32[]{:S(2)}, u32[]{:S(2)}) collective-permute-start(bf16[128,1024]{1,0:T(8,128)(2,1)S(1)} %get-tuple-element.24), channel_id=1, source_target_pairs={{0,1},{1,0},{2,3},{3,2},{4,5},{5,4},{6,7},{7,6},{8,9},{9,8},{10,11... | collective-permute-start | bytes 786440 | tf_op jit(solution)/shard_map/ppermute | solution.py:224
  16.6 1.1 %fusion = f32[8,2,256,128]{3,2,1,0:T(8,128)S(1)} fusion(f32[8,2,128,128]{3,2,1,0:T(8,128)S(1)} %fusion.99, f32[8,2,128,128]{3,2,1,0:T(8,128)S(1)} %get-tuple-element.17), kind=kOutput, calls=%fused_computation | convolution fusion | flops 403177472 | bytes 4194304 | tf_op jit(solution)/shard_map/dot_general | solution.py:58
  20.3 1.1 %fusion.4 = f32[8,2,256,128]{3,2,1,0:T(8,128)S(1)} fusion(f32[8,2,128,128]{3,2,1,0:T(8,128)S(1)} %get-tuple-element.12, f32[8,2,128,128]{3,2,1,0:T(8,128)S(1)} %get-tuple-element.11), kind=kOutput, calls=%fused_computation.4 | convolution fusion | flops 403177472 | bytes 4194304 | tf_op jit(solution)/shard_map/dot_general | solution.py:58
  21.6 1.1 %fusion.8 = f32[8,2,256,128]{3,2,1,0:T(8,128)S(1)} fusion(f32[8,2,128,128]{3,2,1,0:T(8,128)S(1)} %get-tuple-element.10, f32[8,2,128,128]{3,2,1,0:T(8,128)S(1)} %get-tuple-element.9), kind=kOutput, calls=%fused_computation.8 | convolution fusion | flops 403177472 | bytes 4194304 | tf_op jit(solution)/shard_map/dot_general | solution.py:58
  23.0 1.1 %fusion.12 = f32[8,2,256,128]{3,2,1,0:T(8,128)S(1)} fusion(f32[8,2,128,128]{3,2,1,0:T(8,128)S(1)} %get-tuple-element.8, f32[8,2,128,128]{3,2,1,0:T(8,128)S(1)} %get-tuple-element.7), kind=kOutput, calls=%fused_computation.12 | convolution fusion | flops 403177472 | bytes 4194304 | tf_op jit(solution)/shard_map/dot_general | solution.py:58
  24.3 1.1 %fusion.16 = f32[8,2,256,128]{3,2,1,0:T(8,128)S(1)} fusion(f32[8,2,128,128]{3,2,1,0:T(8,128)S(1)} %get-tuple-element.6, f32[8,2,128,128]{3,2,1,0:T(8,128)S(1)} %get-tuple-element.5), kind=kOutput, calls=%fused_computation.16 | convolution fusion | flops 403177472 | bytes 4194304 | tf_op jit(solution)/shard_map/dot_general | solution.py:58
  26.2 1.2 %fusion.20 = f32[8,2,128,256]{3,2,1,0:T(8,128)S(1)} fusion(f32[8,2,128,128]{3,2,1,0:T(8,128)S(1)} %convolution_add_fusion, f32[8,2,128,128]{3,2,1,0:T(8,128)S(1)} %get-tuple-element.25, f32[8,2,128,128]{3,2,1,0:T(8,128)S(1)} %get-tuple-element.41), kind=kOutput, calls=%fused_computation.20 | convolution fusion | flops 403177472 | bytes 5242880 | tf_op jit(solution)/shard_map/dot_general | solution.py:86
  28.4 1.1 %convolution_subtract_fusion = f32[8,2,128,128]{3,2,1,0:T(8,128)S(1)} fusion(f32[8,2,128,128]{3,2,1,0:T(8,128)S(1)} %get-tuple-element.26, f32[8,2,128,256]{3,2,1,0:T(8,128)S(1)} %fusion.20, f32[8,2]{1,0:T(8,128)S(1)} %copy.85, f32[128,128]{1,0:T(8,128)S(1)} %get-tuple-element.47), kind=kOutput, calls=%fused_computation.30 | convolution fusion | flops 201850880 | bytes 3215360 | tf_op jit(solution)/shard_map/hmck,hmcj->hmkj/dot_general | solution.py:91
  30.6 1.8 %fusion.57 = f32[8,128,128]{1,2,0:T(8,128)} fusion(f32[8,128,128]{2,1,0:T(8,128)S(1)} %fusion.56, f32[8,2,128,128]{3,2,1,0:T(8,128)S(1)} %convolution_subtract_fusion), kind=kOutput, calls=%fused_computation.106 | convolution fusion | flops 201326592 | bytes 1572864 | tf_op jit(solution)/shard_map/dot_general | solution.py:21
  33.2 2.0 %copy.128 = f32[8,1,128,128]{3,2,0,1:T(8,128)} copy(f32[8,1,128,128]{2,3,1,0:T(8,128)} %slice.248) | data formatting | bytes 1048576
  35.3 1.8 %convolution_add_fusion.4 = f32[8,128,128]{2,1,0:T(8,128)S(1)} fusion(f32[8,1,128,128]{3,2,0,1:T(8,128)} %copy.128, f32[8,2,128,128]{3,2,1,0:T(8,128)} %copy-done), kind=kOutput, calls=%fused_computation.41 | convolution fusion | flops 201457664 | bytes 1572864 | tf_op jit(solution)/shard_map/dot_general | solution.py:22
  37.1 2.4 %convolution_add_fusion.2 = f32[8,128,128]{1,2,0:T(8,128)S(1)} fusion(f32[8,128,128]{2,1,0:T(8,128)S(1)} %convolution_add_fusion.4, f32[8,2,128,128]{2,3,1,0:T(8,128)} %copy-done.9, f32[8,2,128,128]{3,2,1,0:T(8,128)} %copy-done), kind=kOutput, calls=%fused_computation.38 | convolution fusion | flops 201457664 | bytes 2097152 | tf_op jit(solution)/shard_map/dot_general | solution.py:22
  40.7 2.0 %collective-permute-done.5 = f32[4,128,256]{1,2,0:T(8,128)} collective-permute-done((f32[4,128,256]{1,2,0:T(8,128)}, f32[4,128,256]{1,2,0:T(8,128)}, u32[]{:S(2)}, u32[]{:S(2)}) %collective-permute-start.5) | collective-permute-done | bytes 524320 | tf_op jit(solution)/shard_map/ppermute | solution.py:189
  42.7 1.7 %broadcast_select_fusion.1 = (f32[4,128,256]{1,2,0:T(8,128)S(1)}, f32[4,128,256]{1,2,0:T(8,128)S(1)}) fusion(f32[4,128,256]{1,2,0:T(8,128)} %collective-permute-done.5, pred[]{:T(512)S(6)} %eq.36, f32[8,128,128]{1,2,0:T(8,128)} %copy-done.8, f32[8,128,128]{1,2,0:T(8,128)} %fusion.57), kind=kLoop, calls=%fused_computation.120 | loop fusion | flops 917504 | bytes 2621441 | tf_op jit(solution)/shard_map/jit(_where)/select_n | solution.py:191
  46.7 1.5 %collective-permute-start.6 = (f32[2,128,256]{1,2,0:T(8,128)}, f32[2,128,256]{1,2,0:T(8,128)}, u32[]{:S(2)}, u32[]{:S(2)}) collective-permute-start(f32[2,128,256]{1,2,0:T(8,128)} %broadcast_select_fusion.9), channel_id=1, source_target_pairs={{0,4},{2,6},{4,0},{6,2},{8,12},{10,14},{12,8},{14,10},{16,20},{18,... | collective-permute-start | bytes 786440 | tf_op jit(solution)/shard_map/ppermute | solution.py:189
  48.2 7.2 %collective-permute-done.6 = f32[2,128,256]{1,2,0:T(8,128)} collective-permute-done((f32[2,128,256]{1,2,0:T(8,128)}, f32[2,128,256]{1,2,0:T(8,128)}, u32[]{:S(2)}, u32[]{:S(2)}) %collective-permute-start.6) | collective-permute-done | bytes 262176 | tf_op jit(solution)/shard_map/ppermute | solution.py:189
  55.3 1.2 %broadcast_select_fusion.8 = (f32[2,128,256]{1,2,0:T(8,128)S(1)}, f32[2,128,256]{1,2,0:T(8,128)S(1)}) fusion(f32[2,128,256]{1,2,0:T(8,128)} %collective-permute-done.6, pred[]{:T(512)S(6)} %eq.37, f32[4,128,128]{1,2,0:T(8,128)} %copy-done.10, f32[4,128,128]{1,2,0:T(8,128)S(1)} %fusion.66), kind=kLoop, calls=%fused_computation.139 | loop fusion | flops 458752 | bytes 1310721 | tf_op jit(solution)/shard_map/jit(_where)/select_n | solution.py:191
  57.1 1.7 %collective-permute-start.7 = (f32[1,128,256]{1,2,0:T(8,128)S(1)}, f32[1,128,256]{1,2,0:T(8,128)S(1)}, u32[]{:S(2)}, u32[]{:S(2)}) collective-permute-start(f32[1,128,256]{1,2,0:T(8,128)S(1)} %broadcast_select_fusion.19), channel_id=1, source_target_pairs={{0,8},{2,10},{4,12},{6,14},{8,0},{10,2},{12,4},{14,6},{16,24},{18,... | collective-permute-start | bytes 393224 | tf_op jit(solution)/shard_map/ppermute | solution.py:189
  59.1 3.0 %collective-permute-done.7 = f32[1,128,256]{1,2,0:T(8,128)S(1)} collective-permute-done((f32[1,128,256]{1,2,0:T(8,128)S(1)}, f32[1,128,256]{1,2,0:T(8,128)S(1)}, u32[]{:S(2)}, u32[]{:S(2)}) %collective-permute-start.7) | collective-permute-done | bytes 131104 | tf_op jit(solution)/shard_map/ppermute | solution.py:189
  62.3 4.5 %collective-permute-start.8 = (f32[1,128,128]{1,2,0:T(8,128)S(1)}, f32[1,128,128]{1,2,0:T(8,128)S(1)}, u32[]{:S(2)}, u32[]{:S(2)}) collective-permute-start(f32[1,128,128]{1,2,0:T(8,128)S(1)} %fusion.27), channel_id=1, source_target_pairs={{0,16},{2,18},{4,20},{6,22},{8,24},{10,26},{12,28},{14,30},{1,17},... | collective-permute-start | bytes 196616 | tf_op jit(solution)/shard_map/ppermute | solution.py:167
  67.5 1.4 %collective-permute-done.8 = f32[1,128,128]{1,2,0:T(8,128)S(1)} collective-permute-done((f32[1,128,128]{1,2,0:T(8,128)S(1)}, f32[1,128,128]{1,2,0:T(8,128)S(1)}, u32[]{:S(2)}, u32[]{:S(2)}) %collective-permute-start.8) | collective-permute-done | bytes 65568 | tf_op jit(solution)/shard_map/ppermute | solution.py:167
  69.0 2.1 %collective-permute-start.9 = (f32[1,128,128]{1,2,0:T(8,128)S(1)}, f32[1,128,128]{1,2,0:T(8,128)S(1)}, u32[]{:S(2)}, u32[]{:S(2)}) collective-permute-start(f32[1,128,128]{1,2,0:T(8,128)S(1)} %get-tuple-element.35), channel_id=1, source_target_pairs={{0,8},{2,10},{4,12},{6,14},{8,0},{10,2},{12,4},{14,6},{16,24},{18,... | collective-permute-start | bytes 196616 | tf_op jit(solution)/shard_map/ppermute | solution.py:202
  72.1 1.3 %collective-permute-done.9 = f32[1,128,128]{1,2,0:T(8,128)S(1)} collective-permute-done((f32[1,128,128]{1,2,0:T(8,128)S(1)}, f32[1,128,128]{1,2,0:T(8,128)S(1)}, u32[]{:S(2)}, u32[]{:S(2)}) %collective-permute-start.9) | collective-permute-done | bytes 65568 | tf_op jit(solution)/shard_map/ppermute | solution.py:202
  73.6 1.6 %collective-permute-start.10 = (f32[2,128,128]{1,2,0:T(8,128)S(1)}, f32[2,128,128]{1,2,0:T(8,128)S(1)}, u32[]{:S(2)}, u32[]{:S(2)}) collective-permute-start(f32[2,128,128]{1,2,0:T(8,128)S(1)} %get-tuple-element.29), channel_id=1, source_target_pairs={{0,4},{2,6},{4,0},{6,2},{8,12},{10,14},{12,8},{14,10},{16,20},{18,... | collective-permute-start | bytes 393224 | tf_op jit(solution)/shard_map/ppermute | solution.py:202
  75.8 2.9 %collective-permute-done.10 = f32[2,128,128]{1,2,0:T(8,128)S(1)} collective-permute-done((f32[2,128,128]{1,2,0:T(8,128)S(1)}, f32[2,128,128]{1,2,0:T(8,128)S(1)}, u32[]{:S(2)}, u32[]{:S(2)}) %collective-permute-start.10) | collective-permute-done | bytes 131104 | tf_op jit(solution)/shard_map/ppermute | solution.py:202
  79.6 1.0 %collective-permute-done.11 = f32[4,128,128]{1,2,0:T(8,128)S(1)} collective-permute-done((f32[4,128,128]{1,2,0:T(8,128)S(1)}, f32[4,128,128]{1,2,0:T(8,128)S(1)}, u32[]{:S(2)}, u32[]{:S(2)}) %collective-permute-start.11) | collective-permute-done | bytes 262176 | tf_op jit(solution)/shard_map/ppermute | solution.py:202
  80.7 1.2 %fusion.25 = bf16[2,128,8,128]{1,3,2,0:T(8,128)(2,1)S(1)} fusion(f32[8,1,128,128]{2,3,0,1:T(8,128)S(1)} %fusion.26, f32[8,1,128,128]{2,3,0,1:T(8,128)S(1)} %slice_bitcast_fusion.5, f32[4,128,128]{1,2,0:T(8,128)S(1)} %get-tuple-element.22, f32[4,128,128]{1,2,0:T(8,128)S(1)} %collective-permute-done.11, pred[]{:T(512)S(6)} %eq.36, ...), kind=kOutput, calls=%fused_computation.37 | convolution fusion | flops 404094976 | bytes 3145729 | tf_op jit(solution)/shard_map/hmck,hkv->hmcv/dot_general | solution.py:135
  82.5 7.8 %collective-permute-done.12 = bf16[128,1024]{0,1:T(8,128)(2,1)S(1)} collective-permute-done((bf16[128,1024]{0,1:T(8,128)(2,1)S(1)}, bf16[128,1024]{0,1:T(8,128)(2,1)S(1)}, u32[]{:S(2)}, u32[]{:S(2)}) %collective-permute-start.12) | collective-permute-done | bytes 262176 | tf_op jit(solution)/shard_map/ppermute | solution.py:233
  91.4 1.1 %fusion.41 = bf16[128,2048]{1,0:T(8,128)(2,1)} fusion(bf16[128,2048]{1,0:T(8,128)(2,1)S(1)} %copy-done.13, f32[128,2048]{1,0:T(8,128)S(1)} %copy.106, f32[2048]{0:T(1024)S(1)} %broadcast_bitcast_fusion), kind=kLoop, calls=%fused_computation.74 | loop fusion | flops 2097152 | bytes 2105344 | tf_op jit(solution)/shard_map/convert_element_type | solution.py:216
  (110 shorter events, 24.6 us)
Async XLA Ops:
  1.0 11.8 %collective-permute-start = (bf16[128,512]{1,0:T(8,128)(2,1)S(1)}, bf16[128,512]{1,0:T(8,128)(2,1)S(1)}, u32[]{:S(2)}, u32[]{:S(2)}) collective-permute-start(bf16[128,512]{1,0:T(8,128)(2,1)S(1)} %get-tuple-element.32), channel_id=1, source_target_pairs={{0,1},{1,0},{2,3},{3,2},{4,5},{5,4},{6,7},{7,6},{8,9},{9,8},{10,11... | collective-permute-start | bytes 393224 | tf_op jit(solution)/shard_map/ppermute | solution.py:224
  5.0 8.4 %collective-permute-start.1 = (bf16[128,512]{1,0:T(8,128)(2,1)S(1)}, bf16[128,512]{1,0:T(8,128)(2,1)S(1)}, u32[]{:S(2)}, u32[]{:S(2)}) collective-permute-start(bf16[128,512]{1,0:T(8,128)(2,1)S(1)} %get-tuple-element.34), channel_id=1, source_target_pairs={{0,1},{1,0},{2,3},{3,2},{4,5},{5,4},{6,7},{7,6},{8,9},{9,8},{10,11... | collective-permute-start | bytes 393224 | tf_op jit(solution)/shard_map/ppermute | solution.py:224
  5.8 5.9 %collective-permute-start.2 = (bf16[128,8]{0,1:T(8,128)(2,1)S(1)}, bf16[128,8]{0,1:T(8,128)(2,1)S(1)}, u32[]{:S(2)}, u32[]{:S(2)}) collective-permute-start(bf16[128,8]{0,1:T(8,128)(2,1)S(1)} %get-tuple-element.45), channel_id=1, source_target_pairs={{0,1},{1,0},{2,3},{3,2},{4,5},{5,4},{6,7},{7,6},{8,9},{9,8},{10,11... | collective-permute-start | bytes 6152 | tf_op jit(solution)/shard_map/ppermute | solution.py:224
  8.5 4.0 %collective-permute-start.3 = (bf16[128,8]{0,1:T(8,128)(2,1)S(1)}, bf16[128,8]{0,1:T(8,128)(2,1)S(1)}, u32[]{:S(2)}, u32[]{:S(2)}) collective-permute-start(bf16[128,8]{0,1:T(8,128)(2,1)S(1)} %get-tuple-element.43), channel_id=1, source_target_pairs={{0,1},{1,0},{2,3},{3,2},{4,5},{5,4},{6,7},{7,6},{8,9},{9,8},{10,11... | collective-permute-start | bytes 6152 | tf_op jit(solution)/shard_map/ppermute | solution.py:224
  9.6 9.3 %collective-permute-start.4 = (bf16[128,1024]{1,0:T(8,128)(2,1)S(1)}, bf16[128,1024]{1,0:T(8,128)(2,1)S(1)}, u32[]{:S(2)}, u32[]{:S(2)}) collective-permute-start(bf16[128,1024]{1,0:T(8,128)(2,1)S(1)} %get-tuple-element.24), channel_id=1, source_target_pairs={{0,1},{1,0},{2,3},{3,2},{4,5},{5,4},{6,7},{7,6},{8,9},{9,8},{10,11... | collective-permute-start | bytes 786440 | tf_op jit(solution)/shard_map/ppermute | solution.py:224
  14.6 3.6 %copy-start.3 = (f32[4,2,128,128]{3,0,2,1:T(4,128)}, f32[4,2,128,128]{3,0,2,1:T(4,128)S(1)}, u32[]{:S(2)}) copy-start(f32[4,2,128,128]{3,0,2,1:T(4,128)S(1)} %get-tuple-element.49) | copy-start | bytes 1572868
  28.4 4.0 %copy-start.9 = (f32[8,2,128,128]{2,3,1,0:T(8,128)}, f32[8,2,128,128]{2,3,1,0:T(8,128)S(1)}, u32[]{:S(2)}) copy-start(f32[8,2,128,128]{2,3,1,0:T(8,128)S(1)} %fusion.44) | copy-start | bytes 3145732
  29.6 1.0 %copy-start = (f32[8,2,128,128]{3,2,1,0:T(8,128)}, f32[8,2,128,128]{3,2,1,0:T(8,128)S(1)}, u32[]{:S(2)}) copy-start(f32[8,2,128,128]{3,2,1,0:T(8,128)S(1)} %convolution_subtract_fusion) | copy-start | bytes 3145732
  30.6 1.8 %copy-start.1 = (f32[8,128,128]{2,1,0:T(8,128)}, f32[8,128,128]{2,1,0:T(8,128)S(1)}, u32[]{:S(2)}) copy-start(f32[8,128,128]{2,1,0:T(8,128)S(1)} %fusion.56) | copy-start | bytes 1572868
  35.3 4.2 %copy-start.5 = (f32[8,128,128]{1,2,0:T(8,128)S(1)}, f32[8,128,128]{1,2,0:T(8,128)}, u32[]{:S(2)}) copy-start(f32[8,128,128]{1,2,0:T(8,128)} %fusion.57) | copy-start | bytes 1572868
  37.1 3.4 %copy-start.6 = (f32[8,128,128]{2,1,0:T(8,128)}, f32[8,128,128]{2,1,0:T(8,128)S(1)}, u32[]{:S(2)}) copy-start(f32[8,128,128]{2,1,0:T(8,128)S(1)} %convolution_add_fusion.4) | copy-start | bytes 1572868
  39.5 1.0 %copy-start.8 = (f32[8,128,128]{1,2,0:T(8,128)}, f32[8,128,128]{1,2,0:T(8,128)S(1)}, u32[]{:S(2)}) copy-start(f32[8,128,128]{1,2,0:T(8,128)S(1)} %convolution_add_fusion.2) | copy-start | bytes 1572868
  40.5 2.3 %collective-permute-start.5 = (f32[4,128,256]{1,2,0:T(8,128)}, f32[4,128,256]{1,2,0:T(8,128)}, u32[]{:S(2)}, u32[]{:S(2)}) collective-permute-start(f32[4,128,256]{1,2,0:T(8,128)} %broadcast_select_fusion.2), channel_id=1, source_target_pairs={{0,2},{2,0},{4,6},{6,4},{8,10},{10,8},{12,14},{14,12},{16,18},{18,... | collective-permute-start | bytes 1572872 | tf_op jit(solution)/shard_map/ppermute | solution.py:189
  44.5 2.2 %copy-start.11 = (f32[4,128,256]{1,2,0:T(8,128)}, f32[4,128,256]{1,2,0:T(8,128)S(1)}, u32[]{:S(2)}) copy-start(f32[4,128,256]{1,2,0:T(8,128)S(1)} %get-tuple-element.14) | copy-start | bytes 1572868
  45.2 0.7 copy-start.10
  46.7 8.7 %collective-permute-start.6 = (f32[2,128,256]{1,2,0:T(8,128)}, f32[2,128,256]{1,2,0:T(8,128)}, u32[]{:S(2)}, u32[]{:S(2)}) collective-permute-start(f32[2,128,256]{1,2,0:T(8,128)} %broadcast_select_fusion.9), channel_id=1, source_target_pairs={{0,4},{2,6},{4,0},{6,2},{8,12},{10,14},{12,8},{14,10},{16,20},{18,... | collective-permute-start | bytes 786440 | tf_op jit(solution)/shard_map/ppermute | solution.py:189
  48.2 10.6 %copy-start.4 = (f32[4,2,128,128]{3,0,2,1:T(4,128)S(1)}, f32[4,2,128,128]{3,0,2,1:T(4,128)}, u32[]{:S(2)}) copy-start(f32[4,2,128,128]{3,0,2,1:T(4,128)} %copy-done.3) | copy-start | bytes 1572868
  57.1 5.0 %collective-permute-start.7 = (f32[1,128,256]{1,2,0:T(8,128)S(1)}, f32[1,128,256]{1,2,0:T(8,128)S(1)}, u32[]{:S(2)}, u32[]{:S(2)}) collective-permute-start(f32[1,128,256]{1,2,0:T(8,128)S(1)} %broadcast_select_fusion.19), channel_id=1, source_target_pairs={{0,8},{2,10},{4,12},{6,14},{8,0},{10,2},{12,4},{14,6},{16,24},{18,... | collective-permute-start | bytes 393224 | tf_op jit(solution)/shard_map/ppermute | solution.py:189
  62.3 6.5 %collective-permute-start.8 = (f32[1,128,128]{1,2,0:T(8,128)S(1)}, f32[1,128,128]{1,2,0:T(8,128)S(1)}, u32[]{:S(2)}, u32[]{:S(2)}) collective-permute-start(f32[1,128,128]{1,2,0:T(8,128)S(1)} %fusion.27), channel_id=1, source_target_pairs={{0,16},{2,18},{4,20},{6,22},{8,24},{10,26},{12,28},{14,30},{1,17},... | collective-permute-start | bytes 196616 | tf_op jit(solution)/shard_map/ppermute | solution.py:167
  67.5 7.8 %copy-start.7 = (f32[8,128,128]{2,1,0:T(8,128)S(1)}, f32[8,128,128]{2,1,0:T(8,128)}, u32[]{:S(2)}) copy-start(f32[8,128,128]{2,1,0:T(8,128)} %copy-done.6) | copy-start | bytes 1572868
  69.0 4.3 %collective-permute-start.9 = (f32[1,128,128]{1,2,0:T(8,128)S(1)}, f32[1,128,128]{1,2,0:T(8,128)S(1)}, u32[]{:S(2)}, u32[]{:S(2)}) collective-permute-start(f32[1,128,128]{1,2,0:T(8,128)S(1)} %get-tuple-element.35), channel_id=1, source_target_pairs={{0,8},{2,10},{4,12},{6,14},{8,0},{10,2},{12,4},{14,6},{16,24},{18,... | collective-permute-start | bytes 196616 | tf_op jit(solution)/shard_map/ppermute | solution.py:202
  72.1 6.6 %copy-start.12 = (f32[4,128,256]{1,2,0:T(8,128)S(1)}, f32[4,128,256]{1,2,0:T(8,128)}, u32[]{:S(2)}) copy-start(f32[4,128,256]{1,2,0:T(8,128)} %copy-done.11) | copy-start | bytes 1572868
  73.4 5.8 %copy-start.2 = (f32[8,128,128]{2,1,0:T(8,128)S(1)}, f32[8,128,128]{2,1,0:T(8,128)}, u32[]{:S(2)}) copy-start(f32[8,128,128]{2,1,0:T(8,128)} %copy-done.1) | copy-start | bytes 1572868
  73.6 5.0 %collective-permute-start.10 = (f32[2,128,128]{1,2,0:T(8,128)S(1)}, f32[2,128,128]{1,2,0:T(8,128)S(1)}, u32[]{:S(2)}, u32[]{:S(2)}) collective-permute-start(f32[2,128,128]{1,2,0:T(8,128)S(1)} %get-tuple-element.29), channel_id=1, source_target_pairs={{0,4},{2,6},{4,0},{6,2},{8,12},{10,14},{12,8},{14,10},{16,20},{18,... | collective-permute-start | bytes 393224 | tf_op jit(solution)/shard_map/ppermute | solution.py:202
  79.1 1.6 %collective-permute-start.11 = (f32[4,128,128]{1,2,0:T(8,128)S(1)}, f32[4,128,128]{1,2,0:T(8,128)S(1)}, u32[]{:S(2)}, u32[]{:S(2)}) collective-permute-start(f32[4,128,128]{1,2,0:T(8,128)S(1)} %get-tuple-element.21), channel_id=1, source_target_pairs={{0,2},{2,0},{4,6},{6,4},{8,10},{10,8},{12,14},{14,12},{16,18},{18,... | collective-permute-start | bytes 786440 | tf_op jit(solution)/shard_map/ppermute | solution.py:202
  80.7 1.8 %copy-start.14 = (bf16[128]{0:T(256)(128)(2,1)S(1)}, bf16[128]{0:T(256)(128)(2,1)}, u32[]{:S(2)}) copy-start(bf16[128]{0:T(256)(128)(2,1)} %param.13) | copy-start | bytes 772
  81.9 8.4 %collective-permute-start.12 = (bf16[128,1024]{0,1:T(8,128)(2,1)S(1)}, bf16[128,1024]{0,1:T(8,128)(2,1)S(1)}, u32[]{:S(2)}, u32[]{:S(2)}) collective-permute-start(bf16[128,1024]{0,1:T(8,128)(2,1)S(1)} %bitcast.120), channel_id=1, source_target_pairs={{0,1},{1,0},{2,3},{3,2},{4,5},{5,4},{6,7},{7,6},{8,9},{9,8},{10,11... | collective-permute-start | bytes 786440 | tf_op jit(solution)/shard_map/ppermute | solution.py:233
  90.3 1.0 %copy-start.13 = (bf16[128,2048]{1,0:T(8,128)(2,1)S(1)}, bf16[128,2048]{1,0:T(8,128)(2,1)}, u32[]{:S(2)}) copy-start(bf16[128,2048]{1,0:T(8,128)(2,1)} %param.10) | copy-start | bytes 1572868

commit v3 on v2

--- a/solution.py
+++ b/solution.py
@@ -184,8 +184,9 @@
         stride = 2**level
         upper = (me // stride) % 2 == 1
         half = current.shape[0] // 2
-        mine = jnp.where(upper, current[half:], current[:half])
-        other = jnp.where(upper, current[:half], current[half:])
+        bit = (me // stride) % 2
+        mine = lax.dynamic_slice_in_dim(current, bit * half, half, 0)
+        other = lax.dynamic_slice_in_dim(current, (1 - bit) * half, half, 0)
         got = lax.ppermute(other, "ctx", [(i, i ^ stride) for i in range(size)])
         earlier = jnp.where(upper, got, mine)
         later = jnp.where(upper, mine, got)
@@ -216,13 +217,20 @@
     return gated_rows.reshape(token_count, head_count * DV).astype(jnp.bfloat16)
 
 
-def head_swap(rows):
-    width = rows.shape[1] // 2
-    first = lax.axis_index("head") == 0
-    own = jnp.where(first, rows[:, :width], rows[:, width:])
-    sent = jnp.where(first, rows[:, width:], rows[:, :width])
+def head_swap(pieces_in):
+    half = lax.axis_index("head")
+    widths = [part.shape[1] // 2 for part in pieces_in]
+    own = jnp.concatenate(
+        [lax.dynamic_slice_in_dim(p, half * w, w, 1) for p, w in zip(pieces_in, widths)], axis=1
+    )
+    sent = jnp.concatenate(
+        [lax.dynamic_slice_in_dim(p, (1 - half) * w, w, 1) for p, w in zip(pieces_in, widths)],
+        axis=1,
+    )
     got = lax.ppermute(sent, "head", [(0, 1), (1, 0)])
-    return jnp.where(first, jnp.concatenate([own, got], 0), jnp.concatenate([got, own], 0))
+    rows = jnp.where(half == 0, jnp.concatenate([own, got], 0), jnp.concatenate([got, own], 0))
+    ends = [sum(widths[: i + 1]) for i in range(len(widths))]
+    return [rows[:, end - w : end] for end, w in zip(ends, widths)]
 
 
 def head_return(rows):
@@ -237,7 +245,8 @@
 def head_inputs(pieces_in):
     parts = lax.axis_size("head")
     if parts == 2:
-        return [head_swap(part) for part in pieces_in]
+        wide = head_swap(pieces_in[:3])
+        return wide + head_swap(pieces_in[3:])
     tokens = pieces_in[0].shape[0]
     widths = [part.shape[1] // parts for part in pieces_in]
     packed = jnp.concatenate(

time: 92.9 us -> 103 us (1.11)
  waiting for transfers between devices: 26.5 us -> 36.3 us
  local copies, waits for them, and re-layouts: 5.74 us -> 11.9 us
  other arithmetic: 16.1 us -> 13 us
  starting transfers between devices: 19.2 us -> 16.6 us
    ppermute x5 -> x2, waiting for transfers between devices: 0.01 us -> 11.8 us  [head_swap(): got = lax.ppermute(sent, 'head', [(0, 1), (1, 0)])]
    select_n x8 -> x2, other arithmetic: 6.11 us -> 0.28 us  [head_swap(): jnp.where(half == 0, jnp.concatenate([own, got], 0), jnp.concatenate([got...]
    ppermute x5 -> x2, starting transfers between devices: 7.21 us -> 3.15 us  [head_swap(): got = lax.ppermute(sent, 'head', [(0, 1), (1, 0)])]
    concatenate x0 -> x5, other arithmetic: none -> 2.26 us  [the longest x3 2.21 us: joined(): return jnp.concatenate([carry, write], axis=-1)]
    dynamic_slice x0 -> x3, local copies, waits for them, and re-layouts: none -> 2.23 us  [head_swap(): lax.dynamic_slice_in_dim(p, half * w, w, 1)]
    unnamed x33 -> x41, local copies, waits for them, and re-layouts: 3.83 us -> 5.65 us
    reshape x0 -> x2, local copies, waits for them, and re-layouts: none -> 1.39 us  [the longest x1 1.21 us: arrange_query(): query_part.astype(jnp.float32).reshape(blocks, SPAN, key_heads, DK)]
    ppermute x6, waiting for transfers between devices: 17.3 us -> 16.3 us  [chain_states(): got = lax.ppermute(other, 'ctx', [(i, i ^ stride) for i in range(size)])]
  transfers between devices with their start and end apart: 13 -> 10, of which waited for: 8 -> 9; matrix products, arithmetic and copies ran while one was open for 15% -> 5% of each run, Pallas kernels for 0% -> 0%
where the time goes in v3:
time: 103 us
  waiting for transfers between devices  36.3 us (35%)
  matrix products  24.3 us (24%)
  starting transfers between devices  16.6 us (16%)
  other arithmetic  13 us (13%)
  local copies, waits for them, and re-layouts  11.9 us (12%)
    ppermute x6, waiting for transfers between devices, chain_states(): got = lax.ppermute(other, 'ctx', [(i, i ^ stride) for i in range(size)])  16.3 us
    ppermute x2, waiting for transfers between devices, head_swap(): got = lax.ppermute(sent, 'head', [(0, 1), (1, 0)])  11.8 us
    ppermute x6, starting transfers between devices, chain_states(): got = lax.ppermute(other, 'ctx', [(i, i ^ stride) for i in range(size)])  7.19 us
    ppermute x1, waiting for transfers between devices, head_return(): got = lax.ppermute(sent, 'head', [(0, 1), (1, 0)])  6.82 us
    unnamed x41, local copies, waits for them, and re-layouts  5.65 us
    dot_general x5, matrix products, unit_lower_inverse(): jnp.matmul(jnp.concatenate([inverse, power], axis=-2), power, precision=L...  5.37 us
    dot_general x5, matrix products, compose(): jnp.matmul(later[0], earlier[1], precision=FULL_PRECISION) + later[1]  5.11 us
    ppermute x1, starting transfers between devices, exclusive_scan(): return lax.ppermute(write, 'ctx', near)  4.72 us
  transfers between devices with their start and end apart: 10, of which 9 were waited for; matrix products, arithmetic and copies ran while one was open for 5% of the time, Pallas kernels for 0%

profile of v3, /device:TPU:0, one launch (start us, length us, event | category | flops | bytes accessed | tf_op | source)
XLA Modules:
  0.0 102.8 jit_solution(3444738453277561958)
XLA Ops:
  0.0 1.1 %constant_dynamic-slice_fusion.7 = (bf16[128,1024]{1,0:T(8,128)(2,1)S(1)}, bf16[128,1024]{1,0:T(8,128)(2,1)S(1)}) fusion(bf16[128,2048]{1,0:T(8,128)(2,1)} %param.9, s32[]{:T(128)S(6)} %select_n.218, s32[]{:T(128)S(6)} %select_n.220), kind=kLoop, calls=%fused_computation.177 | loop fusion | bytes 1048584 | tf_op jit(solution)/shard_map/dynamic_slice | solution.py:224
  1.1 1.1 %constant_dynamic-slice_fusion.8 = (bf16[128,512]{1,0:T(8,128)(2,1)S(1)}, bf16[128,512]{1,0:T(8,128)(2,1)S(1)}, bf16[128,512]{1,0:T(8,128)(2,1)S(1)}, bf16[128,512]{1,0:T(8,128)(2,1)S(1)}) fusion(bf16[128,1024]{1,0:T(8,128)(2,1)} %param.8, s32[]{:T(128)S(6)} %select_n.217, s32[]{:T(128)S(6)} %select_n.219, bf16[128,1024]{1,0:T(8,128)(2,1)} %param.7), kind=kLoop, calls=%fused_computation.178 | loop fusion | bytes 1048584 | tf_op jit(solution)/shard_map/dynamic_slice | solution.py:224
  2.3 3.0 %collective-permute-start = (bf16[128,2048]{1,0:T(8,128)(2,1)S(1)}, bf16[128,2048]{1,0:T(8,128)(2,1)S(1)}, u32[]{:S(2)}, u32[]{:S(2)}) collective-permute-start(bf16[128,2048]{1,0:T(8,128)(2,1)S(1)} %pad_maximum_fusion.1), channel_id=1, source_target_pairs={{0,1},{1,0},{2,3},{3,2},{4,5},{5,4},{6,7},{7,6},{8,9},{9,8},{10,11... | collective-permute-start | bytes 1572872 | tf_op jit(solution)/shard_map/ppermute | solution.py:230
  5.5 11.8 %collective-permute-done.1 = bf16[128,16]{0,1:T(8,128)(2,1)S(1)} collective-permute-done((bf16[128,16]{0,1:T(8,128)(2,1)S(1)}, bf16[128,16]{0,1:T(8,128)(2,1)S(1)}, u32[]{:S(2)}, u32[]{:S(2)}) %collective-permute-start.1) | collective-permute-done | bytes 4128 | tf_op jit(solution)/shard_map/ppermute | solution.py:230
  21.2 1.2 %reshape.116 = f32[2,128,4,128]{3,2,1,0:T(4,128)S(1)} reshape(f32[256,512]{1,0:T(8,128)} %get-tuple-element.15) | data formatting | bytes 1048576 | tf_op jit(solution)/shard_map/reshape | solution.py:48
  25.3 1.1 %fusion = f32[8,2,256,128]{3,2,1,0:T(8,128)S(1)} fusion(f32[8,2,128,128]{3,2,1,0:T(8,128)S(1)} %fusion.99, f32[8,2,128,128]{3,2,1,0:T(8,128)S(1)} %get-tuple-element.19), kind=kOutput, calls=%fused_computation | convolution fusion | flops 403177472 | bytes 4194304 | tf_op jit(solution)/shard_map/dot_general | solution.py:58
  27.4 1.1 %fusion.4 = f32[8,2,256,128]{3,2,1,0:T(8,128)S(1)} fusion(f32[8,2,128,128]{3,2,1,0:T(8,128)S(1)} %get-tuple-element.12, f32[8,2,128,128]{3,2,1,0:T(8,128)S(1)} %get-tuple-element.11), kind=kOutput, calls=%fused_computation.4 | convolution fusion | flops 403177472 | bytes 4194304 | tf_op jit(solution)/shard_map/dot_general | solution.py:58
  33.9 1.2 %fusion.20 = f32[8,2,128,256]{3,2,1,0:T(8,128)S(1)} fusion(f32[8,2,128,128]{3,2,1,0:T(8,128)S(1)} %convolution_add_fusion, f32[8,2,128,128]{3,2,1,0:T(8,128)S(1)} %get-tuple-element.25, f32[8,2,128,128]{3,2,1,0:T(8,128)S(1)} %get-tuple-element.43), kind=kOutput, calls=%fused_computation.20 | convolution fusion | flops 403177472 | bytes 5242880 | tf_op jit(solution)/shard_map/dot_general | solution.py:86
  36.1 1.1 %convolution_subtract_fusion = f32[8,2,128,128]{3,2,1,0:T(8,128)S(1)} fusion(f32[8,2,128,128]{3,2,1,0:T(8,128)S(1)} %get-tuple-element.26, f32[8,2,128,256]{3,2,1,0:T(8,128)S(1)} %fusion.20, f32[8,2]{1,0:T(8,128)S(1)} %copy.85, f32[128,128]{1,0:T(8,128)S(1)} %get-tuple-element.53), kind=kOutput, calls=%fused_computation.30 | convolution fusion | flops 201850880 | bytes 3215360 | tf_op jit(solution)/shard_map/hmck,hmcj->hmkj/dot_general | solution.py:91
  38.2 1.4 %fusion.57 = f32[8,128,128]{2,1,0:T(8,128)} fusion(f32[8,2,128,128]{3,2,1,0:T(8,128)S(1)} %convolution_subtract_fusion, f32[128,128]{1,0:T(8,128)S(1)} %get-tuple-element.53), kind=kOutput, calls=%fused_computation.110 | convolution fusion | flops 201326592 | bytes 1114112 | tf_op jit(solution)/shard_map/dot_general | solution.py:21
  40.4 2.0 %copy.128 = f32[8,1,128,128]{3,2,0,1:T(8,128)} copy(f32[8,1,128,128]{2,3,1,0:T(8,128)} %slice.193) | data formatting | bytes 1048576
  42.5 1.9 %convolution_add_fusion.4 = f32[8,128,128]{2,1,0:T(8,128)S(1)} fusion(f32[8,1,128,128]{3,2,0,1:T(8,128)} %copy.128, f32[8,2,128,128]{3,2,1,0:T(8,128)} %copy-done), kind=kOutput, calls=%fused_computation.45 | convolution fusion | flops 201457664 | bytes 1572864 | tf_op jit(solution)/shard_map/dot_general | solution.py:22
  44.4 2.4 %convolution_add_fusion.2 = f32[8,128,128]{1,2,0:T(8,128)S(1)} fusion(f32[8,128,128]{2,1,0:T(8,128)S(1)} %convolution_add_fusion.4, f32[8,2,128,128]{2,3,1,0:T(8,128)} %copy-done.9, f32[8,2,128,128]{3,2,1,0:T(8,128)} %copy-done), kind=kOutput, calls=%fused_computation.42 | convolution fusion | flops 201457664 | bytes 2097152 | tf_op jit(solution)/shard_map/dot_general | solution.py:22
  46.8 1.2 %fusion.58 = f32[8,128,128]{1,2,0:T(8,128)S(1)} fusion(f32[8,128,128]{2,1,0:T(8,128)S(1)} %copy-done.2, f32[8,2,128,128]{3,2,1,0:T(8,128)S(1)} %copy-done.1), kind=kOutput, calls=%fused_computation.111 | convolution fusion | flops 201326592 | bytes 1572864 | tf_op jit(solution)/shard_map/dot_general | solution.py:21
  49.7 2.2 %collective-permute-done.2 = f32[4,128,256]{1,2,0:T(8,128)} collective-permute-done((f32[4,128,256]{1,2,0:T(8,128)}, f32[4,128,256]{1,2,0:T(8,128)}, u32[]{:S(2)}, u32[]{:S(2)}) %collective-permute-start.2) | collective-permute-done | bytes 524320 | tf_op jit(solution)/shard_map/ppermute | solution.py:190
  51.9 1.4 %broadcast_select_fusion.1 = (f32[4,128,256]{1,2,0:T(8,128)S(1)}, f32[4,128,256]{1,2,0:T(8,128)S(1)}) fusion(f32[4,128,256]{1,2,0:T(8,128)} %collective-permute-done.2, pred[]{:T(512)S(6)} %eq.36, s32[]{:T(128)S(6)} %select_n.242, f32[8,128,128]{1,2,0:T(8,128)} %copy-done.6, f32[8,128,128]{1,2,0:T(8,128)} %copy-done.4), kind=kLoop, calls=%fused_computation.125 | loop fusion | flops 524288 | bytes 2621445 | tf_op jit(solution)/shard_map/jit(_where)/select_n | solution.py:192
  55.6 1.7 %collective-permute-start.3 = (f32[2,128,256]{1,2,0:T(8,128)}, f32[2,128,256]{1,2,0:T(8,128)}, u32[]{:S(2)}, u32[]{:S(2)}) collective-permute-start(f32[2,128,256]{1,2,0:T(8,128)} %fusion.59), channel_id=1, source_target_pairs={{0,4},{2,6},{4,0},{6,2},{8,12},{10,14},{12,8},{14,10},{16,20},{18,... | collective-permute-start | bytes 786440 | tf_op jit(solution)/shard_map/ppermute | solution.py:190
  57.3 6.9 %collective-permute-done.3 = f32[2,128,256]{1,2,0:T(8,128)} collective-permute-done((f32[2,128,256]{1,2,0:T(8,128)}, f32[2,128,256]{1,2,0:T(8,128)}, u32[]{:S(2)}, u32[]{:S(2)}) %collective-permute-start.3) | collective-permute-done | bytes 262176 | tf_op jit(solution)/shard_map/ppermute | solution.py:190
  64.2 1.1 %broadcast_select_fusion.4 = (f32[2,128,256]{1,2,0:T(8,128)S(1)}, f32[2,128,256]{1,2,0:T(8,128)S(1)}) fusion(f32[2,128,256]{1,2,0:T(8,128)} %collective-permute-done.3, pred[]{:T(512)S(6)} %eq.37, s32[]{:T(128)S(6)} %select_n.246, f32[4,128,128]{1,2,0:T(8,128)S(1)} %convolution_add_fusion.6, f32[4,128,128]{1,2,0:T(8,128)} %copy-done.10), kind=kLoop, calls=%fused_computation.140 | loop fusion | flops 262144 | bytes 1310725 | tf_op jit(solution)/shard_map/jit(_where)/select_n | solution.py:192
  67.0 1.8 %collective-permute-start.4 = (f32[1,128,256]{1,2,0:T(8,128)}, f32[1,128,256]{1,2,0:T(8,128)S(1)}, u32[]{:S(2)}, u32[]{:S(2)}) collective-permute-start(f32[1,128,256]{1,2,0:T(8,128)} %fusion.70), channel_id=1, source_target_pairs={{0,8},{2,10},{4,12},{6,14},{8,0},{10,2},{12,4},{14,6},{16,24},{18,... | collective-permute-start | bytes 393224 | tf_op jit(solution)/shard_map/ppermute | solution.py:190
  68.8 1.1 %copy.71 = f32[4,2,128,128]{3,2,1,0:T(8,128)S(1)} copy(f32[4,2,128,128]{3,0,2,1:T(4,128)} %copy-done.5) | data formatting | bytes 1048576 | tf_op jit(solution)/shard_map/transpose | solution.py:49
  70.2 2.0 %collective-permute-done.4 = f32[1,128,256]{1,2,0:T(8,128)S(1)} collective-permute-done((f32[1,128,256]{1,2,0:T(8,128)}, f32[1,128,256]{1,2,0:T(8,128)S(1)}, u32[]{:S(2)}, u32[]{:S(2)}) %collective-permute-start.4) | collective-permute-done | bytes 131104 | tf_op jit(solution)/shard_map/ppermute | solution.py:190
  72.4 4.7 %collective-permute-start.5 = (f32[1,128,128]{1,2,0:T(8,128)S(1)}, f32[1,128,128]{1,2,0:T(8,128)S(1)}, u32[]{:S(2)}, u32[]{:S(2)}) collective-permute-start(f32[1,128,128]{1,2,0:T(8,128)S(1)} %fusion.27), channel_id=1, source_target_pairs={{0,16},{2,18},{4,20},{6,22},{8,24},{10,26},{12,28},{14,30},{1,17},... | collective-permute-start | bytes 196616 | tf_op jit(solution)/shard_map/ppermute | solution.py:167
  77.8 1.4 %collective-permute-done.5 = f32[1,128,128]{1,2,0:T(8,128)S(1)} collective-permute-done((f32[1,128,128]{1,2,0:T(8,128)S(1)}, f32[1,128,128]{1,2,0:T(8,128)S(1)}, u32[]{:S(2)}, u32[]{:S(2)}) %collective-permute-start.5) | collective-permute-done | bytes 65568 | tf_op jit(solution)/shard_map/ppermute | solution.py:167
  79.3 2.1 %collective-permute-start.6 = (f32[1,128,128]{1,2,0:T(8,128)S(1)}, f32[1,128,128]{1,2,0:T(8,128)S(1)}, u32[]{:S(2)}, u32[]{:S(2)}) collective-permute-start(f32[1,128,128]{1,2,0:T(8,128)S(1)} %get-tuple-element.37), channel_id=1, source_target_pairs={{0,8},{2,10},{4,12},{6,14},{8,0},{10,2},{12,4},{14,6},{16,24},{18,... | collective-permute-start | bytes 196616 | tf_op jit(solution)/shard_map/ppermute | solution.py:203
  82.4 1.3 %collective-permute-done.6 = f32[1,128,128]{1,2,0:T(8,128)S(1)} collective-permute-done((f32[1,128,128]{1,2,0:T(8,128)S(1)}, f32[1,128,128]{1,2,0:T(8,128)S(1)}, u32[]{:S(2)}, u32[]{:S(2)}) %collective-permute-start.6) | collective-permute-done | bytes 65568 | tf_op jit(solution)/shard_map/ppermute | solution.py:203
  83.9 1.6 %collective-permute-start.7 = (f32[2,128,128]{1,2,0:T(8,128)S(1)}, f32[2,128,128]{1,2,0:T(8,128)S(1)}, u32[]{:S(2)}, u32[]{:S(2)}) collective-permute-start(f32[2,128,128]{1,2,0:T(8,128)S(1)} %get-tuple-element.31), channel_id=1, source_target_pairs={{0,4},{2,6},{4,0},{6,2},{8,12},{10,14},{12,8},{14,10},{16,20},{18,... | collective-permute-start | bytes 393224 | tf_op jit(solution)/shard_map/ppermute | solution.py:203
  86.1 2.9 %collective-permute-done.7 = f32[2,128,128]{1,2,0:T(8,128)S(1)} collective-permute-done((f32[2,128,128]{1,2,0:T(8,128)S(1)}, f32[2,128,128]{1,2,0:T(8,128)S(1)}, u32[]{:S(2)}, u32[]{:S(2)}) %collective-permute-start.7) | collective-permute-done | bytes 131104 | tf_op jit(solution)/shard_map/ppermute | solution.py:203
  91.0 1.2 %fusion.25 = bf16[2,128,8,128]{1,3,2,0:T(8,128)(2,1)S(1)} fusion(f32[8,1,128,128]{2,3,0,1:T(8,128)S(1)} %fusion.26, f32[8,1,128,128]{2,3,0,1:T(8,128)S(1)} %slice_bitcast_fusion.5, f32[4,128,128]{1,2,0:T(8,128)S(1)} %get-tuple-element.24, f32[4,128,128]{1,2,0:T(8,128)S(1)} %collective-permute-done.8, pred[]{:T(512)S(6)} %eq.36, ...), kind=kOutput, calls=%fused_computation.41 | convolution fusion | flops 404094976 | bytes 3145729 | tf_op jit(solution)/shard_map/hmck,hkv->hmcv/dot_general | solution.py:135
  92.2 1.6 %collective-permute-start.9 = (bf16[128,1024]{0,1:T(8,128)(2,1)S(1)}, bf16[128,1024]{0,1:T(8,128)(2,1)S(1)}, u32[]{:S(2)}, u32[]{:S(2)}) collective-permute-start(bf16[128,1024]{0,1:T(8,128)(2,1)S(1)} %bitcast.120), channel_id=1, source_target_pairs={{0,1},{1,0},{2,3},{3,2},{4,5},{5,4},{6,7},{7,6},{8,9},{9,8},{10,11... | collective-permute-start | bytes 786440 | tf_op jit(solution)/shard_map/ppermute | solution.py:241
  93.8 6.8 %collective-permute-done.9 = bf16[128,1024]{0,1:T(8,128)(2,1)S(1)} collective-permute-done((bf16[128,1024]{0,1:T(8,128)(2,1)S(1)}, bf16[128,1024]{0,1:T(8,128)(2,1)S(1)}, u32[]{:S(2)}, u32[]{:S(2)}) %collective-permute-start.9) | collective-permute-done | bytes 262176 | tf_op jit(solution)/shard_map/ppermute | solution.py:241
  101.7 1.1 %fusion.41 = bf16[128,2048]{1,0:T(8,128)(2,1)} fusion(bf16[128,2048]{1,0:T(8,128)(2,1)S(1)} %copy-done.15, f32[128,2048]{1,0:T(8,128)S(1)} %copy.106, f32[2048]{0:T(1024)S(1)} %broadcast_bitcast_fusion), kind=kLoop, calls=%fused_computation.77 | loop fusion | flops 2097152 | bytes 2105344 | tf_op jit(solution)/shard_map/convert_element_type | solution.py:217
  (114 shorter events, 27.7 us)
Async XLA Ops:
  0.0 5.3 %copy-start.17 = (bf16[128,16]{0,1:T(8,128)(2,1)S(1)}, bf16[128,16]{0,1:T(8,128)(2,1)}, u32[]{:S(2)}) copy-start(bf16[128,16]{0,1:T(8,128)(2,1)} %param.11) | copy-start | bytes 12292
  0.0 5.3 %copy-start.16 = (bf16[128,16]{0,1:T(8,128)(2,1)S(1)}, bf16[128,16]{0,1:T(8,128)(2,1)}, u32[]{:S(2)}) copy-start(bf16[128,16]{0,1:T(8,128)(2,1)} %param.12) | copy-start | bytes 12292
  2.3 16.0 %collective-permute-start = (bf16[128,2048]{1,0:T(8,128)(2,1)S(1)}, bf16[128,2048]{1,0:T(8,128)(2,1)S(1)}, u32[]{:S(2)}, u32[]{:S(2)}) collective-permute-start(bf16[128,2048]{1,0:T(8,128)(2,1)S(1)} %pad_maximum_fusion.1), channel_id=1, source_target_pairs={{0,1},{1,0},{2,3},{3,2},{4,5},{5,4},{6,7},{7,6},{8,9},{9,8},{10,11... | collective-permute-start | bytes 1572872 | tf_op jit(solution)/shard_map/ppermute | solution.py:230
  5.3 12.0 %collective-permute-start.1 = (bf16[128,16]{0,1:T(8,128)(2,1)S(1)}, bf16[128,16]{0,1:T(8,128)(2,1)S(1)}, u32[]{:S(2)}, u32[]{:S(2)}) collective-permute-start(bf16[128,16]{0,1:T(8,128)(2,1)S(1)} %pad_maximum_fusion.2), channel_id=1, source_target_pairs={{0,1},{1,0},{2,3},{3,2},{4,5},{5,4},{6,7},{7,6},{8,9},{9,8},{10,11... | collective-permute-start | bytes 12296 | tf_op jit(solution)/shard_map/ppermute | solution.py:230
  23.2 1.3 %copy-start.5 = (f32[4,2,128,128]{3,0,2,1:T(4,128)}, f32[4,2,128,128]{3,0,2,1:T(4,128)S(1)}, u32[]{:S(2)}) copy-start(f32[4,2,128,128]{3,0,2,1:T(4,128)S(1)} %multiply_bitcast_fusion.1) | copy-start | bytes 1572868
  36.1 3.5 %copy-start.9 = (f32[8,2,128,128]{2,3,1,0:T(8,128)}, f32[8,2,128,128]{2,3,1,0:T(8,128)S(1)}, u32[]{:S(2)}) copy-start(f32[8,2,128,128]{2,3,1,0:T(8,128)S(1)} %fusion.44) | copy-start | bytes 3145732
  37.2 1.0 copy-start
  42.5 4.3 %copy-start.1 = (f32[8,2,128,128]{3,2,1,0:T(8,128)S(1)}, f32[8,2,128,128]{3,2,1,0:T(8,128)}, u32[]{:S(2)}) copy-start(f32[8,2,128,128]{3,2,1,0:T(8,128)} %copy-done) | copy-start | bytes 3145732
  42.5 4.3 %copy-start.2 = (f32[8,128,128]{2,1,0:T(8,128)S(1)}, f32[8,128,128]{2,1,0:T(8,128)}, u32[]{:S(2)}) copy-start(f32[8,128,128]{2,1,0:T(8,128)} %fusion.57) | copy-start | bytes 1572868
  44.4 5.3 %copy-start.7 = (f32[8,128,128]{2,1,0:T(8,128)}, f32[8,128,128]{2,1,0:T(8,128)S(1)}, u32[]{:S(2)}) copy-start(f32[8,128,128]{2,1,0:T(8,128)S(1)} %convolution_add_fusion.4) | copy-start | bytes 1572868
  46.8 2.9 %copy-start.6 = (f32[8,128,128]{1,2,0:T(8,128)}, f32[8,128,128]{1,2,0:T(8,128)S(1)}, u32[]{:S(2)}) copy-start(f32[8,128,128]{1,2,0:T(8,128)S(1)} %convolution_add_fusion.2) | copy-start | bytes 1572868
  48.0 0.8 copy-start.4
  49.7 2.3 %collective-permute-start.2 = (f32[4,128,256]{1,2,0:T(8,128)}, f32[4,128,256]{1,2,0:T(8,128)}, u32[]{:S(2)}, u32[]{:S(2)}) collective-permute-start(f32[4,128,256]{1,2,0:T(8,128)} %fusion.48), channel_id=1, source_target_pairs={{0,2},{2,0},{4,6},{6,4},{8,10},{10,8},{12,14},{14,12},{16,18},{18,... | collective-permute-start | bytes 1572872 | tf_op jit(solution)/shard_map/ppermute | solution.py:190
  53.4 2.2 %copy-start.11 = (f32[4,128,256]{1,2,0:T(8,128)}, f32[4,128,256]{1,2,0:T(8,128)S(1)}, u32[]{:S(2)}) copy-start(f32[4,128,256]{1,2,0:T(8,128)S(1)} %get-tuple-element.14) | copy-start | bytes 1572868
  54.1 0.7 copy-start.10
  55.6 8.7 %collective-permute-start.3 = (f32[2,128,256]{1,2,0:T(8,128)}, f32[2,128,256]{1,2,0:T(8,128)}, u32[]{:S(2)}, u32[]{:S(2)}) collective-permute-start(f32[2,128,256]{1,2,0:T(8,128)} %fusion.59), channel_id=1, source_target_pairs={{0,4},{2,6},{4,0},{6,2},{8,12},{10,14},{12,8},{14,10},{16,20},{18,... | collective-permute-start | bytes 786440 | tf_op jit(solution)/shard_map/ppermute | solution.py:190
  65.3 0.7 copy-start.13
  67.0 5.2 %collective-permute-start.4 = (f32[1,128,256]{1,2,0:T(8,128)}, f32[1,128,256]{1,2,0:T(8,128)S(1)}, u32[]{:S(2)}, u32[]{:S(2)}) collective-permute-start(f32[1,128,256]{1,2,0:T(8,128)} %fusion.70), channel_id=1, source_target_pairs={{0,8},{2,10},{4,12},{6,14},{8,0},{10,2},{12,4},{14,6},{16,24},{18,... | collective-permute-start | bytes 393224 | tf_op jit(solution)/shard_map/ppermute | solution.py:190
  72.4 6.7 %collective-permute-start.5 = (f32[1,128,128]{1,2,0:T(8,128)S(1)}, f32[1,128,128]{1,2,0:T(8,128)S(1)}, u32[]{:S(2)}, u32[]{:S(2)}) collective-permute-start(f32[1,128,128]{1,2,0:T(8,128)S(1)} %fusion.27), channel_id=1, source_target_pairs={{0,16},{2,18},{4,20},{6,22},{8,24},{10,26},{12,28},{14,30},{1,17},... | collective-permute-start | bytes 196616 | tf_op jit(solution)/shard_map/ppermute | solution.py:167
  77.7 5.9 %copy-start.14 = (f32[2,128,256]{1,2,0:T(8,128)S(1)}, f32[2,128,256]{1,2,0:T(8,128)}, u32[]{:S(2)}) copy-start(f32[2,128,256]{1,2,0:T(8,128)} %copy-done.13) | copy-start | bytes 786436
  77.7 7.7 %copy-start.8 = (f32[8,128,128]{2,1,0:T(8,128)S(1)}, f32[8,128,128]{2,1,0:T(8,128)}, u32[]{:S(2)}) copy-start(f32[8,128,128]{2,1,0:T(8,128)} %copy-done.7) | copy-start | bytes 1572868
  79.3 4.3 %collective-permute-start.6 = (f32[1,128,128]{1,2,0:T(8,128)S(1)}, f32[1,128,128]{1,2,0:T(8,128)S(1)}, u32[]{:S(2)}, u32[]{:S(2)}) collective-permute-start(f32[1,128,128]{1,2,0:T(8,128)S(1)} %get-tuple-element.37), channel_id=1, source_target_pairs={{0,8},{2,10},{4,12},{6,14},{8,0},{10,2},{12,4},{14,6},{16,24},{18,... | collective-permute-start | bytes 196616 | tf_op jit(solution)/shard_map/ppermute | solution.py:203
  82.4 6.6 %copy-start.12 = (f32[4,128,256]{1,2,0:T(8,128)S(1)}, f32[4,128,256]{1,2,0:T(8,128)}, u32[]{:S(2)}) copy-start(f32[4,128,256]{1,2,0:T(8,128)} %copy-done.11) | copy-start | bytes 1572868
  83.7 5.8 %copy-start.3 = (f32[8,128,128]{2,1,0:T(8,128)S(1)}, f32[8,128,128]{2,1,0:T(8,128)}, u32[]{:S(2)}) copy-start(f32[8,128,128]{2,1,0:T(8,128)} %fusion.57) | copy-start | bytes 1572868
  83.9 5.0 %collective-permute-start.7 = (f32[2,128,128]{1,2,0:T(8,128)S(1)}, f32[2,128,128]{1,2,0:T(8,128)S(1)}, u32[]{:S(2)}, u32[]{:S(2)}) collective-permute-start(f32[2,128,128]{1,2,0:T(8,128)S(1)} %get-tuple-element.31), channel_id=1, source_target_pairs={{0,4},{2,6},{4,0},{6,2},{8,12},{10,14},{12,8},{14,10},{16,20},{18,... | collective-permute-start | bytes 393224 | tf_op jit(solution)/shard_map/ppermute | solution.py:203
  89.4 1.6 %collective-permute-start.8 = (f32[4,128,128]{1,2,0:T(8,128)S(1)}, f32[4,128,128]{1,2,0:T(8,128)S(1)}, u32[]{:S(2)}, u32[]{:S(2)}) collective-permute-start(f32[4,128,128]{1,2,0:T(8,128)S(1)} %get-tuple-element.23), channel_id=1, source_target_pairs={{0,2},{2,0},{4,6},{6,4},{8,10},{10,8},{12,14},{14,12},{16,18},{18,... | collective-permute-start | bytes 786440 | tf_op jit(solution)/shard_map/ppermute | solution.py:203
  91.0 2.8 %copy-start.18 = (bf16[128]{0:T(256)(128)(2,1)S(1)}, bf16[128]{0:T(256)(128)(2,1)}, u32[]{:S(2)}) copy-start(bf16[128]{0:T(256)(128)(2,1)} %param.13) | copy-start | bytes 772
  92.2 8.4 %collective-permute-start.9 = (bf16[128,1024]{0,1:T(8,128)(2,1)S(1)}, bf16[128,1024]{0,1:T(8,128)(2,1)S(1)}, u32[]{:S(2)}, u32[]{:S(2)}) collective-permute-start(bf16[128,1024]{0,1:T(8,128)(2,1)S(1)} %bitcast.120), channel_id=1, source_target_pairs={{0,1},{1,0},{2,3},{3,2},{4,5},{5,4},{6,7},{7,6},{8,9},{9,8},{10,11... | collective-permute-start | bytes 786440 | tf_op jit(solution)/shard_map/ppermute | solution.py:241
  100.6 1.0 %copy-start.15 = (bf16[128,2048]{1,0:T(8,128)(2,1)S(1)}, bf16[128,2048]{1,0:T(8,128)(2,1)}, u32[]{:S(2)}) copy-start(bf16[128,2048]{1,0:T(8,128)(2,1)} %param.10) | copy-start | bytes 1572868

commit v4 on v2

--- a/solution.py
+++ b/solution.py
@@ -113,20 +113,14 @@
     reach = wide_query * jnp.exp(cum_log)[..., None] - jnp.einsum(
         "hmij,hmjk->hmik", scores, weights, precision=LOCAL_PRECISION
     )
-    head_count, blocks = (carry_mat.shape[0], carry_mat.shape[1])
-    reach_map = jnp.broadcast_to(jnp.eye(DK, dtype=jnp.float32), (head_count, DK, DK))
-    reach_add = jnp.zeros((head_count, DK, DV), jnp.float32)
-    fixed, scaled = ([], [])
-    for m in range(blocks):
-        if m == 0:
-            fixed.append(inner[:, m])
-            scaled.append(reach[:, m])
-        else:
-            fixed.append(
-                inner[:, m]
-                + jnp.matmul(reach[:, m], reach_add, precision=LOCAL_PRECISION)
-            )
-            scaled.append(jnp.matmul(reach[:, m], reach_map, precision=LOCAL_PRECISION))
+    blocks = carry_mat.shape[1]
+    fixed, scaled = ([inner[:, 0]], [reach[:, 0]])
+    reach_map, reach_add = (carry_mat[:, 0], write_mat[:, 0])
+    for m in range(1, blocks):
+        fixed.append(
+            inner[:, m] + jnp.matmul(reach[:, m], reach_add, precision=LOCAL_PRECISION)
+        )
+        scaled.append(jnp.matmul(reach[:, m], reach_map, precision=LOCAL_PRECISION))
         reach_map, reach_add = compose((reach_map, reach_add), (carry_mat[:, m], write_mat[:, m]))
     return (jnp.stack(fixed, axis=1), jnp.stack(scaled, axis=1), reach_map, reach_add)
 

time: 92.9 us -> 86.8 us (0.934)
  matrix products: 24.1 us -> 19.7 us
  local copies, waits for them, and re-layouts: 5.74 us -> 2.52 us
  other arithmetic: 16.1 us -> 17.6 us
    dot_general x5 -> x4, matrix products: 5.05 us -> 2.07 us  [compose(): jnp.matmul(later[0], earlier[1], precision=FULL_PRECISION) + later[1]]
    unnamed x33 -> x28, local copies, waits for them, and re-layouts: 3.83 us -> 1.44 us
    dot_general x4 -> x3, matrix products: 3.05 us -> 1.66 us  [compose(): jnp.matmul(later[0], earlier[0], precision=FULL_PRECISION)]
    unnamed x1, other arithmetic: 0.11 us -> 1.16 us
  transfers between devices with their start and end apart: 13 -> 13, of which waited for: 8 -> 8; matrix products, arithmetic and copies ran while one was open for 15% -> 16% of each run, Pallas kernels for 0% -> 0%
where the time goes in v4:
time: 86.8 us; the launch traced here: 86.4 us
  waiting for transfers between devices  26.8 us (31%)
  matrix products  19.7 us (23%)
  starting transfers between devices  19.2 us (22%)
  other arithmetic  17.6 us (20%)
  local copies, waits for them, and re-layouts  2.52 us (3%)
    ppermute x6, waiting for transfers between devices, chain_states(): got = lax.ppermute(other, 'ctx', [(i, i ^ stride) for i in range(size)])  17.6 us
    ppermute x1, waiting for transfers between devices, head_return(): got = lax.ppermute(sent, 'head', [(0, 1), (1, 0)])  7.83 us
    ppermute x5, starting transfers between devices, head_swap(): got = lax.ppermute(sent, 'head', [(0, 1), (1, 0)])  7.15 us
    ppermute x6, starting transfers between devices, chain_states(): got = lax.ppermute(other, 'ctx', [(i, i ^ stride) for i in range(size)])  6.98 us
    dot_general x5, matrix products, unit_lower_inverse(): jnp.matmul(jnp.concatenate([inverse, power], axis=-2), power, precision=L...  5.3 us
    select_n x5, other arithmetic, head_swap(): own = jnp.where(first, rows[:, :width], rows[:, width:])  5.14 us
    ppermute x1, starting transfers between devices, exclusive_scan(): return lax.ppermute(write, 'ctx', near)  4.53 us
    select_n x3, other arithmetic, chain_states(): later = jnp.where(upper, mine, got)  2.8 us
  transfers between devices with their start and end apart: 13, of which 8 were waited for; matrix products, arithmetic and copies ran while one was open for 16% of the time, Pallas kernels for 0%

profile of v4, /device:TPU:0, one launch (start us, length us, event | category | flops | bytes accessed | tf_op | source)
XLA Modules:
  0.0 86.4 jit_solution(11051704666580283295)
XLA Ops:
  1.0 3.0 %collective-permute-start = (bf16[128,512]{1,0:T(8,128)(2,1)S(1)}, bf16[128,512]{1,0:T(8,128)(2,1)S(1)}, u32[]{:S(2)}, u32[]{:S(2)}) collective-permute-start(bf16[128,512]{1,0:T(8,128)(2,1)S(1)} %get-tuple-element.34), channel_id=1, source_target_pairs={{0,1},{1,0},{2,3},{3,2},{4,5},{5,4},{6,7},{7,6},{8,9},{9,8},{10,11... | collective-permute-start | bytes 393224 | tf_op jit(solution)/shard_map/ppermute | solution.py:218
  5.8 2.0 %collective-permute-start.2 = (bf16[128,8]{0,1:T(8,128)(2,1)S(1)}, bf16[128,8]{0,1:T(8,128)(2,1)S(1)}, u32[]{:S(2)}, u32[]{:S(2)}) collective-permute-start(bf16[128,8]{0,1:T(8,128)(2,1)S(1)} %get-tuple-element.45), channel_id=1, source_target_pairs={{0,1},{1,0},{2,3},{3,2},{4,5},{5,4},{6,7},{7,6},{8,9},{9,8},{10,11... | collective-permute-start | bytes 6152 | tf_op jit(solution)/shard_map/ppermute | solution.py:218
  8.5 1.8 %broadcast_select_fusion.5 = (bf16[128,1024]{1,0:T(8,128)(2,1)S(1)}, bf16[128,1024]{1,0:T(8,128)(2,1)}) fusion(pred[]{:T(512)S(6)} %eq.31, bf16[128,2048]{1,0:T(8,128)(2,1)} %param.9), kind=kLoop, calls=%fused_computation.122 | loop fusion | flops 262144 | bytes 1048577 | tf_op jit(solution)/shard_map/jit(_where)/select_n | solution.py:216
  10.3 2.0 %collective-permute-start.4 = (bf16[128,1024]{1,0:T(8,128)(2,1)}, bf16[128,1024]{1,0:T(8,128)(2,1)}, u32[]{:S(2)}, u32[]{:S(2)}) collective-permute-start(bf16[128,1024]{1,0:T(8,128)(2,1)} %get-tuple-element.26), channel_id=1, source_target_pairs={{0,1},{1,0},{2,3},{3,2},{4,5},{5,4},{6,7},{7,6},{8,9},{9,8},{10,11... | collective-permute-start | bytes 786440 | tf_op jit(solution)/shard_map/ppermute | solution.py:218
  17.2 1.1 %fusion = f32[8,2,256,128]{3,2,1,0:T(8,128)S(1)} fusion(f32[8,2,128,128]{3,2,1,0:T(8,128)S(1)} %fusion.94, f32[8,2,128,128]{3,2,1,0:T(8,128)S(1)} %get-tuple-element.17), kind=kOutput, calls=%fused_computation | convolution fusion | flops 403177472 | bytes 4194304 | tf_op jit(solution)/shard_map/dot_general | solution.py:58
  19.6 1.2 %convert_bitcast_fusion = f32[32,8,8,128]{3,1,2,0:T(8,128)S(1)} fusion(bf16[128,1024]{1,0:T(8,128)(2,1)} %collective-permute-done.4, bf16[128,1024]{1,0:T(8,128)(2,1)S(1)} %get-tuple-element.25, pred[]{:T(512)S(6)} %eq.31), kind=kLoop, calls=%fused_computation.72 | loop fusion | flops 2621440 | bytes 1572865
  22.0 1.1 %fusion.4 = f32[8,2,256,128]{3,2,1,0:T(8,128)S(1)} fusion(f32[8,2,128,128]{3,2,1,0:T(8,128)S(1)} %get-tuple-element.12, f32[8,2,128,128]{3,2,1,0:T(8,128)S(1)} %get-tuple-element.11), kind=kOutput, calls=%fused_computation.4 | convolution fusion | flops 403177472 | bytes 4194304 | tf_op jit(solution)/shard_map/dot_general | solution.py:58
  23.3 1.1 %fusion.8 = f32[8,2,256,128]{3,2,1,0:T(8,128)S(1)} fusion(f32[8,2,128,128]{3,2,1,0:T(8,128)S(1)} %get-tuple-element.10, f32[8,2,128,128]{3,2,1,0:T(8,128)S(1)} %get-tuple-element.9), kind=kOutput, calls=%fused_computation.8 | convolution fusion | flops 403177472 | bytes 4194304 | tf_op jit(solution)/shard_map/dot_general | solution.py:58
  24.5 1.0 %fusion.12 = f32[8,2,256,128]{3,2,1,0:T(8,128)S(1)} fusion(f32[8,2,128,128]{3,2,1,0:T(8,128)S(1)} %get-tuple-element.8, f32[8,2,128,128]{3,2,1,0:T(8,128)S(1)} %get-tuple-element.7), kind=kOutput, calls=%fused_computation.12 | convolution fusion | flops 403177472 | bytes 4194304 | tf_op jit(solution)/shard_map/dot_general | solution.py:58
  25.8 1.1 %fusion.16 = f32[8,2,256,128]{3,2,1,0:T(8,128)S(1)} fusion(f32[8,2,128,128]{3,2,1,0:T(8,128)S(1)} %get-tuple-element.6, f32[8,2,128,128]{3,2,1,0:T(8,128)S(1)} %get-tuple-element.5), kind=kOutput, calls=%fused_computation.16 | convolution fusion | flops 403177472 | bytes 4194304 | tf_op jit(solution)/shard_map/dot_general | solution.py:58
  27.6 1.2 %fusion.20 = f32[8,2,128,256]{3,2,1,0:T(8,128)S(1)} fusion(f32[8,2,128,128]{3,2,1,0:T(8,128)S(1)} %convolution_add_fusion, f32[8,2,128,128]{3,2,1,0:T(8,128)S(1)} %get-tuple-element.24, f32[8,2,128,128]{3,2,1,0:T(8,128)S(1)} %get-tuple-element.40), kind=kOutput, calls=%fused_computation.20 | convolution fusion | flops 403177472 | bytes 5242880 | tf_op jit(solution)/shard_map/dot_general | solution.py:86
  28.8 1.0 %fusion.44 = f32[8,2,128,128]{2,3,1,0:T(8,128)S(1)} fusion(f32[8,2,128,128]{3,2,1,0:T(8,128)S(1)} %get-tuple-element.23, f32[8,2,128,256]{3,2,1,0:T(8,128)S(1)} %fusion.20), kind=kOutput, calls=%fused_computation.76 | convolution fusion | flops 201326592 | bytes 3145728 | tf_op jit(solution)/shard_map/hmck,hmcv->hmkv/dot_general | solution.py:94
  29.9 1.1 %convolution_subtract_fusion = f32[8,2,128,128]{3,2,1,0:T(8,128)S(1)} fusion(f32[8,2,128,128]{3,2,1,0:T(8,128)S(1)} %get-tuple-element.23, f32[8,2,128,256]{3,2,1,0:T(8,128)S(1)} %fusion.20, f32[8,2]{1,0:T(8,128)S(1)} %copy.81, f32[128,128]{1,0:T(8,128)S(1)} %get-tuple-element.47), kind=kOutput, calls=%fused_computation.30 | convolution fusion | flops 201850880 | bytes 3215360 | tf_op jit(solution)/shard_map/hmck,hmcj->hmkj/dot_general | solution.py:91
  31.0 1.0 %fusion.56 = f32[8,128,128]{1,2,0:T(8,128)S(1)} fusion(f32[8,2,128,128]{3,2,1,0:T(8,128)S(1)} %convolution_subtract_fusion), kind=kOutput, calls=%fused_computation.105 | convolution fusion | flops 201326592 | bytes 1572864 | tf_op jit(solution)/shard_map/dot_general | solution.py:21
  32.1 1.2 %convolution_add_fusion.2 = f32[8,128,128]{1,2,0:T(8,128)S(1)} fusion(f32[8,2,128,128]{2,3,1,0:T(8,128)S(1)} %fusion.44, f32[8,2,128,128]{3,2,1,0:T(8,128)S(1)} %convolution_subtract_fusion), kind=kOutput, calls=%fused_computation.38 | convolution fusion | flops 201457664 | bytes 2097152 | tf_op jit(solution)/shard_map/dot_general | solution.py:22
  34.3 2.2 %collective-permute-done.5 = f32[4,128,256]{1,2,0:T(8,128)} collective-permute-done((f32[4,128,256]{1,2,0:T(8,128)}, f32[4,128,256]{1,2,0:T(8,128)}, u32[]{:S(2)}, u32[]{:S(2)}) %collective-permute-start.5) | collective-permute-done | bytes 524320 | tf_op jit(solution)/shard_map/ppermute | solution.py:183
  36.6 1.6 %broadcast_select_fusion.1 = (f32[4,128,256]{1,2,0:T(8,128)S(1)}, f32[4,128,256]{1,2,0:T(8,128)S(1)}) fusion(f32[4,128,256]{1,2,0:T(8,128)} %collective-permute-done.5, pred[]{:T(512)S(6)} %eq.33, f32[8,128,128]{1,2,0:T(8,128)} %copy-done.5, f32[8,128,128]{1,2,0:T(8,128)} %copy-done.4), kind=kLoop, calls=%fused_computation.117 | loop fusion | flops 917504 | bytes 2621441 | tf_op jit(solution)/shard_map/jit(_where)/select_n | solution.py:185
  40.4 1.5 %collective-permute-start.6 = (f32[2,128,256]{1,2,0:T(8,128)}, f32[2,128,256]{1,2,0:T(8,128)}, u32[]{:S(2)}, u32[]{:S(2)}) collective-permute-start(f32[2,128,256]{1,2,0:T(8,128)} %broadcast_select_fusion.9), channel_id=1, source_target_pairs={{0,4},{2,6},{4,0},{6,2},{8,12},{10,14},{12,8},{14,10},{16,20},{18,... | collective-permute-start | bytes 786440 | tf_op jit(solution)/shard_map/ppermute | solution.py:183
  41.9 7.2 %collective-permute-done.6 = f32[2,128,256]{1,2,0:T(8,128)} collective-permute-done((f32[2,128,256]{1,2,0:T(8,128)}, f32[2,128,256]{1,2,0:T(8,128)}, u32[]{:S(2)}, u32[]{:S(2)}) %collective-permute-start.6) | collective-permute-done | bytes 262176 | tf_op jit(solution)/shard_map/ppermute | solution.py:183
  49.1 1.2 %broadcast_select_fusion.8 = (f32[2,128,256]{1,2,0:T(8,128)S(1)}, f32[2,128,256]{1,2,0:T(8,128)S(1)}) fusion(f32[2,128,256]{1,2,0:T(8,128)} %collective-permute-done.6, pred[]{:T(512)S(6)} %eq.34, f32[4,128,128]{1,2,0:T(8,128)} %copy-done.8, f32[4,128,128]{1,2,0:T(8,128)S(1)} %fusion.63), kind=kLoop, calls=%fused_computation.136 | loop fusion | flops 458752 | bytes 1310721 | tf_op jit(solution)/shard_map/jit(_where)/select_n | solution.py:185
  50.8 1.9 %collective-permute-start.7 = (f32[1,128,256]{1,2,0:T(8,128)S(1)}, f32[1,128,256]{1,2,0:T(8,128)S(1)}, u32[]{:S(2)}, u32[]{:S(2)}) collective-permute-start(f32[1,128,256]{1,2,0:T(8,128)S(1)} %broadcast_select_fusion.19), channel_id=1, source_target_pairs={{0,8},{2,10},{4,12},{6,14},{8,0},{10,2},{12,4},{14,6},{16,24},{18,... | collective-permute-start | bytes 393224 | tf_op jit(solution)/shard_map/ppermute | solution.py:183
  53.0 3.0 %collective-permute-done.7 = f32[1,128,256]{1,2,0:T(8,128)S(1)} collective-permute-done((f32[1,128,256]{1,2,0:T(8,128)S(1)}, f32[1,128,256]{1,2,0:T(8,128)S(1)}, u32[]{:S(2)}, u32[]{:S(2)}) %collective-permute-start.7) | collective-permute-done | bytes 131104 | tf_op jit(solution)/shard_map/ppermute | solution.py:183
  56.3 4.5 %collective-permute-start.8 = (f32[1,128,128]{1,2,0:T(8,128)S(1)}, f32[1,128,128]{1,2,0:T(8,128)S(1)}, u32[]{:S(2)}, u32[]{:S(2)}) collective-permute-start(f32[1,128,128]{1,2,0:T(8,128)S(1)} %fusion.27), channel_id=1, source_target_pairs={{0,16},{2,18},{4,20},{6,22},{8,24},{10,26},{12,28},{14,30},{1,17},... | collective-permute-start | bytes 196616 | tf_op jit(solution)/shard_map/ppermute | solution.py:161
  61.4 1.4 %collective-permute-done.8 = f32[1,128,128]{1,2,0:T(8,128)S(1)} collective-permute-done((f32[1,128,128]{1,2,0:T(8,128)S(1)}, f32[1,128,128]{1,2,0:T(8,128)S(1)}, u32[]{:S(2)}, u32[]{:S(2)}) %collective-permute-start.8) | collective-permute-done | bytes 65568 | tf_op jit(solution)/shard_map/ppermute | solution.py:161
  63.0 2.0 %collective-permute-start.9 = (f32[1,128,128]{1,2,0:T(8,128)S(1)}, f32[1,128,128]{1,2,0:T(8,128)S(1)}, u32[]{:S(2)}, u32[]{:S(2)}) collective-permute-start(f32[1,128,128]{1,2,0:T(8,128)S(1)} %get-tuple-element.35), channel_id=1, source_target_pairs={{0,8},{2,10},{4,12},{6,14},{8,0},{10,2},{12,4},{14,6},{16,24},{18,... | collective-permute-start | bytes 196616 | tf_op jit(solution)/shard_map/ppermute | solution.py:196
  66.1 1.3 %collective-permute-done.9 = f32[1,128,128]{1,2,0:T(8,128)S(1)} collective-permute-done((f32[1,128,128]{1,2,0:T(8,128)S(1)}, f32[1,128,128]{1,2,0:T(8,128)S(1)}, u32[]{:S(2)}, u32[]{:S(2)}) %collective-permute-start.9) | collective-permute-done | bytes 65568 | tf_op jit(solution)/shard_map/ppermute | solution.py:196
  67.6 1.5 %collective-permute-start.10 = (f32[2,128,128]{1,2,0:T(8,128)S(1)}, f32[2,128,128]{1,2,0:T(8,128)S(1)}, u32[]{:S(2)}, u32[]{:S(2)}) collective-permute-start(f32[2,128,128]{1,2,0:T(8,128)S(1)} %get-tuple-element.29), channel_id=1, source_target_pairs={{0,4},{2,6},{4,0},{6,2},{8,12},{10,14},{12,8},{14,10},{16,20},{18,... | collective-permute-start | bytes 393224 | tf_op jit(solution)/shard_map/ppermute | solution.py:196
  69.8 2.8 %collective-permute-done.10 = f32[2,128,128]{1,2,0:T(8,128)S(1)} collective-permute-done((f32[2,128,128]{1,2,0:T(8,128)S(1)}, f32[2,128,128]{1,2,0:T(8,128)S(1)}, u32[]{:S(2)}, u32[]{:S(2)}) %collective-permute-start.10) | collective-permute-done | bytes 131104 | tf_op jit(solution)/shard_map/ppermute | solution.py:196
  73.6 1.0 %collective-permute-done.11 = f32[4,128,128]{1,2,0:T(8,128)S(1)} collective-permute-done((f32[4,128,128]{1,2,0:T(8,128)S(1)}, f32[4,128,128]{1,2,0:T(8,128)S(1)}, u32[]{:S(2)}, u32[]{:S(2)}) %collective-permute-start.11) | collective-permute-done | bytes 262176 | tf_op jit(solution)/shard_map/ppermute | solution.py:196
  74.7 1.1 %fusion.25 = bf16[2,128,8,128]{1,3,2,0:T(8,128)(2,1)S(1)} fusion(f32[8,1,128,128]{2,3,0,1:T(8,128)S(1)} %fusion.26, f32[8,1,128,128]{2,3,0,1:T(8,128)S(1)} %slice_bitcast_fusion.6, f32[4,128,128]{1,2,0:T(8,128)S(1)} %get-tuple-element.22, f32[4,128,128]{1,2,0:T(8,128)S(1)} %collective-permute-done.11, pred[]{:T(512)S(6)} %eq.33, ...), kind=kOutput, calls=%fused_computation.37 | convolution fusion | flops 404094976 | bytes 3145729 | tf_op jit(solution)/shard_map/hmck,hkv->hmcv/dot_general | solution.py:129
  76.4 7.8 %collective-permute-done.12 = bf16[128,1024]{0,1:T(8,128)(2,1)S(1)} collective-permute-done((bf16[128,1024]{0,1:T(8,128)(2,1)S(1)}, bf16[128,1024]{0,1:T(8,128)(2,1)S(1)}, u32[]{:S(2)}, u32[]{:S(2)}) %collective-permute-start.12) | collective-permute-done | bytes 262176 | tf_op jit(solution)/shard_map/ppermute | solution.py:227
  85.3 1.1 %fusion.41 = bf16[128,2048]{1,0:T(8,128)(2,1)} fusion(bf16[128,2048]{1,0:T(8,128)(2,1)S(1)} %copy-done.11, f32[128,2048]{1,0:T(8,128)S(1)} %copy.97, f32[2048]{0:T(1024)S(1)} %broadcast_bitcast_fusion), kind=kLoop, calls=%fused_computation.73 | loop fusion | flops 2097152 | bytes 2105344 | tf_op jit(solution)/shard_map/convert_element_type | solution.py:210
  (102 shorter events, 21.7 us)
Async XLA Ops:
  1.0 12.4 %collective-permute-start = (bf16[128,512]{1,0:T(8,128)(2,1)S(1)}, bf16[128,512]{1,0:T(8,128)(2,1)S(1)}, u32[]{:S(2)}, u32[]{:S(2)}) collective-permute-start(bf16[128,512]{1,0:T(8,128)(2,1)S(1)} %get-tuple-element.34), channel_id=1, source_target_pairs={{0,1},{1,0},{2,3},{3,2},{4,5},{5,4},{6,7},{7,6},{8,9},{9,8},{10,11... | collective-permute-start | bytes 393224 | tf_op jit(solution)/shard_map/ppermute | solution.py:218
  5.0 9.0 %collective-permute-start.1 = (bf16[128,512]{1,0:T(8,128)(2,1)S(1)}, bf16[128,512]{1,0:T(8,128)(2,1)S(1)}, u32[]{:S(2)}, u32[]{:S(2)}) collective-permute-start(bf16[128,512]{1,0:T(8,128)(2,1)S(1)} %get-tuple-element.32), channel_id=1, source_target_pairs={{0,1},{1,0},{2,3},{3,2},{4,5},{5,4},{6,7},{7,6},{8,9},{9,8},{10,11... | collective-permute-start | bytes 393224 | tf_op jit(solution)/shard_map/ppermute | solution.py:218
  5.8 6.6 %collective-permute-start.2 = (bf16[128,8]{0,1:T(8,128)(2,1)S(1)}, bf16[128,8]{0,1:T(8,128)(2,1)S(1)}, u32[]{:S(2)}, u32[]{:S(2)}) collective-permute-start(bf16[128,8]{0,1:T(8,128)(2,1)S(1)} %get-tuple-element.45), channel_id=1, source_target_pairs={{0,1},{1,0},{2,3},{3,2},{4,5},{5,4},{6,7},{7,6},{8,9},{9,8},{10,11... | collective-permute-start | bytes 6152 | tf_op jit(solution)/shard_map/ppermute | solution.py:218
  8.5 4.6 %collective-permute-start.3 = (bf16[128,8]{0,1:T(8,128)(2,1)S(1)}, bf16[128,8]{0,1:T(8,128)(2,1)S(1)}, u32[]{:S(2)}, u32[]{:S(2)}) collective-permute-start(bf16[128,8]{0,1:T(8,128)(2,1)S(1)} %get-tuple-element.43), channel_id=1, source_target_pairs={{0,1},{1,0},{2,3},{3,2},{4,5},{5,4},{6,7},{7,6},{8,9},{9,8},{10,11... | collective-permute-start | bytes 6152 | tf_op jit(solution)/shard_map/ppermute | solution.py:218
  10.3 9.3 %collective-permute-start.4 = (bf16[128,1024]{1,0:T(8,128)(2,1)}, bf16[128,1024]{1,0:T(8,128)(2,1)}, u32[]{:S(2)}, u32[]{:S(2)}) collective-permute-start(bf16[128,1024]{1,0:T(8,128)(2,1)} %get-tuple-element.26), channel_id=1, source_target_pairs={{0,1},{1,0},{2,3},{3,2},{4,5},{5,4},{6,7},{7,6},{8,9},{9,8},{10,11... | collective-permute-start | bytes 786440 | tf_op jit(solution)/shard_map/ppermute | solution.py:218
  15.3 3.6 %copy-start.2 = (f32[4,2,128,128]{3,0,2,1:T(4,128)}, f32[4,2,128,128]{3,0,2,1:T(4,128)S(1)}, u32[]{:S(2)}) copy-start(f32[4,2,128,128]{3,0,2,1:T(4,128)S(1)} %get-tuple-element.49) | copy-start | bytes 1572868
  29.8 2.2 %copy-start.6 = (f32[8,2,128,128]{2,3,1,0:T(8,128)}, f32[8,2,128,128]{2,3,1,0:T(8,128)S(1)}, u32[]{:S(2)}) copy-start(f32[8,2,128,128]{2,3,1,0:T(8,128)S(1)} %fusion.44) | copy-start | bytes 3145732
  31.0 3.2 %copy-start = (f32[8,2,128,128]{3,2,1,0:T(8,128)}, f32[8,2,128,128]{3,2,1,0:T(8,128)S(1)}, u32[]{:S(2)}) copy-start(f32[8,2,128,128]{3,2,1,0:T(8,128)S(1)} %convolution_subtract_fusion) | copy-start | bytes 3145732
  32.0 1.2 %copy-start.4 = (f32[8,128,128]{1,2,0:T(8,128)}, f32[8,128,128]{1,2,0:T(8,128)S(1)}, u32[]{:S(2)}) copy-start(f32[8,128,128]{1,2,0:T(8,128)S(1)} %fusion.56) | copy-start | bytes 1572868
  33.3 1.0 %copy-start.5 = (f32[8,128,128]{1,2,0:T(8,128)}, f32[8,128,128]{1,2,0:T(8,128)S(1)}, u32[]{:S(2)}) copy-start(f32[8,128,128]{1,2,0:T(8,128)S(1)} %convolution_add_fusion.2) | copy-start | bytes 1572868
  34.3 2.3 %collective-permute-start.5 = (f32[4,128,256]{1,2,0:T(8,128)}, f32[4,128,256]{1,2,0:T(8,128)}, u32[]{:S(2)}, u32[]{:S(2)}) collective-permute-start(f32[4,128,256]{1,2,0:T(8,128)} %broadcast_select_fusion.2), channel_id=1, source_target_pairs={{0,2},{2,0},{4,6},{6,4},{8,10},{10,8},{12,14},{14,12},{16,18},{18,... | collective-permute-start | bytes 1572872 | tf_op jit(solution)/shard_map/ppermute | solution.py:183
  38.2 2.2 %copy-start.9 = (f32[4,128,256]{1,2,0:T(8,128)}, f32[4,128,256]{1,2,0:T(8,128)S(1)}, u32[]{:S(2)}) copy-start(f32[4,128,256]{1,2,0:T(8,128)S(1)} %get-tuple-element.14) | copy-start | bytes 1572868
  39.0 0.7 copy-start.8
  40.4 8.7 %collective-permute-start.6 = (f32[2,128,256]{1,2,0:T(8,128)}, f32[2,128,256]{1,2,0:T(8,128)}, u32[]{:S(2)}, u32[]{:S(2)}) collective-permute-start(f32[2,128,256]{1,2,0:T(8,128)} %broadcast_select_fusion.9), channel_id=1, source_target_pairs={{0,4},{2,6},{4,0},{6,2},{8,12},{10,14},{12,8},{14,10},{16,20},{18,... | collective-permute-start | bytes 786440 | tf_op jit(solution)/shard_map/ppermute | solution.py:183
  41.9 10.8 %copy-start.3 = (f32[4,2,128,128]{3,0,2,1:T(4,128)S(1)}, f32[4,2,128,128]{3,0,2,1:T(4,128)}, u32[]{:S(2)}) copy-start(f32[4,2,128,128]{3,0,2,1:T(4,128)} %copy-done.2) | copy-start | bytes 1572868
  50.8 5.3 %collective-permute-start.7 = (f32[1,128,256]{1,2,0:T(8,128)S(1)}, f32[1,128,256]{1,2,0:T(8,128)S(1)}, u32[]{:S(2)}, u32[]{:S(2)}) collective-permute-start(f32[1,128,256]{1,2,0:T(8,128)S(1)} %broadcast_select_fusion.19), channel_id=1, source_target_pairs={{0,8},{2,10},{4,12},{6,14},{8,0},{10,2},{12,4},{14,6},{16,24},{18,... | collective-permute-start | bytes 393224 | tf_op jit(solution)/shard_map/ppermute | solution.py:183
  56.3 6.5 %collective-permute-start.8 = (f32[1,128,128]{1,2,0:T(8,128)S(1)}, f32[1,128,128]{1,2,0:T(8,128)S(1)}, u32[]{:S(2)}, u32[]{:S(2)}) collective-permute-start(f32[1,128,128]{1,2,0:T(8,128)S(1)} %fusion.27), channel_id=1, source_target_pairs={{0,16},{2,18},{4,20},{6,22},{8,24},{10,26},{12,28},{14,30},{1,17},... | collective-permute-start | bytes 196616 | tf_op jit(solution)/shard_map/ppermute | solution.py:161
  61.4 7.7 %copy-start.7 = (f32[8,2,128,128]{2,3,1,0:T(8,128)S(1)}, f32[8,2,128,128]{2,3,1,0:T(8,128)}, u32[]{:S(2)}) copy-start(f32[8,2,128,128]{2,3,1,0:T(8,128)} %copy-done.6) | copy-start | bytes 3145732
  63.0 4.3 %collective-permute-start.9 = (f32[1,128,128]{1,2,0:T(8,128)S(1)}, f32[1,128,128]{1,2,0:T(8,128)S(1)}, u32[]{:S(2)}, u32[]{:S(2)}) collective-permute-start(f32[1,128,128]{1,2,0:T(8,128)S(1)} %get-tuple-element.35), channel_id=1, source_target_pairs={{0,8},{2,10},{4,12},{6,14},{8,0},{10,2},{12,4},{14,6},{16,24},{18,... | collective-permute-start | bytes 196616 | tf_op jit(solution)/shard_map/ppermute | solution.py:196
  66.1 6.6 %copy-start.10 = (f32[4,128,256]{1,2,0:T(8,128)S(1)}, f32[4,128,256]{1,2,0:T(8,128)}, u32[]{:S(2)}) copy-start(f32[4,128,256]{1,2,0:T(8,128)} %copy-done.9) | copy-start | bytes 1572868
  67.3 5.8 %copy-start.1 = (f32[8,2,128,128]{3,2,1,0:T(8,128)S(1)}, f32[8,2,128,128]{3,2,1,0:T(8,128)}, u32[]{:S(2)}) copy-start(f32[8,2,128,128]{3,2,1,0:T(8,128)} %copy-done) | copy-start | bytes 3145732
  67.6 5.0 %collective-permute-start.10 = (f32[2,128,128]{1,2,0:T(8,128)S(1)}, f32[2,128,128]{1,2,0:T(8,128)S(1)}, u32[]{:S(2)}, u32[]{:S(2)}) collective-permute-start(f32[2,128,128]{1,2,0:T(8,128)S(1)} %get-tuple-element.29), channel_id=1, source_target_pairs={{0,4},{2,6},{4,0},{6,2},{8,12},{10,14},{12,8},{14,10},{16,20},{18,... | collective-permute-start | bytes 393224 | tf_op jit(solution)/shard_map/ppermute | solution.py:196
  73.1 1.6 %collective-permute-start.11 = (f32[4,128,128]{1,2,0:T(8,128)S(1)}, f32[4,128,128]{1,2,0:T(8,128)S(1)}, u32[]{:S(2)}, u32[]{:S(2)}) collective-permute-start(f32[4,128,128]{1,2,0:T(8,128)S(1)} %get-tuple-element.21), channel_id=1, source_target_pairs={{0,2},{2,0},{4,6},{6,4},{8,10},{10,8},{12,14},{14,12},{16,18},{18,... | collective-permute-start | bytes 786440 | tf_op jit(solution)/shard_map/ppermute | solution.py:196
  74.7 1.7 %copy-start.12 = (bf16[128]{0:T(256)(128)(2,1)S(1)}, bf16[128]{0:T(256)(128)(2,1)}, u32[]{:S(2)}) copy-start(bf16[128]{0:T(256)(128)(2,1)} %param.13) | copy-start | bytes 772
  75.8 8.4 %collective-permute-start.12 = (bf16[128,1024]{0,1:T(8,128)(2,1)S(1)}, bf16[128,1024]{0,1:T(8,128)(2,1)S(1)}, u32[]{:S(2)}, u32[]{:S(2)}) collective-permute-start(bf16[128,1024]{0,1:T(8,128)(2,1)S(1)} %bitcast.118), channel_id=1, source_target_pairs={{0,1},{1,0},{2,3},{3,2},{4,5},{5,4},{6,7},{7,6},{8,9},{9,8},{10,11... | collective-permute-start | bytes 786440 | tf_op jit(solution)/shard_map/ppermute | solution.py:227
  84.3 1.0 %copy-start.11 = (bf16[128,2048]{1,0:T(8,128)(2,1)S(1)}, bf16[128,2048]{1,0:T(8,128)(2,1)}, u32[]{:S(2)}) copy-start(bf16[128,2048]{1,0:T(8,128)(2,1)} %param.10) | copy-start | bytes 1572868

commit v5 on v4

--- a/solution.py
+++ b/solution.py
@@ -213,8 +213,9 @@
 def head_swap(rows):
     width = rows.shape[1] // 2
     first = lax.axis_index("head") == 0
-    own = jnp.where(first, rows[:, :width], rows[:, width:])
-    sent = jnp.where(first, rows[:, width:], rows[:, :width])
+    half = lax.axis_index("head")
+    own = lax.dynamic_slice_in_dim(rows, half * width, width, 1)
+    sent = lax.dynamic_slice_in_dim(rows, (1 - half) * width, width, 1)
     got = lax.ppermute(sent, "head", [(0, 1), (1, 0)])
     return jnp.where(first, jnp.concatenate([own, got], 0), jnp.concatenate([got, own], 0))
 

time: 86.8 us -> 87.1 us (level)
  local copies, waits for them, and re-layouts: 2.52 us -> 7.64 us
  other arithmetic: 17.6 us -> 12.7 us
    select_n x5 -> x0, other arithmetic: 5.14 us -> none  [head_swap(): own = jnp.where(first, rows[:, :width], rows[:, width:])]
    dynamic_slice x0 -> x5, local copies, waits for them, and re-layouts: none -> 5.12 us  [head_swap(): own = lax.dynamic_slice_in_dim(rows, half * width, width, 1)]
  transfers between devices with their start and end apart: 13 -> 13, of which waited for: 8 -> 8; matrix products, arithmetic and copies ran while one was open for 16% -> 17% of each run, Pallas kernels for 0% -> 0%
where the time goes in v5:
time: 87.1 us; the launch traced here: 86.8 us
  waiting for transfers between devices  26.8 us (31%)
  matrix products  19.8 us (23%)
  starting transfers between devices  19.2 us (22%)
  other arithmetic  12.7 us (15%)
  local copies, waits for them, and re-layouts  7.64 us (9%)
    ppermute x6, waiting for transfers between devices, chain_states(): got = lax.ppermute(other, 'ctx', [(i, i ^ stride) for i in range(size)])  17.5 us
    ppermute x1, waiting for transfers between devices, head_return(): got = lax.ppermute(sent, 'head', [(0, 1), (1, 0)])  7.86 us
    ppermute x5, starting transfers between devices, head_swap(): got = lax.ppermute(sent, 'head', [(0, 1), (1, 0)])  7.15 us
    ppermute x6, starting transfers between devices, chain_states(): got = lax.ppermute(other, 'ctx', [(i, i ^ stride) for i in range(size)])  7.03 us
    dot_general x5, matrix products, unit_lower_inverse(): jnp.matmul(jnp.concatenate([inverse, power], axis=-2), power, precision=L...  5.37 us
    dynamic_slice x5, local copies, waits for them, and re-layouts, head_swap(): own = lax.dynamic_slice_in_dim(rows, half * width, width, 1)  5.12 us
    ppermute x1, starting transfers between devices, exclusive_scan(): return lax.ppermute(write, 'ctx', near)  4.5 us
    select_n x3, other arithmetic, chain_states(): later = jnp.where(upper, mine, got)  2.8 us
  transfers between devices with their start and end apart: 13, of which 8 were waited for; matrix products, arithmetic and copies ran while one was open for 17% of the time, Pallas kernels for 0%

profile of v5, /device:TPU:0, one launch (start us, length us, event | category | flops | bytes accessed | tf_op | source)
XLA Modules:
  0.0 86.8 jit_solution(16887313011713065913)
XLA Ops:
  1.0 3.0 %collective-permute-start = (bf16[128,512]{1,0:T(8,128)(2,1)S(1)}, bf16[128,512]{1,0:T(8,128)(2,1)S(1)}, u32[]{:S(2)}, u32[]{:S(2)}) collective-permute-start(bf16[128,512]{1,0:T(8,128)(2,1)S(1)} %get-tuple-element.34), channel_id=1, source_target_pairs={{0,1},{1,0},{2,3},{3,2},{4,5},{5,4},{6,7},{7,6},{8,9},{9,8},{10,11... | collective-permute-start | bytes 393224 | tf_op jit(solution)/shard_map/ppermute | solution.py:219
  5.8 2.0 %collective-permute-start.2 = (bf16[128,8]{0,1:T(8,128)(2,1)S(1)}, bf16[128,8]{0,1:T(8,128)(2,1)S(1)}, u32[]{:S(2)}, u32[]{:S(2)}) collective-permute-start(bf16[128,8]{0,1:T(8,128)(2,1)S(1)} %get-tuple-element.45), channel_id=1, source_target_pairs={{0,1},{1,0},{2,3},{3,2},{4,5},{5,4},{6,7},{7,6},{8,9},{9,8},{10,11... | collective-permute-start | bytes 6152 | tf_op jit(solution)/shard_map/ppermute | solution.py:219
  8.5 1.8 %constant_dynamic-slice_fusion.1 = (bf16[128,1024]{1,0:T(8,128)(2,1)S(1)}, bf16[128,1024]{1,0:T(8,128)(2,1)}) fusion(bf16[128,2048]{1,0:T(8,128)(2,1)} %param.9, s32[]{:T(128)S(6)} %select_n.252, s32[]{:T(128)S(6)} %select_n.253), kind=kLoop, calls=%fused_computation.172 | loop fusion | bytes 1048584 | tf_op jit(solution)/shard_map/dynamic_slice | solution.py:217
  10.3 2.0 %collective-permute-start.4 = (bf16[128,1024]{1,0:T(8,128)(2,1)}, bf16[128,1024]{1,0:T(8,128)(2,1)}, u32[]{:S(2)}, u32[]{:S(2)}) collective-permute-start(bf16[128,1024]{1,0:T(8,128)(2,1)} %get-tuple-element.26), channel_id=1, source_target_pairs={{0,1},{1,0},{2,3},{3,2},{4,5},{5,4},{6,7},{7,6},{8,9},{9,8},{10,11... | collective-permute-start | bytes 786440 | tf_op jit(solution)/shard_map/ppermute | solution.py:219
  17.3 1.1 %fusion = f32[8,2,256,128]{3,2,1,0:T(8,128)S(1)} fusion(f32[8,2,128,128]{3,2,1,0:T(8,128)S(1)} %fusion.94, f32[8,2,128,128]{3,2,1,0:T(8,128)S(1)} %get-tuple-element.17), kind=kOutput, calls=%fused_computation | convolution fusion | flops 403177472 | bytes 4194304 | tf_op jit(solution)/shard_map/dot_general | solution.py:58
  19.7 1.2 %convert_bitcast_fusion = f32[32,8,8,128]{3,1,2,0:T(8,128)S(1)} fusion(bf16[128,1024]{1,0:T(8,128)(2,1)} %collective-permute-done.4, bf16[128,1024]{1,0:T(8,128)(2,1)S(1)} %get-tuple-element.25, pred[]{:T(512)S(6)} %eq.31), kind=kLoop, calls=%fused_computation.72 | loop fusion | flops 2621440 | bytes 1572865
  22.1 1.1 %fusion.4 = f32[8,2,256,128]{3,2,1,0:T(8,128)S(1)} fusion(f32[8,2,128,128]{3,2,1,0:T(8,128)S(1)} %get-tuple-element.12, f32[8,2,128,128]{3,2,1,0:T(8,128)S(1)} %get-tuple-element.11), kind=kOutput, calls=%fused_computation.4 | convolution fusion | flops 403177472 | bytes 4194304 | tf_op jit(solution)/shard_map/dot_general | solution.py:58
  23.4 1.1 %fusion.8 = f32[8,2,256,128]{3,2,1,0:T(8,128)S(1)} fusion(f32[8,2,128,128]{3,2,1,0:T(8,128)S(1)} %get-tuple-element.10, f32[8,2,128,128]{3,2,1,0:T(8,128)S(1)} %get-tuple-element.9), kind=kOutput, calls=%fused_computation.8 | convolution fusion | flops 403177472 | bytes 4194304 | tf_op jit(solution)/shard_map/dot_general | solution.py:58
  24.8 1.1 %fusion.12 = f32[8,2,256,128]{3,2,1,0:T(8,128)S(1)} fusion(f32[8,2,128,128]{3,2,1,0:T(8,128)S(1)} %get-tuple-element.8, f32[8,2,128,128]{3,2,1,0:T(8,128)S(1)} %get-tuple-element.7), kind=kOutput, calls=%fused_computation.12 | convolution fusion | flops 403177472 | bytes 4194304 | tf_op jit(solution)/shard_map/dot_general | solution.py:58
  26.1 1.1 %fusion.16 = f32[8,2,256,128]{3,2,1,0:T(8,128)S(1)} fusion(f32[8,2,128,128]{3,2,1,0:T(8,128)S(1)} %get-tuple-element.6, f32[8,2,128,128]{3,2,1,0:T(8,128)S(1)} %get-tuple-element.5), kind=kOutput, calls=%fused_computation.16 | convolution fusion | flops 403177472 | bytes 4194304 | tf_op jit(solution)/shard_map/dot_general | solution.py:58
  27.9 1.2 %fusion.20 = f32[8,2,128,256]{3,2,1,0:T(8,128)S(1)} fusion(f32[8,2,128,128]{3,2,1,0:T(8,128)S(1)} %convolution_add_fusion, f32[8,2,128,128]{3,2,1,0:T(8,128)S(1)} %get-tuple-element.24, f32[8,2,128,128]{3,2,1,0:T(8,128)S(1)} %get-tuple-element.40), kind=kOutput, calls=%fused_computation.20 | convolution fusion | flops 403177472 | bytes 5242880 | tf_op jit(solution)/shard_map/dot_general | solution.py:86
  29.2 1.0 %fusion.44 = f32[8,2,128,128]{2,3,1,0:T(8,128)S(1)} fusion(f32[8,2,128,128]{3,2,1,0:T(8,128)S(1)} %get-tuple-element.23, f32[8,2,128,256]{3,2,1,0:T(8,128)S(1)} %fusion.20), kind=kOutput, calls=%fused_computation.76 | convolution fusion | flops 201326592 | bytes 3145728 | tf_op jit(solution)/shard_map/hmck,hmcv->hmkv/dot_general | solution.py:94
  30.2 1.1 %convolution_subtract_fusion = f32[8,2,128,128]{3,2,1,0:T(8,128)S(1)} fusion(f32[8,2,128,128]{3,2,1,0:T(8,128)S(1)} %get-tuple-element.23, f32[8,2,128,256]{3,2,1,0:T(8,128)S(1)} %fusion.20, f32[8,2]{1,0:T(8,128)S(1)} %copy.81, f32[128,128]{1,0:T(8,128)S(1)} %get-tuple-element.49), kind=kOutput, calls=%fused_computation.30 | convolution fusion | flops 201850880 | bytes 3215360 | tf_op jit(solution)/shard_map/hmck,hmcj->hmkj/dot_general | solution.py:91
  31.3 1.0 %fusion.56 = f32[8,128,128]{1,2,0:T(8,128)S(1)} fusion(f32[8,2,128,128]{3,2,1,0:T(8,128)S(1)} %convolution_subtract_fusion), kind=kOutput, calls=%fused_computation.105 | convolution fusion | flops 201326592 | bytes 1572864 | tf_op jit(solution)/shard_map/dot_general | solution.py:21
  32.4 1.2 %convolution_add_fusion.2 = f32[8,128,128]{1,2,0:T(8,128)S(1)} fusion(f32[8,2,128,128]{2,3,1,0:T(8,128)S(1)} %fusion.44, f32[8,2,128,128]{3,2,1,0:T(8,128)S(1)} %convolution_subtract_fusion), kind=kOutput, calls=%fused_computation.38 | convolution fusion | flops 201457664 | bytes 2097152 | tf_op jit(solution)/shard_map/dot_general | solution.py:22
  34.6 2.2 %collective-permute-done.5 = f32[4,128,256]{1,2,0:T(8,128)} collective-permute-done((f32[4,128,256]{1,2,0:T(8,128)}, f32[4,128,256]{1,2,0:T(8,128)}, u32[]{:S(2)}, u32[]{:S(2)}) %collective-permute-start.5) | collective-permute-done | bytes 524320 | tf_op jit(solution)/shard_map/ppermute | solution.py:183
  36.9 1.6 %broadcast_select_fusion.1 = (f32[4,128,256]{1,2,0:T(8,128)S(1)}, f32[4,128,256]{1,2,0:T(8,128)S(1)}) fusion(f32[4,128,256]{1,2,0:T(8,128)} %collective-permute-done.5, pred[]{:T(512)S(6)} %eq.33, f32[8,128,128]{1,2,0:T(8,128)} %copy-done.5, f32[8,128,128]{1,2,0:T(8,128)} %copy-done.4), kind=kLoop, calls=%fused_computation.117 | loop fusion | flops 917504 | bytes 2621441 | tf_op jit(solution)/shard_map/jit(_where)/select_n | solution.py:185
  40.7 1.5 %collective-permute-start.6 = (f32[2,128,256]{1,2,0:T(8,128)}, f32[2,128,256]{1,2,0:T(8,128)}, u32[]{:S(2)}, u32[]{:S(2)}) collective-permute-start(f32[2,128,256]{1,2,0:T(8,128)} %broadcast_select_fusion.7), channel_id=1, source_target_pairs={{0,4},{2,6},{4,0},{6,2},{8,12},{10,14},{12,8},{14,10},{16,20},{18,... | collective-permute-start | bytes 786440 | tf_op jit(solution)/shard_map/ppermute | solution.py:183
  42.2 7.2 %collective-permute-done.6 = f32[2,128,256]{1,2,0:T(8,128)} collective-permute-done((f32[2,128,256]{1,2,0:T(8,128)}, f32[2,128,256]{1,2,0:T(8,128)}, u32[]{:S(2)}, u32[]{:S(2)}) %collective-permute-start.6) | collective-permute-done | bytes 262176 | tf_op jit(solution)/shard_map/ppermute | solution.py:183
  49.4 1.2 %broadcast_select_fusion.6 = (f32[2,128,256]{1,2,0:T(8,128)S(1)}, f32[2,128,256]{1,2,0:T(8,128)S(1)}) fusion(f32[2,128,256]{1,2,0:T(8,128)} %collective-permute-done.6, pred[]{:T(512)S(6)} %eq.34, f32[4,128,128]{1,2,0:T(8,128)} %copy-done.8, f32[4,128,128]{1,2,0:T(8,128)S(1)} %fusion.63), kind=kLoop, calls=%fused_computation.134 | loop fusion | flops 458752 | bytes 1310721 | tf_op jit(solution)/shard_map/jit(_where)/select_n | solution.py:185
  51.1 1.9 %collective-permute-start.7 = (f32[1,128,256]{1,2,0:T(8,128)S(1)}, f32[1,128,256]{1,2,0:T(8,128)S(1)}, u32[]{:S(2)}, u32[]{:S(2)}) collective-permute-start(f32[1,128,256]{1,2,0:T(8,128)S(1)} %broadcast_select_fusion.13), channel_id=1, source_target_pairs={{0,8},{2,10},{4,12},{6,14},{8,0},{10,2},{12,4},{14,6},{16,24},{18,... | collective-permute-start | bytes 393224 | tf_op jit(solution)/shard_map/ppermute | solution.py:183
  53.4 3.0 %collective-permute-done.7 = f32[1,128,256]{1,2,0:T(8,128)S(1)} collective-permute-done((f32[1,128,256]{1,2,0:T(8,128)S(1)}, f32[1,128,256]{1,2,0:T(8,128)S(1)}, u32[]{:S(2)}, u32[]{:S(2)}) %collective-permute-start.7) | collective-permute-done | bytes 131104 | tf_op jit(solution)/shard_map/ppermute | solution.py:183
  56.6 4.5 %collective-permute-start.8 = (f32[1,128,128]{1,2,0:T(8,128)S(1)}, f32[1,128,128]{1,2,0:T(8,128)S(1)}, u32[]{:S(2)}, u32[]{:S(2)}) collective-permute-start(f32[1,128,128]{1,2,0:T(8,128)S(1)} %fusion.27), channel_id=1, source_target_pairs={{0,16},{2,18},{4,20},{6,22},{8,24},{10,26},{12,28},{14,30},{1,17},... | collective-permute-start | bytes 196616 | tf_op jit(solution)/shard_map/ppermute | solution.py:161
  61.7 1.4 %collective-permute-done.8 = f32[1,128,128]{1,2,0:T(8,128)S(1)} collective-permute-done((f32[1,128,128]{1,2,0:T(8,128)S(1)}, f32[1,128,128]{1,2,0:T(8,128)S(1)}, u32[]{:S(2)}, u32[]{:S(2)}) %collective-permute-start.8) | collective-permute-done | bytes 65568 | tf_op jit(solution)/shard_map/ppermute | solution.py:161
  63.3 2.0 %collective-permute-start.9 = (f32[1,128,128]{1,2,0:T(8,128)S(1)}, f32[1,128,128]{1,2,0:T(8,128)S(1)}, u32[]{:S(2)}, u32[]{:S(2)}) collective-permute-start(f32[1,128,128]{1,2,0:T(8,128)S(1)} %get-tuple-element.35), channel_id=1, source_target_pairs={{0,8},{2,10},{4,12},{6,14},{8,0},{10,2},{12,4},{14,6},{16,24},{18,... | collective-permute-start | bytes 196616 | tf_op jit(solution)/shard_map/ppermute | solution.py:196
  66.4 1.3 %collective-permute-done.9 = f32[1,128,128]{1,2,0:T(8,128)S(1)} collective-permute-done((f32[1,128,128]{1,2,0:T(8,128)S(1)}, f32[1,128,128]{1,2,0:T(8,128)S(1)}, u32[]{:S(2)}, u32[]{:S(2)}) %collective-permute-start.9) | collective-permute-done | bytes 65568 | tf_op jit(solution)/shard_map/ppermute | solution.py:196
  67.9 1.6 %collective-permute-start.10 = (f32[2,128,128]{1,2,0:T(8,128)S(1)}, f32[2,128,128]{1,2,0:T(8,128)S(1)}, u32[]{:S(2)}, u32[]{:S(2)}) collective-permute-start(f32[2,128,128]{1,2,0:T(8,128)S(1)} %get-tuple-element.29), channel_id=1, source_target_pairs={{0,4},{2,6},{4,0},{6,2},{8,12},{10,14},{12,8},{14,10},{16,20},{18,... | collective-permute-start | bytes 393224 | tf_op jit(solution)/shard_map/ppermute | solution.py:196
  70.2 2.8 %collective-permute-done.10 = f32[2,128,128]{1,2,0:T(8,128)S(1)} collective-permute-done((f32[2,128,128]{1,2,0:T(8,128)S(1)}, f32[2,128,128]{1,2,0:T(8,128)S(1)}, u32[]{:S(2)}, u32[]{:S(2)}) %collective-permute-start.10) | collective-permute-done | bytes 131104 | tf_op jit(solution)/shard_map/ppermute | solution.py:196
  74.0 1.0 %collective-permute-done.11 = f32[4,128,128]{1,2,0:T(8,128)S(1)} collective-permute-done((f32[4,128,128]{1,2,0:T(8,128)S(1)}, f32[4,128,128]{1,2,0:T(8,128)S(1)}, u32[]{:S(2)}, u32[]{:S(2)}) %collective-permute-start.11) | collective-permute-done | bytes 262176 | tf_op jit(solution)/shard_map/ppermute | solution.py:196
  75.0 1.2 %fusion.25 = bf16[2,128,8,128]{1,3,2,0:T(8,128)(2,1)S(1)} fusion(f32[8,1,128,128]{2,3,0,1:T(8,128)S(1)} %fusion.26, f32[8,1,128,128]{2,3,0,1:T(8,128)S(1)} %slice_bitcast_fusion.6, f32[4,128,128]{1,2,0:T(8,128)S(1)} %get-tuple-element.22, f32[4,128,128]{1,2,0:T(8,128)S(1)} %collective-permute-done.11, pred[]{:T(512)S(6)} %eq.33, ...), kind=kOutput, calls=%fused_computation.37 | convolution fusion | flops 404094976 | bytes 3145729 | tf_op jit(solution)/shard_map/hmck,hkv->hmcv/dot_general | solution.py:129
  76.8 7.9 %collective-permute-done.12 = bf16[128,1024]{0,1:T(8,128)(2,1)S(1)} collective-permute-done((bf16[128,1024]{0,1:T(8,128)(2,1)S(1)}, bf16[128,1024]{0,1:T(8,128)(2,1)S(1)}, u32[]{:S(2)}, u32[]{:S(2)}) %collective-permute-start.12) | collective-permute-done | bytes 262176 | tf_op jit(solution)/shard_map/ppermute | solution.py:228
  85.7 1.1 %fusion.41 = bf16[128,2048]{1,0:T(8,128)(2,1)} fusion(bf16[128,2048]{1,0:T(8,128)(2,1)S(1)} %copy-done.11, f32[128,2048]{1,0:T(8,128)S(1)} %copy.97, f32[2048]{0:T(1024)S(1)} %broadcast_bitcast_fusion), kind=kLoop, calls=%fused_computation.73 | loop fusion | flops 2097152 | bytes 2105344 | tf_op jit(solution)/shard_map/convert_element_type | solution.py:210
  (102 shorter events, 21.9 us)
Async XLA Ops:
  1.0 12.4 %collective-permute-start = (bf16[128,512]{1,0:T(8,128)(2,1)S(1)}, bf16[128,512]{1,0:T(8,128)(2,1)S(1)}, u32[]{:S(2)}, u32[]{:S(2)}) collective-permute-start(bf16[128,512]{1,0:T(8,128)(2,1)S(1)} %get-tuple-element.34), channel_id=1, source_target_pairs={{0,1},{1,0},{2,3},{3,2},{4,5},{5,4},{6,7},{7,6},{8,9},{9,8},{10,11... | collective-permute-start | bytes 393224 | tf_op jit(solution)/shard_map/ppermute | solution.py:219
  5.0 8.3 %collective-permute-start.1 = (bf16[128,512]{1,0:T(8,128)(2,1)S(1)}, bf16[128,512]{1,0:T(8,128)(2,1)S(1)}, u32[]{:S(2)}, u32[]{:S(2)}) collective-permute-start(bf16[128,512]{1,0:T(8,128)(2,1)S(1)} %get-tuple-element.32), channel_id=1, source_target_pairs={{0,1},{1,0},{2,3},{3,2},{4,5},{5,4},{6,7},{7,6},{8,9},{9,8},{10,11... | collective-permute-start | bytes 393224 | tf_op jit(solution)/shard_map/ppermute | solution.py:219
  5.8 6.6 %collective-permute-start.2 = (bf16[128,8]{0,1:T(8,128)(2,1)S(1)}, bf16[128,8]{0,1:T(8,128)(2,1)S(1)}, u32[]{:S(2)}, u32[]{:S(2)}) collective-permute-start(bf16[128,8]{0,1:T(8,128)(2,1)S(1)} %get-tuple-element.45), channel_id=1, source_target_pairs={{0,1},{1,0},{2,3},{3,2},{4,5},{5,4},{6,7},{7,6},{8,9},{9,8},{10,11... | collective-permute-start | bytes 6152 | tf_op jit(solution)/shard_map/ppermute | solution.py:219
  8.5 4.6 %collective-permute-start.3 = (bf16[128,8]{0,1:T(8,128)(2,1)S(1)}, bf16[128,8]{0,1:T(8,128)(2,1)S(1)}, u32[]{:S(2)}, u32[]{:S(2)}) collective-permute-start(bf16[128,8]{0,1:T(8,128)(2,1)S(1)} %get-tuple-element.43), channel_id=1, source_target_pairs={{0,1},{1,0},{2,3},{3,2},{4,5},{5,4},{6,7},{7,6},{8,9},{9,8},{10,11... | collective-permute-start | bytes 6152 | tf_op jit(solution)/shard_map/ppermute | solution.py:219
  10.3 9.4 %collective-permute-start.4 = (bf16[128,1024]{1,0:T(8,128)(2,1)}, bf16[128,1024]{1,0:T(8,128)(2,1)}, u32[]{:S(2)}, u32[]{:S(2)}) collective-permute-start(bf16[128,1024]{1,0:T(8,128)(2,1)} %get-tuple-element.26), channel_id=1, source_target_pairs={{0,1},{1,0},{2,3},{3,2},{4,5},{5,4},{6,7},{7,6},{8,9},{9,8},{10,11... | collective-permute-start | bytes 786440 | tf_op jit(solution)/shard_map/ppermute | solution.py:219
  16.1 2.9 %copy-start.2 = (f32[4,2,128,128]{3,0,2,1:T(4,128)}, f32[4,2,128,128]{3,0,2,1:T(4,128)S(1)}, u32[]{:S(2)}) copy-start(f32[4,2,128,128]{3,0,2,1:T(4,128)S(1)} %multiply_bitcast_fusion.1) | copy-start | bytes 1572868
  30.2 2.2 %copy-start.6 = (f32[8,2,128,128]{2,3,1,0:T(8,128)}, f32[8,2,128,128]{2,3,1,0:T(8,128)S(1)}, u32[]{:S(2)}) copy-start(f32[8,2,128,128]{2,3,1,0:T(8,128)S(1)} %fusion.44) | copy-start | bytes 3145732
  31.3 3.2 %copy-start = (f32[8,2,128,128]{3,2,1,0:T(8,128)}, f32[8,2,128,128]{3,2,1,0:T(8,128)S(1)}, u32[]{:S(2)}) copy-start(f32[8,2,128,128]{3,2,1,0:T(8,128)S(1)} %convolution_subtract_fusion) | copy-start | bytes 3145732
  32.4 1.2 %copy-start.4 = (f32[8,128,128]{1,2,0:T(8,128)}, f32[8,128,128]{1,2,0:T(8,128)S(1)}, u32[]{:S(2)}) copy-start(f32[8,128,128]{1,2,0:T(8,128)S(1)} %fusion.56) | copy-start | bytes 1572868
  33.6 1.0 %copy-start.5 = (f32[8,128,128]{1,2,0:T(8,128)}, f32[8,128,128]{1,2,0:T(8,128)S(1)}, u32[]{:S(2)}) copy-start(f32[8,128,128]{1,2,0:T(8,128)S(1)} %convolution_add_fusion.2) | copy-start | bytes 1572868
  34.6 2.3 %collective-permute-start.5 = (f32[4,128,256]{1,2,0:T(8,128)}, f32[4,128,256]{1,2,0:T(8,128)}, u32[]{:S(2)}, u32[]{:S(2)}) collective-permute-start(f32[4,128,256]{1,2,0:T(8,128)} %broadcast_select_fusion.2), channel_id=1, source_target_pairs={{0,2},{2,0},{4,6},{6,4},{8,10},{10,8},{12,14},{14,12},{16,18},{18,... | collective-permute-start | bytes 1572872 | tf_op jit(solution)/shard_map/ppermute | solution.py:183
  38.5 2.2 %copy-start.9 = (f32[4,128,256]{1,2,0:T(8,128)}, f32[4,128,256]{1,2,0:T(8,128)S(1)}, u32[]{:S(2)}) copy-start(f32[4,128,256]{1,2,0:T(8,128)S(1)} %get-tuple-element.14) | copy-start | bytes 1572868
  39.3 0.7 copy-start.8
  40.7 8.7 %collective-permute-start.6 = (f32[2,128,256]{1,2,0:T(8,128)}, f32[2,128,256]{1,2,0:T(8,128)}, u32[]{:S(2)}, u32[]{:S(2)}) collective-permute-start(f32[2,128,256]{1,2,0:T(8,128)} %broadcast_select_fusion.7), channel_id=1, source_target_pairs={{0,4},{2,6},{4,0},{6,2},{8,12},{10,14},{12,8},{14,10},{16,20},{18,... | collective-permute-start | bytes 786440 | tf_op jit(solution)/shard_map/ppermute | solution.py:183
  42.2 10.8 %copy-start.3 = (f32[4,2,128,128]{3,0,2,1:T(4,128)S(1)}, f32[4,2,128,128]{3,0,2,1:T(4,128)}, u32[]{:S(2)}) copy-start(f32[4,2,128,128]{3,0,2,1:T(4,128)} %copy-done.2) | copy-start | bytes 1572868
  51.1 5.3 %collective-permute-start.7 = (f32[1,128,256]{1,2,0:T(8,128)S(1)}, f32[1,128,256]{1,2,0:T(8,128)S(1)}, u32[]{:S(2)}, u32[]{:S(2)}) collective-permute-start(f32[1,128,256]{1,2,0:T(8,128)S(1)} %broadcast_select_fusion.13), channel_id=1, source_target_pairs={{0,8},{2,10},{4,12},{6,14},{8,0},{10,2},{12,4},{14,6},{16,24},{18,... | collective-permute-start | bytes 393224 | tf_op jit(solution)/shard_map/ppermute | solution.py:183
  56.6 6.5 %collective-permute-start.8 = (f32[1,128,128]{1,2,0:T(8,128)S(1)}, f32[1,128,128]{1,2,0:T(8,128)S(1)}, u32[]{:S(2)}, u32[]{:S(2)}) collective-permute-start(f32[1,128,128]{1,2,0:T(8,128)S(1)} %fusion.27), channel_id=1, source_target_pairs={{0,16},{2,18},{4,20},{6,22},{8,24},{10,26},{12,28},{14,30},{1,17},... | collective-permute-start | bytes 196616 | tf_op jit(solution)/shard_map/ppermute | solution.py:161
  61.7 7.8 %copy-start.7 = (f32[8,2,128,128]{2,3,1,0:T(8,128)S(1)}, f32[8,2,128,128]{2,3,1,0:T(8,128)}, u32[]{:S(2)}) copy-start(f32[8,2,128,128]{2,3,1,0:T(8,128)} %copy-done.6) | copy-start | bytes 3145732
  63.3 4.3 %collective-permute-start.9 = (f32[1,128,128]{1,2,0:T(8,128)S(1)}, f32[1,128,128]{1,2,0:T(8,128)S(1)}, u32[]{:S(2)}, u32[]{:S(2)}) collective-permute-start(f32[1,128,128]{1,2,0:T(8,128)S(1)} %get-tuple-element.35), channel_id=1, source_target_pairs={{0,8},{2,10},{4,12},{6,14},{8,0},{10,2},{12,4},{14,6},{16,24},{18,... | collective-permute-start | bytes 196616 | tf_op jit(solution)/shard_map/ppermute | solution.py:196
  66.4 6.6 %copy-start.10 = (f32[4,128,256]{1,2,0:T(8,128)S(1)}, f32[4,128,256]{1,2,0:T(8,128)}, u32[]{:S(2)}) copy-start(f32[4,128,256]{1,2,0:T(8,128)} %copy-done.9) | copy-start | bytes 1572868
  67.7 5.8 %copy-start.1 = (f32[8,2,128,128]{3,2,1,0:T(8,128)S(1)}, f32[8,2,128,128]{3,2,1,0:T(8,128)}, u32[]{:S(2)}) copy-start(f32[8,2,128,128]{3,2,1,0:T(8,128)} %copy-done) | copy-start | bytes 3145732
  67.9 5.0 %collective-permute-start.10 = (f32[2,128,128]{1,2,0:T(8,128)S(1)}, f32[2,128,128]{1,2,0:T(8,128)S(1)}, u32[]{:S(2)}, u32[]{:S(2)}) collective-permute-start(f32[2,128,128]{1,2,0:T(8,128)S(1)} %get-tuple-element.29), channel_id=1, source_target_pairs={{0,4},{2,6},{4,0},{6,2},{8,12},{10,14},{12,8},{14,10},{16,20},{18,... | collective-permute-start | bytes 393224 | tf_op jit(solution)/shard_map/ppermute | solution.py:196
  73.4 1.6 %collective-permute-start.11 = (f32[4,128,128]{1,2,0:T(8,128)S(1)}, f32[4,128,128]{1,2,0:T(8,128)S(1)}, u32[]{:S(2)}, u32[]{:S(2)}) collective-permute-start(f32[4,128,128]{1,2,0:T(8,128)S(1)} %get-tuple-element.21), channel_id=1, source_target_pairs={{0,2},{2,0},{4,6},{6,4},{8,10},{10,8},{12,14},{14,12},{16,18},{18,... | collective-permute-start | bytes 786440 | tf_op jit(solution)/shard_map/ppermute | solution.py:196
  75.0 1.8 %copy-start.12 = (bf16[128]{0:T(256)(128)(2,1)S(1)}, bf16[128]{0:T(256)(128)(2,1)}, u32[]{:S(2)}) copy-start(bf16[128]{0:T(256)(128)(2,1)} %param.13) | copy-start | bytes 772
  76.2 8.4 %collective-permute-start.12 = (bf16[128,1024]{0,1:T(8,128)(2,1)S(1)}, bf16[128,1024]{0,1:T(8,128)(2,1)S(1)}, u32[]{:S(2)}, u32[]{:S(2)}) collective-permute-start(bf16[128,1024]{0,1:T(8,128)(2,1)S(1)} %bitcast.118), channel_id=1, source_target_pairs={{0,1},{1,0},{2,3},{3,2},{4,5},{5,4},{6,7},{7,6},{8,9},{9,8},{10,11... | collective-permute-start | bytes 786440 | tf_op jit(solution)/shard_map/ppermute | solution.py:228
  84.6 1.0 %copy-start.11 = (bf16[128,2048]{1,0:T(8,128)(2,1)S(1)}, bf16[128,2048]{1,0:T(8,128)(2,1)}, u32[]{:S(2)}) copy-start(bf16[128,2048]{1,0:T(8,128)(2,1)} %param.10) | copy-start | bytes 1572868

commit v6 on v4

--- a/solution.py
+++ b/solution.py
@@ -8,7 +8,7 @@
 SPAN = 128
 
 
-FULL_PRECISION = lax.Precision.HIGHEST
+FULL_PRECISION = lax.Precision.HIGH
 LOCAL_PRECISION = lax.Precision.HIGH
 
 

time: 86.8 us -> 84.6 us (0.975)
  matrix products: 19.7 us -> 17.6 us
  transfers between devices with their start and end apart: 13 -> 13, of which waited for: 8 -> 8; matrix products, arithmetic and copies ran while one was open for 16% -> 17% of each run, Pallas kernels for 0% -> 0%
where the time goes in v6:
time: 84.6 us; the launch traced here: 84.2 us
  waiting for transfers between devices  26.5 us (31%)
  starting transfers between devices  19.3 us (23%)
  other arithmetic  17.6 us (21%)
  matrix products  17.6 us (21%)
  local copies, waits for them, and re-layouts  2.64 us (3%)
    ppermute x6, waiting for transfers between devices, chain_states(): got = lax.ppermute(other, 'ctx', [(i, i ^ stride) for i in range(size)])  17.5 us
    ppermute x1, waiting for transfers between devices, head_return(): got = lax.ppermute(sent, 'head', [(0, 1), (1, 0)])  7.83 us
    ppermute x5, starting transfers between devices, head_swap(): got = lax.ppermute(sent, 'head', [(0, 1), (1, 0)])  7.15 us
    ppermute x6, starting transfers between devices, chain_states(): got = lax.ppermute(other, 'ctx', [(i, i ^ stride) for i in range(size)])  6.8 us
    dot_general x5, matrix products, unit_lower_inverse(): jnp.matmul(jnp.concatenate([inverse, power], axis=-2), power, precision=L...  5.3 us
    select_n x5, other arithmetic, head_swap(): own = jnp.where(first, rows[:, :width], rows[:, width:])  5.14 us
    ppermute x1, starting transfers between devices, exclusive_scan(): return lax.ppermute(write, 'ctx', near)  4.74 us
    select_n x3, other arithmetic, chain_states(): later = jnp.where(upper, mine, got)  2.8 us
  transfers between devices with their start and end apart: 13, of which 8 were waited for; matrix products, arithmetic and copies ran while one was open for 17% of the time, Pallas kernels for 0%

profile of v6, /device:TPU:0, one launch (start us, length us, event | category | flops | bytes accessed | tf_op | source)
XLA Modules:
  0.0 84.2 jit_solution(13444849533097280441)
XLA Ops:
  0.0 1.0 %broadcast_select_fusion.16 = (bf16[128,512]{1,0:T(8,128)(2,1)S(1)}, bf16[128,512]{1,0:T(8,128)(2,1)S(1)}) fusion(pred[]{:T(512)S(6)} %eq.31, bf16[128,1024]{1,0:T(8,128)(2,1)} %param.7), kind=kLoop, calls=%fused_computation.144 | loop fusion | flops 131072 | bytes 524289 | tf_op jit(solution)/shard_map/jit(_where)/select_n | solution.py:216
  1.0 3.0 %collective-permute-start = (bf16[128,512]{1,0:T(8,128)(2,1)S(1)}, bf16[128,512]{1,0:T(8,128)(2,1)S(1)}, u32[]{:S(2)}, u32[]{:S(2)}) collective-permute-start(bf16[128,512]{1,0:T(8,128)(2,1)S(1)} %get-tuple-element.34), channel_id=1, source_target_pairs={{0,1},{1,0},{2,3},{3,2},{4,5},{5,4},{6,7},{7,6},{8,9},{9,8},{10,11... | collective-permute-start | bytes 393224 | tf_op jit(solution)/shard_map/ppermute | solution.py:218
  5.8 2.0 %collective-permute-start.2 = (bf16[128,8]{0,1:T(8,128)(2,1)S(1)}, bf16[128,8]{0,1:T(8,128)(2,1)S(1)}, u32[]{:S(2)}, u32[]{:S(2)}) collective-permute-start(bf16[128,8]{0,1:T(8,128)(2,1)S(1)} %get-tuple-element.45), channel_id=1, source_target_pairs={{0,1},{1,0},{2,3},{3,2},{4,5},{5,4},{6,7},{7,6},{8,9},{9,8},{10,11... | collective-permute-start | bytes 6152 | tf_op jit(solution)/shard_map/ppermute | solution.py:218
  8.5 1.8 %broadcast_select_fusion.5 = (bf16[128,1024]{1,0:T(8,128)(2,1)S(1)}, bf16[128,1024]{1,0:T(8,128)(2,1)}) fusion(pred[]{:T(512)S(6)} %eq.31, bf16[128,2048]{1,0:T(8,128)(2,1)} %param.9), kind=kLoop, calls=%fused_computation.122 | loop fusion | flops 262144 | bytes 1048577 | tf_op jit(solution)/shard_map/jit(_where)/select_n | solution.py:216
  10.3 2.0 %collective-permute-start.4 = (bf16[128,1024]{1,0:T(8,128)(2,1)}, bf16[128,1024]{1,0:T(8,128)(2,1)}, u32[]{:S(2)}, u32[]{:S(2)}) collective-permute-start(bf16[128,1024]{1,0:T(8,128)(2,1)} %get-tuple-element.26), channel_id=1, source_target_pairs={{0,1},{1,0},{2,3},{3,2},{4,5},{5,4},{6,7},{7,6},{8,9},{9,8},{10,11... | collective-permute-start | bytes 786440 | tf_op jit(solution)/shard_map/ppermute | solution.py:218
  17.2 1.1 %fusion = f32[8,2,256,128]{3,2,1,0:T(8,128)S(1)} fusion(f32[8,2,128,128]{3,2,1,0:T(8,128)S(1)} %fusion.94, f32[8,2,128,128]{3,2,1,0:T(8,128)S(1)} %get-tuple-element.17), kind=kOutput, calls=%fused_computation | convolution fusion | flops 403177472 | bytes 4194304 | tf_op jit(solution)/shard_map/dot_general | solution.py:58
  19.6 1.2 %convert_bitcast_fusion = f32[32,8,8,128]{3,1,2,0:T(8,128)S(1)} fusion(bf16[128,1024]{1,0:T(8,128)(2,1)} %collective-permute-done.4, bf16[128,1024]{1,0:T(8,128)(2,1)S(1)} %get-tuple-element.25, pred[]{:T(512)S(6)} %eq.31), kind=kLoop, calls=%fused_computation.72 | loop fusion | flops 2621440 | bytes 1572865
  20.9 1.0 %slice_add_fusion.5 = (f32[8,2,128,128]{3,2,1,0:T(8,128)S(1)}, f32[8,2,128,128]{3,2,1,0:T(8,128)S(1)}, f32[8,2,128,128]{3,2,1,0:T(8,128)S(1)}, f32[8,2,128,128]{3,2,1,0:T(8,128)S(1)}) fusion(f32[8,2,256,128]{3,2,1,0:T(8,128)S(1)} %fusion, f32[4,2,128,128]{3,2,1,0:T(8,128)S(1)} %fusion.91, f32[8,2,128]{2,1,0:T(2,128)S(1)} %copy.67, ...), kind=kLoop, calls=%fused_computation.65 | loop fusion | flops 2359296 | bytes 8511488 | tf_op jit(solution)/shard_map/add | solution.py:61
  22.0 1.1 %fusion.4 = f32[8,2,256,128]{3,2,1,0:T(8,128)S(1)} fusion(f32[8,2,128,128]{3,2,1,0:T(8,128)S(1)} %get-tuple-element.12, f32[8,2,128,128]{3,2,1,0:T(8,128)S(1)} %get-tuple-element.11), kind=kOutput, calls=%fused_computation.4 | convolution fusion | flops 403177472 | bytes 4194304 | tf_op jit(solution)/shard_map/dot_general | solution.py:58
  23.3 1.1 %fusion.8 = f32[8,2,256,128]{3,2,1,0:T(8,128)S(1)} fusion(f32[8,2,128,128]{3,2,1,0:T(8,128)S(1)} %get-tuple-element.10, f32[8,2,128,128]{3,2,1,0:T(8,128)S(1)} %get-tuple-element.9), kind=kOutput, calls=%fused_computation.8 | convolution fusion | flops 403177472 | bytes 4194304 | tf_op jit(solution)/shard_map/dot_general | solution.py:58
  24.5 1.0 %fusion.12 = f32[8,2,256,128]{3,2,1,0:T(8,128)S(1)} fusion(f32[8,2,128,128]{3,2,1,0:T(8,128)S(1)} %get-tuple-element.8, f32[8,2,128,128]{3,2,1,0:T(8,128)S(1)} %get-tuple-element.7), kind=kOutput, calls=%fused_computation.12 | convolution fusion | flops 403177472 | bytes 4194304 | tf_op jit(solution)/shard_map/dot_general | solution.py:58
  25.8 1.1 %fusion.16 = f32[8,2,256,128]{3,2,1,0:T(8,128)S(1)} fusion(f32[8,2,128,128]{3,2,1,0:T(8,128)S(1)} %get-tuple-element.6, f32[8,2,128,128]{3,2,1,0:T(8,128)S(1)} %get-tuple-element.5), kind=kOutput, calls=%fused_computation.16 | convolution fusion | flops 403177472 | bytes 4194304 | tf_op jit(solution)/shard_map/dot_general | solution.py:58
  27.6 1.2 %fusion.20 = f32[8,2,128,256]{3,2,1,0:T(8,128)S(1)} fusion(f32[8,2,128,128]{3,2,1,0:T(8,128)S(1)} %convolution_add_fusion, f32[8,2,128,128]{3,2,1,0:T(8,128)S(1)} %get-tuple-element.24, f32[8,2,128,128]{3,2,1,0:T(8,128)S(1)} %get-tuple-element.40), kind=kOutput, calls=%fused_computation.20 | convolution fusion | flops 403177472 | bytes 5242880 | tf_op jit(solution)/shard_map/dot_general | solution.py:86
  28.8 1.0 %fusion.44 = f32[8,2,128,128]{2,3,1,0:T(8,128)S(1)} fusion(f32[8,2,128,128]{3,2,1,0:T(8,128)S(1)} %get-tuple-element.23, f32[8,2,128,256]{3,2,1,0:T(8,128)S(1)} %fusion.20), kind=kOutput, calls=%fused_computation.76 | convolution fusion | flops 201326592 | bytes 3145728 | tf_op jit(solution)/shard_map/hmck,hmcv->hmkv/dot_general | solution.py:94
  29.9 1.1 %convolution_subtract_fusion = f32[8,2,128,128]{3,2,1,0:T(8,128)S(1)} fusion(f32[8,2,128,128]{3,2,1,0:T(8,128)S(1)} %get-tuple-element.23, f32[8,2,128,256]{3,2,1,0:T(8,128)S(1)} %fusion.20, f32[8,2]{1,0:T(8,128)S(1)} %copy.81, f32[128,128]{1,0:T(8,128)S(1)} %get-tuple-element.47), kind=kOutput, calls=%fused_computation.30 | convolution fusion | flops 201850880 | bytes 3215360 | tf_op jit(solution)/shard_map/hmck,hmcj->hmkj/dot_general | solution.py:91
  33.4 2.2 %collective-permute-done.5 = f32[4,128,256]{1,2,0:T(8,128)} collective-permute-done((f32[4,128,256]{1,2,0:T(8,128)}, f32[4,128,256]{1,2,0:T(8,128)}, u32[]{:S(2)}, u32[]{:S(2)}) %collective-permute-start.5) | collective-permute-done | bytes 524320 | tf_op jit(solution)/shard_map/ppermute | solution.py:183
  35.7 1.6 %broadcast_select_fusion.1 = (f32[4,128,256]{1,2,0:T(8,128)S(1)}, f32[4,128,256]{1,2,0:T(8,128)S(1)}) fusion(f32[4,128,256]{1,2,0:T(8,128)} %collective-permute-done.5, pred[]{:T(512)S(6)} %eq.33, f32[8,128,128]{1,2,0:T(8,128)} %copy-done.5, f32[8,128,128]{1,2,0:T(8,128)} %copy-done.4), kind=kLoop, calls=%fused_computation.117 | loop fusion | flops 917504 | bytes 2621441 | tf_op jit(solution)/shard_map/jit(_where)/select_n | solution.py:185
  39.3 1.5 %collective-permute-start.6 = (f32[2,128,256]{1,2,0:T(8,128)}, f32[2,128,256]{1,2,0:T(8,128)}, u32[]{:S(2)}, u32[]{:S(2)}) collective-permute-start(f32[2,128,256]{1,2,0:T(8,128)} %broadcast_select_fusion.9), channel_id=1, source_target_pairs={{0,4},{2,6},{4,0},{6,2},{8,12},{10,14},{12,8},{14,10},{16,20},{18,... | collective-permute-start | bytes 786440 | tf_op jit(solution)/shard_map/ppermute | solution.py:183
  40.8 7.2 %collective-permute-done.6 = f32[2,128,256]{1,2,0:T(8,128)} collective-permute-done((f32[2,128,256]{1,2,0:T(8,128)}, f32[2,128,256]{1,2,0:T(8,128)}, u32[]{:S(2)}, u32[]{:S(2)}) %collective-permute-start.6) | collective-permute-done | bytes 262176 | tf_op jit(solution)/shard_map/ppermute | solution.py:183
  48.0 1.2 %broadcast_select_fusion.8 = (f32[2,128,256]{1,2,0:T(8,128)S(1)}, f32[2,128,256]{1,2,0:T(8,128)S(1)}) fusion(f32[2,128,256]{1,2,0:T(8,128)} %collective-permute-done.6, pred[]{:T(512)S(6)} %eq.34, f32[4,128,128]{1,2,0:T(8,128)} %copy-done.8, f32[4,128,128]{1,2,0:T(8,128)S(1)} %fusion.63), kind=kLoop, calls=%fused_computation.136 | loop fusion | flops 458752 | bytes 1310721 | tf_op jit(solution)/shard_map/jit(_where)/select_n | solution.py:185
  49.6 1.6 %collective-permute-start.7 = (f32[1,128,256]{1,2,0:T(8,128)S(1)}, f32[1,128,256]{1,2,0:T(8,128)S(1)}, u32[]{:S(2)}, u32[]{:S(2)}) collective-permute-start(f32[1,128,256]{1,2,0:T(8,128)S(1)} %broadcast_select_fusion.19), channel_id=1, source_target_pairs={{0,8},{2,10},{4,12},{6,14},{8,0},{10,2},{12,4},{14,6},{16,24},{18,... | collective-permute-start | bytes 393224 | tf_op jit(solution)/shard_map/ppermute | solution.py:183
  51.6 3.0 %collective-permute-done.7 = f32[1,128,256]{1,2,0:T(8,128)S(1)} collective-permute-done((f32[1,128,256]{1,2,0:T(8,128)S(1)}, f32[1,128,256]{1,2,0:T(8,128)S(1)}, u32[]{:S(2)}, u32[]{:S(2)}) %collective-permute-start.7) | collective-permute-done | bytes 131104 | tf_op jit(solution)/shard_map/ppermute | solution.py:183
  54.8 4.7 %collective-permute-start.8 = (f32[1,128,128]{1,2,0:T(8,128)S(1)}, f32[1,128,128]{1,2,0:T(8,128)S(1)}, u32[]{:S(2)}, u32[]{:S(2)}) collective-permute-start(f32[1,128,128]{1,2,0:T(8,128)S(1)} %fusion.27), channel_id=1, source_target_pairs={{0,16},{2,18},{4,20},{6,22},{8,24},{10,26},{12,28},{14,30},{1,17},... | collective-permute-start | bytes 196616 | tf_op jit(solution)/shard_map/ppermute | solution.py:161
  60.2 1.2 %collective-permute-done.8 = f32[1,128,128]{1,2,0:T(8,128)S(1)} collective-permute-done((f32[1,128,128]{1,2,0:T(8,128)S(1)}, f32[1,128,128]{1,2,0:T(8,128)S(1)}, u32[]{:S(2)}, u32[]{:S(2)}) %collective-permute-start.8) | collective-permute-done | bytes 65568 | tf_op jit(solution)/shard_map/ppermute | solution.py:161
  61.5 2.0 %collective-permute-start.9 = (f32[1,128,128]{1,2,0:T(8,128)S(1)}, f32[1,128,128]{1,2,0:T(8,128)S(1)}, u32[]{:S(2)}, u32[]{:S(2)}) collective-permute-start(f32[1,128,128]{1,2,0:T(8,128)S(1)} %get-tuple-element.35), channel_id=1, source_target_pairs={{0,8},{2,10},{4,12},{6,14},{8,0},{10,2},{12,4},{14,6},{16,24},{18,... | collective-permute-start | bytes 196616 | tf_op jit(solution)/shard_map/ppermute | solution.py:196
  63.6 1.0 %fusion.46 = f32[8,2,128,128]{2,3,1,0:T(8,128)S(1)} fusion(f32[8,2,128,128]{3,2,1,0:T(8,128)S(1)} %get-tuple-element.41, f32[8,2,128,256]{3,2,1,0:T(8,128)S(1)} %fusion.20), kind=kOutput, calls=%fused_computation.78 | convolution fusion | flops 201326592 | bytes 3145728 | tf_op jit(solution)/shard_map/hmij,hmjv->hmiv/dot_general | solution.py:112
  64.6 1.3 %collective-permute-done.9 = f32[1,128,128]{1,2,0:T(8,128)S(1)} collective-permute-done((f32[1,128,128]{1,2,0:T(8,128)S(1)}, f32[1,128,128]{1,2,0:T(8,128)S(1)}, u32[]{:S(2)}, u32[]{:S(2)}) %collective-permute-start.9) | collective-permute-done | bytes 65568 | tf_op jit(solution)/shard_map/ppermute | solution.py:196
  66.1 1.6 %collective-permute-start.10 = (f32[2,128,128]{1,2,0:T(8,128)S(1)}, f32[2,128,128]{1,2,0:T(8,128)S(1)}, u32[]{:S(2)}, u32[]{:S(2)}) collective-permute-start(f32[2,128,128]{1,2,0:T(8,128)S(1)} %get-tuple-element.29), channel_id=1, source_target_pairs={{0,4},{2,6},{4,0},{6,2},{8,12},{10,14},{12,8},{14,10},{16,20},{18,... | collective-permute-start | bytes 393224 | tf_op jit(solution)/shard_map/ppermute | solution.py:196
  68.3 2.8 %collective-permute-done.10 = f32[2,128,128]{1,2,0:T(8,128)S(1)} collective-permute-done((f32[2,128,128]{1,2,0:T(8,128)S(1)}, f32[2,128,128]{1,2,0:T(8,128)S(1)}, u32[]{:S(2)}, u32[]{:S(2)}) %collective-permute-start.10) | collective-permute-done | bytes 131104 | tf_op jit(solution)/shard_map/ppermute | solution.py:196
  72.0 1.0 %collective-permute-done.11 = f32[4,128,128]{1,2,0:T(8,128)S(1)} collective-permute-done((f32[4,128,128]{1,2,0:T(8,128)S(1)}, f32[4,128,128]{1,2,0:T(8,128)S(1)}, u32[]{:S(2)}, u32[]{:S(2)}) %collective-permute-start.11) | collective-permute-done | bytes 262176 | tf_op jit(solution)/shard_map/ppermute | solution.py:196
  74.3 7.8 %collective-permute-done.12 = bf16[128,1024]{0,1:T(8,128)(2,1)S(1)} collective-permute-done((bf16[128,1024]{0,1:T(8,128)(2,1)S(1)}, bf16[128,1024]{0,1:T(8,128)(2,1)S(1)}, u32[]{:S(2)}, u32[]{:S(2)}) %collective-permute-start.12) | collective-permute-done | bytes 262176 | tf_op jit(solution)/shard_map/ppermute | solution.py:227
  83.1 1.1 %fusion.41 = bf16[128,2048]{1,0:T(8,128)(2,1)} fusion(bf16[128,2048]{1,0:T(8,128)(2,1)S(1)} %copy-done.11, f32[128,2048]{1,0:T(8,128)S(1)} %copy.97, f32[2048]{0:T(1024)S(1)} %broadcast_bitcast_fusion), kind=kLoop, calls=%fused_computation.73 | loop fusion | flops 2097152 | bytes 2105344 | tf_op jit(solution)/shard_map/convert_element_type | solution.py:210
  (102 shorter events, 20.1 us)
Async XLA Ops:
  1.0 12.4 %collective-permute-start = (bf16[128,512]{1,0:T(8,128)(2,1)S(1)}, bf16[128,512]{1,0:T(8,128)(2,1)S(1)}, u32[]{:S(2)}, u32[]{:S(2)}) collective-permute-start(bf16[128,512]{1,0:T(8,128)(2,1)S(1)} %get-tuple-element.34), channel_id=1, source_target_pairs={{0,1},{1,0},{2,3},{3,2},{4,5},{5,4},{6,7},{7,6},{8,9},{9,8},{10,11... | collective-permute-start | bytes 393224 | tf_op jit(solution)/shard_map/ppermute | solution.py:218
  5.0 9.0 %collective-permute-start.1 = (bf16[128,512]{1,0:T(8,128)(2,1)S(1)}, bf16[128,512]{1,0:T(8,128)(2,1)S(1)}, u32[]{:S(2)}, u32[]{:S(2)}) collective-permute-start(bf16[128,512]{1,0:T(8,128)(2,1)S(1)} %get-tuple-element.32), channel_id=1, source_target_pairs={{0,1},{1,0},{2,3},{3,2},{4,5},{5,4},{6,7},{7,6},{8,9},{9,8},{10,11... | collective-permute-start | bytes 393224 | tf_op jit(solution)/shard_map/ppermute | solution.py:218
  5.8 6.6 %collective-permute-start.2 = (bf16[128,8]{0,1:T(8,128)(2,1)S(1)}, bf16[128,8]{0,1:T(8,128)(2,1)S(1)}, u32[]{:S(2)}, u32[]{:S(2)}) collective-permute-start(bf16[128,8]{0,1:T(8,128)(2,1)S(1)} %get-tuple-element.45), channel_id=1, source_target_pairs={{0,1},{1,0},{2,3},{3,2},{4,5},{5,4},{6,7},{7,6},{8,9},{9,8},{10,11... | collective-permute-start | bytes 6152 | tf_op jit(solution)/shard_map/ppermute | solution.py:218
  8.5 4.6 %collective-permute-start.3 = (bf16[128,8]{0,1:T(8,128)(2,1)S(1)}, bf16[128,8]{0,1:T(8,128)(2,1)S(1)}, u32[]{:S(2)}, u32[]{:S(2)}) collective-permute-start(bf16[128,8]{0,1:T(8,128)(2,1)S(1)} %get-tuple-element.43), channel_id=1, source_target_pairs={{0,1},{1,0},{2,3},{3,2},{4,5},{5,4},{6,7},{7,6},{8,9},{9,8},{10,11... | collective-permute-start | bytes 6152 | tf_op jit(solution)/shard_map/ppermute | solution.py:218
  10.3 9.3 %collective-permute-start.4 = (bf16[128,1024]{1,0:T(8,128)(2,1)}, bf16[128,1024]{1,0:T(8,128)(2,1)}, u32[]{:S(2)}, u32[]{:S(2)}) collective-permute-start(bf16[128,1024]{1,0:T(8,128)(2,1)} %get-tuple-element.26), channel_id=1, source_target_pairs={{0,1},{1,0},{2,3},{3,2},{4,5},{5,4},{6,7},{7,6},{8,9},{9,8},{10,11... | collective-permute-start | bytes 786440 | tf_op jit(solution)/shard_map/ppermute | solution.py:218
  15.3 3.6 %copy-start.2 = (f32[4,2,128,128]{3,0,2,1:T(4,128)}, f32[4,2,128,128]{3,0,2,1:T(4,128)S(1)}, u32[]{:S(2)}) copy-start(f32[4,2,128,128]{3,0,2,1:T(4,128)S(1)} %get-tuple-element.49) | copy-start | bytes 1572868
  29.8 1.8 %copy-start.6 = (f32[8,2,128,128]{2,3,1,0:T(8,128)}, f32[8,2,128,128]{2,3,1,0:T(8,128)S(1)}, u32[]{:S(2)}) copy-start(f32[8,2,128,128]{2,3,1,0:T(8,128)S(1)} %fusion.44) | copy-start | bytes 3145732
  31.0 2.4 %copy-start = (f32[8,2,128,128]{3,2,1,0:T(8,128)}, f32[8,2,128,128]{3,2,1,0:T(8,128)S(1)}, u32[]{:S(2)}) copy-start(f32[8,2,128,128]{3,2,1,0:T(8,128)S(1)} %convolution_subtract_fusion) | copy-start | bytes 3145732
  31.6 0.8 copy-start.4
  32.4 1.0 %copy-start.5 = (f32[8,128,128]{1,2,0:T(8,128)}, f32[8,128,128]{1,2,0:T(8,128)S(1)}, u32[]{:S(2)}) copy-start(f32[8,128,128]{1,2,0:T(8,128)S(1)} %convolution_add_fusion.2) | copy-start | bytes 1572868
  33.4 2.3 %collective-permute-start.5 = (f32[4,128,256]{1,2,0:T(8,128)}, f32[4,128,256]{1,2,0:T(8,128)}, u32[]{:S(2)}, u32[]{:S(2)}) collective-permute-start(f32[4,128,256]{1,2,0:T(8,128)} %broadcast_select_fusion.2), channel_id=1, source_target_pairs={{0,2},{2,0},{4,6},{6,4},{8,10},{10,8},{12,14},{14,12},{16,18},{18,... | collective-permute-start | bytes 1572872 | tf_op jit(solution)/shard_map/ppermute | solution.py:183
  37.3 2.0 %copy-start.9 = (f32[4,128,256]{1,2,0:T(8,128)}, f32[4,128,256]{1,2,0:T(8,128)S(1)}, u32[]{:S(2)}) copy-start(f32[4,128,256]{1,2,0:T(8,128)S(1)} %get-tuple-element.14) | copy-start | bytes 1572868
  37.9 0.7 copy-start.8
  39.3 8.7 %collective-permute-start.6 = (f32[2,128,256]{1,2,0:T(8,128)}, f32[2,128,256]{1,2,0:T(8,128)}, u32[]{:S(2)}, u32[]{:S(2)}) collective-permute-start(f32[2,128,256]{1,2,0:T(8,128)} %broadcast_select_fusion.9), channel_id=1, source_target_pairs={{0,4},{2,6},{4,0},{6,2},{8,12},{10,14},{12,8},{14,10},{16,20},{18,... | collective-permute-start | bytes 786440 | tf_op jit(solution)/shard_map/ppermute | solution.py:183
  40.8 10.4 %copy-start.3 = (f32[4,2,128,128]{3,0,2,1:T(4,128)S(1)}, f32[4,2,128,128]{3,0,2,1:T(4,128)}, u32[]{:S(2)}) copy-start(f32[4,2,128,128]{3,0,2,1:T(4,128)} %copy-done.2) | copy-start | bytes 1572868
  49.6 5.0 %collective-permute-start.7 = (f32[1,128,256]{1,2,0:T(8,128)S(1)}, f32[1,128,256]{1,2,0:T(8,128)S(1)}, u32[]{:S(2)}, u32[]{:S(2)}) collective-permute-start(f32[1,128,256]{1,2,0:T(8,128)S(1)} %broadcast_select_fusion.19), channel_id=1, source_target_pairs={{0,8},{2,10},{4,12},{6,14},{8,0},{10,2},{12,4},{14,6},{16,24},{18,... | collective-permute-start | bytes 393224 | tf_op jit(solution)/shard_map/ppermute | solution.py:183
  54.8 6.5 %collective-permute-start.8 = (f32[1,128,128]{1,2,0:T(8,128)S(1)}, f32[1,128,128]{1,2,0:T(8,128)S(1)}, u32[]{:S(2)}, u32[]{:S(2)}) collective-permute-start(f32[1,128,128]{1,2,0:T(8,128)S(1)} %fusion.27), channel_id=1, source_target_pairs={{0,16},{2,18},{4,20},{6,22},{8,24},{10,26},{12,28},{14,30},{1,17},... | collective-permute-start | bytes 196616 | tf_op jit(solution)/shard_map/ppermute | solution.py:161
  60.2 7.5 %copy-start.7 = (f32[8,2,128,128]{2,3,1,0:T(8,128)S(1)}, f32[8,2,128,128]{2,3,1,0:T(8,128)}, u32[]{:S(2)}) copy-start(f32[8,2,128,128]{2,3,1,0:T(8,128)} %copy-done.6) | copy-start | bytes 3145732
  61.5 4.3 %collective-permute-start.9 = (f32[1,128,128]{1,2,0:T(8,128)S(1)}, f32[1,128,128]{1,2,0:T(8,128)S(1)}, u32[]{:S(2)}, u32[]{:S(2)}) collective-permute-start(f32[1,128,128]{1,2,0:T(8,128)S(1)} %get-tuple-element.35), channel_id=1, source_target_pairs={{0,8},{2,10},{4,12},{6,14},{8,0},{10,2},{12,4},{14,6},{16,24},{18,... | collective-permute-start | bytes 196616 | tf_op jit(solution)/shard_map/ppermute | solution.py:196
  64.6 6.5 %copy-start.10 = (f32[4,128,256]{1,2,0:T(8,128)S(1)}, f32[4,128,256]{1,2,0:T(8,128)}, u32[]{:S(2)}) copy-start(f32[4,128,256]{1,2,0:T(8,128)} %copy-done.9) | copy-start | bytes 1572868
  65.9 5.6 %copy-start.1 = (f32[8,2,128,128]{3,2,1,0:T(8,128)S(1)}, f32[8,2,128,128]{3,2,1,0:T(8,128)}, u32[]{:S(2)}) copy-start(f32[8,2,128,128]{3,2,1,0:T(8,128)} %copy-done) | copy-start | bytes 3145732
  66.1 5.0 %collective-permute-start.10 = (f32[2,128,128]{1,2,0:T(8,128)S(1)}, f32[2,128,128]{1,2,0:T(8,128)S(1)}, u32[]{:S(2)}, u32[]{:S(2)}) collective-permute-start(f32[2,128,128]{1,2,0:T(8,128)S(1)} %get-tuple-element.29), channel_id=1, source_target_pairs={{0,4},{2,6},{4,0},{6,2},{8,12},{10,14},{12,8},{14,10},{16,20},{18,... | collective-permute-start | bytes 393224 | tf_op jit(solution)/shard_map/ppermute | solution.py:196
  71.4 1.6 %collective-permute-start.11 = (f32[4,128,128]{1,2,0:T(8,128)S(1)}, f32[4,128,128]{1,2,0:T(8,128)S(1)}, u32[]{:S(2)}, u32[]{:S(2)}) collective-permute-start(f32[4,128,128]{1,2,0:T(8,128)S(1)} %get-tuple-element.21), channel_id=1, source_target_pairs={{0,2},{2,0},{4,6},{6,4},{8,10},{10,8},{12,14},{14,12},{16,18},{18,... | collective-permute-start | bytes 786440 | tf_op jit(solution)/shard_map/ppermute | solution.py:196
  73.0 1.2 %copy-start.12 = (bf16[128]{0:T(256)(128)(2,1)S(1)}, bf16[128]{0:T(256)(128)(2,1)}, u32[]{:S(2)}) copy-start(bf16[128]{0:T(256)(128)(2,1)} %param.13) | copy-start | bytes 772
  73.7 8.4 %collective-permute-start.12 = (bf16[128,1024]{0,1:T(8,128)(2,1)S(1)}, bf16[128,1024]{0,1:T(8,128)(2,1)S(1)}, u32[]{:S(2)}, u32[]{:S(2)}) collective-permute-start(bf16[128,1024]{0,1:T(8,128)(2,1)S(1)} %bitcast.118), channel_id=1, source_target_pairs={{0,1},{1,0},{2,3},{3,2},{4,5},{5,4},{6,7},{7,6},{8,9},{9,8},{10,11... | collective-permute-start | bytes 786440 | tf_op jit(solution)/shard_map/ppermute | solution.py:227
  82.1 1.0 %copy-start.11 = (bf16[128,2048]{1,0:T(8,128)(2,1)S(1)}, bf16[128,2048]{1,0:T(8,128)(2,1)}, u32[]{:S(2)}) copy-start(bf16[128,2048]{1,0:T(8,128)(2,1)} %param.10) | copy-start | bytes 1572868

commit v7 on v6

--- a/solution.py
+++ b/solution.py
@@ -211,12 +211,15 @@
 
 
 def head_swap(rows):
-    width = rows.shape[1] // 2
+    width = rows.shape[-1] // 2
     first = lax.axis_index("head") == 0
-    own = jnp.where(first, rows[:, :width], rows[:, width:])
-    sent = jnp.where(first, rows[:, width:], rows[:, :width])
+    own = jnp.where(first, rows[..., :width], rows[..., width:])
+    sent = jnp.where(first, rows[..., width:], rows[..., :width])
     got = lax.ppermute(sent, "head", [(0, 1), (1, 0)])
-    return jnp.where(first, jnp.concatenate([own, got], 0), jnp.concatenate([got, own], 0))
+    axis = rows.ndim - 2
+    return jnp.where(
+        first, jnp.concatenate([own, got], axis), jnp.concatenate([got, own], axis)
+    )
 
 
 def head_return(rows):
@@ -231,7 +234,10 @@
 def head_inputs(pieces_in):
     parts = lax.axis_size("head")
     if parts == 2:
-        return [head_swap(part) for part in pieces_in]
+        query_rows, key_rows, value_rows, beta_logit, log_decay = pieces_in
+        query_key = head_swap(jnp.stack([query_rows, key_rows]))
+        gates = head_swap(jnp.stack([beta_logit, log_decay]))
+        return [query_key[0], query_key[1], head_swap(value_rows), gates[0], gates[1]]
     tokens = pieces_in[0].shape[0]
     widths = [part.shape[1] // parts for part in pieces_in]
     packed = jnp.concatenate(

time: 84.6 us -> 83.7 us (0.989)
  other arithmetic: 17.6 us -> 14.9 us
  waiting for transfers between devices: 26.5 us -> 28.3 us
    ppermute x5 -> x3, waiting for transfers between devices: 0.01 us -> 3.18 us  [head_swap(): got = lax.ppermute(sent, 'head', [(0, 1), (1, 0)])]
    ppermute x5 -> x3, starting transfers between devices: 7.15 us -> 5.18 us  [head_swap(): got = lax.ppermute(sent, 'head', [(0, 1), (1, 0)])]
    select_n x5, other arithmetic: 5.14 us -> 3.37 us  [the longest x3 3.15 us: head_swap(): own = jnp.where(first, rows[..., :width], rows[..., width:])]
    unnamed x1, other arithmetic: 1.16 us -> 0.11 us
    ppermute x1, waiting for transfers between devices: 7.83 us -> 6.82 us  [head_return(): got = lax.ppermute(sent, 'head', [(0, 1), (1, 0)])]
    ppermute x1, starting transfers between devices: 0.57 us -> 1.58 us  [head_return(): got = lax.ppermute(sent, 'head', [(0, 1), (1, 0)])]
  transfers between devices with their start and end apart: 13 -> 11, of which waited for: 8 -> 9; matrix products, arithmetic and copies ran while one was open for 17% -> 13% of each run, Pallas kernels for 0% -> 0%
where the time goes in v7:
time: 83.7 us; the launch traced here: 83.4 us
  waiting for transfers between devices  28.3 us (34%)
  starting transfers between devices  19.3 us (23%)
  matrix products  17.7 us (21%)
  other arithmetic  14.9 us (18%)
  local copies, waits for them, and re-layouts  2.66 us (3%)
    ppermute x6, waiting for transfers between devices, chain_states(): got = lax.ppermute(other, 'ctx', [(i, i ^ stride) for i in range(size)])  17.1 us
    ppermute x6, starting transfers between devices, chain_states(): got = lax.ppermute(other, 'ctx', [(i, i ^ stride) for i in range(size)])  7.58 us
    ppermute x1, waiting for transfers between devices, head_return(): got = lax.ppermute(sent, 'head', [(0, 1), (1, 0)])  6.82 us
    dot_general x5, matrix products, unit_lower_inverse(): jnp.matmul(jnp.concatenate([inverse, power], axis=-2), power, precision=L...  5.37 us
    ppermute x3, starting transfers between devices, head_swap(): got = lax.ppermute(sent, 'head', [(0, 1), (1, 0)])  5.18 us
    ppermute x1, starting transfers between devices, exclusive_scan(): return lax.ppermute(write, 'ctx', near)  4.92 us
    ppermute x3, waiting for transfers between devices, head_swap(): got = lax.ppermute(sent, 'head', [(0, 1), (1, 0)])  3.18 us
    select_n x3, other arithmetic, head_swap(): own = jnp.where(first, rows[..., :width], rows[..., width:])  3.15 us
  transfers between devices with their start and end apart: 11, of which 9 were waited for; matrix products, arithmetic and copies ran while one was open for 13% of the time, Pallas kernels for 0%

profile of v7, /device:TPU:0, one launch (start us, length us, event | category | flops | bytes accessed | tf_op | source)
XLA Modules:
  0.0 83.4 jit_solution(14289868462287489439)
XLA Ops:
  0.0 1.3 %broadcast_select_fusion.7 = (bf16[2,128,512]{2,1,0:T(8,128)(2,1)S(1)}, bf16[2,128,512]{2,1,0:T(8,128)(2,1)S(1)}) fusion(pred[]{:T(512)S(6)} %eq.29, bf16[1,128,1024]{2,1,0:T(8,128)(2,1)} %bitcast.122, bf16[1,128,1024]{2,1,0:T(8,128)(2,1)} %bitcast.123), kind=kLoop, calls=%fused_computation.127 | loop fusion | flops 1835008 | bytes 1048577 | tf_op jit(solution)/shard_map/jit(_where)/select_n | solution.py:216
  1.3 3.0 %collective-permute-start = (bf16[2,128,512]{2,1,0:T(8,128)(2,1)S(1)}, bf16[2,128,512]{2,1,0:T(8,128)(2,1)S(1)}, u32[]{:S(2)}, u32[]{:S(2)}) collective-permute-start(bf16[2,128,512]{2,1,0:T(8,128)(2,1)S(1)} %get-tuple-element.30), channel_id=1, source_target_pairs={{0,1},{1,0},{2,3},{3,2},{4,5},{5,4},{6,7},{7,6},{8,9},{9,8},{10,11... | collective-permute-start | bytes 786440 | tf_op jit(solution)/shard_map/ppermute | solution.py:218
  5.2 1.1 %broadcast_select_fusion.5 = (bf16[128,1024]{1,0:T(8,128)(2,1)S(1)}, bf16[128,1024]{1,0:T(8,128)(2,1)S(1)}) fusion(pred[]{:T(512)S(6)} %eq.29, bf16[128,2048]{1,0:T(8,128)(2,1)} %param.9), kind=kLoop, calls=%fused_computation.125 | loop fusion | flops 262144 | bytes 1048577 | tf_op jit(solution)/shard_map/jit(_where)/select_n | solution.py:216
  6.3 2.1 %collective-permute-start.2 = (bf16[128,1024]{1,0:T(8,128)(2,1)S(1)}, bf16[128,1024]{1,0:T(8,128)(2,1)S(1)}, u32[]{:S(2)}, u32[]{:S(2)}) collective-permute-start(bf16[128,1024]{1,0:T(8,128)(2,1)S(1)} %get-tuple-element.26), channel_id=1, source_target_pairs={{0,1},{1,0},{2,3},{3,2},{4,5},{5,4},{6,7},{7,6},{8,9},{9,8},{10,11... | collective-permute-start | bytes 786440 | tf_op jit(solution)/shard_map/ppermute | solution.py:218
  8.4 3.2 %collective-permute-done.1 = bf16[2,128,8]{1,2,0:T(8,128)(2,1)S(1)} collective-permute-done((bf16[2,128,8]{1,2,0:T(8,128)(2,1)S(1)}, bf16[2,128,8]{1,2,0:T(8,128)(2,1)S(1)}, u32[]{:S(2)}, u32[]{:S(2)}) %collective-permute-start.1) | collective-permute-done | bytes 4128 | tf_op jit(solution)/shard_map/ppermute | solution.py:218
  17.6 1.1 %fusion = f32[8,2,256,128]{3,2,1,0:T(8,128)S(1)} fusion(f32[8,2,128,128]{3,2,1,0:T(8,128)S(1)} %fusion.92, f32[8,2,128,128]{3,2,1,0:T(8,128)S(1)} %get-tuple-element.17), kind=kOutput, calls=%fused_computation | convolution fusion | flops 403177472 | bytes 4194304 | tf_op jit(solution)/shard_map/dot_general | solution.py:58
  18.7 1.0 %slice_add_fusion.5 = (f32[8,2,128,128]{3,2,1,0:T(8,128)S(1)}, f32[8,2,128,128]{3,2,1,0:T(8,128)S(1)}, f32[8,2,128,128]{3,2,1,0:T(8,128)S(1)}, f32[8,2,128,128]{3,2,1,0:T(8,128)S(1)}) fusion(f32[8,2,256,128]{3,2,1,0:T(8,128)S(1)} %fusion, f32[4,2,128,128]{3,2,1,0:T(8,128)S(1)} %fusion.89, f32[8,2,128]{2,1,0:T(2,128)S(1)} %copy.67, ...), kind=kLoop, calls=%fused_computation.65 | loop fusion | flops 2359296 | bytes 8511488 | tf_op jit(solution)/shard_map/add | solution.py:61
  19.7 1.1 %fusion.4 = f32[8,2,256,128]{3,2,1,0:T(8,128)S(1)} fusion(f32[8,2,128,128]{3,2,1,0:T(8,128)S(1)} %get-tuple-element.12, f32[8,2,128,128]{3,2,1,0:T(8,128)S(1)} %get-tuple-element.11), kind=kOutput, calls=%fused_computation.4 | convolution fusion | flops 403177472 | bytes 4194304 | tf_op jit(solution)/shard_map/dot_general | solution.py:58
  21.1 1.1 %fusion.8 = f32[8,2,256,128]{3,2,1,0:T(8,128)S(1)} fusion(f32[8,2,128,128]{3,2,1,0:T(8,128)S(1)} %get-tuple-element.10, f32[8,2,128,128]{3,2,1,0:T(8,128)S(1)} %get-tuple-element.9), kind=kOutput, calls=%fused_computation.8 | convolution fusion | flops 403177472 | bytes 4194304 | tf_op jit(solution)/shard_map/dot_general | solution.py:58
  22.4 1.1 %fusion.12 = f32[8,2,256,128]{3,2,1,0:T(8,128)S(1)} fusion(f32[8,2,128,128]{3,2,1,0:T(8,128)S(1)} %get-tuple-element.8, f32[8,2,128,128]{3,2,1,0:T(8,128)S(1)} %get-tuple-element.7), kind=kOutput, calls=%fused_computation.12 | convolution fusion | flops 403177472 | bytes 4194304 | tf_op jit(solution)/shard_map/dot_general | solution.py:58
  23.7 1.1 %fusion.16 = f32[8,2,256,128]{3,2,1,0:T(8,128)S(1)} fusion(f32[8,2,128,128]{3,2,1,0:T(8,128)S(1)} %get-tuple-element.6, f32[8,2,128,128]{3,2,1,0:T(8,128)S(1)} %get-tuple-element.5), kind=kOutput, calls=%fused_computation.16 | convolution fusion | flops 403177472 | bytes 4194304 | tf_op jit(solution)/shard_map/dot_general | solution.py:58
  26.2 1.2 %fusion.20 = f32[8,2,128,256]{3,2,1,0:T(8,128)S(1)} fusion(f32[8,2,128,128]{3,2,1,0:T(8,128)S(1)} %convolution_add_fusion, f32[8,2,128,128]{3,2,1,0:T(8,128)S(1)} %get-tuple-element.24, f32[8,2,128,128]{3,2,1,0:T(8,128)S(1)} %get-tuple-element.40), kind=kOutput, calls=%fused_computation.20 | convolution fusion | flops 403177472 | bytes 5242880 | tf_op jit(solution)/shard_map/dot_general | solution.py:86
  27.4 1.0 %fusion.44 = f32[8,2,128,128]{2,3,1,0:T(8,128)S(1)} fusion(f32[8,2,128,128]{3,2,1,0:T(8,128)S(1)} %get-tuple-element.23, f32[8,2,128,256]{3,2,1,0:T(8,128)S(1)} %fusion.20), kind=kOutput, calls=%fused_computation.76 | convolution fusion | flops 201326592 | bytes 3145728 | tf_op jit(solution)/shard_map/hmck,hmcv->hmkv/dot_general | solution.py:94
  28.4 1.1 %convolution_subtract_fusion = f32[8,2,128,128]{3,2,1,0:T(8,128)S(1)} fusion(f32[8,2,128,128]{3,2,1,0:T(8,128)S(1)} %get-tuple-element.23, f32[8,2,128,256]{3,2,1,0:T(8,128)S(1)} %fusion.20, f32[8,2]{1,0:T(8,128)S(1)} %copy.81, f32[128,128]{1,0:T(8,128)S(1)} %get-tuple-element.45), kind=kOutput, calls=%fused_computation.30 | convolution fusion | flops 201850880 | bytes 3215360 | tf_op jit(solution)/shard_map/hmck,hmcj->hmkj/dot_general | solution.py:91
  32.0 2.2 %collective-permute-done.3 = f32[4,128,256]{1,2,0:T(8,128)} collective-permute-done((f32[4,128,256]{1,2,0:T(8,128)}, f32[4,128,256]{1,2,0:T(8,128)}, u32[]{:S(2)}, u32[]{:S(2)}) %collective-permute-start.3) | collective-permute-done | bytes 524320 | tf_op jit(solution)/shard_map/ppermute | solution.py:183
  34.2 1.6 %broadcast_select_fusion.1 = (f32[4,128,256]{1,2,0:T(8,128)S(1)}, f32[4,128,256]{1,2,0:T(8,128)S(1)}) fusion(f32[4,128,256]{1,2,0:T(8,128)} %collective-permute-done.3, pred[]{:T(512)S(6)} %eq.31, f32[8,128,128]{1,2,0:T(8,128)} %copy-done.5, f32[8,128,128]{1,2,0:T(8,128)} %copy-done.4), kind=kLoop, calls=%fused_computation.120 | loop fusion | flops 917504 | bytes 2621441 | tf_op jit(solution)/shard_map/jit(_where)/select_n | solution.py:185
  37.9 2.0 %collective-permute-start.4 = (f32[2,128,256]{1,2,0:T(8,128)}, f32[2,128,256]{1,2,0:T(8,128)}, u32[]{:S(2)}, u32[]{:S(2)}) collective-permute-start(f32[2,128,256]{1,2,0:T(8,128)} %broadcast_select_fusion.11), channel_id=1, source_target_pairs={{0,4},{2,6},{4,0},{6,2},{8,12},{10,14},{12,8},{14,10},{16,20},{18,... | collective-permute-start | bytes 786440 | tf_op jit(solution)/shard_map/ppermute | solution.py:183
  39.9 6.9 %collective-permute-done.4 = f32[2,128,256]{1,2,0:T(8,128)} collective-permute-done((f32[2,128,256]{1,2,0:T(8,128)}, f32[2,128,256]{1,2,0:T(8,128)}, u32[]{:S(2)}, u32[]{:S(2)}) %collective-permute-start.4) | collective-permute-done | bytes 262176 | tf_op jit(solution)/shard_map/ppermute | solution.py:183
  46.8 1.2 %broadcast_select_fusion.10 = (f32[2,128,256]{1,2,0:T(8,128)S(1)}, f32[2,128,256]{1,2,0:T(8,128)S(1)}) fusion(f32[2,128,256]{1,2,0:T(8,128)} %collective-permute-done.4, pred[]{:T(512)S(6)} %eq.32, f32[4,128,128]{1,2,0:T(8,128)} %copy-done.8, f32[4,128,128]{1,2,0:T(8,128)S(1)} %fusion.62), kind=kLoop, calls=%fused_computation.141 | loop fusion | flops 458752 | bytes 1310721 | tf_op jit(solution)/shard_map/jit(_where)/select_n | solution.py:185
  48.4 1.9 %collective-permute-start.5 = (f32[1,128,256]{1,2,0:T(8,128)S(1)}, f32[1,128,256]{1,2,0:T(8,128)S(1)}, u32[]{:S(2)}, u32[]{:S(2)}) collective-permute-start(f32[1,128,256]{1,2,0:T(8,128)S(1)} %broadcast_select_fusion.17), channel_id=1, source_target_pairs={{0,8},{2,10},{4,12},{6,14},{8,0},{10,2},{12,4},{14,6},{16,24},{18,... | collective-permute-start | bytes 393224 | tf_op jit(solution)/shard_map/ppermute | solution.py:183
  50.7 2.8 %collective-permute-done.5 = f32[1,128,256]{1,2,0:T(8,128)S(1)} collective-permute-done((f32[1,128,256]{1,2,0:T(8,128)S(1)}, f32[1,128,256]{1,2,0:T(8,128)S(1)}, u32[]{:S(2)}, u32[]{:S(2)}) %collective-permute-start.5) | collective-permute-done | bytes 131104 | tf_op jit(solution)/shard_map/ppermute | solution.py:183
  53.7 4.9 %collective-permute-start.6 = (f32[1,128,128]{1,2,0:T(8,128)S(1)}, f32[1,128,128]{1,2,0:T(8,128)S(1)}, u32[]{:S(2)}, u32[]{:S(2)}) collective-permute-start(f32[1,128,128]{1,2,0:T(8,128)S(1)} %fusion.27), channel_id=1, source_target_pairs={{0,16},{2,18},{4,20},{6,22},{8,24},{10,26},{12,28},{14,30},{1,17},... | collective-permute-start | bytes 196616 | tf_op jit(solution)/shard_map/ppermute | solution.py:161
  59.3 1.2 %collective-permute-done.6 = f32[1,128,128]{1,2,0:T(8,128)S(1)} collective-permute-done((f32[1,128,128]{1,2,0:T(8,128)S(1)}, f32[1,128,128]{1,2,0:T(8,128)S(1)}, u32[]{:S(2)}, u32[]{:S(2)}) %collective-permute-start.6) | collective-permute-done | bytes 65568 | tf_op jit(solution)/shard_map/ppermute | solution.py:161
  60.6 2.0 %collective-permute-start.7 = (f32[1,128,128]{1,2,0:T(8,128)S(1)}, f32[1,128,128]{1,2,0:T(8,128)S(1)}, u32[]{:S(2)}, u32[]{:S(2)}) collective-permute-start(f32[1,128,128]{1,2,0:T(8,128)S(1)} %get-tuple-element.35), channel_id=1, source_target_pairs={{0,8},{2,10},{4,12},{6,14},{8,0},{10,2},{12,4},{14,6},{16,24},{18,... | collective-permute-start | bytes 196616 | tf_op jit(solution)/shard_map/ppermute | solution.py:196
  62.7 1.0 %fusion.46 = f32[8,2,128,128]{2,3,1,0:T(8,128)S(1)} fusion(f32[8,2,128,128]{3,2,1,0:T(8,128)S(1)} %get-tuple-element.41, f32[8,2,128,256]{3,2,1,0:T(8,128)S(1)} %fusion.20), kind=kOutput, calls=%fused_computation.78 | convolution fusion | flops 201326592 | bytes 3145728 | tf_op jit(solution)/shard_map/hmij,hmjv->hmiv/dot_general | solution.py:112
  63.7 1.3 %collective-permute-done.7 = f32[1,128,128]{1,2,0:T(8,128)S(1)} collective-permute-done((f32[1,128,128]{1,2,0:T(8,128)S(1)}, f32[1,128,128]{1,2,0:T(8,128)S(1)}, u32[]{:S(2)}, u32[]{:S(2)}) %collective-permute-start.7) | collective-permute-done | bytes 65568 | tf_op jit(solution)/shard_map/ppermute | solution.py:196
  65.2 1.6 %collective-permute-start.8 = (f32[2,128,128]{1,2,0:T(8,128)S(1)}, f32[2,128,128]{1,2,0:T(8,128)S(1)}, u32[]{:S(2)}, u32[]{:S(2)}) collective-permute-start(f32[2,128,128]{1,2,0:T(8,128)S(1)} %get-tuple-element.33), channel_id=1, source_target_pairs={{0,4},{2,6},{4,0},{6,2},{8,12},{10,14},{12,8},{14,10},{16,20},{18,... | collective-permute-start | bytes 393224 | tf_op jit(solution)/shard_map/ppermute | solution.py:196
  67.4 2.8 %collective-permute-done.8 = f32[2,128,128]{1,2,0:T(8,128)S(1)} collective-permute-done((f32[2,128,128]{1,2,0:T(8,128)S(1)}, f32[2,128,128]{1,2,0:T(8,128)S(1)}, u32[]{:S(2)}, u32[]{:S(2)}) %collective-permute-start.8) | collective-permute-done | bytes 131104 | tf_op jit(solution)/shard_map/ppermute | solution.py:196
  71.1 1.0 %collective-permute-done.9 = f32[4,128,128]{1,2,0:T(8,128)S(1)} collective-permute-done((f32[4,128,128]{1,2,0:T(8,128)S(1)}, f32[4,128,128]{1,2,0:T(8,128)S(1)}, u32[]{:S(2)}, u32[]{:S(2)}) %collective-permute-start.9) | collective-permute-done | bytes 262176 | tf_op jit(solution)/shard_map/ppermute | solution.py:196
  72.8 1.6 %collective-permute-start.10 = (bf16[128,1024]{0,1:T(8,128)(2,1)S(1)}, bf16[128,1024]{0,1:T(8,128)(2,1)S(1)}, u32[]{:S(2)}, u32[]{:S(2)}) collective-permute-start(bf16[128,1024]{0,1:T(8,128)(2,1)S(1)} %bitcast.124), channel_id=1, source_target_pairs={{0,1},{1,0},{2,3},{3,2},{4,5},{5,4},{6,7},{7,6},{8,9},{9,8},{10,11... | collective-permute-start | bytes 786440 | tf_op jit(solution)/shard_map/ppermute | solution.py:230
  74.4 6.8 %collective-permute-done.10 = bf16[128,1024]{0,1:T(8,128)(2,1)S(1)} collective-permute-done((bf16[128,1024]{0,1:T(8,128)(2,1)S(1)}, bf16[128,1024]{0,1:T(8,128)(2,1)S(1)}, u32[]{:S(2)}, u32[]{:S(2)}) %collective-permute-start.10) | collective-permute-done | bytes 262176 | tf_op jit(solution)/shard_map/ppermute | solution.py:230
  82.3 1.1 %fusion.41 = bf16[128,2048]{1,0:T(8,128)(2,1)} fusion(bf16[128,2048]{1,0:T(8,128)(2,1)S(1)} %copy-done.11, f32[128,2048]{1,0:T(8,128)S(1)} %copy.97, f32[2048]{0:T(1024)S(1)} %broadcast_bitcast_fusion), kind=kLoop, calls=%fused_computation.73 | loop fusion | flops 2097152 | bytes 2105344 | tf_op jit(solution)/shard_map/convert_element_type | solution.py:210
  (97 shorter events, 18.4 us)
Async XLA Ops:
  1.3 11.2 %collective-permute-start = (bf16[2,128,512]{2,1,0:T(8,128)(2,1)S(1)}, bf16[2,128,512]{2,1,0:T(8,128)(2,1)S(1)}, u32[]{:S(2)}, u32[]{:S(2)}) collective-permute-start(bf16[2,128,512]{2,1,0:T(8,128)(2,1)S(1)} %get-tuple-element.30), channel_id=1, source_target_pairs={{0,1},{1,0},{2,3},{3,2},{4,5},{5,4},{6,7},{7,6},{8,9},{9,8},{10,11... | collective-permute-start | bytes 786440 | tf_op jit(solution)/shard_map/ppermute | solution.py:218
  5.1 6.5 %collective-permute-start.1 = (bf16[2,128,8]{1,2,0:T(8,128)(2,1)S(1)}, bf16[2,128,8]{1,2,0:T(8,128)(2,1)S(1)}, u32[]{:S(2)}, u32[]{:S(2)}) collective-permute-start(bf16[2,128,8]{1,2,0:T(8,128)(2,1)S(1)} %get-tuple-element.43), channel_id=1, source_target_pairs={{0,1},{1,0},{2,3},{3,2},{4,5},{5,4},{6,7},{7,6},{8,9},{9,8},{10,11... | collective-permute-start | bytes 12296 | tf_op jit(solution)/shard_map/ppermute | solution.py:218
  6.3 11.0 %collective-permute-start.2 = (bf16[128,1024]{1,0:T(8,128)(2,1)S(1)}, bf16[128,1024]{1,0:T(8,128)(2,1)S(1)}, u32[]{:S(2)}, u32[]{:S(2)}) collective-permute-start(bf16[128,1024]{1,0:T(8,128)(2,1)S(1)} %get-tuple-element.26), channel_id=1, source_target_pairs={{0,1},{1,0},{2,3},{3,2},{4,5},{5,4},{6,7},{7,6},{8,9},{9,8},{10,11... | collective-permute-start | bytes 786440 | tf_op jit(solution)/shard_map/ppermute | solution.py:218
  14.7 1.9 %copy-start.2 = (f32[4,2,128,128]{3,0,2,1:T(4,128)}, f32[4,2,128,128]{3,0,2,1:T(4,128)S(1)}, u32[]{:S(2)}) copy-start(f32[4,2,128,128]{3,0,2,1:T(4,128)S(1)} %get-tuple-element.47) | copy-start | bytes 1572868
  28.4 1.7 %copy-start.6 = (f32[8,2,128,128]{2,3,1,0:T(8,128)}, f32[8,2,128,128]{2,3,1,0:T(8,128)S(1)}, u32[]{:S(2)}) copy-start(f32[8,2,128,128]{2,3,1,0:T(8,128)S(1)} %fusion.44) | copy-start | bytes 3145732
  29.6 2.3 %copy-start = (f32[8,2,128,128]{3,2,1,0:T(8,128)}, f32[8,2,128,128]{3,2,1,0:T(8,128)S(1)}, u32[]{:S(2)}) copy-start(f32[8,2,128,128]{3,2,1,0:T(8,128)S(1)} %convolution_subtract_fusion) | copy-start | bytes 3145732
  30.2 0.8 copy-start.4
  31.0 1.0 %copy-start.5 = (f32[8,128,128]{1,2,0:T(8,128)}, f32[8,128,128]{1,2,0:T(8,128)S(1)}, u32[]{:S(2)}) copy-start(f32[8,128,128]{1,2,0:T(8,128)S(1)} %convolution_add_fusion.2) | copy-start | bytes 1572868
  32.0 2.3 %collective-permute-start.3 = (f32[4,128,256]{1,2,0:T(8,128)}, f32[4,128,256]{1,2,0:T(8,128)}, u32[]{:S(2)}, u32[]{:S(2)}) collective-permute-start(f32[4,128,256]{1,2,0:T(8,128)} %broadcast_select_fusion.2), channel_id=1, source_target_pairs={{0,2},{2,0},{4,6},{6,4},{8,10},{10,8},{12,14},{14,12},{16,18},{18,... | collective-permute-start | bytes 1572872 | tf_op jit(solution)/shard_map/ppermute | solution.py:183
  35.9 2.0 %copy-start.9 = (f32[4,128,256]{1,2,0:T(8,128)}, f32[4,128,256]{1,2,0:T(8,128)S(1)}, u32[]{:S(2)}) copy-start(f32[4,128,256]{1,2,0:T(8,128)S(1)} %get-tuple-element.14) | copy-start | bytes 1572868
  36.4 0.7 copy-start.8
  37.9 8.9 %collective-permute-start.4 = (f32[2,128,256]{1,2,0:T(8,128)}, f32[2,128,256]{1,2,0:T(8,128)}, u32[]{:S(2)}, u32[]{:S(2)}) collective-permute-start(f32[2,128,256]{1,2,0:T(8,128)} %broadcast_select_fusion.11), channel_id=1, source_target_pairs={{0,4},{2,6},{4,0},{6,2},{8,12},{10,14},{12,8},{14,10},{16,20},{18,... | collective-permute-start | bytes 786440 | tf_op jit(solution)/shard_map/ppermute | solution.py:183
  39.9 10.4 %copy-start.3 = (f32[4,2,128,128]{3,0,2,1:T(4,128)S(1)}, f32[4,2,128,128]{3,0,2,1:T(4,128)}, u32[]{:S(2)}) copy-start(f32[4,2,128,128]{3,0,2,1:T(4,128)} %copy-done.2) | copy-start | bytes 1572868
  48.4 5.1 %collective-permute-start.5 = (f32[1,128,256]{1,2,0:T(8,128)S(1)}, f32[1,128,256]{1,2,0:T(8,128)S(1)}, u32[]{:S(2)}, u32[]{:S(2)}) collective-permute-start(f32[1,128,256]{1,2,0:T(8,128)S(1)} %broadcast_select_fusion.17), channel_id=1, source_target_pairs={{0,8},{2,10},{4,12},{6,14},{8,0},{10,2},{12,4},{14,6},{16,24},{18,... | collective-permute-start | bytes 393224 | tf_op jit(solution)/shard_map/ppermute | solution.py:183
  53.7 6.7 %collective-permute-start.6 = (f32[1,128,128]{1,2,0:T(8,128)S(1)}, f32[1,128,128]{1,2,0:T(8,128)S(1)}, u32[]{:S(2)}, u32[]{:S(2)}) collective-permute-start(f32[1,128,128]{1,2,0:T(8,128)S(1)} %fusion.27), channel_id=1, source_target_pairs={{0,16},{2,18},{4,20},{6,22},{8,24},{10,26},{12,28},{14,30},{1,17},... | collective-permute-start | bytes 196616 | tf_op jit(solution)/shard_map/ppermute | solution.py:161
  59.3 7.5 %copy-start.7 = (f32[8,2,128,128]{2,3,1,0:T(8,128)S(1)}, f32[8,2,128,128]{2,3,1,0:T(8,128)}, u32[]{:S(2)}) copy-start(f32[8,2,128,128]{2,3,1,0:T(8,128)} %copy-done.6) | copy-start | bytes 3145732
  60.6 4.3 %collective-permute-start.7 = (f32[1,128,128]{1,2,0:T(8,128)S(1)}, f32[1,128,128]{1,2,0:T(8,128)S(1)}, u32[]{:S(2)}, u32[]{:S(2)}) collective-permute-start(f32[1,128,128]{1,2,0:T(8,128)S(1)} %get-tuple-element.35), channel_id=1, source_target_pairs={{0,8},{2,10},{4,12},{6,14},{8,0},{10,2},{12,4},{14,6},{16,24},{18,... | collective-permute-start | bytes 196616 | tf_op jit(solution)/shard_map/ppermute | solution.py:196
  63.7 6.6 %copy-start.10 = (f32[4,128,256]{1,2,0:T(8,128)S(1)}, f32[4,128,256]{1,2,0:T(8,128)}, u32[]{:S(2)}) copy-start(f32[4,128,256]{1,2,0:T(8,128)} %copy-done.9) | copy-start | bytes 1572868
  65.0 5.6 %copy-start.1 = (f32[8,2,128,128]{3,2,1,0:T(8,128)S(1)}, f32[8,2,128,128]{3,2,1,0:T(8,128)}, u32[]{:S(2)}) copy-start(f32[8,2,128,128]{3,2,1,0:T(8,128)} %copy-done) | copy-start | bytes 3145732
  65.2 5.0 %collective-permute-start.8 = (f32[2,128,128]{1,2,0:T(8,128)S(1)}, f32[2,128,128]{1,2,0:T(8,128)S(1)}, u32[]{:S(2)}, u32[]{:S(2)}) collective-permute-start(f32[2,128,128]{1,2,0:T(8,128)S(1)} %get-tuple-element.33), channel_id=1, source_target_pairs={{0,4},{2,6},{4,0},{6,2},{8,12},{10,14},{12,8},{14,10},{16,20},{18,... | collective-permute-start | bytes 393224 | tf_op jit(solution)/shard_map/ppermute | solution.py:196
  70.5 1.6 %collective-permute-start.9 = (f32[4,128,128]{1,2,0:T(8,128)S(1)}, f32[4,128,128]{1,2,0:T(8,128)S(1)}, u32[]{:S(2)}, u32[]{:S(2)}) collective-permute-start(f32[4,128,128]{1,2,0:T(8,128)S(1)} %get-tuple-element.21), channel_id=1, source_target_pairs={{0,2},{2,0},{4,6},{6,4},{8,10},{10,8},{12,14},{14,12},{16,18},{18,... | collective-permute-start | bytes 786440 | tf_op jit(solution)/shard_map/ppermute | solution.py:196
  72.1 2.3 %copy-start.12 = (bf16[128]{0:T(256)(128)(2,1)S(1)}, bf16[128]{0:T(256)(128)(2,1)}, u32[]{:S(2)}) copy-start(bf16[128]{0:T(256)(128)(2,1)} %param.13) | copy-start | bytes 772
  72.8 8.4 %collective-permute-start.10 = (bf16[128,1024]{0,1:T(8,128)(2,1)S(1)}, bf16[128,1024]{0,1:T(8,128)(2,1)S(1)}, u32[]{:S(2)}, u32[]{:S(2)}) collective-permute-start(bf16[128,1024]{0,1:T(8,128)(2,1)S(1)} %bitcast.124), channel_id=1, source_target_pairs={{0,1},{1,0},{2,3},{3,2},{4,5},{5,4},{6,7},{7,6},{8,9},{9,8},{10,11... | collective-permute-start | bytes 786440 | tf_op jit(solution)/shard_map/ppermute | solution.py:230
  81.2 1.0 %copy-start.11 = (bf16[128,2048]{1,0:T(8,128)(2,1)S(1)}, bf16[128,2048]{1,0:T(8,128)(2,1)}, u32[]{:S(2)}) copy-start(bf16[128,2048]{1,0:T(8,128)(2,1)} %param.10) | copy-start | bytes 1572868

commit v8 on v7

--- a/solution.py
+++ b/solution.py
@@ -170,7 +170,11 @@
     size = lax.axis_size("ctx")
     me = lax.axis_index("ctx")
     levels = 0
-    while size % 2 ** (levels + 1) == 0 and block_carry.shape[0] % 2 ** (levels + 1) == 0:
+    while (
+        levels < 2
+        and size % 2 ** (levels + 1) == 0
+        and block_carry.shape[0] % 2 ** (levels + 1) == 0
+    ):
         levels += 1
     current = joined(block_carry, block_write)
     saved = []

time: 83.7 us -> 87.2 us (1.042)
  starting transfers between devices: 19.3 us -> 22.3 us
  waiting for transfers between devices: 28.3 us -> 31 us
  other arithmetic: 14.9 us -> 13.1 us
    ppermute x1 -> x3, waiting for transfers between devices: 1.16 us -> 8.67 us  [the longest x1 4.19 us: exclusive_scan(): got = lax.ppermute(joined(carry, write), 'ctx', pairs)]
    ppermute x1 -> x3, starting transfers between devices: 4.92 us -> 11.8 us  [the longest x1 6.41 us: exclusive_scan(): lax.ppermute(write, 'ctx', [(i, i + far * stride) for i in range(size - f...]
    ppermute x6 -> x4, waiting for transfers between devices: 17.1 us -> 12.3 us  [chain_states(): got = lax.ppermute(other, 'ctx', [(i, i ^ stride) for i in range(size)])]
    ppermute x6 -> x4, starting transfers between devices: 7.58 us -> 3.72 us  [chain_states(): got = lax.ppermute(other, 'ctx', [(i, i ^ stride) for i in range(size)])]
    select_n x3 -> x1, other arithmetic: 2.8 us -> 1.61 us  [chain_states(): later = jnp.where(upper, mine, got)]
  transfers between devices with their start and end apart: 11 -> 11, of which waited for: 9 -> 9; matrix products, arithmetic and copies ran while one was open for 13% -> 12% of each run, Pallas kernels for 0% -> 0%
where the time goes in v8:
time: 87.2 us; the launch traced here: 86.9 us
  waiting for transfers between devices  31 us (36%)
  starting transfers between devices  22.3 us (26%)
  matrix products  18 us (21%)
  other arithmetic  13.1 us (15%)
  local copies, waits for them, and re-layouts  1.94 us (2%)
    ppermute x4, waiting for transfers between devices, chain_states(): got = lax.ppermute(other, 'ctx', [(i, i ^ stride) for i in range(size)])  12.3 us
    ppermute x1, waiting for transfers between devices, head_return(): got = lax.ppermute(sent, 'head', [(0, 1), (1, 0)])  6.8 us
    ppermute x1, starting transfers between devices, exclusive_scan(): lax.ppermute(write, 'ctx', [(i, i + far * stride) for i in range(size - f...  6.41 us
    dot_general x5, matrix products, unit_lower_inverse(): jnp.matmul(jnp.concatenate([inverse, power], axis=-2), power, precision=L...  5.37 us
    ppermute x3, starting transfers between devices, head_swap(): got = lax.ppermute(sent, 'head', [(0, 1), (1, 0)])  5.18 us
    ppermute x1, waiting for transfers between devices, exclusive_scan(): got = lax.ppermute(joined(carry, write), 'ctx', pairs)  4.19 us
    ppermute x1, starting transfers between devices, exclusive_scan(): got = lax.ppermute(joined(carry, write), 'ctx', pairs)  3.98 us
    ppermute x4, starting transfers between devices, chain_states(): got = lax.ppermute(other, 'ctx', [(i, i ^ stride) for i in range(size)])  3.72 us
  transfers between devices with their start and end apart: 11, of which 9 were waited for; matrix products, arithmetic and copies ran while one was open for 12% of the time, Pallas kernels for 0%

profile of v8, /device:TPU:0, one launch (start us, length us, event | category | flops | bytes accessed | tf_op | source)
XLA Modules:
  0.0 86.9 jit_solution(14440275804787341849)
XLA Ops:
  0.0 1.3 %broadcast_select_fusion.7 = (bf16[2,128,512]{2,1,0:T(8,128)(2,1)S(1)}, bf16[2,128,512]{2,1,0:T(8,128)(2,1)S(1)}) fusion(pred[]{:T(512)S(6)} %eq.25, bf16[1,128,1024]{2,1,0:T(8,128)(2,1)} %bitcast.102, bf16[1,128,1024]{2,1,0:T(8,128)(2,1)} %bitcast.103), kind=kLoop, calls=%fused_computation.125 | loop fusion | flops 1835008 | bytes 1048577 | tf_op jit(solution)/shard_map/jit(_where)/select_n | solution.py:220
  1.3 3.0 %collective-permute-start = (bf16[2,128,512]{2,1,0:T(8,128)(2,1)S(1)}, bf16[2,128,512]{2,1,0:T(8,128)(2,1)S(1)}, u32[]{:S(2)}, u32[]{:S(2)}) collective-permute-start(bf16[2,128,512]{2,1,0:T(8,128)(2,1)S(1)} %get-tuple-element.30), channel_id=1, source_target_pairs={{0,1},{1,0},{2,3},{3,2},{4,5},{5,4},{6,7},{7,6},{8,9},{9,8},{10,11... | collective-permute-start | bytes 786440 | tf_op jit(solution)/shard_map/ppermute | solution.py:222
  5.2 1.1 %broadcast_select_fusion.5 = (bf16[128,1024]{1,0:T(8,128)(2,1)S(1)}, bf16[128,1024]{1,0:T(8,128)(2,1)S(1)}) fusion(pred[]{:T(512)S(6)} %eq.25, bf16[128,2048]{1,0:T(8,128)(2,1)} %param.9), kind=kLoop, calls=%fused_computation.123 | loop fusion | flops 262144 | bytes 1048577 | tf_op jit(solution)/shard_map/jit(_where)/select_n | solution.py:220
  6.3 2.1 %collective-permute-start.2 = (bf16[128,1024]{1,0:T(8,128)(2,1)S(1)}, bf16[128,1024]{1,0:T(8,128)(2,1)S(1)}, u32[]{:S(2)}, u32[]{:S(2)}) collective-permute-start(bf16[128,1024]{1,0:T(8,128)(2,1)S(1)} %get-tuple-element.26), channel_id=1, source_target_pairs={{0,1},{1,0},{2,3},{3,2},{4,5},{5,4},{6,7},{7,6},{8,9},{9,8},{10,11... | collective-permute-start | bytes 786440 | tf_op jit(solution)/shard_map/ppermute | solution.py:222
  8.4 3.2 %collective-permute-done.1 = bf16[2,128,8]{1,2,0:T(8,128)(2,1)S(1)} collective-permute-done((bf16[2,128,8]{1,2,0:T(8,128)(2,1)S(1)}, bf16[2,128,8]{1,2,0:T(8,128)(2,1)S(1)}, u32[]{:S(2)}, u32[]{:S(2)}) %collective-permute-start.1) | collective-permute-done | bytes 4128 | tf_op jit(solution)/shard_map/ppermute | solution.py:222
  17.6 1.1 %fusion = f32[8,2,256,128]{3,2,1,0:T(8,128)S(1)} fusion(f32[8,2,128,128]{3,2,1,0:T(8,128)S(1)} %fusion.89, f32[8,2,128,128]{3,2,1,0:T(8,128)S(1)} %get-tuple-element.17), kind=kOutput, calls=%fused_computation | convolution fusion | flops 403177472 | bytes 4194304 | tf_op jit(solution)/shard_map/dot_general | solution.py:58
  18.7 1.0 %slice_add_fusion.5 = (f32[8,2,128,128]{3,2,1,0:T(8,128)S(1)}, f32[8,2,128,128]{3,2,1,0:T(8,128)S(1)}, f32[8,2,128,128]{3,2,1,0:T(8,128)S(1)}, f32[8,2,128,128]{3,2,1,0:T(8,128)S(1)}) fusion(f32[8,2,256,128]{3,2,1,0:T(8,128)S(1)} %fusion, f32[4,2,128,128]{3,2,1,0:T(8,128)S(1)} %fusion.86, f32[8,2,128]{2,1,0:T(2,128)S(1)} %copy.73, ...), kind=kLoop, calls=%fused_computation.63 | loop fusion | flops 2359296 | bytes 8511488 | tf_op jit(solution)/shard_map/add | solution.py:61
  19.7 1.1 %fusion.4 = f32[8,2,256,128]{3,2,1,0:T(8,128)S(1)} fusion(f32[8,2,128,128]{3,2,1,0:T(8,128)S(1)} %get-tuple-element.12, f32[8,2,128,128]{3,2,1,0:T(8,128)S(1)} %get-tuple-element.11), kind=kOutput, calls=%fused_computation.4 | convolution fusion | flops 403177472 | bytes 4194304 | tf_op jit(solution)/shard_map/dot_general | solution.py:58
  21.1 1.1 %fusion.8 = f32[8,2,256,128]{3,2,1,0:T(8,128)S(1)} fusion(f32[8,2,128,128]{3,2,1,0:T(8,128)S(1)} %get-tuple-element.10, f32[8,2,128,128]{3,2,1,0:T(8,128)S(1)} %get-tuple-element.9), kind=kOutput, calls=%fused_computation.8 | convolution fusion | flops 403177472 | bytes 4194304 | tf_op jit(solution)/shard_map/dot_general | solution.py:58
  22.4 1.1 %fusion.12 = f32[8,2,256,128]{3,2,1,0:T(8,128)S(1)} fusion(f32[8,2,128,128]{3,2,1,0:T(8,128)S(1)} %get-tuple-element.8, f32[8,2,128,128]{3,2,1,0:T(8,128)S(1)} %get-tuple-element.7), kind=kOutput, calls=%fused_computation.12 | convolution fusion | flops 403177472 | bytes 4194304 | tf_op jit(solution)/shard_map/dot_general | solution.py:58
  23.7 1.1 %fusion.16 = f32[8,2,256,128]{3,2,1,0:T(8,128)S(1)} fusion(f32[8,2,128,128]{3,2,1,0:T(8,128)S(1)} %get-tuple-element.6, f32[8,2,128,128]{3,2,1,0:T(8,128)S(1)} %get-tuple-element.5), kind=kOutput, calls=%fused_computation.16 | convolution fusion | flops 403177472 | bytes 4194304 | tf_op jit(solution)/shard_map/dot_general | solution.py:58
  26.2 1.2 %fusion.20 = f32[8,2,128,256]{3,2,1,0:T(8,128)S(1)} fusion(f32[8,2,128,128]{3,2,1,0:T(8,128)S(1)} %convolution_add_fusion, f32[8,2,128,128]{3,2,1,0:T(8,128)S(1)} %get-tuple-element.24, f32[8,2,128,128]{3,2,1,0:T(8,128)S(1)} %get-tuple-element.36), kind=kOutput, calls=%fused_computation.20 | convolution fusion | flops 403177472 | bytes 5242880 | tf_op jit(solution)/shard_map/dot_general | solution.py:86
  27.4 1.0 %fusion.42 = f32[8,2,128,128]{2,3,1,0:T(8,128)S(1)} fusion(f32[8,2,128,128]{3,2,1,0:T(8,128)S(1)} %get-tuple-element.23, f32[8,2,128,256]{3,2,1,0:T(8,128)S(1)} %fusion.20), kind=kOutput, calls=%fused_computation.74 | convolution fusion | flops 201326592 | bytes 3145728 | tf_op jit(solution)/shard_map/hmck,hmcv->hmkv/dot_general | solution.py:94
  28.4 1.1 %convolution_subtract_fusion = f32[8,2,128,128]{3,2,1,0:T(8,128)S(1)} fusion(f32[8,2,128,128]{3,2,1,0:T(8,128)S(1)} %get-tuple-element.23, f32[8,2,128,256]{3,2,1,0:T(8,128)S(1)} %fusion.20, f32[8,2]{1,0:T(8,128)S(1)} %copy.87, f32[128,128]{1,0:T(8,128)S(1)} %get-tuple-element.41), kind=kOutput, calls=%fused_computation.30 | convolution fusion | flops 201850880 | bytes 3215360 | tf_op jit(solution)/shard_map/hmck,hmcj->hmkj/dot_general | solution.py:91
  31.0 0.9 %broadcast_select_fusion.2 = f32[4,128,256]{1,2,0:T(8,128)} fusion(pred[]{:T(512)S(6)} %eq.27, f32[8,128,128]{1,2,0:T(8,128)S(1)} %convolution_add_fusion.2, f32[8,128,128]{1,2,0:T(8,128)S(1)} %fusion.54), kind=kLoop, calls=%fused_computation.119 | loop fusion | flops 393216 | bytes 1572865 | tf_op jit(solution)/shard_map/jit(_where)/select_n | solution.py:186
  32.0 2.2 %collective-permute-done.3 = f32[4,128,256]{1,2,0:T(8,128)} collective-permute-done((f32[4,128,256]{1,2,0:T(8,128)}, f32[4,128,256]{1,2,0:T(8,128)}, u32[]{:S(2)}, u32[]{:S(2)}) %collective-permute-start.3) | collective-permute-done | bytes 524320 | tf_op jit(solution)/shard_map/ppermute | solution.py:187
  34.2 1.6 %broadcast_select_fusion.1 = (f32[4,128,256]{1,2,0:T(8,128)S(1)}, f32[4,128,256]{1,2,0:T(8,128)S(1)}) fusion(f32[4,128,256]{1,2,0:T(8,128)} %collective-permute-done.3, pred[]{:T(512)S(6)} %eq.27, f32[8,128,128]{1,2,0:T(8,128)} %copy-done.5, f32[8,128,128]{1,2,0:T(8,128)} %copy-done.4), kind=kLoop, calls=%fused_computation.118 | loop fusion | flops 917504 | bytes 2621441 | tf_op jit(solution)/shard_map/jit(_where)/select_n | solution.py:189
  36.4 2.1 %collective-permute-start.4 = (f32[2,128,256]{1,2,0:T(8,128)S(1)}, f32[2,128,256]{1,2,0:T(8,128)S(1)}, u32[]{:S(2)}, u32[]{:S(2)}) collective-permute-start(f32[2,128,256]{1,2,0:T(8,128)S(1)} %broadcast_select_fusion.11), channel_id=1, source_target_pairs={{0,4},{2,6},{4,0},{6,2},{8,12},{10,14},{12,8},{14,10},{16,20},{18,... | collective-permute-start | bytes 786440 | tf_op jit(solution)/shard_map/ppermute | solution.py:187
  38.9 6.2 %collective-permute-done.4 = f32[2,128,256]{1,2,0:T(8,128)S(1)} collective-permute-done((f32[2,128,256]{1,2,0:T(8,128)S(1)}, f32[2,128,256]{1,2,0:T(8,128)S(1)}, u32[]{:S(2)}, u32[]{:S(2)}) %collective-permute-start.4) | collective-permute-done | bytes 262176 | tf_op jit(solution)/shard_map/ppermute | solution.py:187
  45.7 4.0 %collective-permute-start.5 = (f32[2,128,256]{1,2,0:T(8,128)S(1)}, f32[2,128,256]{1,2,0:T(8,128)S(1)}, u32[]{:S(2)}, u32[]{:S(2)}) collective-permute-start(f32[2,128,256]{1,2,0:T(8,128)S(1)} %pad_maximum_fusion.4), channel_id=1, source_target_pairs={{0,8},{2,10},{4,12},{6,14},{8,16},{10,18},{12,20},{14,22},{16,24},... | collective-permute-start | bytes 786440 | tf_op jit(solution)/shard_map/ppermute | solution.py:155
  50.2 4.2 %collective-permute-done.5 = f32[2,128,256]{1,2,0:T(8,128)S(1)} collective-permute-done((f32[2,128,256]{1,2,0:T(8,128)S(1)}, f32[2,128,256]{1,2,0:T(8,128)S(1)}, u32[]{:S(2)}, u32[]{:S(2)}) %collective-permute-start.5) | collective-permute-done | bytes 262176 | tf_op jit(solution)/shard_map/ppermute | solution.py:155
  54.6 6.4 %collective-permute-start.7 = (f32[2,128,128]{1,2,0:T(8,128)S(1)}, f32[2,128,128]{1,2,0:T(8,128)S(1)}, u32[]{:S(2)}, u32[]{:S(2)}) collective-permute-start(f32[2,128,128]{1,2,0:T(8,128)S(1)} %convolution_add_fusion.8), channel_id=1, source_target_pairs={{0,24},{2,26},{4,28},{6,30},{1,25},{3,27},{5,29},{7,31}} | collective-permute-start | bytes 393224 | tf_op jit(solution)/shard_map/ppermute | solution.py:163
  61.3 1.4 %collective-permute-start.6 = (f32[2,128,256]{1,2,0:T(8,128)S(1)}, f32[2,128,256]{1,2,0:T(8,128)S(1)}, u32[]{:S(2)}, u32[]{:S(2)}) collective-permute-start(f32[2,128,256]{1,2,0:T(8,128)S(1)} %pad_maximum_fusion.5), channel_id=1, source_target_pairs={{0,8},{2,10},{4,12},{6,14},{8,16},{10,18},{12,20},{14,22},{16,24},... | collective-permute-start | bytes 786440 | tf_op jit(solution)/shard_map/ppermute | solution.py:162
  62.8 1.0 %fusion.44 = f32[8,2,128,128]{2,3,1,0:T(8,128)S(1)} fusion(f32[8,2,128,128]{3,2,1,0:T(8,128)S(1)} %get-tuple-element.37, f32[8,2,128,256]{3,2,1,0:T(8,128)S(1)} %fusion.20), kind=kOutput, calls=%fused_computation.76 | convolution fusion | flops 201326592 | bytes 3145728 | tf_op jit(solution)/shard_map/hmij,hmjv->hmiv/dot_general | solution.py:112
  63.8 1.1 %collective-permute-done.7 = f32[2,128,128]{1,2,0:T(8,128)S(1)} collective-permute-done((f32[2,128,128]{1,2,0:T(8,128)S(1)}, f32[2,128,128]{1,2,0:T(8,128)S(1)}, u32[]{:S(2)}, u32[]{:S(2)}) %collective-permute-start.7) | collective-permute-done | bytes 131104 | tf_op jit(solution)/shard_map/ppermute | solution.py:163
  64.9 3.3 %collective-permute-done.6 = f32[2,128,256]{1,2,0:T(8,128)S(1)} collective-permute-done((f32[2,128,256]{1,2,0:T(8,128)S(1)}, f32[2,128,256]{1,2,0:T(8,128)S(1)}, u32[]{:S(2)}, u32[]{:S(2)}) %collective-permute-start.6) | collective-permute-done | bytes 262176 | tf_op jit(solution)/shard_map/ppermute | solution.py:162
  68.7 1.6 %collective-permute-start.8 = (f32[2,128,128]{1,2,0:T(8,128)S(1)}, f32[2,128,128]{1,2,0:T(8,128)S(1)}, u32[]{:S(2)}, u32[]{:S(2)}) collective-permute-start(f32[2,128,128]{1,2,0:T(8,128)S(1)} %get-tuple-element.31), channel_id=1, source_target_pairs={{0,4},{2,6},{4,0},{6,2},{8,12},{10,14},{12,8},{14,10},{16,20},{18,... | collective-permute-start | bytes 393224 | tf_op jit(solution)/shard_map/ppermute | solution.py:200
  70.9 2.8 %collective-permute-done.8 = f32[2,128,128]{1,2,0:T(8,128)S(1)} collective-permute-done((f32[2,128,128]{1,2,0:T(8,128)S(1)}, f32[2,128,128]{1,2,0:T(8,128)S(1)}, u32[]{:S(2)}, u32[]{:S(2)}) %collective-permute-start.8) | collective-permute-done | bytes 131104 | tf_op jit(solution)/shard_map/ppermute | solution.py:200
  74.6 1.0 %collective-permute-done.9 = f32[4,128,128]{1,2,0:T(8,128)S(1)} collective-permute-done((f32[4,128,128]{1,2,0:T(8,128)S(1)}, f32[4,128,128]{1,2,0:T(8,128)S(1)}, u32[]{:S(2)}, u32[]{:S(2)}) %collective-permute-start.9) | collective-permute-done | bytes 262176 | tf_op jit(solution)/shard_map/ppermute | solution.py:200
  76.3 1.6 %collective-permute-start.10 = (bf16[128,1024]{0,1:T(8,128)(2,1)S(1)}, bf16[128,1024]{0,1:T(8,128)(2,1)S(1)}, u32[]{:S(2)}, u32[]{:S(2)}) collective-permute-start(bf16[128,1024]{0,1:T(8,128)(2,1)S(1)} %bitcast.104), channel_id=1, source_target_pairs={{0,1},{1,0},{2,3},{3,2},{4,5},{5,4},{6,7},{7,6},{8,9},{9,8},{10,11... | collective-permute-start | bytes 786440 | tf_op jit(solution)/shard_map/ppermute | solution.py:234
  77.9 6.8 %collective-permute-done.10 = bf16[128,1024]{0,1:T(8,128)(2,1)S(1)} collective-permute-done((bf16[128,1024]{0,1:T(8,128)(2,1)S(1)}, bf16[128,1024]{0,1:T(8,128)(2,1)S(1)}, u32[]{:S(2)}, u32[]{:S(2)}) %collective-permute-start.10) | collective-permute-done | bytes 262176 | tf_op jit(solution)/shard_map/ppermute | solution.py:234
  85.8 1.1 %fusion.39 = bf16[128,2048]{1,0:T(8,128)(2,1)} fusion(bf16[128,2048]{1,0:T(8,128)(2,1)S(1)} %copy-done.8, f32[128,2048]{1,0:T(8,128)S(1)} %copy.106, f32[2048]{0:T(1024)S(1)} %broadcast_bitcast_fusion), kind=kLoop, calls=%fused_computation.71 | loop fusion | flops 2097152 | bytes 2105344 | tf_op jit(solution)/shard_map/convert_element_type | solution.py:214
  (92 shorter events, 16.4 us)
Async XLA Ops:
  1.3 11.2 %collective-permute-start = (bf16[2,128,512]{2,1,0:T(8,128)(2,1)S(1)}, bf16[2,128,512]{2,1,0:T(8,128)(2,1)S(1)}, u32[]{:S(2)}, u32[]{:S(2)}) collective-permute-start(bf16[2,128,512]{2,1,0:T(8,128)(2,1)S(1)} %get-tuple-element.30), channel_id=1, source_target_pairs={{0,1},{1,0},{2,3},{3,2},{4,5},{5,4},{6,7},{7,6},{8,9},{9,8},{10,11... | collective-permute-start | bytes 786440 | tf_op jit(solution)/shard_map/ppermute | solution.py:222
  5.1 6.5 %collective-permute-start.1 = (bf16[2,128,8]{1,2,0:T(8,128)(2,1)S(1)}, bf16[2,128,8]{1,2,0:T(8,128)(2,1)S(1)}, u32[]{:S(2)}, u32[]{:S(2)}) collective-permute-start(bf16[2,128,8]{1,2,0:T(8,128)(2,1)S(1)} %get-tuple-element.39), channel_id=1, source_target_pairs={{0,1},{1,0},{2,3},{3,2},{4,5},{5,4},{6,7},{7,6},{8,9},{9,8},{10,11... | collective-permute-start | bytes 12296 | tf_op jit(solution)/shard_map/ppermute | solution.py:222
  6.3 11.0 %collective-permute-start.2 = (bf16[128,1024]{1,0:T(8,128)(2,1)S(1)}, bf16[128,1024]{1,0:T(8,128)(2,1)S(1)}, u32[]{:S(2)}, u32[]{:S(2)}) collective-permute-start(bf16[128,1024]{1,0:T(8,128)(2,1)S(1)} %get-tuple-element.26), channel_id=1, source_target_pairs={{0,1},{1,0},{2,3},{3,2},{4,5},{5,4},{6,7},{7,6},{8,9},{9,8},{10,11... | collective-permute-start | bytes 786440 | tf_op jit(solution)/shard_map/ppermute | solution.py:222
  14.7 1.9 %copy-start.2 = (f32[4,2,128,128]{3,0,2,1:T(4,128)}, f32[4,2,128,128]{3,0,2,1:T(4,128)S(1)}, u32[]{:S(2)}) copy-start(f32[4,2,128,128]{3,0,2,1:T(4,128)S(1)} %get-tuple-element.43) | copy-start | bytes 1572868
  28.4 1.7 %copy-start.6 = (f32[8,2,128,128]{2,3,1,0:T(8,128)}, f32[8,2,128,128]{2,3,1,0:T(8,128)S(1)}, u32[]{:S(2)}) copy-start(f32[8,2,128,128]{2,3,1,0:T(8,128)S(1)} %fusion.42) | copy-start | bytes 3145732
  29.6 2.3 %copy-start = (f32[8,2,128,128]{3,2,1,0:T(8,128)}, f32[8,2,128,128]{3,2,1,0:T(8,128)S(1)}, u32[]{:S(2)}) copy-start(f32[8,2,128,128]{3,2,1,0:T(8,128)S(1)} %convolution_subtract_fusion) | copy-start | bytes 3145732
  30.2 0.8 copy-start.4
  31.0 1.0 %copy-start.5 = (f32[8,128,128]{1,2,0:T(8,128)}, f32[8,128,128]{1,2,0:T(8,128)S(1)}, u32[]{:S(2)}) copy-start(f32[8,128,128]{1,2,0:T(8,128)S(1)} %convolution_add_fusion.2) | copy-start | bytes 1572868
  32.0 2.3 %collective-permute-start.3 = (f32[4,128,256]{1,2,0:T(8,128)}, f32[4,128,256]{1,2,0:T(8,128)}, u32[]{:S(2)}, u32[]{:S(2)}) collective-permute-start(f32[4,128,256]{1,2,0:T(8,128)} %broadcast_select_fusion.2), channel_id=1, source_target_pairs={{0,2},{2,0},{4,6},{6,4},{8,10},{10,8},{12,14},{14,12},{16,18},{18,... | collective-permute-start | bytes 1572872 | tf_op jit(solution)/shard_map/ppermute | solution.py:187
  32.0 6.6 %copy-start.3 = (f32[4,2,128,128]{3,0,2,1:T(4,128)S(1)}, f32[4,2,128,128]{3,0,2,1:T(4,128)}, u32[]{:S(2)}) copy-start(f32[4,2,128,128]{3,0,2,1:T(4,128)} %copy-done.2) | copy-start | bytes 1572868
  36.4 8.7 %collective-permute-start.4 = (f32[2,128,256]{1,2,0:T(8,128)S(1)}, f32[2,128,256]{1,2,0:T(8,128)S(1)}, u32[]{:S(2)}, u32[]{:S(2)}) collective-permute-start(f32[2,128,256]{1,2,0:T(8,128)S(1)} %broadcast_select_fusion.11), channel_id=1, source_target_pairs={{0,4},{2,6},{4,0},{6,2},{8,12},{10,14},{12,8},{14,10},{16,20},{18,... | collective-permute-start | bytes 786440 | tf_op jit(solution)/shard_map/ppermute | solution.py:187
  45.7 8.8 %collective-permute-start.5 = (f32[2,128,256]{1,2,0:T(8,128)S(1)}, f32[2,128,256]{1,2,0:T(8,128)S(1)}, u32[]{:S(2)}, u32[]{:S(2)}) collective-permute-start(f32[2,128,256]{1,2,0:T(8,128)S(1)} %pad_maximum_fusion.4), channel_id=1, source_target_pairs={{0,8},{2,10},{4,12},{6,14},{8,16},{10,18},{12,20},{14,22},{16,24},... | collective-permute-start | bytes 786440 | tf_op jit(solution)/shard_map/ppermute | solution.py:155
  54.6 10.3 %collective-permute-start.7 = (f32[2,128,128]{1,2,0:T(8,128)S(1)}, f32[2,128,128]{1,2,0:T(8,128)S(1)}, u32[]{:S(2)}, u32[]{:S(2)}) collective-permute-start(f32[2,128,128]{1,2,0:T(8,128)S(1)} %convolution_add_fusion.8), channel_id=1, source_target_pairs={{0,24},{2,26},{4,28},{6,30},{1,25},{3,27},{5,29},{7,31}} | collective-permute-start | bytes 393224 | tf_op jit(solution)/shard_map/ppermute | solution.py:163
  61.3 8.9 %copy-start.7 = (f32[8,2,128,128]{2,3,1,0:T(8,128)S(1)}, f32[8,2,128,128]{2,3,1,0:T(8,128)}, u32[]{:S(2)}) copy-start(f32[8,2,128,128]{2,3,1,0:T(8,128)} %copy-done.6) | copy-start | bytes 3145732
  61.3 6.9 %collective-permute-start.6 = (f32[2,128,256]{1,2,0:T(8,128)S(1)}, f32[2,128,256]{1,2,0:T(8,128)S(1)}, u32[]{:S(2)}, u32[]{:S(2)}) collective-permute-start(f32[2,128,256]{1,2,0:T(8,128)S(1)} %pad_maximum_fusion.5), channel_id=1, source_target_pairs={{0,8},{2,10},{4,12},{6,14},{8,16},{10,18},{12,20},{14,22},{16,24},... | collective-permute-start | bytes 786440 | tf_op jit(solution)/shard_map/ppermute | solution.py:162
  68.5 5.6 %copy-start.1 = (f32[8,2,128,128]{3,2,1,0:T(8,128)S(1)}, f32[8,2,128,128]{3,2,1,0:T(8,128)}, u32[]{:S(2)}) copy-start(f32[8,2,128,128]{3,2,1,0:T(8,128)} %copy-done) | copy-start | bytes 3145732
  68.7 5.0 %collective-permute-start.8 = (f32[2,128,128]{1,2,0:T(8,128)S(1)}, f32[2,128,128]{1,2,0:T(8,128)S(1)}, u32[]{:S(2)}, u32[]{:S(2)}) collective-permute-start(f32[2,128,128]{1,2,0:T(8,128)S(1)} %get-tuple-element.31), channel_id=1, source_target_pairs={{0,4},{2,6},{4,0},{6,2},{8,12},{10,14},{12,8},{14,10},{16,20},{18,... | collective-permute-start | bytes 393224 | tf_op jit(solution)/shard_map/ppermute | solution.py:200
  74.0 1.6 %collective-permute-start.9 = (f32[4,128,128]{1,2,0:T(8,128)S(1)}, f32[4,128,128]{1,2,0:T(8,128)S(1)}, u32[]{:S(2)}, u32[]{:S(2)}) collective-permute-start(f32[4,128,128]{1,2,0:T(8,128)S(1)} %get-tuple-element.21), channel_id=1, source_target_pairs={{0,2},{2,0},{4,6},{6,4},{8,10},{10,8},{12,14},{14,12},{16,18},{18,... | collective-permute-start | bytes 786440 | tf_op jit(solution)/shard_map/ppermute | solution.py:200
  75.6 2.3 %copy-start.9 = (bf16[128]{0:T(256)(128)(2,1)S(1)}, bf16[128]{0:T(256)(128)(2,1)}, u32[]{:S(2)}) copy-start(bf16[128]{0:T(256)(128)(2,1)} %param.13) | copy-start | bytes 772
  76.3 8.4 %collective-permute-start.10 = (bf16[128,1024]{0,1:T(8,128)(2,1)S(1)}, bf16[128,1024]{0,1:T(8,128)(2,1)S(1)}, u32[]{:S(2)}, u32[]{:S(2)}) collective-permute-start(bf16[128,1024]{0,1:T(8,128)(2,1)S(1)} %bitcast.104), channel_id=1, source_target_pairs={{0,1},{1,0},{2,3},{3,2},{4,5},{5,4},{6,7},{7,6},{8,9},{9,8},{10,11... | collective-permute-start | bytes 786440 | tf_op jit(solution)/shard_map/ppermute | solution.py:234
  84.7 1.0 %copy-start.8 = (bf16[128,2048]{1,0:T(8,128)(2,1)S(1)}, bf16[128,2048]{1,0:T(8,128)(2,1)}, u32[]{:S(2)}) copy-start(bf16[128,2048]{1,0:T(8,128)(2,1)} %param.10) | copy-start | bytes 1572868

commit v9 on v7

--- a/solution.py
+++ b/solution.py
@@ -266,8 +266,21 @@
     fixed, scaled, total_carry, total_write = span_prep(query_unit, key_unit, group_size, pieces)
     state_in = chain_states(total_carry, total_write)
     core_out = span_out(fixed, scaled, state_in)
-    core_rows = head_outputs(to_rows(core_out).astype(jnp.bfloat16))
-    return gated_norm(core_rows, output_gate, norm_gain)
+    core_rows = to_rows(core_out).astype(jnp.bfloat16)
+    if lax.axis_size("head") != 2:
+        return gated_norm(head_outputs(core_rows), output_gate, norm_gain)
+    width = output_gate.shape[1] // 2
+    tokens = output_gate.shape[0]
+    first = lax.axis_index("head") == 0
+    own_gate = jnp.where(first, output_gate[:, :width], output_gate[:, width:])
+    sent_gate = jnp.where(first, output_gate[:, width:], output_gate[:, :width])
+    sent_gate, v_head = lax.optimization_barrier((sent_gate, v_head))
+    got_gate = lax.ppermute(sent_gate, "head", [(0, 1), (1, 0)])
+    own_core = jnp.where(first, core_rows[:tokens], core_rows[tokens:])
+    sent_core = jnp.where(first, core_rows[tokens:], core_rows[:tokens])
+    got = lax.ppermute(gated_norm(sent_core, got_gate, norm_gain), "head", [(0, 1), (1, 0)])
+    own = gated_norm(own_core, own_gate, norm_gain)
+    return jnp.where(first, jnp.concatenate([own, got], 1), jnp.concatenate([got, own], 1))
 
 
 def solution(mesh):

time: 83.7 us -> 85.2 us (1.018)
  waiting for transfers between devices: 28.3 us -> 26 us
  other arithmetic: 14.9 us -> 16.9 us
  starting transfers between devices: 19.3 us -> 20.8 us
    ppermute x6, waiting for transfers between devices: 17.1 us -> 14.8 us  [chain_states(): got = lax.ppermute(other, 'ctx', [(i, i ^ stride) for i in range(size)])]
    select_n x1 -> x3, other arithmetic: 0.04 us -> 1.72 us  [the longest x1 0.93 us: on_device(): jnp.where(first, jnp.concatenate([own, got], 1), jnp.concatenate([got, ow...]
    ppermute x1 -> x2, starting transfers between devices: 1.58 us -> 3.1 us  [the longest x1 1.58 us: on_device(): lax.ppermute(gated_norm(sent_core, got_gate, norm_gain), 'head', [(0, 1),...]
    ppermute x1 -> x2, waiting for transfers between devices: 6.82 us -> 6.83 us  [the longest x1 6.83 us: on_device(): lax.ppermute(gated_norm(sent_core, got_gate, norm_gain), 'head', [(0, 1),...]
  transfers between devices with their start and end apart: 11 -> 12, of which waited for: 9 -> 9; matrix products, arithmetic and copies ran while one was open for 13% -> 18% of each run, Pallas kernels for 0% -> 0%
where the time goes in v9:
time: 85.2 us; the launch traced here: 84.9 us
  waiting for transfers between devices  26 us (31%)
  starting transfers between devices  20.8 us (24%)
  matrix products  17.7 us (21%)
  other arithmetic  16.9 us (20%)
  local copies, waits for them, and re-layouts  2.92 us (3%)
    ppermute x6, waiting for transfers between devices, chain_states(): got = lax.ppermute(other, 'ctx', [(i, i ^ stride) for i in range(size)])  14.8 us
    ppermute x6, starting transfers between devices, chain_states(): got = lax.ppermute(other, 'ctx', [(i, i ^ stride) for i in range(size)])  7.58 us
    ppermute x1, waiting for transfers between devices, on_device(): lax.ppermute(gated_norm(sent_core, got_gate, norm_gain), 'head', [(0, 1),...  6.83 us
    dot_general x5, matrix products, unit_lower_inverse(): jnp.matmul(jnp.concatenate([inverse, power], axis=-2), power, precision=L...  5.37 us
    ppermute x3, starting transfers between devices, head_swap(): got = lax.ppermute(sent, 'head', [(0, 1), (1, 0)])  5.18 us
    ppermute x1, starting transfers between devices, exclusive_scan(): return lax.ppermute(write, 'ctx', near)  4.92 us
    ppermute x3, waiting for transfers between devices, head_swap(): got = lax.ppermute(sent, 'head', [(0, 1), (1, 0)])  3.18 us
    select_n x3, other arithmetic, head_swap(): own = jnp.where(first, rows[..., :width], rows[..., width:])  3.15 us
  transfers between devices with their start and end apart: 12, of which 9 were waited for; matrix products, arithmetic and copies ran while one was open for 18% of the time, Pallas kernels for 0%

profile of v9, /device:TPU:0, one launch (start us, length us, event | category | flops | bytes accessed | tf_op | source)
XLA Modules:
  0.0 84.9 jit_solution(17346874293113060728)
XLA Ops:
  0.0 1.3 %broadcast_select_fusion.8 = (bf16[2,128,512]{2,1,0:T(8,128)(2,1)S(1)}, bf16[2,128,512]{2,1,0:T(8,128)(2,1)S(1)}) fusion(pred[]{:T(512)S(6)} %eq.29, bf16[1,128,1024]{2,1,0:T(8,128)(2,1)} %bitcast.152, bf16[1,128,1024]{2,1,0:T(8,128)(2,1)} %bitcast.153), kind=kLoop, calls=%fused_computation.139 | loop fusion | flops 1835008 | bytes 1048577 | tf_op jit(solution)/shard_map/jit(_where)/select_n | solution.py:216
  1.3 3.0 %collective-permute-start = (bf16[2,128,512]{2,1,0:T(8,128)(2,1)S(1)}, bf16[2,128,512]{2,1,0:T(8,128)(2,1)S(1)}, u32[]{:S(2)}, u32[]{:S(2)}) collective-permute-start(bf16[2,128,512]{2,1,0:T(8,128)(2,1)S(1)} %get-tuple-element.30), channel_id=1, source_target_pairs={{0,1},{1,0},{2,3},{3,2},{4,5},{5,4},{6,7},{7,6},{8,9},{9,8},{10,11... | collective-permute-start | bytes 786440 | tf_op jit(solution)/shard_map/ppermute | solution.py:218
  5.2 1.1 %broadcast_select_fusion.6 = (bf16[128,1024]{1,0:T(8,128)(2,1)S(1)}, bf16[128,1024]{1,0:T(8,128)(2,1)S(1)}) fusion(pred[]{:T(512)S(6)} %eq.29, bf16[128,2048]{1,0:T(8,128)(2,1)} %param.9), kind=kLoop, calls=%fused_computation.137 | loop fusion | flops 262144 | bytes 1048577 | tf_op jit(solution)/shard_map/jit(_where)/select_n | solution.py:216
  6.3 2.1 %collective-permute-start.2 = (bf16[128,1024]{1,0:T(8,128)(2,1)S(1)}, bf16[128,1024]{1,0:T(8,128)(2,1)S(1)}, u32[]{:S(2)}, u32[]{:S(2)}) collective-permute-start(bf16[128,1024]{1,0:T(8,128)(2,1)S(1)} %get-tuple-element.26), channel_id=1, source_target_pairs={{0,1},{1,0},{2,3},{3,2},{4,5},{5,4},{6,7},{7,6},{8,9},{9,8},{10,11... | collective-permute-start | bytes 786440 | tf_op jit(solution)/shard_map/ppermute | solution.py:218
  8.4 3.2 %collective-permute-done.1 = bf16[2,128,8]{1,2,0:T(8,128)(2,1)S(1)} collective-permute-done((bf16[2,128,8]{1,2,0:T(8,128)(2,1)S(1)}, bf16[2,128,8]{1,2,0:T(8,128)(2,1)S(1)}, u32[]{:S(2)}, u32[]{:S(2)}) %collective-permute-start.1) | collective-permute-done | bytes 4128 | tf_op jit(solution)/shard_map/ppermute | solution.py:218
  17.6 1.1 %fusion = f32[8,2,256,128]{3,2,1,0:T(8,128)S(1)} fusion(f32[8,2,128,128]{3,2,1,0:T(8,128)S(1)} %fusion.100, f32[8,2,128,128]{3,2,1,0:T(8,128)S(1)} %get-tuple-element.17), kind=kOutput, calls=%fused_computation | convolution fusion | flops 403177472 | bytes 4194304 | tf_op jit(solution)/shard_map/dot_general | solution.py:58
  18.7 1.0 %slice_add_fusion.5 = (f32[8,2,128,128]{3,2,1,0:T(8,128)S(1)}, f32[8,2,128,128]{3,2,1,0:T(8,128)S(1)}, f32[8,2,128,128]{3,2,1,0:T(8,128)S(1)}, f32[8,2,128,128]{3,2,1,0:T(8,128)S(1)}) fusion(f32[8,2,256,128]{3,2,1,0:T(8,128)S(1)} %fusion, f32[4,2,128,128]{3,2,1,0:T(8,128)S(1)} %fusion.97, f32[8,2,128]{2,1,0:T(2,128)S(1)} %copy.69, ...), kind=kLoop, calls=%fused_computation.56 | loop fusion | flops 2359296 | bytes 8511488 | tf_op jit(solution)/shard_map/add | solution.py:61
  19.7 1.1 %fusion.4 = f32[8,2,256,128]{3,2,1,0:T(8,128)S(1)} fusion(f32[8,2,128,128]{3,2,1,0:T(8,128)S(1)} %get-tuple-element.12, f32[8,2,128,128]{3,2,1,0:T(8,128)S(1)} %get-tuple-element.11), kind=kOutput, calls=%fused_computation.4 | convolution fusion | flops 403177472 | bytes 4194304 | tf_op jit(solution)/shard_map/dot_general | solution.py:58
  21.1 1.1 %fusion.8 = f32[8,2,256,128]{3,2,1,0:T(8,128)S(1)} fusion(f32[8,2,128,128]{3,2,1,0:T(8,128)S(1)} %get-tuple-element.10, f32[8,2,128,128]{3,2,1,0:T(8,128)S(1)} %get-tuple-element.9), kind=kOutput, calls=%fused_computation.8 | convolution fusion | flops 403177472 | bytes 4194304 | tf_op jit(solution)/shard_map/dot_general | solution.py:58
  22.4 1.1 %fusion.12 = f32[8,2,256,128]{3,2,1,0:T(8,128)S(1)} fusion(f32[8,2,128,128]{3,2,1,0:T(8,128)S(1)} %get-tuple-element.8, f32[8,2,128,128]{3,2,1,0:T(8,128)S(1)} %get-tuple-element.7), kind=kOutput, calls=%fused_computation.12 | convolution fusion | flops 403177472 | bytes 4194304 | tf_op jit(solution)/shard_map/dot_general | solution.py:58
  23.7 1.1 %fusion.16 = f32[8,2,256,128]{3,2,1,0:T(8,128)S(1)} fusion(f32[8,2,128,128]{3,2,1,0:T(8,128)S(1)} %get-tuple-element.6, f32[8,2,128,128]{3,2,1,0:T(8,128)S(1)} %get-tuple-element.5), kind=kOutput, calls=%fused_computation.16 | convolution fusion | flops 403177472 | bytes 4194304 | tf_op jit(solution)/shard_map/dot_general | solution.py:58
  26.2 1.2 %fusion.20 = f32[8,2,128,256]{3,2,1,0:T(8,128)S(1)} fusion(f32[8,2,128,128]{3,2,1,0:T(8,128)S(1)} %convolution_add_fusion, f32[8,2,128,128]{3,2,1,0:T(8,128)S(1)} %get-tuple-element.24, f32[8,2,128,128]{3,2,1,0:T(8,128)S(1)} %get-tuple-element.40), kind=kOutput, calls=%fused_computation.20 | convolution fusion | flops 403177472 | bytes 5242880 | tf_op jit(solution)/shard_map/dot_general | solution.py:86
  27.4 1.0 %fusion.38 = f32[8,2,128,128]{2,3,1,0:T(8,128)S(1)} fusion(f32[8,2,128,128]{3,2,1,0:T(8,128)S(1)} %get-tuple-element.23, f32[8,2,128,256]{3,2,1,0:T(8,128)S(1)} %fusion.20), kind=kOutput, calls=%fused_computation.66 | convolution fusion | flops 201326592 | bytes 3145728 | tf_op jit(solution)/shard_map/hmck,hmcv->hmkv/dot_general | solution.py:94
  28.4 1.1 %convolution_subtract_fusion = f32[8,2,128,128]{3,2,1,0:T(8,128)S(1)} fusion(f32[8,2,128,128]{3,2,1,0:T(8,128)S(1)} %get-tuple-element.23, f32[8,2,128,256]{3,2,1,0:T(8,128)S(1)} %fusion.20, f32[8,2]{1,0:T(8,128)S(1)} %copy.83, f32[128,128]{1,0:T(8,128)S(1)} %get-tuple-element.47), kind=kOutput, calls=%fused_computation.30 | convolution fusion | flops 201850880 | bytes 3215360 | tf_op jit(solution)/shard_map/hmck,hmcj->hmkj/dot_general | solution.py:91
  32.0 2.2 %collective-permute-done.3 = f32[4,128,256]{1,2,0:T(8,128)} collective-permute-done((f32[4,128,256]{1,2,0:T(8,128)}, f32[4,128,256]{1,2,0:T(8,128)}, u32[]{:S(2)}, u32[]{:S(2)}) %collective-permute-start.3) | collective-permute-done | bytes 524320 | tf_op jit(solution)/shard_map/ppermute | solution.py:183
  34.2 1.6 %broadcast_select_fusion.1 = (f32[4,128,256]{1,2,0:T(8,128)S(1)}, f32[4,128,256]{1,2,0:T(8,128)S(1)}) fusion(f32[4,128,256]{1,2,0:T(8,128)} %collective-permute-done.3, pred[]{:T(512)S(6)} %eq.31, f32[8,128,128]{1,2,0:T(8,128)} %copy-done.5, f32[8,128,128]{1,2,0:T(8,128)} %copy-done.4), kind=kLoop, calls=%fused_computation.131 | loop fusion | flops 917504 | bytes 2621441 | tf_op jit(solution)/shard_map/jit(_where)/select_n | solution.py:185
  37.9 2.0 %collective-permute-start.4 = (f32[2,128,256]{1,2,0:T(8,128)}, f32[2,128,256]{1,2,0:T(8,128)}, u32[]{:S(2)}, u32[]{:S(2)}) collective-permute-start(f32[2,128,256]{1,2,0:T(8,128)} %broadcast_select_fusion.13), channel_id=1, source_target_pairs={{0,4},{2,6},{4,0},{6,2},{8,12},{10,14},{12,8},{14,10},{16,20},{18,... | collective-permute-start | bytes 786440 | tf_op jit(solution)/shard_map/ppermute | solution.py:183
  40.6 1.5 %collective-permute-start.10 = (bf16[128,1024]{1,0:T(8,128)(2,1)}, bf16[128,1024]{1,0:T(8,128)(2,1)}, u32[]{:S(2)}, u32[]{:S(2)}) collective-permute-start(bf16[128,1024]{1,0:T(8,128)(2,1)} %broadcast_select_fusion.4), channel_id=1, source_target_pairs={{0,1},{1,0},{2,3},{3,2},{4,5},{5,4},{6,7},{7,6},{8,9},{9,8},{10,11... | collective-permute-start | bytes 786440 | tf_op jit(solution)/shard_map/ppermute | solution.py:278
  42.2 4.6 %collective-permute-done.4 = f32[2,128,256]{1,2,0:T(8,128)} collective-permute-done((f32[2,128,256]{1,2,0:T(8,128)}, f32[2,128,256]{1,2,0:T(8,128)}, u32[]{:S(2)}, u32[]{:S(2)}) %collective-permute-start.4) | collective-permute-done | bytes 262176 | tf_op jit(solution)/shard_map/ppermute | solution.py:183
  46.8 1.2 %broadcast_select_fusion.12 = (f32[2,128,256]{1,2,0:T(8,128)S(1)}, f32[2,128,256]{1,2,0:T(8,128)S(1)}) fusion(f32[2,128,256]{1,2,0:T(8,128)} %collective-permute-done.4, pred[]{:T(512)S(6)} %eq.32, f32[4,128,128]{1,2,0:T(8,128)} %copy-done.8, f32[4,128,128]{1,2,0:T(8,128)S(1)} %fusion.68), kind=kLoop, calls=%fused_computation.156 | loop fusion | flops 458752 | bytes 1310721 | tf_op jit(solution)/shard_map/jit(_where)/select_n | solution.py:185
  48.4 1.9 %collective-permute-start.5 = (f32[1,128,256]{1,2,0:T(8,128)S(1)}, f32[1,128,256]{1,2,0:T(8,128)S(1)}, u32[]{:S(2)}, u32[]{:S(2)}) collective-permute-start(f32[1,128,256]{1,2,0:T(8,128)S(1)} %broadcast_select_fusion.19), channel_id=1, source_target_pairs={{0,8},{2,10},{4,12},{6,14},{8,0},{10,2},{12,4},{14,6},{16,24},{18,... | collective-permute-start | bytes 393224 | tf_op jit(solution)/shard_map/ppermute | solution.py:183
  50.7 2.8 %collective-permute-done.5 = f32[1,128,256]{1,2,0:T(8,128)S(1)} collective-permute-done((f32[1,128,256]{1,2,0:T(8,128)S(1)}, f32[1,128,256]{1,2,0:T(8,128)S(1)}, u32[]{:S(2)}, u32[]{:S(2)}) %collective-permute-start.5) | collective-permute-done | bytes 131104 | tf_op jit(solution)/shard_map/ppermute | solution.py:183
  53.7 4.9 %collective-permute-start.6 = (f32[1,128,128]{1,2,0:T(8,128)S(1)}, f32[1,128,128]{1,2,0:T(8,128)S(1)}, u32[]{:S(2)}, u32[]{:S(2)}) collective-permute-start(f32[1,128,128]{1,2,0:T(8,128)S(1)} %fusion.27), channel_id=1, source_target_pairs={{0,16},{2,18},{4,20},{6,22},{8,24},{10,26},{12,28},{14,30},{1,17},... | collective-permute-start | bytes 196616 | tf_op jit(solution)/shard_map/ppermute | solution.py:161
  59.3 1.2 %collective-permute-done.6 = f32[1,128,128]{1,2,0:T(8,128)S(1)} collective-permute-done((f32[1,128,128]{1,2,0:T(8,128)S(1)}, f32[1,128,128]{1,2,0:T(8,128)S(1)}, u32[]{:S(2)}, u32[]{:S(2)}) %collective-permute-start.6) | collective-permute-done | bytes 65568 | tf_op jit(solution)/shard_map/ppermute | solution.py:161
  60.6 2.0 %collective-permute-start.7 = (f32[1,128,128]{1,2,0:T(8,128)S(1)}, f32[1,128,128]{1,2,0:T(8,128)S(1)}, u32[]{:S(2)}, u32[]{:S(2)}) collective-permute-start(f32[1,128,128]{1,2,0:T(8,128)S(1)} %get-tuple-element.35), channel_id=1, source_target_pairs={{0,8},{2,10},{4,12},{6,14},{8,0},{10,2},{12,4},{14,6},{16,24},{18,... | collective-permute-start | bytes 196616 | tf_op jit(solution)/shard_map/ppermute | solution.py:196
  63.6 1.3 %collective-permute-done.7 = f32[1,128,128]{1,2,0:T(8,128)S(1)} collective-permute-done((f32[1,128,128]{1,2,0:T(8,128)S(1)}, f32[1,128,128]{1,2,0:T(8,128)S(1)}, u32[]{:S(2)}, u32[]{:S(2)}) %collective-permute-start.7) | collective-permute-done | bytes 65568 | tf_op jit(solution)/shard_map/ppermute | solution.py:196
  65.1 1.6 %collective-permute-start.8 = (f32[2,128,128]{1,2,0:T(8,128)S(1)}, f32[2,128,128]{1,2,0:T(8,128)S(1)}, u32[]{:S(2)}, u32[]{:S(2)}) collective-permute-start(f32[2,128,128]{1,2,0:T(8,128)S(1)} %get-tuple-element.33), channel_id=1, source_target_pairs={{0,4},{2,6},{4,0},{6,2},{8,12},{10,14},{12,8},{14,10},{16,20},{18,... | collective-permute-start | bytes 393224 | tf_op jit(solution)/shard_map/ppermute | solution.py:196
  67.4 2.8 %collective-permute-done.8 = f32[2,128,128]{1,2,0:T(8,128)S(1)} collective-permute-done((f32[2,128,128]{1,2,0:T(8,128)S(1)}, f32[2,128,128]{1,2,0:T(8,128)S(1)}, u32[]{:S(2)}, u32[]{:S(2)}) %collective-permute-start.8) | collective-permute-done | bytes 131104 | tf_op jit(solution)/shard_map/ppermute | solution.py:196
  71.0 1.0 %collective-permute-done.9 = f32[4,128,128]{1,2,0:T(8,128)S(1)} collective-permute-done((f32[4,128,128]{1,2,0:T(8,128)S(1)}, f32[4,128,128]{1,2,0:T(8,128)S(1)}, u32[]{:S(2)}, u32[]{:S(2)}) %collective-permute-start.9) | collective-permute-done | bytes 262176 | tf_op jit(solution)/shard_map/ppermute | solution.py:196
  74.1 1.4 %fusion.61 = (bf16[128,1024]{1,0:T(8,128)(2,1)S(1)}, bf16[128,1024]{1,0:T(8,128)(2,1)S(1)}) fusion(f32[128,1024]{1,0:T(8,128)S(1)} %copy.100, f32[16,8,8,128]{3,2,1,0:T(8,128)S(1)} %bitcast.150, f32[1024]{0:T(1024)S(1)} %broadcast_bitcast_fusion, pred[]{:T(512)S(6)} %eq.29, bf16[128,2048]{1,0:T(8,128)(2,1)S(1)} %copy-done.12, ...), kind=kLoop, calls=%fused_computation.117 | loop fusion | flops 2490368 | bytes 3411969 | tf_op jit(solution)/shard_map/convert_element_type | solution.py:210
  75.6 1.6 %collective-permute-start.11 = (bf16[128,1024]{1,0:T(8,128)(2,1)S(1)}, bf16[128,1024]{1,0:T(8,128)(2,1)S(1)}, u32[]{:S(2)}, u32[]{:S(2)}) collective-permute-start(bf16[128,1024]{1,0:T(8,128)(2,1)S(1)} %get-tuple-element.45), channel_id=1, source_target_pairs={{0,1},{1,0},{2,3},{3,2},{4,5},{5,4},{6,7},{7,6},{8,9},{9,8},{10,11... | collective-permute-start | bytes 786440 | tf_op jit(solution)/shard_map/ppermute | solution.py:281
  77.2 6.8 %collective-permute-done.11 = bf16[128,1024]{1,0:T(8,128)(2,1)S(1)} collective-permute-done((bf16[128,1024]{1,0:T(8,128)(2,1)S(1)}, bf16[128,1024]{1,0:T(8,128)(2,1)S(1)}, u32[]{:S(2)}, u32[]{:S(2)}) %collective-permute-start.11) | collective-permute-done | bytes 262176 | tf_op jit(solution)/shard_map/ppermute | solution.py:281
  (111 shorter events, 21.3 us)
Async XLA Ops:
  1.3 11.2 %collective-permute-start = (bf16[2,128,512]{2,1,0:T(8,128)(2,1)S(1)}, bf16[2,128,512]{2,1,0:T(8,128)(2,1)S(1)}, u32[]{:S(2)}, u32[]{:S(2)}) collective-permute-start(bf16[2,128,512]{2,1,0:T(8,128)(2,1)S(1)} %get-tuple-element.30), channel_id=1, source_target_pairs={{0,1},{1,0},{2,3},{3,2},{4,5},{5,4},{6,7},{7,6},{8,9},{9,8},{10,11... | collective-permute-start | bytes 786440 | tf_op jit(solution)/shard_map/ppermute | solution.py:218
  5.1 6.5 %collective-permute-start.1 = (bf16[2,128,8]{1,2,0:T(8,128)(2,1)S(1)}, bf16[2,128,8]{1,2,0:T(8,128)(2,1)S(1)}, u32[]{:S(2)}, u32[]{:S(2)}) collective-permute-start(bf16[2,128,8]{1,2,0:T(8,128)(2,1)S(1)} %get-tuple-element.43), channel_id=1, source_target_pairs={{0,1},{1,0},{2,3},{3,2},{4,5},{5,4},{6,7},{7,6},{8,9},{9,8},{10,11... | collective-permute-start | bytes 12296 | tf_op jit(solution)/shard_map/ppermute | solution.py:218
  6.3 11.0 %collective-permute-start.2 = (bf16[128,1024]{1,0:T(8,128)(2,1)S(1)}, bf16[128,1024]{1,0:T(8,128)(2,1)S(1)}, u32[]{:S(2)}, u32[]{:S(2)}) collective-permute-start(bf16[128,1024]{1,0:T(8,128)(2,1)S(1)} %get-tuple-element.26), channel_id=1, source_target_pairs={{0,1},{1,0},{2,3},{3,2},{4,5},{5,4},{6,7},{7,6},{8,9},{9,8},{10,11... | collective-permute-start | bytes 786440 | tf_op jit(solution)/shard_map/ppermute | solution.py:218
  14.7 1.9 %copy-start.2 = (f32[4,2,128,128]{3,0,2,1:T(4,128)}, f32[4,2,128,128]{3,0,2,1:T(4,128)S(1)}, u32[]{:S(2)}) copy-start(f32[4,2,128,128]{3,0,2,1:T(4,128)S(1)} %get-tuple-element.49) | copy-start | bytes 1572868
  28.4 1.7 %copy-start.6 = (f32[8,2,128,128]{2,3,1,0:T(8,128)}, f32[8,2,128,128]{2,3,1,0:T(8,128)S(1)}, u32[]{:S(2)}) copy-start(f32[8,2,128,128]{2,3,1,0:T(8,128)S(1)} %fusion.38) | copy-start | bytes 3145732
  29.6 2.3 %copy-start = (f32[8,2,128,128]{3,2,1,0:T(8,128)}, f32[8,2,128,128]{3,2,1,0:T(8,128)S(1)}, u32[]{:S(2)}) copy-start(f32[8,2,128,128]{3,2,1,0:T(8,128)S(1)} %convolution_subtract_fusion) | copy-start | bytes 3145732
  30.2 0.8 copy-start.4
  31.0 1.0 %copy-start.5 = (f32[8,128,128]{1,2,0:T(8,128)}, f32[8,128,128]{1,2,0:T(8,128)S(1)}, u32[]{:S(2)}) copy-start(f32[8,128,128]{1,2,0:T(8,128)S(1)} %convolution_add_fusion.2) | copy-start | bytes 1572868
  32.0 2.3 %collective-permute-start.3 = (f32[4,128,256]{1,2,0:T(8,128)}, f32[4,128,256]{1,2,0:T(8,128)}, u32[]{:S(2)}, u32[]{:S(2)}) collective-permute-start(f32[4,128,256]{1,2,0:T(8,128)} %broadcast_select_fusion.2), channel_id=1, source_target_pairs={{0,2},{2,0},{4,6},{6,4},{8,10},{10,8},{12,14},{14,12},{16,18},{18,... | collective-permute-start | bytes 1572872 | tf_op jit(solution)/shard_map/ppermute | solution.py:183
  32.0 7.9 %copy-start.11 = (bf16[128,2048]{1,0:T(8,128)(2,1)S(1)}, bf16[128,2048]{1,0:T(8,128)(2,1)}, u32[]{:S(2)}) copy-start(bf16[128,2048]{1,0:T(8,128)(2,1)} %param.10) | copy-start | bytes 1572868
  35.9 2.0 %copy-start.9 = (f32[4,128,256]{1,2,0:T(8,128)}, f32[4,128,256]{1,2,0:T(8,128)S(1)}, u32[]{:S(2)}) copy-start(f32[4,128,256]{1,2,0:T(8,128)S(1)} %get-tuple-element.14) | copy-start | bytes 1572868
  35.9 6.3 %copy-start.13 = (bf16[128]{0:T(256)(128)(2,1)S(1)}, bf16[128]{0:T(256)(128)(2,1)}, u32[]{:S(2)}) copy-start(bf16[128]{0:T(256)(128)(2,1)} %param.13) | copy-start | bytes 772
  36.4 0.7 copy-start.8
  37.9 8.9 %collective-permute-start.4 = (f32[2,128,256]{1,2,0:T(8,128)}, f32[2,128,256]{1,2,0:T(8,128)}, u32[]{:S(2)}, u32[]{:S(2)}) collective-permute-start(f32[2,128,256]{1,2,0:T(8,128)} %broadcast_select_fusion.13), channel_id=1, source_target_pairs={{0,4},{2,6},{4,0},{6,2},{8,12},{10,14},{12,8},{14,10},{16,20},{18,... | collective-permute-start | bytes 786440 | tf_op jit(solution)/shard_map/ppermute | solution.py:183
  40.6 33.1 %collective-permute-start.10 = (bf16[128,1024]{1,0:T(8,128)(2,1)}, bf16[128,1024]{1,0:T(8,128)(2,1)}, u32[]{:S(2)}, u32[]{:S(2)}) collective-permute-start(bf16[128,1024]{1,0:T(8,128)(2,1)} %broadcast_select_fusion.4), channel_id=1, source_target_pairs={{0,1},{1,0},{2,3},{3,2},{4,5},{5,4},{6,7},{7,6},{8,9},{9,8},{10,11... | collective-permute-start | bytes 786440 | tf_op jit(solution)/shard_map/ppermute | solution.py:278
  42.1 8.2 %copy-start.3 = (f32[4,2,128,128]{3,0,2,1:T(4,128)S(1)}, f32[4,2,128,128]{3,0,2,1:T(4,128)}, u32[]{:S(2)}) copy-start(f32[4,2,128,128]{3,0,2,1:T(4,128)} %copy-done.2) | copy-start | bytes 1572868
  48.4 5.1 %collective-permute-start.5 = (f32[1,128,256]{1,2,0:T(8,128)S(1)}, f32[1,128,256]{1,2,0:T(8,128)S(1)}, u32[]{:S(2)}, u32[]{:S(2)}) collective-permute-start(f32[1,128,256]{1,2,0:T(8,128)S(1)} %broadcast_select_fusion.19), channel_id=1, source_target_pairs={{0,8},{2,10},{4,12},{6,14},{8,0},{10,2},{12,4},{14,6},{16,24},{18,... | collective-permute-start | bytes 393224 | tf_op jit(solution)/shard_map/ppermute | solution.py:183
  53.7 6.7 %collective-permute-start.6 = (f32[1,128,128]{1,2,0:T(8,128)S(1)}, f32[1,128,128]{1,2,0:T(8,128)S(1)}, u32[]{:S(2)}, u32[]{:S(2)}) collective-permute-start(f32[1,128,128]{1,2,0:T(8,128)S(1)} %fusion.27), channel_id=1, source_target_pairs={{0,16},{2,18},{4,20},{6,22},{8,24},{10,26},{12,28},{14,30},{1,17},... | collective-permute-start | bytes 196616 | tf_op jit(solution)/shard_map/ppermute | solution.py:161
  59.2 7.5 %copy-start.7 = (f32[8,2,128,128]{2,3,1,0:T(8,128)S(1)}, f32[8,2,128,128]{2,3,1,0:T(8,128)}, u32[]{:S(2)}) copy-start(f32[8,2,128,128]{2,3,1,0:T(8,128)} %copy-done.6) | copy-start | bytes 3145732
  60.6 4.3 %collective-permute-start.7 = (f32[1,128,128]{1,2,0:T(8,128)S(1)}, f32[1,128,128]{1,2,0:T(8,128)S(1)}, u32[]{:S(2)}, u32[]{:S(2)}) collective-permute-start(f32[1,128,128]{1,2,0:T(8,128)S(1)} %get-tuple-element.35), channel_id=1, source_target_pairs={{0,8},{2,10},{4,12},{6,14},{8,0},{10,2},{12,4},{14,6},{16,24},{18,... | collective-permute-start | bytes 196616 | tf_op jit(solution)/shard_map/ppermute | solution.py:196
  63.6 6.6 %copy-start.10 = (f32[4,128,256]{1,2,0:T(8,128)S(1)}, f32[4,128,256]{1,2,0:T(8,128)}, u32[]{:S(2)}) copy-start(f32[4,128,256]{1,2,0:T(8,128)} %copy-done.9) | copy-start | bytes 1572868
  64.9 5.6 %copy-start.1 = (f32[8,2,128,128]{3,2,1,0:T(8,128)S(1)}, f32[8,2,128,128]{3,2,1,0:T(8,128)}, u32[]{:S(2)}) copy-start(f32[8,2,128,128]{3,2,1,0:T(8,128)} %copy-done) | copy-start | bytes 3145732
  65.1 5.0 %collective-permute-start.8 = (f32[2,128,128]{1,2,0:T(8,128)S(1)}, f32[2,128,128]{1,2,0:T(8,128)S(1)}, u32[]{:S(2)}, u32[]{:S(2)}) collective-permute-start(f32[2,128,128]{1,2,0:T(8,128)S(1)} %get-tuple-element.33), channel_id=1, source_target_pairs={{0,4},{2,6},{4,0},{6,2},{8,12},{10,14},{12,8},{14,10},{16,20},{18,... | collective-permute-start | bytes 393224 | tf_op jit(solution)/shard_map/ppermute | solution.py:196
  70.5 1.6 %collective-permute-start.9 = (f32[4,128,128]{1,2,0:T(8,128)S(1)}, f32[4,128,128]{1,2,0:T(8,128)S(1)}, u32[]{:S(2)}, u32[]{:S(2)}) collective-permute-start(f32[4,128,128]{1,2,0:T(8,128)S(1)} %get-tuple-element.21), channel_id=1, source_target_pairs={{0,2},{2,0},{4,6},{6,4},{8,10},{10,8},{12,14},{14,12},{16,18},{18,... | collective-permute-start | bytes 786440 | tf_op jit(solution)/shard_map/ppermute | solution.py:196
  72.9 1.2 %copy-start.12 = (bf16[128,2048]{1,0:T(8,128)(2,1)S(1)}, bf16[128,2048]{1,0:T(8,128)(2,1)}, u32[]{:S(2)}) copy-start(bf16[128,2048]{1,0:T(8,128)(2,1)} %param.10) | copy-start | bytes 1572868
  75.6 8.4 %collective-permute-start.11 = (bf16[128,1024]{1,0:T(8,128)(2,1)S(1)}, bf16[128,1024]{1,0:T(8,128)(2,1)S(1)}, u32[]{:S(2)}, u32[]{:S(2)}) collective-permute-start(bf16[128,1024]{1,0:T(8,128)(2,1)S(1)} %get-tuple-element.45), channel_id=1, source_target_pairs={{0,1},{1,0},{2,3},{3,2},{4,5},{5,4},{6,7},{7,6},{8,9},{9,8},{10,11... | collective-permute-start | bytes 786440 | tf_op jit(solution)/shard_map/ppermute | solution.py:281

commit v10 on v7

--- a/solution.py
+++ b/solution.py
@@ -181,10 +181,14 @@
         mine = jnp.where(upper, current[half:], current[:half])
         other = jnp.where(upper, current[:half], current[half:])
         got = lax.ppermute(other, "ctx", [(i, i ^ stride) for i in range(size)])
-        earlier = jnp.where(upper, got, mine)
-        later = jnp.where(upper, mine, got)
+
+        def ordered(earlier, later):
+            return (joined(*compose(split(earlier), split(later))), earlier)
+
+        current, earlier = lax.cond(
+            upper, lambda a, b: ordered(b, a), lambda a, b: ordered(a, b), mine, got
+        )
         saved.append((upper, earlier))
-        current = joined(*compose(split(earlier), split(later)))
     state = exclusive_scan(*split(current), size, 2**levels)
     for level in reversed(range(levels)):
         stride = 2**level

time: 83.7 us -> 98 us (1.17)
  matrix products: 17.7 us -> 28 us
  local copies, waits for them, and re-layouts: 2.66 us -> 9.97 us
  waiting for transfers between devices: 28.3 us -> 24.1 us
  other arithmetic: 14.9 us -> 16 us
    another operation x0 -> x5, local copies, waits for them, and re-layouts: none -> 6.46 us
    ppermute x6, waiting for transfers between devices: 17.1 us -> 14.1 us  [chain_states(): got = lax.ppermute(other, 'ctx', [(i, i ^ stride) for i in range(size)])]
    dot_general x1, matrix products: 0.59 us -> 3.2 us  [span_prep(): jnp.einsum('hmij,hmjk->hmik', scores, weights, precision=LOCAL_PRECISION)]
    dot_general x3 -> x4, matrix products: 1.06 us -> 3.35 us  [compose(): jnp.matmul(later[0], earlier[0], precision=FULL_PRECISION)]
    dot_general x1, matrix products: 0.67 us -> 2.95 us  [span_prep(): jnp.matmul(reach[:, m], reach_add, precision=LOCAL_PRECISION)]
    dot_general x4, matrix products: 1.32 us -> 3.49 us  [compose(): jnp.matmul(later[0], earlier[1], precision=FULL_PRECISION) + later[1]]
    ppermute x1, waiting for transfers between devices: 1.16 us -> 0.01 us  [exclusive_scan(): return lax.ppermute(write, 'ctx', near)]
    select_n x6 -> x3, other arithmetic: 4.46 us -> 3.32 us  [chain_states(): mine = jnp.where(upper, current[half:], current[:half])]
  transfers between devices with their start and end apart: 11 -> 11, of which waited for: 9 -> 8; matrix products, arithmetic and copies ran while one was open for 13% -> 18% of each run, Pallas kernels for 0% -> 0%
where the time goes in v10:
time: 98 us; the launch traced here: 97.5 us
  matrix products  28 us (29%)
  waiting for transfers between devices  24.1 us (25%)
  starting transfers between devices  18.7 us (19%)
  other arithmetic  16 us (16%)
  local copies, waits for them, and re-layouts  9.97 us (10%)
    ppermute x6, waiting for transfers between devices, chain_states(): got = lax.ppermute(other, 'ctx', [(i, i ^ stride) for i in range(size)])  14.1 us
    ppermute x6, starting transfers between devices, chain_states(): got = lax.ppermute(other, 'ctx', [(i, i ^ stride) for i in range(size)])  7.31 us
    ppermute x1, waiting for transfers between devices, head_return(): got = lax.ppermute(sent, 'head', [(0, 1), (1, 0)])  6.82 us
    another operation x5, local copies, waits for them, and re-layouts  6.46 us
    dot_general x5, matrix products, unit_lower_inverse(): jnp.matmul(jnp.concatenate([inverse, power], axis=-2), power, precision=L...  5.35 us
    ppermute x3, starting transfers between devices, head_swap(): got = lax.ppermute(sent, 'head', [(0, 1), (1, 0)])  5.18 us
    ppermute x1, starting transfers between devices, exclusive_scan(): return lax.ppermute(write, 'ctx', near)  4.65 us
    dot_general x4, matrix products, compose(): jnp.matmul(later[0], earlier[1], precision=FULL_PRECISION) + later[1]  3.49 us
  transfers between devices with their start and end apart: 11, of which 8 were waited for; matrix products, arithmetic and copies ran while one was open for 18% of the time, Pallas kernels for 0%

profile of v10, /device:TPU:0, one launch (start us, length us, event | category | flops | bytes accessed | tf_op | source)
XLA Modules:
  0.0 97.5 jit_solution(12791998968278711382)
XLA Ops:
  0.0 1.3 %broadcast_select_fusion.5 = (bf16[2,128,512]{2,1,0:T(8,128)(2,1)S(1)}, bf16[2,128,512]{2,1,0:T(8,128)(2,1)S(1)}) fusion(pred[]{:T(512)S(6)} %eq.29, bf16[1,128,1024]{2,1,0:T(8,128)(2,1)} %bitcast.144, bf16[1,128,1024]{2,1,0:T(8,128)(2,1)} %bitcast.145), kind=kLoop, calls=%fused_computation.174 | loop fusion | flops 1835008 | bytes 1048577 | tf_op jit(solution)/shard_map/jit(_where)/select_n | solution.py:220
  1.3 3.0 %collective-permute-start = (bf16[2,128,512]{2,1,0:T(8,128)(2,1)S(1)}, bf16[2,128,512]{2,1,0:T(8,128)(2,1)S(1)}, u32[]{:S(2)}, u32[]{:S(2)}) collective-permute-start(bf16[2,128,512]{2,1,0:T(8,128)(2,1)S(1)} %get-tuple-element.188), channel_id=1, source_target_pairs={{0,1},{1,0},{2,3},{3,2},{4,5},{5,4},{6,7},{7,6},{8,9},{9,8},{10,11... | collective-permute-start | bytes 786440 | tf_op jit(solution)/shard_map/ppermute | solution.py:222
  6.3 2.1 %collective-permute-start.2 = (bf16[128,1024]{1,0:T(8,128)(2,1)S(1)}, bf16[128,1024]{1,0:T(8,128)(2,1)S(1)}, u32[]{:S(2)}, u32[]{:S(2)}) collective-permute-start(bf16[128,1024]{1,0:T(8,128)(2,1)S(1)} %get-tuple-element.184), channel_id=1, source_target_pairs={{0,1},{1,0},{2,3},{3,2},{4,5},{5,4},{6,7},{7,6},{8,9},{9,8},{10,11... | collective-permute-start | bytes 786440 | tf_op jit(solution)/shard_map/ppermute | solution.py:222
  8.4 3.2 %collective-permute-done.1 = bf16[2,128,8]{1,2,0:T(8,128)(2,1)S(1)} collective-permute-done((bf16[2,128,8]{1,2,0:T(8,128)(2,1)S(1)}, bf16[2,128,8]{1,2,0:T(8,128)(2,1)S(1)}, u32[]{:S(2)}, u32[]{:S(2)}) %collective-permute-start.1) | collective-permute-done | bytes 4128 | tf_op jit(solution)/shard_map/ppermute | solution.py:222
  18.7 1.7 %slice_add_fusion.5 = (f32[8,2,128,128]{3,2,1,0:T(8,128)S(1)}, f32[8,2,128,128]{3,2,1,0:T(8,128)S(1)}, f32[8,2,128,128]{3,2,1,0:T(8,128)S(1)}, f32[8,2,128,128]{3,2,1,0:T(8,128)}) fusion(f32[8,2,256,128]{3,2,1,0:T(8,128)S(1)} %fusion.34, f32[4,2,128,128]{3,2,1,0:T(8,128)S(1)} %fusion.110, f32[8,2,128]{2,1,0:T(2,128)S(1)} %copy.111, ...), kind=kLoop, calls=%fused_computation.119 | loop fusion | flops 2359296 | bytes 8511488 | tf_op jit(solution)/shard_map/add | solution.py:61
  26.6 1.2 %fusion.54 = f32[8,2,128,256]{3,2,1,0:T(8,128)S(1)} fusion(f32[8,2,128,128]{3,2,1,0:T(8,128)S(1)} %convolution_add_fusion.4, f32[8,2,128,128]{3,2,1,0:T(8,128)S(1)} %get-tuple-element.182, f32[8,2,128,128]{3,2,1,0:T(8,128)S(1)} %get-tuple-element.198), kind=kOutput, calls=%fused_computation.78 | convolution fusion | flops 403177472 | bytes 5242880 | tf_op jit(solution)/shard_map/dot_general | solution.py:86
  28.9 1.1 %convolution_subtract_fusion = f32[8,2,128,128]{3,2,1,0:T(8,128)S(1)} fusion(f32[8,2,128,128]{3,2,1,0:T(8,128)S(1)} %get-tuple-element.181, f32[8,2,128,256]{3,2,1,0:T(8,128)S(1)} %fusion.54, f32[8,2]{1,0:T(8,128)S(1)} %copy.125, f32[128,128]{1,0:T(8,128)S(1)} %get-tuple-element.203), kind=kOutput, calls=%fused_computation.88 | convolution fusion | flops 201850880 | bytes 3215360 | tf_op jit(solution)/shard_map/hmck,hmcj->hmkj/dot_general | solution.py:91
  32.2 2.1 %collective-permute-done.3 = f32[4,128,256]{1,2,0:T(8,128)S(1)} collective-permute-done((f32[4,128,256]{1,2,0:T(8,128)}, f32[4,128,256]{1,2,0:T(8,128)S(1)}, u32[]{:S(2)}, u32[]{:S(2)}) %collective-permute-start.3) | collective-permute-done | bytes 524320 | tf_op jit(solution)/shard_map/ppermute | solution.py:183
  34.3 3.7 %conditional.3 = (f32[4,128,256]{1,2,0:T(8,128)S(1)}, f32[2,128,256]{1,2,0:T(8,128)S(1)}, f32[2,128,256]{1,2,0:T(8,128)S(1)}) conditional(s32[]{:T(128)} %convert_element_type.88, (f32[4,128,256]{1,2,0:T(8,128)S(1)}, f32[4,128,256]{1,2,0:T(8,128)S(1)}) %tuple.41, (f32[4,128,256]{1,2,0:T(8,128)S(1)}, f32[4,128,256]{1,2,0:T(8,128)S(1)}) %tuple.42), branch_computations={%region_3.4_spmd, %region_4.5_spmd} | conditional | flops 100859904 | bytes 4980760 | solution.py:188
  35.3 1.3 %convolution_add_fusion = f32[4,128,128]{1,2,0:T(8,128)S(1)} fusion(f32[4,128,256]{1,2,0:T(8,128)S(1)} %get-tuple-element.141, f32[4,128,256]{1,2,0:T(8,128)S(1)} %get-tuple-element.206, f32[4,128,256]{2,1,0:T(8,128)} %copy.128), kind=kOutput, calls=%fused_computation | convolution fusion | flops 50397184 | bytes 1048576 | tf_op jit(solution)/shard_map/cond/branch_0_fun/dot_general | solution.py:22
  36.6 1.3 %fusion.2 = f32[4,128,128]{1,2,0:T(8,128)S(1)} fusion(f32[4,128,256]{1,2,0:T(8,128)S(1)} %get-tuple-element.206, f32[4,128,256]{2,1,0:T(8,128)} %copy.128), kind=kOutput, calls=%fused_computation.6 | convolution fusion | flops 50331648 | bytes 786432 | tf_op jit(solution)/shard_map/cond/branch_0_fun/dot_general | solution.py:21
  38.8 2.0 %collective-permute-start.4 = (f32[2,128,256]{1,2,0:T(8,128)}, f32[2,128,256]{1,2,0:T(8,128)S(1)}, u32[]{:S(2)}, u32[]{:S(2)}) collective-permute-start(f32[2,128,256]{1,2,0:T(8,128)} %get-tuple-element.180), channel_id=1, source_target_pairs={{0,4},{2,6},{4,0},{6,2},{8,12},{10,14},{12,8},{14,10},{16,20},{18,... | collective-permute-start | bytes 786440 | tf_op jit(solution)/shard_map/ppermute | solution.py:183
  40.9 6.9 %collective-permute-done.4 = f32[2,128,256]{1,2,0:T(8,128)S(1)} collective-permute-done((f32[2,128,256]{1,2,0:T(8,128)}, f32[2,128,256]{1,2,0:T(8,128)S(1)}, u32[]{:S(2)}, u32[]{:S(2)}) %collective-permute-start.4) | collective-permute-done | bytes 262176 | tf_op jit(solution)/shard_map/ppermute | solution.py:183
  48.4 7.6 %conditional.4 = (f32[2,128,256]{1,2,0:T(8,128)S(1)}, f32[1,128,256]{2,1,0:T(8,128)S(1)}, f32[1,128,256]{2,1,0:T(8,128)}) conditional(s32[]{:T(128)} %convert_element_type.87, (f32[2,128,256]{1,2,0:T(8,128)}, f32[2,128,256]{1,2,0:T(8,128)S(1)}) %tuple.114, (f32[2,128,256]{1,2,0:T(8,128)S(1)}, f32[2,128,256]{1,2,0:T(8,128)}) %tuple.115), branch_computations={%region_5.6_spmd, %region_6.7_spmd} | conditional | flops 50429952 | bytes 3014680 | solution.py:188
  48.4 1.8 %copy.134 = f32[2,128,256]{2,1,0:T(8,128)} copy(f32[2,128,256]{1,2,0:T(8,128)} %get-tuple-element.145) | data formatting | bytes 524288 | tf_op jit(solution)/shard_map
  50.3 1.2 %convolution_add_fusion.2 = f32[2,128,128]{1,2,0:T(8,128)S(1)} fusion(f32[2,128,256]{1,2,0:T(8,128)} %get-tuple-element.145, f32[2,128,256]{1,2,0:T(8,128)S(1)} %get-tuple-element.212, f32[2,128,256]{2,1,0:T(8,128)} %copy.134), kind=kOutput, calls=%fused_computation.20 | convolution fusion | flops 25198592 | bytes 524288 | tf_op jit(solution)/shard_map/cond/branch_0_fun/dot_general | solution.py:22
  51.5 1.2 %fusion.14 = f32[2,128,128]{1,2,0:T(8,128)S(1)} fusion(f32[2,128,256]{1,2,0:T(8,128)S(1)} %get-tuple-element.212, f32[2,128,256]{2,1,0:T(8,128)} %copy.134), kind=kOutput, calls=%fused_computation.26 | convolution fusion | flops 25165824 | bytes 393216 | tf_op jit(solution)/shard_map/cond/branch_0_fun/dot_general | solution.py:21
  54.4 1.7 %copy.105 = f32[1,128,256]{2,1,0:T(8,128)} copy(f32[1,128,256]{1,2,0:T(8,128)} %get-tuple-element.159) | data formatting | bytes 262144 | tf_op jit(solution)/shard_map
  56.7 1.7 %broadcast_select_fusion.11 = (f32[1,128,256]{2,1,0:T(8,128)S(1)}, f32[1,128,256]{2,1,0:T(8,128)}) fusion(f32[1,128,256]{2,1,0:T(8,128)} %copy-done.9, f32[1,128,256]{2,1,0:T(8,128)} %get-tuple-element.75, pred[]{:T(512)S(6)} %eq.33), kind=kLoop, calls=%fused_computation.191 | loop fusion | flops 65536 | bytes 524289 | tf_op jit(solution)/shard_map/jit(_where)/select_n | solution.py:181
  58.3 1.8 %collective-permute-start.5 = (f32[1,128,256]{2,1,0:T(8,128)}, f32[1,128,256]{2,1,0:T(8,128)}, u32[]{:S(2)}, u32[]{:S(2)}) collective-permute-start(f32[1,128,256]{2,1,0:T(8,128)} %get-tuple-element.192), channel_id=1, source_target_pairs={{0,8},{2,10},{4,12},{6,14},{8,0},{10,2},{12,4},{14,6},{16,24},{18,... | collective-permute-start | bytes 393224 | tf_op jit(solution)/shard_map/ppermute | solution.py:183
  60.2 1.3 %bitcast_multiply_fusion.2 = f32[8,2,128,128]{3,2,1,0:T(8,128)} fusion(f32[8,2,128]{2,1,0:T(2,128)S(1)} %copy.122, f32[4,2,128,128]{3,2,1,0:T(8,128)S(1)} %copy.109), kind=kLoop, calls=%fused_computation.123 | loop fusion | flops 262144 | bytes 1581056 | tf_op jit(solution)/shard_map/mul | solution.py:113
  61.5 2.2 %collective-permute-done.5 = f32[1,128,256]{2,1,0:T(8,128)} collective-permute-done((f32[1,128,256]{2,1,0:T(8,128)}, f32[1,128,256]{2,1,0:T(8,128)}, u32[]{:S(2)}, u32[]{:S(2)}) %collective-permute-start.5) | collective-permute-done | bytes 131104 | tf_op jit(solution)/shard_map/ppermute | solution.py:183
  63.7 1.5 %conditional.5 = (f32[1,128,256]{1,2,0:T(8,128)S(1)}, f32[1,128,256]{2,1,0:T(8,128)S(1)}) conditional(s32[]{:T(128)} %convert_element_type.86, (f32[1,128,256]{2,1,0:T(8,128)}, f32[1,128,256]{2,1,0:T(8,128)S(1)}) %tuple.45, (f32[1,128,256]{2,1,0:T(8,128)S(1)}, f32[1,128,256]{2,1,0:T(8,128)}) %tuple.46), branch_computations={%region_7.8_spmd, %region_8.9_spmd} | conditional | flops 25214976 | bytes 1245200 | solution.py:188
  65.4 4.7 %collective-permute-start.6 = (f32[1,128,128]{2,1,0:T(8,128)S(1)}, f32[1,128,128]{2,1,0:T(8,128)S(1)}, u32[]{:S(2)}, u32[]{:S(2)}) collective-permute-start(f32[1,128,128]{2,1,0:T(8,128)S(1)} %slice.357), channel_id=1, source_target_pairs={{0,16},{2,18},{4,20},{6,22},{8,24},{10,26},{12,28},{14,30},{1,17},... | collective-permute-start | bytes 196616 | tf_op jit(solution)/shard_map/ppermute | solution.py:161
  70.0 3.2 %convolution_subtract_fusion.1 = f32[8,2,128,128]{3,2,1,0:T(8,128)} fusion(f32[8,2,128,128]{3,2,1,0:T(8,128)} %bitcast_multiply_fusion.2, f32[8,2,128,128]{3,2,1,0:T(8,128)} %get-tuple-element.199, f32[8,2,128,256]{3,2,1,0:T(8,128)S(1)} %fusion.54), kind=kOutput, calls=%fused_computation.89 | convolution fusion | flops 201588736 | bytes 4194304 | tf_op jit(solution)/shard_map/hmij,hmjk->hmik/dot_general | solution.py:113
  73.4 3.3 %collective-permute-start.7 = (f32[1,128,128]{2,1,0:T(8,128)S(1)}, f32[1,128,128]{2,1,0:T(8,128)S(1)}, u32[]{:S(2)}, u32[]{:S(2)}) collective-permute-start(f32[1,128,128]{2,1,0:T(8,128)S(1)} %get-tuple-element.193), channel_id=1, source_target_pairs={{0,8},{2,10},{4,12},{6,14},{8,0},{10,2},{12,4},{14,6},{16,24},{18,... | collective-permute-start | bytes 196616 | tf_op jit(solution)/shard_map/ppermute | solution.py:200
  76.7 2.0 %fusion.79 = f32[8,2,128,128]{2,3,1,0:T(8,128)} fusion(f32[8,2,128,128]{3,2,1,0:T(8,128)S(1)} %copy-done, f32[8,2,128,256]{3,2,1,0:T(8,128)S(1)} %fusion.54), kind=kOutput, calls=%fused_computation.132 | convolution fusion | flops 201326592 | bytes 3145728 | tf_op jit(solution)/shard_map/hmij,hmjv->hmiv/dot_general | solution.py:112
  79.3 3.0 %fusion.60 = f32[8,1,128,128]{2,3,0,1:T(8,128)} fusion(f32[8,2,128,128]{2,3,1,0:T(8,128)} %fusion.79, f32[8,2,128,128]{3,2,1,0:T(8,128)} %convolution_subtract_fusion.1, f32[8,2,128,128]{2,3,1,0:T(8,128)} %copy-done.6), kind=kOutput, calls=%fused_computation.98 | convolution fusion | flops 100794368 | bytes 2097152 | tf_op jit(solution)/shard_map/dot_general | solution.py:121
  82.5 1.8 %collective-permute-done.8 = f32[2,128,128]{2,1,0:T(8,128)S(1)} collective-permute-done((f32[2,128,128]{2,1,0:T(8,128)S(1)}, f32[2,128,128]{2,1,0:T(8,128)S(1)}, u32[]{:S(2)}, u32[]{:S(2)}) %collective-permute-start.8) | collective-permute-done | bytes 131104 | tf_op jit(solution)/shard_map/ppermute | solution.py:200
  86.9 1.6 %collective-permute-start.10 = (bf16[128,1024]{0,1:T(8,128)(2,1)S(1)}, bf16[128,1024]{0,1:T(8,128)(2,1)S(1)}, u32[]{:S(2)}, u32[]{:S(2)}) collective-permute-start(bf16[128,1024]{0,1:T(8,128)(2,1)S(1)} %bitcast.146), channel_id=1, source_target_pairs={{0,1},{1,0},{2,3},{3,2},{4,5},{5,4},{6,7},{7,6},{8,9},{9,8},{10,11... | collective-permute-start | bytes 786440 | tf_op jit(solution)/shard_map/ppermute | solution.py:234
  88.5 6.8 %collective-permute-done.10 = bf16[128,1024]{0,1:T(8,128)(2,1)S(1)} collective-permute-done((bf16[128,1024]{0,1:T(8,128)(2,1)S(1)}, bf16[128,1024]{0,1:T(8,128)(2,1)S(1)}, u32[]{:S(2)}, u32[]{:S(2)}) %collective-permute-start.10) | collective-permute-done | bytes 262176 | tf_op jit(solution)/shard_map/ppermute | solution.py:234
  96.3 1.1 %fusion.74 = bf16[128,2048]{1,0:T(8,128)(2,1)} fusion(bf16[128,2048]{1,0:T(8,128)(2,1)S(1)} %copy-done.10, f32[128,2048]{1,0:T(8,128)S(1)} %copy.145, f32[2048]{0:T(1024)S(1)} %broadcast_bitcast_fusion), kind=kLoop, calls=%fused_computation.127 | loop fusion | flops 2097152 | bytes 2105344 | tf_op jit(solution)/shard_map/convert_element_type | solution.py:214
  (111 shorter events, 29.3 us)
Async XLA Ops:
  1.3 11.2 %collective-permute-start = (bf16[2,128,512]{2,1,0:T(8,128)(2,1)S(1)}, bf16[2,128,512]{2,1,0:T(8,128)(2,1)S(1)}, u32[]{:S(2)}, u32[]{:S(2)}) collective-permute-start(bf16[2,128,512]{2,1,0:T(8,128)(2,1)S(1)} %get-tuple-element.188), channel_id=1, source_target_pairs={{0,1},{1,0},{2,3},{3,2},{4,5},{5,4},{6,7},{7,6},{8,9},{9,8},{10,11... | collective-permute-start | bytes 786440 | tf_op jit(solution)/shard_map/ppermute | solution.py:222
  5.1 6.5 %collective-permute-start.1 = (bf16[2,128,8]{1,2,0:T(8,128)(2,1)S(1)}, bf16[2,128,8]{1,2,0:T(8,128)(2,1)S(1)}, u32[]{:S(2)}, u32[]{:S(2)}) collective-permute-start(bf16[2,128,8]{1,2,0:T(8,128)(2,1)S(1)} %get-tuple-element.201), channel_id=1, source_target_pairs={{0,1},{1,0},{2,3},{3,2},{4,5},{5,4},{6,7},{7,6},{8,9},{9,8},{10,11... | collective-permute-start | bytes 12296 | tf_op jit(solution)/shard_map/ppermute | solution.py:222
  6.3 11.0 %collective-permute-start.2 = (bf16[128,1024]{1,0:T(8,128)(2,1)S(1)}, bf16[128,1024]{1,0:T(8,128)(2,1)S(1)}, u32[]{:S(2)}, u32[]{:S(2)}) collective-permute-start(bf16[128,1024]{1,0:T(8,128)(2,1)S(1)} %get-tuple-element.184), channel_id=1, source_target_pairs={{0,1},{1,0},{2,3},{3,2},{4,5},{5,4},{6,7},{7,6},{8,9},{9,8},{10,11... | collective-permute-start | bytes 786440 | tf_op jit(solution)/shard_map/ppermute | solution.py:222
  14.7 1.9 %copy-start.4 = (f32[4,2,128,128]{3,0,2,1:T(4,128)}, f32[4,2,128,128]{3,0,2,1:T(4,128)S(1)}, u32[]{:S(2)}) copy-start(f32[4,2,128,128]{3,0,2,1:T(4,128)S(1)} %get-tuple-element.205) | copy-start | bytes 1572868
  28.9 1.7 %copy-start.6 = (f32[8,2,128,128]{2,3,1,0:T(8,128)}, f32[8,2,128,128]{2,3,1,0:T(8,128)S(1)}, u32[]{:S(2)}) copy-start(f32[8,2,128,128]{2,3,1,0:T(8,128)S(1)} %fusion.77) | copy-start | bytes 3145732
  30.0 2.2 %copy-start.1 = (f32[8,2,128,128]{3,2,1,0:T(8,128)}, f32[8,2,128,128]{3,2,1,0:T(8,128)S(1)}, u32[]{:S(2)}) copy-start(f32[8,2,128,128]{3,2,1,0:T(8,128)S(1)} %convolution_subtract_fusion) | copy-start | bytes 3145732
  32.2 2.1 %collective-permute-start.3 = (f32[4,128,256]{1,2,0:T(8,128)}, f32[4,128,256]{1,2,0:T(8,128)S(1)}, u32[]{:S(2)}, u32[]{:S(2)}) collective-permute-start(f32[4,128,256]{1,2,0:T(8,128)} %get-tuple-element.172), channel_id=1, source_target_pairs={{0,2},{2,0},{4,6},{6,4},{8,10},{10,8},{12,14},{14,12},{16,18},{18,... | collective-permute-start | bytes 1572872 | tf_op jit(solution)/shard_map/ppermute | solution.py:183
  38.8 8.9 %collective-permute-start.4 = (f32[2,128,256]{1,2,0:T(8,128)}, f32[2,128,256]{1,2,0:T(8,128)S(1)}, u32[]{:S(2)}, u32[]{:S(2)}) collective-permute-start(f32[2,128,256]{1,2,0:T(8,128)} %get-tuple-element.180), channel_id=1, source_target_pairs={{0,4},{2,6},{4,0},{6,2},{8,12},{10,14},{12,8},{14,10},{16,20},{18,... | collective-permute-start | bytes 786440 | tf_op jit(solution)/shard_map/ppermute | solution.py:183
  47.7 0.7 copy-start.8
  48.4 11.7 %copy-start.5 = (f32[4,2,128,128]{3,0,2,1:T(4,128)S(1)}, f32[4,2,128,128]{3,0,2,1:T(4,128)}, u32[]{:S(2)}) copy-start(f32[4,2,128,128]{3,0,2,1:T(4,128)} %copy-done.4) | copy-start | bytes 1572868
  56.0 0.6 copy-start.9
  58.3 5.4 %collective-permute-start.5 = (f32[1,128,256]{2,1,0:T(8,128)}, f32[1,128,256]{2,1,0:T(8,128)}, u32[]{:S(2)}, u32[]{:S(2)}) collective-permute-start(f32[1,128,256]{2,1,0:T(8,128)} %get-tuple-element.192), channel_id=1, source_target_pairs={{0,8},{2,10},{4,12},{6,14},{8,0},{10,2},{12,4},{14,6},{16,24},{18,... | collective-permute-start | bytes 393224 | tf_op jit(solution)/shard_map/ppermute | solution.py:183
  65.4 7.9 %collective-permute-start.6 = (f32[1,128,128]{2,1,0:T(8,128)S(1)}, f32[1,128,128]{2,1,0:T(8,128)S(1)}, u32[]{:S(2)}, u32[]{:S(2)}) collective-permute-start(f32[1,128,128]{2,1,0:T(8,128)S(1)} %slice.357), channel_id=1, source_target_pairs={{0,16},{2,18},{4,20},{6,22},{8,24},{10,26},{12,28},{14,30},{1,17},... | collective-permute-start | bytes 196616 | tf_op jit(solution)/shard_map/ppermute | solution.py:161
  70.0 6.7 %copy-start = (f32[8,2,128,128]{3,2,1,0:T(8,128)S(1)}, f32[8,2,128,128]{3,2,1,0:T(8,128)}, u32[]{:S(2)}) copy-start(f32[8,2,128,128]{3,2,1,0:T(8,128)} %get-tuple-element.199) | copy-start | bytes 3145732
  73.4 5.6 %collective-permute-start.7 = (f32[1,128,128]{2,1,0:T(8,128)S(1)}, f32[1,128,128]{2,1,0:T(8,128)S(1)}, u32[]{:S(2)}, u32[]{:S(2)}) collective-permute-start(f32[1,128,128]{2,1,0:T(8,128)S(1)} %get-tuple-element.193), channel_id=1, source_target_pairs={{0,8},{2,10},{4,12},{6,14},{8,0},{10,2},{12,4},{14,6},{16,24},{18,... | collective-permute-start | bytes 196616 | tf_op jit(solution)/shard_map/ppermute | solution.py:200
  79.2 5.5 %copy-start.2 = (f32[8,2,128,128]{3,2,1,0:T(8,128)S(1)}, f32[8,2,128,128]{3,2,1,0:T(8,128)}, u32[]{:S(2)}) copy-start(f32[8,2,128,128]{3,2,1,0:T(8,128)} %copy-done.1) | copy-start | bytes 3145732
  79.2 5.5 %copy-start.3 = (f32[8,2,128,128]{3,2,1,0:T(8,128)S(1)}, f32[8,2,128,128]{3,2,1,0:T(8,128)}, u32[]{:S(2)}) copy-start(f32[8,2,128,128]{3,2,1,0:T(8,128)} %convolution_subtract_fusion.1) | copy-start | bytes 3145732
  79.2 5.0 %collective-permute-start.8 = (f32[2,128,128]{2,1,0:T(8,128)S(1)}, f32[2,128,128]{2,1,0:T(8,128)S(1)}, u32[]{:S(2)}, u32[]{:S(2)}) collective-permute-start(f32[2,128,128]{2,1,0:T(8,128)S(1)} %get-tuple-element.189), channel_id=1, source_target_pairs={{0,4},{2,6},{4,0},{6,2},{8,12},{10,14},{12,8},{14,10},{16,20},{18,... | collective-permute-start | bytes 393224 | tf_op jit(solution)/shard_map/ppermute | solution.py:200
  82.5 2.6 %copy-start.7 = (f32[8,2,128,128]{2,3,1,0:T(8,128)S(1)}, f32[8,2,128,128]{2,3,1,0:T(8,128)}, u32[]{:S(2)}) copy-start(f32[8,2,128,128]{2,3,1,0:T(8,128)} %fusion.79) | copy-start | bytes 3145732
  84.5 1.6 %slice-start = ((f32[8,2,128,128]{3,2,1,0:T(8,128)}), f32[8,1,128,128]{3,2,1,0:T(8,128)S(1)}, s32[]{:S(2)}) async-start(f32[8,2,128,128]{3,2,1,0:T(8,128)} %convolution_subtract_fusion.1), calls=%async_computation | async-start | bytes 1048576 | tf_op jit(solution)/shard_map/slice | solution.py:117
  84.6 1.6 %copy-start.11 = (f32[8,1,128,128]{2,3,0,1:T(8,128)S(1)}, f32[8,1,128,128]{2,3,0,1:T(8,128)}, u32[]{:S(2)}) copy-start(f32[8,1,128,128]{2,3,0,1:T(8,128)} %fusion.60) | copy-start | bytes 1572868
  84.6 1.6 %collective-permute-start.9 = (f32[4,128,128]{2,1,0:T(8,128)S(1)}, f32[4,128,128]{2,1,0:T(8,128)S(1)}, u32[]{:S(2)}, u32[]{:S(2)}) collective-permute-start(f32[4,128,128]{2,1,0:T(8,128)S(1)} %get-tuple-element.177), channel_id=1, source_target_pairs={{0,2},{2,0},{4,6},{6,4},{8,10},{10,8},{12,14},{14,12},{16,18},{18,... | collective-permute-start | bytes 786440 | tf_op jit(solution)/shard_map/ppermute | solution.py:200
  86.2 2.3 %copy-start.12 = (bf16[128]{0:T(256)(128)(2,1)S(1)}, bf16[128]{0:T(256)(128)(2,1)}, u32[]{:S(2)}) copy-start(bf16[128]{0:T(256)(128)(2,1)} %param.19) | copy-start | bytes 772
  86.9 8.4 %collective-permute-start.10 = (bf16[128,1024]{0,1:T(8,128)(2,1)S(1)}, bf16[128,1024]{0,1:T(8,128)(2,1)S(1)}, u32[]{:S(2)}, u32[]{:S(2)}) collective-permute-start(bf16[128,1024]{0,1:T(8,128)(2,1)S(1)} %bitcast.146), channel_id=1, source_target_pairs={{0,1},{1,0},{2,3},{3,2},{4,5},{5,4},{6,7},{7,6},{8,9},{9,8},{10,11... | collective-permute-start | bytes 786440 | tf_op jit(solution)/shard_map/ppermute | solution.py:234
  95.3 1.0 %copy-start.10 = (bf16[128,2048]{1,0:T(8,128)(2,1)S(1)}, bf16[128,2048]{1,0:T(8,128)(2,1)}, u32[]{:S(2)}) copy-start(bf16[128,2048]{1,0:T(8,128)(2,1)} %param.16) | copy-start | bytes 1572868

commit v11 on v7

--- a/solution.py
+++ b/solution.py
@@ -88,10 +88,9 @@
     weights = solved[..., DV:]
     faded_keys = wide_keys * jnp.exp(cum_log[..., -1:] - cum_log)[..., None]
     tail_decay = jnp.exp(cum_log[..., -1])
-    carry_mat = tail_decay[..., None, None] * jnp.eye(DK, dtype=jnp.float32) - jnp.einsum(
-        "hmck,hmcj->hmkj", faded_keys, weights, precision=LOCAL_PRECISION
-    )
-    write_mat = jnp.einsum("hmck,hmcv->hmkv", faded_keys, written, precision=LOCAL_PRECISION)
+    maps = jnp.einsum("hmck,hmcj->hmkj", faded_keys, solved, precision=LOCAL_PRECISION)
+    carry_mat = tail_decay[..., None, None] * jnp.eye(DK, dtype=jnp.float32) - maps[..., DV:]
+    write_mat = maps[..., :DV]
     return (cum_log, spread, written, weights, carry_mat, write_mat)
 
 

time: 83.7 us -> 82.7 us (0.988)
  waiting for transfers between devices: 28.3 us -> 27.2 us
    ppermute x6, waiting for transfers between devices: 17.1 us -> 16.1 us  [chain_states(): got = lax.ppermute(other, 'ctx', [(i, i ^ stride) for i in range(size)])]
    dot_general x2 -> x1, matrix products: 2.13 us -> 1.11 us  [span_pass(): jnp.einsum('hmck,hmcj->hmkj', faded_keys, solved, precision=LOCAL_PRECISION)]
    dot_general x1, matrix products: 0.67 us -> 1.66 us  [span_prep(): jnp.matmul(reach[:, m], reach_add, precision=LOCAL_PRECISION)]
    unnamed x28 -> x26, local copies, waits for them, and re-layouts: 1.58 us -> 1.74 us
  transfers between devices with their start and end apart: 11 -> 11, of which waited for: 9 -> 9; matrix products, arithmetic and copies ran while one was open for 13% -> 14% of each run, Pallas kernels for 0% -> 0%
where the time goes in v11:
time: 82.7 us; the launch traced here: 82.3 us
  waiting for transfers between devices  27.2 us (33%)
  starting transfers between devices  19.3 us (23%)
  matrix products  17.2 us (21%)
  other arithmetic  15.1 us (18%)
  local copies, waits for them, and re-layouts  2.81 us (3%)
    ppermute x6, waiting for transfers between devices, chain_states(): got = lax.ppermute(other, 'ctx', [(i, i ^ stride) for i in range(size)])  16.1 us
    ppermute x6, starting transfers between devices, chain_states(): got = lax.ppermute(other, 'ctx', [(i, i ^ stride) for i in range(size)])  7.62 us
    ppermute x1, waiting for transfers between devices, head_return(): got = lax.ppermute(sent, 'head', [(0, 1), (1, 0)])  6.81 us
    dot_general x5, matrix products, unit_lower_inverse(): jnp.matmul(jnp.concatenate([inverse, power], axis=-2), power, precision=L...  5.37 us
    ppermute x3, starting transfers between devices, head_swap(): got = lax.ppermute(sent, 'head', [(0, 1), (1, 0)])  5.18 us
    ppermute x1, starting transfers between devices, exclusive_scan(): return lax.ppermute(write, 'ctx', near)  4.92 us
    ppermute x3, waiting for transfers between devices, head_swap(): got = lax.ppermute(sent, 'head', [(0, 1), (1, 0)])  3.18 us
    select_n x3, other arithmetic, head_swap(): own = jnp.where(first, rows[..., :width], rows[..., width:])  3.15 us
  transfers between devices with their start and end apart: 11, of which 9 were waited for; matrix products, arithmetic and copies ran while one was open for 14% of the time, Pallas kernels for 0%

profile of v11, /device:TPU:0, one launch (start us, length us, event | category | flops | bytes accessed | tf_op | source)
XLA Modules:
  0.0 82.3 jit_solution(8802767792781897155)
XLA Ops:
  0.0 1.3 %broadcast_select_fusion.7 = (bf16[2,128,512]{2,1,0:T(8,128)(2,1)S(1)}, bf16[2,128,512]{2,1,0:T(8,128)(2,1)S(1)}) fusion(pred[]{:T(512)S(6)} %eq.29, bf16[1,128,1024]{2,1,0:T(8,128)(2,1)} %bitcast.122, bf16[1,128,1024]{2,1,0:T(8,128)(2,1)} %bitcast.123), kind=kLoop, calls=%fused_computation.124 | loop fusion | flops 1835008 | bytes 1048577 | tf_op jit(solution)/shard_map/jit(_where)/select_n | solution.py:215
  1.3 3.0 %collective-permute-start = (bf16[2,128,512]{2,1,0:T(8,128)(2,1)S(1)}, bf16[2,128,512]{2,1,0:T(8,128)(2,1)S(1)}, u32[]{:S(2)}, u32[]{:S(2)}) collective-permute-start(bf16[2,128,512]{2,1,0:T(8,128)(2,1)S(1)} %get-tuple-element.30), channel_id=1, source_target_pairs={{0,1},{1,0},{2,3},{3,2},{4,5},{5,4},{6,7},{7,6},{8,9},{9,8},{10,11... | collective-permute-start | bytes 786440 | tf_op jit(solution)/shard_map/ppermute | solution.py:217
  5.2 1.1 %broadcast_select_fusion.5 = (bf16[128,1024]{1,0:T(8,128)(2,1)S(1)}, bf16[128,1024]{1,0:T(8,128)(2,1)S(1)}) fusion(pred[]{:T(512)S(6)} %eq.29, bf16[128,2048]{1,0:T(8,128)(2,1)} %param.9), kind=kLoop, calls=%fused_computation.122 | loop fusion | flops 262144 | bytes 1048577 | tf_op jit(solution)/shard_map/jit(_where)/select_n | solution.py:215
  6.3 2.1 %collective-permute-start.2 = (bf16[128,1024]{1,0:T(8,128)(2,1)S(1)}, bf16[128,1024]{1,0:T(8,128)(2,1)S(1)}, u32[]{:S(2)}, u32[]{:S(2)}) collective-permute-start(bf16[128,1024]{1,0:T(8,128)(2,1)S(1)} %get-tuple-element.26), channel_id=1, source_target_pairs={{0,1},{1,0},{2,3},{3,2},{4,5},{5,4},{6,7},{7,6},{8,9},{9,8},{10,11... | collective-permute-start | bytes 786440 | tf_op jit(solution)/shard_map/ppermute | solution.py:217
  8.4 3.2 %collective-permute-done.1 = bf16[2,128,8]{1,2,0:T(8,128)(2,1)S(1)} collective-permute-done((bf16[2,128,8]{1,2,0:T(8,128)(2,1)S(1)}, bf16[2,128,8]{1,2,0:T(8,128)(2,1)S(1)}, u32[]{:S(2)}, u32[]{:S(2)}) %collective-permute-start.1) | collective-permute-done | bytes 4128 | tf_op jit(solution)/shard_map/ppermute | solution.py:217
  17.6 1.1 %fusion = f32[8,2,256,128]{3,2,1,0:T(8,128)S(1)} fusion(f32[8,2,128,128]{3,2,1,0:T(8,128)S(1)} %fusion.89, f32[8,2,128,128]{3,2,1,0:T(8,128)S(1)} %get-tuple-element.17), kind=kOutput, calls=%fused_computation | convolution fusion | flops 403177472 | bytes 4194304 | tf_op jit(solution)/shard_map/dot_general | solution.py:58
  18.7 1.0 %slice_add_fusion.5 = (f32[8,2,128,128]{3,2,1,0:T(8,128)S(1)}, f32[8,2,128,128]{3,2,1,0:T(8,128)S(1)}, f32[8,2,128,128]{3,2,1,0:T(8,128)S(1)}, f32[8,2,128,128]{3,2,1,0:T(8,128)S(1)}) fusion(f32[8,2,256,128]{3,2,1,0:T(8,128)S(1)} %fusion, f32[4,2,128,128]{3,2,1,0:T(8,128)S(1)} %fusion.86, f32[8,2,128]{2,1,0:T(2,128)S(1)} %copy.67, ...), kind=kLoop, calls=%fused_computation.68 | loop fusion | flops 2359296 | bytes 8511488 | tf_op jit(solution)/shard_map/add | solution.py:61
  19.7 1.1 %fusion.4 = f32[8,2,256,128]{3,2,1,0:T(8,128)S(1)} fusion(f32[8,2,128,128]{3,2,1,0:T(8,128)S(1)} %get-tuple-element.12, f32[8,2,128,128]{3,2,1,0:T(8,128)S(1)} %get-tuple-element.11), kind=kOutput, calls=%fused_computation.4 | convolution fusion | flops 403177472 | bytes 4194304 | tf_op jit(solution)/shard_map/dot_general | solution.py:58
  21.1 1.1 %fusion.8 = f32[8,2,256,128]{3,2,1,0:T(8,128)S(1)} fusion(f32[8,2,128,128]{3,2,1,0:T(8,128)S(1)} %get-tuple-element.10, f32[8,2,128,128]{3,2,1,0:T(8,128)S(1)} %get-tuple-element.9), kind=kOutput, calls=%fused_computation.8 | convolution fusion | flops 403177472 | bytes 4194304 | tf_op jit(solution)/shard_map/dot_general | solution.py:58
  22.4 1.1 %fusion.12 = f32[8,2,256,128]{3,2,1,0:T(8,128)S(1)} fusion(f32[8,2,128,128]{3,2,1,0:T(8,128)S(1)} %get-tuple-element.8, f32[8,2,128,128]{3,2,1,0:T(8,128)S(1)} %get-tuple-element.7), kind=kOutput, calls=%fused_computation.12 | convolution fusion | flops 403177472 | bytes 4194304 | tf_op jit(solution)/shard_map/dot_general | solution.py:58
  23.7 1.1 %fusion.16 = f32[8,2,256,128]{3,2,1,0:T(8,128)S(1)} fusion(f32[8,2,128,128]{3,2,1,0:T(8,128)S(1)} %get-tuple-element.6, f32[8,2,128,128]{3,2,1,0:T(8,128)S(1)} %get-tuple-element.5), kind=kOutput, calls=%fused_computation.16 | convolution fusion | flops 403177472 | bytes 4194304 | tf_op jit(solution)/shard_map/dot_general | solution.py:58
  26.2 1.2 %fusion.20 = f32[8,2,128,256]{3,2,1,0:T(8,128)S(1)} fusion(f32[8,2,128,128]{3,2,1,0:T(8,128)S(1)} %convolution_add_fusion, f32[8,2,128,128]{3,2,1,0:T(8,128)S(1)} %get-tuple-element.24, f32[8,2,128,128]{3,2,1,0:T(8,128)S(1)} %get-tuple-element.40), kind=kOutput, calls=%fused_computation.20 | convolution fusion | flops 403177472 | bytes 5242880 | tf_op jit(solution)/shard_map/dot_general | solution.py:86
  27.4 1.1 %fusion.90 = f32[8,2,128,256]{3,2,1,0:T(8,128)S(1)} fusion(f32[8,2,128,128]{3,2,1,0:T(8,128)S(1)} %get-tuple-element.23, f32[8,2,128,256]{3,2,1,0:T(8,128)S(1)} %fusion.20), kind=kOutput, calls=%fused_computation.196 | convolution fusion | flops 402653184 | bytes 5242880 | tf_op jit(solution)/shard_map/hmck,hmcj->hmkj/dot_general | solution.py:91
  30.9 2.2 %collective-permute-done.3 = f32[4,128,256]{2,1,0:T(8,128)} collective-permute-done((f32[4,128,256]{2,1,0:T(8,128)}, f32[4,128,256]{2,1,0:T(8,128)}, u32[]{:S(2)}, u32[]{:S(2)}) %collective-permute-start.3) | collective-permute-done | bytes 524320 | tf_op jit(solution)/shard_map/ppermute | solution.py:182
  33.1 1.7 %broadcast_select_fusion.1 = (f32[4,128,256]{2,1,0:T(8,128)S(1)}, f32[4,128,256]{2,1,0:T(8,128)S(1)}) fusion(f32[4,128,256]{2,1,0:T(8,128)} %collective-permute-done.3, pred[]{:T(512)S(6)} %eq.31, f32[8,128,128]{2,1,0:T(8,128)} %copy-done.5, f32[8,128,128]{2,1,0:T(8,128)} %copy-done.6), kind=kLoop, calls=%fused_computation.117 | loop fusion | flops 917504 | bytes 2621441 | tf_op jit(solution)/shard_map/jit(_where)/select_n | solution.py:184
  36.8 2.0 %collective-permute-start.4 = (f32[2,128,256]{2,1,0:T(8,128)}, f32[2,128,256]{2,1,0:T(8,128)}, u32[]{:S(2)}, u32[]{:S(2)}) collective-permute-start(f32[2,128,256]{2,1,0:T(8,128)} %broadcast_select_fusion.11), channel_id=1, source_target_pairs={{0,4},{2,6},{4,0},{6,2},{8,12},{10,14},{12,8},{14,10},{16,20},{18,... | collective-permute-start | bytes 786440 | tf_op jit(solution)/shard_map/ppermute | solution.py:182
  38.8 6.9 %collective-permute-done.4 = f32[2,128,256]{2,1,0:T(8,128)} collective-permute-done((f32[2,128,256]{2,1,0:T(8,128)}, f32[2,128,256]{2,1,0:T(8,128)}, u32[]{:S(2)}, u32[]{:S(2)}) %collective-permute-start.4) | collective-permute-done | bytes 262176 | tf_op jit(solution)/shard_map/ppermute | solution.py:182
  45.7 1.2 %broadcast_select_fusion.10 = (f32[2,128,256]{2,1,0:T(8,128)S(1)}, f32[2,128,256]{2,1,0:T(8,128)S(1)}) fusion(f32[2,128,256]{2,1,0:T(8,128)} %collective-permute-done.4, pred[]{:T(512)S(6)} %eq.32, f32[4,128,128]{2,1,0:T(8,128)} %copy-done.7, f32[4,128,128]{2,1,0:T(8,128)S(1)} %fusion.59), kind=kLoop, calls=%fused_computation.138 | loop fusion | flops 458752 | bytes 1310721 | tf_op jit(solution)/shard_map/jit(_where)/select_n | solution.py:184
  47.4 1.9 %collective-permute-start.5 = (f32[1,128,256]{2,1,0:T(8,128)S(1)}, f32[1,128,256]{2,1,0:T(8,128)S(1)}, u32[]{:S(2)}, u32[]{:S(2)}) collective-permute-start(f32[1,128,256]{2,1,0:T(8,128)S(1)} %broadcast_select_fusion.17), channel_id=1, source_target_pairs={{0,8},{2,10},{4,12},{6,14},{8,0},{10,2},{12,4},{14,6},{16,24},{18,... | collective-permute-start | bytes 393224 | tf_op jit(solution)/shard_map/ppermute | solution.py:182
  49.7 2.8 %collective-permute-done.5 = f32[1,128,256]{2,1,0:T(8,128)S(1)} collective-permute-done((f32[1,128,256]{2,1,0:T(8,128)S(1)}, f32[1,128,256]{2,1,0:T(8,128)S(1)}, u32[]{:S(2)}, u32[]{:S(2)}) %collective-permute-start.5) | collective-permute-done | bytes 131104 | tf_op jit(solution)/shard_map/ppermute | solution.py:182
  52.7 4.9 %collective-permute-start.6 = (f32[1,128,128]{2,1,0:T(8,128)S(1)}, f32[1,128,128]{2,1,0:T(8,128)S(1)}, u32[]{:S(2)}, u32[]{:S(2)}) collective-permute-start(f32[1,128,128]{2,1,0:T(8,128)S(1)} %fusion.27), channel_id=1, source_target_pairs={{0,16},{2,18},{4,20},{6,22},{8,24},{10,26},{12,28},{14,30},{1,17},... | collective-permute-start | bytes 196616 | tf_op jit(solution)/shard_map/ppermute | solution.py:160
  58.2 1.2 %collective-permute-done.6 = f32[1,128,128]{2,1,0:T(8,128)S(1)} collective-permute-done((f32[1,128,128]{2,1,0:T(8,128)S(1)}, f32[1,128,128]{2,1,0:T(8,128)S(1)}, u32[]{:S(2)}, u32[]{:S(2)}) %collective-permute-start.6) | collective-permute-done | bytes 65568 | tf_op jit(solution)/shard_map/ppermute | solution.py:160
  59.6 2.0 %collective-permute-start.7 = (f32[1,128,128]{2,1,0:T(8,128)S(1)}, f32[1,128,128]{2,1,0:T(8,128)S(1)}, u32[]{:S(2)}, u32[]{:S(2)}) collective-permute-start(f32[1,128,128]{2,1,0:T(8,128)S(1)} %get-tuple-element.35), channel_id=1, source_target_pairs={{0,8},{2,10},{4,12},{6,14},{8,0},{10,2},{12,4},{14,6},{16,24},{18,... | collective-permute-start | bytes 196616 | tf_op jit(solution)/shard_map/ppermute | solution.py:195
  61.6 1.0 %fusion.40 = f32[8,2,128,128]{2,3,1,0:T(8,128)S(1)} fusion(f32[8,2,128,128]{3,2,1,0:T(8,128)S(1)} %get-tuple-element.41, f32[8,2,128,256]{3,2,1,0:T(8,128)S(1)} %fusion.20), kind=kOutput, calls=%fused_computation.61 | convolution fusion | flops 201326592 | bytes 3145728 | tf_op jit(solution)/shard_map/hmij,hmjv->hmiv/dot_general | solution.py:111
  62.6 1.3 %collective-permute-done.7 = f32[1,128,128]{2,1,0:T(8,128)S(1)} collective-permute-done((f32[1,128,128]{2,1,0:T(8,128)S(1)}, f32[1,128,128]{2,1,0:T(8,128)S(1)}, u32[]{:S(2)}, u32[]{:S(2)}) %collective-permute-start.7) | collective-permute-done | bytes 65568 | tf_op jit(solution)/shard_map/ppermute | solution.py:195
  64.1 1.6 %collective-permute-start.8 = (f32[2,128,128]{2,1,0:T(8,128)S(1)}, f32[2,128,128]{2,1,0:T(8,128)S(1)}, u32[]{:S(2)}, u32[]{:S(2)}) collective-permute-start(f32[2,128,128]{2,1,0:T(8,128)S(1)} %get-tuple-element.33), channel_id=1, source_target_pairs={{0,4},{2,6},{4,0},{6,2},{8,12},{10,14},{12,8},{14,10},{16,20},{18,... | collective-permute-start | bytes 393224 | tf_op jit(solution)/shard_map/ppermute | solution.py:195
  65.7 1.7 %fusion.26 = f32[8,1,128,128]{2,3,0,1:T(8,128)S(1)} fusion(f32[8,2,128,128]{2,3,1,0:T(8,128)S(1)} %fusion.40, f32[8,2,128,128]{3,2,1,0:T(8,128)S(1)} %convolution_subtract_fusion, f32[8,2,128,256]{3,2,1,0:T(8,128)} %copy-done.2), kind=kOutput, calls=%fused_computation.39 | convolution fusion | flops 100794368 | bytes 2097152 | tf_op jit(solution)/shard_map/dot_general | solution.py:120
  67.3 1.8 %collective-permute-done.8 = f32[2,128,128]{2,1,0:T(8,128)S(1)} collective-permute-done((f32[2,128,128]{2,1,0:T(8,128)S(1)}, f32[2,128,128]{2,1,0:T(8,128)S(1)}, u32[]{:S(2)}, u32[]{:S(2)}) %collective-permute-start.8) | collective-permute-done | bytes 131104 | tf_op jit(solution)/shard_map/ppermute | solution.py:195
  70.0 1.0 %collective-permute-done.9 = f32[4,128,128]{2,1,0:T(8,128)S(1)} collective-permute-done((f32[4,128,128]{2,1,0:T(8,128)S(1)}, f32[4,128,128]{2,1,0:T(8,128)S(1)}, u32[]{:S(2)}, u32[]{:S(2)}) %collective-permute-start.9) | collective-permute-done | bytes 262176 | tf_op jit(solution)/shard_map/ppermute | solution.py:195
  71.8 1.6 %collective-permute-start.10 = (bf16[128,1024]{0,1:T(8,128)(2,1)S(1)}, bf16[128,1024]{0,1:T(8,128)(2,1)S(1)}, u32[]{:S(2)}, u32[]{:S(2)}) collective-permute-start(bf16[128,1024]{0,1:T(8,128)(2,1)S(1)} %bitcast.124), channel_id=1, source_target_pairs={{0,1},{1,0},{2,3},{3,2},{4,5},{5,4},{6,7},{7,6},{8,9},{9,8},{10,11... | collective-permute-start | bytes 786440 | tf_op jit(solution)/shard_map/ppermute | solution.py:229
  73.4 6.8 %collective-permute-done.10 = bf16[128,1024]{0,1:T(8,128)(2,1)S(1)} collective-permute-done((bf16[128,1024]{0,1:T(8,128)(2,1)S(1)}, bf16[128,1024]{0,1:T(8,128)(2,1)S(1)}, u32[]{:S(2)}, u32[]{:S(2)}) %collective-permute-start.10) | collective-permute-done | bytes 262176 | tf_op jit(solution)/shard_map/ppermute | solution.py:229
  81.2 1.1 %fusion.44 = bf16[128,2048]{1,0:T(8,128)(2,1)} fusion(bf16[128,2048]{1,0:T(8,128)(2,1)S(1)} %copy-done.10, f32[128,2048]{1,0:T(8,128)S(1)} %copy.97, f32[2048]{0:T(1024)S(1)} %broadcast_bitcast_fusion), kind=kLoop, calls=%fused_computation.76 | loop fusion | flops 2097152 | bytes 2105344 | tf_op jit(solution)/shard_map/convert_element_type | solution.py:209
  (95 shorter events, 17.7 us)
Async XLA Ops:
  1.3 11.2 %collective-permute-start = (bf16[2,128,512]{2,1,0:T(8,128)(2,1)S(1)}, bf16[2,128,512]{2,1,0:T(8,128)(2,1)S(1)}, u32[]{:S(2)}, u32[]{:S(2)}) collective-permute-start(bf16[2,128,512]{2,1,0:T(8,128)(2,1)S(1)} %get-tuple-element.30), channel_id=1, source_target_pairs={{0,1},{1,0},{2,3},{3,2},{4,5},{5,4},{6,7},{7,6},{8,9},{9,8},{10,11... | collective-permute-start | bytes 786440 | tf_op jit(solution)/shard_map/ppermute | solution.py:217
  5.1 6.5 %collective-permute-start.1 = (bf16[2,128,8]{1,2,0:T(8,128)(2,1)S(1)}, bf16[2,128,8]{1,2,0:T(8,128)(2,1)S(1)}, u32[]{:S(2)}, u32[]{:S(2)}) collective-permute-start(bf16[2,128,8]{1,2,0:T(8,128)(2,1)S(1)} %get-tuple-element.43), channel_id=1, source_target_pairs={{0,1},{1,0},{2,3},{3,2},{4,5},{5,4},{6,7},{7,6},{8,9},{9,8},{10,11... | collective-permute-start | bytes 12296 | tf_op jit(solution)/shard_map/ppermute | solution.py:217
  6.3 11.0 %collective-permute-start.2 = (bf16[128,1024]{1,0:T(8,128)(2,1)S(1)}, bf16[128,1024]{1,0:T(8,128)(2,1)S(1)}, u32[]{:S(2)}, u32[]{:S(2)}) collective-permute-start(bf16[128,1024]{1,0:T(8,128)(2,1)S(1)} %get-tuple-element.26), channel_id=1, source_target_pairs={{0,1},{1,0},{2,3},{3,2},{4,5},{5,4},{6,7},{7,6},{8,9},{9,8},{10,11... | collective-permute-start | bytes 786440 | tf_op jit(solution)/shard_map/ppermute | solution.py:217
  14.7 1.9 %copy-start.3 = (f32[4,2,128,128]{3,0,2,1:T(4,128)}, f32[4,2,128,128]{3,0,2,1:T(4,128)S(1)}, u32[]{:S(2)}) copy-start(f32[4,2,128,128]{3,0,2,1:T(4,128)S(1)} %get-tuple-element.47) | copy-start | bytes 1572868
  28.5 1.3 %copy-start.2 = (f32[8,2,128,256]{3,2,1,0:T(8,128)}, f32[8,2,128,256]{3,2,1,0:T(8,128)S(1)}, u32[]{:S(2)}) copy-start(f32[8,2,128,256]{3,2,1,0:T(8,128)S(1)} %fusion.90) | copy-start | bytes 6291460
  28.7 2.1 %copy-start = (f32[8,2,128,128]{3,2,1,0:T(8,128)}, f32[8,2,128,128]{3,2,1,0:T(8,128)S(1)}, u32[]{:S(2)}) copy-start(f32[8,2,128,128]{3,2,1,0:T(8,128)S(1)} %slice_subtract_fusion) | copy-start | bytes 3145732
  29.1 1.7 %copy-start.5 = (f32[8,128,128]{2,1,0:T(8,128)}, f32[8,128,128]{2,1,0:T(8,128)S(1)}, u32[]{:S(2)}) copy-start(f32[8,128,128]{2,1,0:T(8,128)S(1)} %convolution_add_fusion.2) | copy-start | bytes 1572868
  29.9 1.0 %copy-start.6 = (f32[8,128,128]{2,1,0:T(8,128)}, f32[8,128,128]{2,1,0:T(8,128)S(1)}, u32[]{:S(2)}) copy-start(f32[8,128,128]{2,1,0:T(8,128)S(1)} %fusion.53) | copy-start | bytes 1572868
  30.9 2.3 %collective-permute-start.3 = (f32[4,128,256]{2,1,0:T(8,128)}, f32[4,128,256]{2,1,0:T(8,128)}, u32[]{:S(2)}, u32[]{:S(2)}) collective-permute-start(f32[4,128,256]{2,1,0:T(8,128)} %broadcast_select_fusion.2), channel_id=1, source_target_pairs={{0,2},{2,0},{4,6},{6,4},{8,10},{10,8},{12,14},{14,12},{16,18},{18,... | collective-permute-start | bytes 1572872 | tf_op jit(solution)/shard_map/ppermute | solution.py:182
  34.8 2.0 %copy-start.8 = (f32[4,128,256]{2,1,0:T(8,128)}, f32[4,128,256]{2,1,0:T(8,128)S(1)}, u32[]{:S(2)}) copy-start(f32[4,128,256]{2,1,0:T(8,128)S(1)} %get-tuple-element.14) | copy-start | bytes 1572868
  35.4 0.7 copy-start.7
  36.8 8.9 %collective-permute-start.4 = (f32[2,128,256]{2,1,0:T(8,128)}, f32[2,128,256]{2,1,0:T(8,128)}, u32[]{:S(2)}, u32[]{:S(2)}) collective-permute-start(f32[2,128,256]{2,1,0:T(8,128)} %broadcast_select_fusion.11), channel_id=1, source_target_pairs={{0,4},{2,6},{4,0},{6,2},{8,12},{10,14},{12,8},{14,10},{16,20},{18,... | collective-permute-start | bytes 786440 | tf_op jit(solution)/shard_map/ppermute | solution.py:182
  38.8 10.5 %copy-start.4 = (f32[4,2,128,128]{3,0,2,1:T(4,128)S(1)}, f32[4,2,128,128]{3,0,2,1:T(4,128)}, u32[]{:S(2)}) copy-start(f32[4,2,128,128]{3,0,2,1:T(4,128)} %copy-done.3) | copy-start | bytes 1572868
  47.4 5.1 %collective-permute-start.5 = (f32[1,128,256]{2,1,0:T(8,128)S(1)}, f32[1,128,256]{2,1,0:T(8,128)S(1)}, u32[]{:S(2)}, u32[]{:S(2)}) collective-permute-start(f32[1,128,256]{2,1,0:T(8,128)S(1)} %broadcast_select_fusion.17), channel_id=1, source_target_pairs={{0,8},{2,10},{4,12},{6,14},{8,0},{10,2},{12,4},{14,6},{16,24},{18,... | collective-permute-start | bytes 393224 | tf_op jit(solution)/shard_map/ppermute | solution.py:182
  52.7 6.7 %collective-permute-start.6 = (f32[1,128,128]{2,1,0:T(8,128)S(1)}, f32[1,128,128]{2,1,0:T(8,128)S(1)}, u32[]{:S(2)}, u32[]{:S(2)}) collective-permute-start(f32[1,128,128]{2,1,0:T(8,128)S(1)} %fusion.27), channel_id=1, source_target_pairs={{0,16},{2,18},{4,20},{6,22},{8,24},{10,26},{12,28},{14,30},{1,17},... | collective-permute-start | bytes 196616 | tf_op jit(solution)/shard_map/ppermute | solution.py:160
  59.6 4.3 %collective-permute-start.7 = (f32[1,128,128]{2,1,0:T(8,128)S(1)}, f32[1,128,128]{2,1,0:T(8,128)S(1)}, u32[]{:S(2)}, u32[]{:S(2)}) collective-permute-start(f32[1,128,128]{2,1,0:T(8,128)S(1)} %get-tuple-element.35), channel_id=1, source_target_pairs={{0,8},{2,10},{4,12},{6,14},{8,0},{10,2},{12,4},{14,6},{16,24},{18,... | collective-permute-start | bytes 196616 | tf_op jit(solution)/shard_map/ppermute | solution.py:195
  62.6 6.6 %copy-start.9 = (f32[4,128,256]{2,1,0:T(8,128)S(1)}, f32[4,128,256]{2,1,0:T(8,128)}, u32[]{:S(2)}) copy-start(f32[4,128,256]{2,1,0:T(8,128)} %copy-done.8) | copy-start | bytes 1572868
  63.9 5.6 %copy-start.1 = (f32[8,2,128,128]{3,2,1,0:T(8,128)S(1)}, f32[8,2,128,128]{3,2,1,0:T(8,128)}, u32[]{:S(2)}) copy-start(f32[8,2,128,128]{3,2,1,0:T(8,128)} %copy-done) | copy-start | bytes 3145732
  64.1 5.0 %collective-permute-start.8 = (f32[2,128,128]{2,1,0:T(8,128)S(1)}, f32[2,128,128]{2,1,0:T(8,128)S(1)}, u32[]{:S(2)}, u32[]{:S(2)}) collective-permute-start(f32[2,128,128]{2,1,0:T(8,128)S(1)} %get-tuple-element.33), channel_id=1, source_target_pairs={{0,4},{2,6},{4,0},{6,2},{8,12},{10,14},{12,8},{14,10},{16,20},{18,... | collective-permute-start | bytes 393224 | tf_op jit(solution)/shard_map/ppermute | solution.py:195
  69.4 1.6 %collective-permute-start.9 = (f32[4,128,128]{2,1,0:T(8,128)S(1)}, f32[4,128,128]{2,1,0:T(8,128)S(1)}, u32[]{:S(2)}, u32[]{:S(2)}) collective-permute-start(f32[4,128,128]{2,1,0:T(8,128)S(1)} %get-tuple-element.21), channel_id=1, source_target_pairs={{0,2},{2,0},{4,6},{6,4},{8,10},{10,8},{12,14},{14,12},{16,18},{18,... | collective-permute-start | bytes 786440 | tf_op jit(solution)/shard_map/ppermute | solution.py:195
  71.0 2.3 %copy-start.11 = (bf16[128]{0:T(256)(128)(2,1)S(1)}, bf16[128]{0:T(256)(128)(2,1)}, u32[]{:S(2)}) copy-start(bf16[128]{0:T(256)(128)(2,1)} %param.13) | copy-start | bytes 772
  71.8 8.4 %collective-permute-start.10 = (bf16[128,1024]{0,1:T(8,128)(2,1)S(1)}, bf16[128,1024]{0,1:T(8,128)(2,1)S(1)}, u32[]{:S(2)}, u32[]{:S(2)}) collective-permute-start(bf16[128,1024]{0,1:T(8,128)(2,1)S(1)} %bitcast.124), channel_id=1, source_target_pairs={{0,1},{1,0},{2,3},{3,2},{4,5},{5,4},{6,7},{7,6},{8,9},{9,8},{10,11... | collective-permute-start | bytes 786440 | tf_op jit(solution)/shard_map/ppermute | solution.py:229
  80.2 1.0 %copy-start.10 = (bf16[128,2048]{1,0:T(8,128)(2,1)S(1)}, bf16[128,2048]{1,0:T(8,128)(2,1)}, u32[]{:S(2)}) copy-start(bf16[128,2048]{1,0:T(8,128)(2,1)} %param.10) | copy-start | bytes 1572868

commit v12 on v11

--- a/solution.py
+++ b/solution.py
@@ -17,10 +17,10 @@
 
 
 def compose(earlier, later):
-    return (
-        jnp.matmul(later[0], earlier[0], precision=FULL_PRECISION),
-        jnp.matmul(later[0], earlier[1], precision=FULL_PRECISION) + later[1],
-    )
+    both = jnp.matmul(
+        later[0], jnp.concatenate([earlier[0], earlier[1]], axis=-1), precision=FULL_PRECISION
+    )
+    return (both[..., : earlier[0].shape[-1]], both[..., earlier[0].shape[-1] :] + later[1])
 
 
 def arrange(key_part, value_part, beta_part, decay_part):
@@ -108,18 +108,23 @@
         * within
     )
     wide_query = jnp.repeat(query_unit, group_size, axis=0)
-    inner = jnp.einsum("hmij,hmjv->hmiv", scores, written, precision=LOCAL_PRECISION)
-    reach = wide_query * jnp.exp(cum_log)[..., None] - jnp.einsum(
-        "hmij,hmjk->hmik", scores, weights, precision=LOCAL_PRECISION
-    )
+    mixed = jnp.einsum(
+        "hmij,hmjv->hmiv",
+        scores,
+        jnp.concatenate([written, weights], axis=-1),
+        precision=LOCAL_PRECISION,
+    )
+    inner = mixed[..., :DV]
+    reach = wide_query * jnp.exp(cum_log)[..., None] - mixed[..., DV:]
     blocks = carry_mat.shape[1]
     fixed, scaled = ([inner[:, 0]], [reach[:, 0]])
     reach_map, reach_add = (carry_mat[:, 0], write_mat[:, 0])
     for m in range(1, blocks):
-        fixed.append(
-            inner[:, m] + jnp.matmul(reach[:, m], reach_add, precision=LOCAL_PRECISION)
+        both = jnp.matmul(
+            reach[:, m], jnp.concatenate([reach_add, reach_map], axis=-1), precision=LOCAL_PRECISION
         )
-        scaled.append(jnp.matmul(reach[:, m], reach_map, precision=LOCAL_PRECISION))
+        fixed.append(inner[:, m] + both[..., :DV])
+        scaled.append(both[..., DV:])
         reach_map, reach_add = compose((reach_map, reach_add), (carry_mat[:, m], write_mat[:, m]))
     return (jnp.stack(fixed, axis=1), jnp.stack(scaled, axis=1), reach_map, reach_add)
 

time: 82.7 us -> 80.7 us (0.976)
  local copies, waits for them, and re-layouts: 2.81 us -> 6.55 us
  matrix products: 17.2 us -> 14.9 us
  waiting for transfers between devices: 27.2 us -> 25 us
  other arithmetic: 15.1 us -> 14 us
    dot_general x11 -> x6, matrix products: 5.52 us -> 3.28 us  [the longest x4 1.44 us: compose(): jnp.matmul(later[0], jnp.concatenate([earlier[0], earlier[1]], axis=-1),...]
    convert_element_type x1, local copies, waits for them, and re-layouts: 0.18 us -> 2.01 us  [arrange_query(): query_part.astype(jnp.float32).reshape(blocks, SPAN, key_heads, DK)]
    ppermute x6, waiting for transfers between devices: 16.1 us -> 14.3 us  [chain_states(): got = lax.ppermute(other, 'ctx', [(i, i ^ stride) for i in range(size)])]
    select_n x3, other arithmetic: 2.85 us -> 1.73 us  [chain_states(): later = jnp.where(upper, mine, got)]
    convert_element_type x0 -> x1, local copies, waits for them, and re-layouts: none -> 1.01 us  [gated_norm(): return gated_rows.reshape(token_count, head_count * DV).astype(jnp.bfloat16)]
    unnamed x26 -> x17, local copies, waits for them, and re-layouts: 1.74 us -> 2.12 us
  transfers between devices with their start and end apart: 11 -> 11, of which waited for: 9 -> 9; matrix products, arithmetic and copies ran while one was open for 14% -> 16% of each run, Pallas kernels for 0% -> 0%
where the time goes in v12:
time: 80.7 us; the launch traced here: 80.4 us
  waiting for transfers between devices  25 us (31%)
  starting transfers between devices  19.2 us (24%)
  matrix products  14.9 us (18%)
  other arithmetic  14 us (17%)
  local copies, waits for them, and re-layouts  6.55 us (8%)
    ppermute x6, waiting for transfers between devices, chain_states(): got = lax.ppermute(other, 'ctx', [(i, i ^ stride) for i in range(size)])  14.3 us
    ppermute x6, starting transfers between devices, chain_states(): got = lax.ppermute(other, 'ctx', [(i, i ^ stride) for i in range(size)])  7.73 us
    ppermute x1, waiting for transfers between devices, head_return(): got = lax.ppermute(sent, 'head', [(0, 1), (1, 0)])  6.51 us
    dot_general x5, matrix products, unit_lower_inverse(): jnp.matmul(jnp.concatenate([inverse, power], axis=-2), power, precision=L...  5.37 us
    ppermute x3, starting transfers between devices, head_swap(): got = lax.ppermute(sent, 'head', [(0, 1), (1, 0)])  5.18 us
    ppermute x1, starting transfers between devices, exclusive_scan(): return lax.ppermute(write, 'ctx', near)  4.71 us
    ppermute x3, waiting for transfers between devices, head_swap(): got = lax.ppermute(sent, 'head', [(0, 1), (1, 0)])  3.2 us
    select_n x3, other arithmetic, head_swap(): own = jnp.where(first, rows[..., :width], rows[..., width:])  3.15 us
  transfers between devices with their start and end apart: 11, of which 9 were waited for; matrix products, arithmetic and copies ran while one was open for 16% of the time, Pallas kernels for 0%

profile of v12, /device:TPU:0, one launch (start us, length us, event | category | flops | bytes accessed | tf_op | source)
XLA Modules:
  0.0 80.4 jit_solution(17351595046117223544)
XLA Ops:
  0.0 1.3 %broadcast_select_fusion.7 = (bf16[2,128,512]{2,1,0:T(8,128)(2,1)S(1)}, bf16[2,128,512]{2,1,0:T(8,128)(2,1)S(1)}) fusion(pred[]{:T(512)S(6)} %eq.29, bf16[1,128,1024]{2,1,0:T(8,128)(2,1)} %bitcast.123, bf16[1,128,1024]{2,1,0:T(8,128)(2,1)} %bitcast.124), kind=kLoop, calls=%fused_computation.135 | loop fusion | flops 1835008 | bytes 1048577 | tf_op jit(solution)/shard_map/jit(_where)/select_n | solution.py:220
  1.3 3.0 %collective-permute-start = (bf16[2,128,512]{2,1,0:T(8,128)(2,1)S(1)}, bf16[2,128,512]{2,1,0:T(8,128)(2,1)S(1)}, u32[]{:S(2)}, u32[]{:S(2)}) collective-permute-start(bf16[2,128,512]{2,1,0:T(8,128)(2,1)S(1)} %get-tuple-element.36), channel_id=1, source_target_pairs={{0,1},{1,0},{2,3},{3,2},{4,5},{5,4},{6,7},{7,6},{8,9},{9,8},{10,11... | collective-permute-start | bytes 786440 | tf_op jit(solution)/shard_map/ppermute | solution.py:222
  5.2 1.1 %broadcast_select_fusion.5 = (bf16[128,1024]{1,0:T(8,128)(2,1)S(1)}, bf16[128,1024]{1,0:T(8,128)(2,1)S(1)}) fusion(pred[]{:T(512)S(6)} %eq.29, bf16[128,2048]{1,0:T(8,128)(2,1)} %param.9), kind=kLoop, calls=%fused_computation.133 | loop fusion | flops 262144 | bytes 1048577 | tf_op jit(solution)/shard_map/jit(_where)/select_n | solution.py:220
  6.3 2.1 %collective-permute-start.2 = (bf16[128,1024]{1,0:T(8,128)(2,1)S(1)}, bf16[128,1024]{1,0:T(8,128)(2,1)S(1)}, u32[]{:S(2)}, u32[]{:S(2)}) collective-permute-start(bf16[128,1024]{1,0:T(8,128)(2,1)S(1)} %get-tuple-element.32), channel_id=1, source_target_pairs={{0,1},{1,0},{2,3},{3,2},{4,5},{5,4},{6,7},{7,6},{8,9},{9,8},{10,11... | collective-permute-start | bytes 786440 | tf_op jit(solution)/shard_map/ppermute | solution.py:222
  8.4 3.2 %collective-permute-done.1 = bf16[2,128,8]{1,2,0:T(8,128)(2,1)S(1)} collective-permute-done((bf16[2,128,8]{1,2,0:T(8,128)(2,1)S(1)}, bf16[2,128,8]{1,2,0:T(8,128)(2,1)S(1)}, u32[]{:S(2)}, u32[]{:S(2)}) %collective-permute-start.1) | collective-permute-done | bytes 4128 | tf_op jit(solution)/shard_map/ppermute | solution.py:222
  12.8 0.9 %slice_convert_fusion.1 = (f32[1,256,512]{2,1,0:T(8,128)}, f32[1,256,512]{2,1,0:T(8,128)S(1)}) fusion(bf16[2,256,512]{2,1,0:T(8,128)(2,1)S(1)} %maximum_select_fusion), kind=kLoop, calls=%fused_computation.121 | loop fusion | flops 262144 | bytes 1572864 | tf_op jit(solution)/shard_map/convert_element_type | solution.py:48
  16.9 1.1 %fusion = f32[8,2,256,128]{3,2,1,0:T(8,128)S(1)} fusion(f32[8,2,128,128]{3,2,1,0:T(8,128)S(1)} %fusion.99, f32[8,2,128,128]{3,2,1,0:T(8,128)S(1)} %get-tuple-element.21), kind=kOutput, calls=%fused_computation | convolution fusion | flops 403177472 | bytes 4194304 | tf_op jit(solution)/shard_map/dot_general | solution.py:58
  17.9 1.0 %slice_add_fusion.5 = (f32[8,2,128,128]{3,2,1,0:T(8,128)S(1)}, f32[8,2,128,128]{3,2,1,0:T(8,128)S(1)}, f32[8,2,128,128]{3,2,1,0:T(8,128)S(1)}) fusion(f32[8,2,256,128]{3,2,1,0:T(8,128)S(1)} %fusion, f32[4,2,128,128]{3,2,1,0:T(8,128)S(1)} %fusion.92, f32[8,2,128]{2,1,0:T(2,128)S(1)} %copy.45, pred[128,128]{1,0:T(8,128)(4,1)S(1)} %get-tuple-element.51, ...), kind=kLoop, calls=%fused_computation.59 | loop fusion | flops 1835008 | bytes 6922240 | tf_op jit(solution)/shard_map/add | solution.py:61
  18.9 1.1 %fusion.4 = f32[8,2,256,128]{3,2,1,0:T(8,128)S(1)} fusion(f32[8,2,128,128]{3,2,1,0:T(8,128)S(1)} %get-tuple-element.12, f32[8,2,128,128]{3,2,1,0:T(8,128)S(1)} %get-tuple-element.11), kind=kOutput, calls=%fused_computation.4 | convolution fusion | flops 403177472 | bytes 4194304 | tf_op jit(solution)/shard_map/dot_general | solution.py:58
  20.3 1.1 %fusion.8 = f32[8,2,256,128]{3,2,1,0:T(8,128)S(1)} fusion(f32[8,2,128,128]{3,2,1,0:T(8,128)S(1)} %get-tuple-element.10, f32[8,2,128,128]{3,2,1,0:T(8,128)S(1)} %get-tuple-element.9), kind=kOutput, calls=%fused_computation.8 | convolution fusion | flops 403177472 | bytes 4194304 | tf_op jit(solution)/shard_map/dot_general | solution.py:58
  21.6 1.1 %fusion.12 = f32[8,2,256,128]{3,2,1,0:T(8,128)S(1)} fusion(f32[8,2,128,128]{3,2,1,0:T(8,128)S(1)} %get-tuple-element.8, f32[8,2,128,128]{3,2,1,0:T(8,128)S(1)} %get-tuple-element.7), kind=kOutput, calls=%fused_computation.12 | convolution fusion | flops 403177472 | bytes 4194304 | tf_op jit(solution)/shard_map/dot_general | solution.py:58
  23.0 1.1 %fusion.16 = f32[8,2,256,128]{3,2,1,0:T(8,128)S(1)} fusion(f32[8,2,128,128]{3,2,1,0:T(8,128)S(1)} %get-tuple-element.6, f32[8,2,128,128]{3,2,1,0:T(8,128)S(1)} %get-tuple-element.5), kind=kOutput, calls=%fused_computation.16 | convolution fusion | flops 403177472 | bytes 4194304 | tf_op jit(solution)/shard_map/dot_general | solution.py:58
  25.4 1.2 %fusion.20 = f32[8,2,128,256]{3,2,1,0:T(8,128)S(1)} fusion(f32[8,2,128,128]{3,2,1,0:T(8,128)S(1)} %convolution_add_fusion, f32[8,2,128,128]{3,2,1,0:T(8,128)S(1)} %get-tuple-element.33, f32[8,2,128,128]{3,2,1,0:T(8,128)S(1)} %get-tuple-element.48), kind=kOutput, calls=%fused_computation.20 | convolution fusion | flops 403177472 | bytes 5242880 | tf_op jit(solution)/shard_map/dot_general | solution.py:86
  26.6 1.1 %fusion.100 = f32[8,2,128,256]{3,2,1,0:T(8,128)S(1)} fusion(f32[8,2,128,128]{3,2,1,0:T(8,128)S(1)} %get-tuple-element.34, f32[8,2,128,256]{3,2,1,0:T(8,128)S(1)} %fusion.20), kind=kOutput, calls=%fused_computation.206 | convolution fusion | flops 402653184 | bytes 5242880 | tf_op jit(solution)/shard_map/hmck,hmcj->hmkj/dot_general | solution.py:91
  29.5 0.8 copy-done.3
  30.3 0.9 %broadcast_select_fusion.2 = f32[4,128,256]{2,1,0:T(8,128)} fusion(pred[]{:T(512)S(6)} %eq.31, f32[8,128,128]{2,1,0:T(8,128)S(1)} %get-tuple-element.16, f32[8,128,128]{2,1,0:T(8,128)S(1)} %get-tuple-element.15), kind=kLoop, calls=%fused_computation.129 | loop fusion | flops 393216 | bytes 1572865 | tf_op jit(solution)/shard_map/jit(_where)/select_n | solution.py:186
  31.2 2.0 %reshape.111 = f32[2,128,4,128]{3,2,1,0:T(4,128)} reshape(f32[1,256,512]{2,1,0:T(8,128)} %get-tuple-element.29) | data formatting | bytes 1048576 | tf_op jit(solution)/shard_map/convert_element_type | solution.py:48
  33.4 1.6 %broadcast_select_fusion.1 = (f32[4,128,256]{2,1,0:T(8,128)S(1)}, f32[4,128,256]{2,1,0:T(8,128)S(1)}) fusion(f32[4,128,256]{2,1,0:T(8,128)} %collective-permute-done.3, pred[]{:T(512)S(6)} %eq.31, f32[8,128,128]{2,1,0:T(8,128)} %copy-done.4, f32[8,128,128]{2,1,0:T(8,128)} %copy-done.3), kind=kLoop, calls=%fused_computation.128 | loop fusion | flops 917504 | bytes 2621441 | tf_op jit(solution)/shard_map/jit(_where)/select_n | solution.py:189
  35.6 2.1 %collective-permute-start.4 = (f32[2,128,256]{2,1,0:T(8,128)S(1)}, f32[2,128,256]{2,1,0:T(8,128)S(1)}, u32[]{:S(2)}, u32[]{:S(2)}) collective-permute-start(f32[2,128,256]{2,1,0:T(8,128)S(1)} %broadcast_select_fusion.11), channel_id=1, source_target_pairs={{0,4},{2,6},{4,0},{6,2},{8,12},{10,14},{12,8},{14,10},{16,20},{18,... | collective-permute-start | bytes 786440 | tf_op jit(solution)/shard_map/ppermute | solution.py:187
  38.1 6.4 %collective-permute-done.4 = f32[2,128,256]{2,1,0:T(8,128)S(1)} collective-permute-done((f32[2,128,256]{2,1,0:T(8,128)S(1)}, f32[2,128,256]{2,1,0:T(8,128)S(1)}, u32[]{:S(2)}, u32[]{:S(2)}) %collective-permute-start.4) | collective-permute-done | bytes 262176 | tf_op jit(solution)/shard_map/ppermute | solution.py:187
  44.9 1.9 %collective-permute-start.5 = (f32[1,128,256]{2,1,0:T(8,128)S(1)}, f32[1,128,256]{2,1,0:T(8,128)S(1)}, u32[]{:S(2)}, u32[]{:S(2)}) collective-permute-start(f32[1,128,256]{2,1,0:T(8,128)S(1)} %broadcast_select_fusion.17), channel_id=1, source_target_pairs={{0,8},{2,10},{4,12},{6,14},{8,0},{10,2},{12,4},{14,6},{16,24},{18,... | collective-permute-start | bytes 393224 | tf_op jit(solution)/shard_map/ppermute | solution.py:187
  47.1 3.0 %collective-permute-done.5 = f32[1,128,256]{2,1,0:T(8,128)S(1)} collective-permute-done((f32[1,128,256]{2,1,0:T(8,128)S(1)}, f32[1,128,256]{2,1,0:T(8,128)S(1)}, u32[]{:S(2)}, u32[]{:S(2)}) %collective-permute-start.5) | collective-permute-done | bytes 131104 | tf_op jit(solution)/shard_map/ppermute | solution.py:187
  50.4 4.7 %collective-permute-start.6 = (f32[1,128,128]{2,1,0:T(8,128)S(1)}, f32[1,128,128]{2,1,0:T(8,128)S(1)}, u32[]{:S(2)}, u32[]{:S(2)}) collective-permute-start(f32[1,128,128]{2,1,0:T(8,128)S(1)} %slice_add_fusion.9), channel_id=1, source_target_pairs={{0,16},{2,18},{4,20},{6,22},{8,24},{10,26},{12,28},{14,30},{1,17},... | collective-permute-start | bytes 196616 | tf_op jit(solution)/shard_map/ppermute | solution.py:165
  55.8 1.0 %collective-permute-done.6 = f32[1,128,128]{2,1,0:T(8,128)S(1)} collective-permute-done((f32[1,128,128]{2,1,0:T(8,128)S(1)}, f32[1,128,128]{2,1,0:T(8,128)S(1)}, u32[]{:S(2)}, u32[]{:S(2)}) %collective-permute-start.6) | collective-permute-done | bytes 65568 | tf_op jit(solution)/shard_map/ppermute | solution.py:165
  57.0 2.1 %collective-permute-start.7 = (f32[1,128,128]{2,1,0:T(8,128)S(1)}, f32[1,128,128]{2,1,0:T(8,128)S(1)}, u32[]{:S(2)}, u32[]{:S(2)}) collective-permute-start(f32[1,128,128]{2,1,0:T(8,128)S(1)} %get-tuple-element.43), channel_id=1, source_target_pairs={{0,8},{2,10},{4,12},{6,14},{8,0},{10,2},{12,4},{14,6},{16,24},{18,... | collective-permute-start | bytes 196616 | tf_op jit(solution)/shard_map/ppermute | solution.py:200
  59.2 1.2 %fusion.34 = f32[8,2,128,256]{3,2,1,0:T(8,128)S(1)} fusion(f32[8,2,128,256]{3,2,1,0:T(8,128)S(1)} %fusion.20, f32[8,2,128,128]{3,2,1,0:T(8,128)S(1)} %bitcast.119, f32[8,2,128]{2,1,0:T(2,128)S(1)} %copy.45, pred[128,128]{1,0:T(8,128)(4,1)S(1)} %iota_compare_fusion.2), kind=kOutput, calls=%fused_computation.48 | convolution fusion | flops 403439616 | bytes 5267456 | tf_op jit(solution)/shard_map/hmij,hmjv->hmiv/dot_general | solution.py:111
  61.5 1.6 %collective-permute-start.8 = (f32[2,128,128]{2,1,0:T(8,128)S(1)}, f32[2,128,128]{2,1,0:T(8,128)S(1)}, u32[]{:S(2)}, u32[]{:S(2)}) collective-permute-start(f32[2,128,128]{2,1,0:T(8,128)S(1)} %get-tuple-element.39), channel_id=1, source_target_pairs={{0,4},{2,6},{4,0},{6,2},{8,12},{10,14},{12,8},{14,10},{16,20},{18,... | collective-permute-start | bytes 393224 | tf_op jit(solution)/shard_map/ppermute | solution.py:200
  63.7 2.9 %collective-permute-done.8 = f32[2,128,128]{2,1,0:T(8,128)S(1)} collective-permute-done((f32[2,128,128]{2,1,0:T(8,128)S(1)}, f32[2,128,128]{2,1,0:T(8,128)S(1)}, u32[]{:S(2)}, u32[]{:S(2)}) %collective-permute-start.8) | collective-permute-done | bytes 131104 | tf_op jit(solution)/shard_map/ppermute | solution.py:200
  67.2 1.3 %collective-permute-done.9 = f32[4,128,128]{2,1,0:T(8,128)S(1)} collective-permute-done((f32[4,128,128]{2,1,0:T(8,128)S(1)}, f32[4,128,128]{2,1,0:T(8,128)S(1)}, u32[]{:S(2)}, u32[]{:S(2)}) %collective-permute-start.9) | collective-permute-done | bytes 262176 | tf_op jit(solution)/shard_map/ppermute | solution.py:200
  69.3 1.6 %collective-permute-start.10 = (bf16[128,1024]{0,1:T(8,128)(2,1)S(1)}, bf16[128,1024]{0,1:T(8,128)(2,1)S(1)}, u32[]{:S(2)}, u32[]{:S(2)}) collective-permute-start(bf16[128,1024]{0,1:T(8,128)(2,1)S(1)} %bitcast.121), channel_id=1, source_target_pairs={{0,1},{1,0},{2,3},{3,2},{4,5},{5,4},{6,7},{7,6},{8,9},{9,8},{10,11... | collective-permute-start | bytes 786440 | tf_op jit(solution)/shard_map/ppermute | solution.py:234
  71.2 6.5 %collective-permute-done.10 = bf16[128,1024]{0,1:T(8,128)(2,1)S(1)} collective-permute-done((bf16[128,1024]{0,1:T(8,128)(2,1)S(1)}, bf16[128,1024]{0,1:T(8,128)(2,1)S(1)}, u32[]{:S(2)}, u32[]{:S(2)}) %collective-permute-start.10) | collective-permute-done | bytes 262176 | tf_op jit(solution)/shard_map/ppermute | solution.py:234
  79.4 1.0 %copy.67 = bf16[128,2048]{1,0:T(8,128)(2,1)} copy(bf16[128,2048]{0,1:T(8,128)(2,1)S(1)} %fusion.49) | data formatting | bytes 1048576 | tf_op jit(solution)/shard_map/convert_element_type | solution.py:214
  (93 shorter events, 16.8 us)
Async XLA Ops:
  1.3 11.2 %collective-permute-start = (bf16[2,128,512]{2,1,0:T(8,128)(2,1)S(1)}, bf16[2,128,512]{2,1,0:T(8,128)(2,1)S(1)}, u32[]{:S(2)}, u32[]{:S(2)}) collective-permute-start(bf16[2,128,512]{2,1,0:T(8,128)(2,1)S(1)} %get-tuple-element.36), channel_id=1, source_target_pairs={{0,1},{1,0},{2,3},{3,2},{4,5},{5,4},{6,7},{7,6},{8,9},{9,8},{10,11... | collective-permute-start | bytes 786440 | tf_op jit(solution)/shard_map/ppermute | solution.py:222
  5.1 6.5 %collective-permute-start.1 = (bf16[2,128,8]{1,2,0:T(8,128)(2,1)S(1)}, bf16[2,128,8]{1,2,0:T(8,128)(2,1)S(1)}, u32[]{:S(2)}, u32[]{:S(2)}) collective-permute-start(bf16[2,128,8]{1,2,0:T(8,128)(2,1)S(1)} %get-tuple-element.50), channel_id=1, source_target_pairs={{0,1},{1,0},{2,3},{3,2},{4,5},{5,4},{6,7},{7,6},{8,9},{9,8},{10,11... | collective-permute-start | bytes 12296 | tf_op jit(solution)/shard_map/ppermute | solution.py:222
  6.3 10.2 %collective-permute-start.2 = (bf16[128,1024]{1,0:T(8,128)(2,1)S(1)}, bf16[128,1024]{1,0:T(8,128)(2,1)S(1)}, u32[]{:S(2)}, u32[]{:S(2)}) collective-permute-start(bf16[128,1024]{1,0:T(8,128)(2,1)S(1)} %get-tuple-element.32), channel_id=1, source_target_pairs={{0,1},{1,0},{2,3},{3,2},{4,5},{5,4},{6,7},{7,6},{8,9},{9,8},{10,11... | collective-permute-start | bytes 786440 | tf_op jit(solution)/shard_map/ppermute | solution.py:222
  28.0 0.8 copy-start
  29.5 0.8 %copy-start.3 = (f32[8,128,128]{2,1,0:T(8,128)}, f32[8,128,128]{2,1,0:T(8,128)S(1)}, u32[]{:S(2)}) copy-start(f32[8,128,128]{2,1,0:T(8,128)S(1)} %get-tuple-element.15) | copy-start | bytes 1572868
  29.5 1.7 %copy-start.4 = (f32[8,128,128]{2,1,0:T(8,128)}, f32[8,128,128]{2,1,0:T(8,128)S(1)}, u32[]{:S(2)}) copy-start(f32[8,128,128]{2,1,0:T(8,128)S(1)} %get-tuple-element.16) | copy-start | bytes 1572868
  31.2 2.3 %collective-permute-start.3 = (f32[4,128,256]{2,1,0:T(8,128)}, f32[4,128,256]{2,1,0:T(8,128)}, u32[]{:S(2)}, u32[]{:S(2)}) collective-permute-start(f32[4,128,256]{2,1,0:T(8,128)} %broadcast_select_fusion.2), channel_id=1, source_target_pairs={{0,2},{2,0},{4,6},{6,4},{8,10},{10,8},{12,14},{14,12},{16,18},{18,... | collective-permute-start | bytes 1572872 | tf_op jit(solution)/shard_map/ppermute | solution.py:187
  35.1 2.6 %copy-start.2 = (f32[2,128,4,128]{3,2,1,0:T(4,128)S(1)}, f32[2,128,4,128]{3,2,1,0:T(4,128)}, u32[]{:S(2)}) copy-start(f32[2,128,4,128]{3,2,1,0:T(4,128)} %reshape.111) | copy-start | bytes 1572868
  35.6 8.9 %collective-permute-start.4 = (f32[2,128,256]{2,1,0:T(8,128)S(1)}, f32[2,128,256]{2,1,0:T(8,128)S(1)}, u32[]{:S(2)}, u32[]{:S(2)}) collective-permute-start(f32[2,128,256]{2,1,0:T(8,128)S(1)} %broadcast_select_fusion.11), channel_id=1, source_target_pairs={{0,4},{2,6},{4,0},{6,2},{8,12},{10,14},{12,8},{14,10},{16,20},{18,... | collective-permute-start | bytes 786440 | tf_op jit(solution)/shard_map/ppermute | solution.py:187
  44.9 5.3 %collective-permute-start.5 = (f32[1,128,256]{2,1,0:T(8,128)S(1)}, f32[1,128,256]{2,1,0:T(8,128)S(1)}, u32[]{:S(2)}, u32[]{:S(2)}) collective-permute-start(f32[1,128,256]{2,1,0:T(8,128)S(1)} %broadcast_select_fusion.17), channel_id=1, source_target_pairs={{0,8},{2,10},{4,12},{6,14},{8,0},{10,2},{12,4},{14,6},{16,24},{18,... | collective-permute-start | bytes 393224 | tf_op jit(solution)/shard_map/ppermute | solution.py:187
  50.4 6.4 %collective-permute-start.6 = (f32[1,128,128]{2,1,0:T(8,128)S(1)}, f32[1,128,128]{2,1,0:T(8,128)S(1)}, u32[]{:S(2)}, u32[]{:S(2)}) collective-permute-start(f32[1,128,128]{2,1,0:T(8,128)S(1)} %slice_add_fusion.9), channel_id=1, source_target_pairs={{0,16},{2,18},{4,20},{6,22},{8,24},{10,26},{12,28},{14,30},{1,17},... | collective-permute-start | bytes 196616 | tf_op jit(solution)/shard_map/ppermute | solution.py:165
  57.0 4.4 %collective-permute-start.7 = (f32[1,128,128]{2,1,0:T(8,128)S(1)}, f32[1,128,128]{2,1,0:T(8,128)S(1)}, u32[]{:S(2)}, u32[]{:S(2)}) collective-permute-start(f32[1,128,128]{2,1,0:T(8,128)S(1)} %get-tuple-element.43), channel_id=1, source_target_pairs={{0,8},{2,10},{4,12},{6,14},{8,0},{10,2},{12,4},{14,6},{16,24},{18,... | collective-permute-start | bytes 196616 | tf_op jit(solution)/shard_map/ppermute | solution.py:200
  60.4 2.7 %copy-start.1 = (f32[8,128,128]{2,1,0:T(8,128)S(1)}, f32[8,128,128]{2,1,0:T(8,128)}, u32[]{:S(2)}) copy-start(f32[8,128,128]{2,1,0:T(8,128)} %copy-done) | copy-start | bytes 1572868
  61.5 5.0 %collective-permute-start.8 = (f32[2,128,128]{2,1,0:T(8,128)S(1)}, f32[2,128,128]{2,1,0:T(8,128)S(1)}, u32[]{:S(2)}, u32[]{:S(2)}) collective-permute-start(f32[2,128,128]{2,1,0:T(8,128)S(1)} %get-tuple-element.39), channel_id=1, source_target_pairs={{0,4},{2,6},{4,0},{6,2},{8,12},{10,14},{12,8},{14,10},{16,20},{18,... | collective-permute-start | bytes 393224 | tf_op jit(solution)/shard_map/ppermute | solution.py:200
  66.9 1.6 %collective-permute-start.9 = (f32[4,128,128]{2,1,0:T(8,128)S(1)}, f32[4,128,128]{2,1,0:T(8,128)S(1)}, u32[]{:S(2)}, u32[]{:S(2)}) collective-permute-start(f32[4,128,128]{2,1,0:T(8,128)S(1)} %get-tuple-element.25), channel_id=1, source_target_pairs={{0,2},{2,0},{4,6},{6,4},{8,10},{10,8},{12,14},{14,12},{16,18},{18,... | collective-permute-start | bytes 786440 | tf_op jit(solution)/shard_map/ppermute | solution.py:200
  68.5 2.5 %copy-start.5 = (bf16[128,2048]{1,0:T(8,128)(2,1)S(1)}, bf16[128,2048]{1,0:T(8,128)(2,1)}, u32[]{:S(2)}) copy-start(bf16[128,2048]{1,0:T(8,128)(2,1)} %param.10) | copy-start | bytes 1572868
  69.1 2.1 %copy-start.6 = (bf16[128]{0:T(256)(128)(2,1)S(1)}, bf16[128]{0:T(256)(128)(2,1)}, u32[]{:S(2)}) copy-start(bf16[128]{0:T(256)(128)(2,1)} %param.13) | copy-start | bytes 772
  69.3 8.4 %collective-permute-start.10 = (bf16[128,1024]{0,1:T(8,128)(2,1)S(1)}, bf16[128,1024]{0,1:T(8,128)(2,1)S(1)}, u32[]{:S(2)}, u32[]{:S(2)}) collective-permute-start(bf16[128,1024]{0,1:T(8,128)(2,1)S(1)} %bitcast.121), channel_id=1, source_target_pairs={{0,1},{1,0},{2,3},{3,2},{4,5},{5,4},{6,7},{7,6},{8,9},{9,8},{10,11... | collective-permute-start | bytes 786440 | tf_op jit(solution)/shard_map/ppermute | solution.py:234

commit v13 on v12

--- a/solution.py
+++ b/solution.py
@@ -21,6 +21,13 @@
         later[0], jnp.concatenate([earlier[0], earlier[1]], axis=-1), precision=FULL_PRECISION
     )
     return (both[..., : earlier[0].shape[-1]], both[..., earlier[0].shape[-1] :] + later[1])
+
+
+def compose_joined(earlier, later):
+    lane = lax.broadcasted_iota(jnp.int32, later.shape, later.ndim - 1)
+    return jnp.matmul(
+        later[..., : later.shape[-2]], earlier, precision=FULL_PRECISION
+    ) + jnp.where(lane >= later.shape[-2], later, 0.0)
 
 
 def arrange(key_part, value_part, beta_part, decay_part):
@@ -118,15 +125,14 @@
     reach = wide_query * jnp.exp(cum_log)[..., None] - mixed[..., DV:]
     blocks = carry_mat.shape[1]
     fixed, scaled = ([inner[:, 0]], [reach[:, 0]])
-    reach_map, reach_add = (carry_mat[:, 0], write_mat[:, 0])
+    reach_both = jnp.concatenate([carry_mat, write_mat], axis=-1)
+    total = reach_both[:, 0]
     for m in range(1, blocks):
-        both = jnp.matmul(
-            reach[:, m], jnp.concatenate([reach_add, reach_map], axis=-1), precision=LOCAL_PRECISION
-        )
-        fixed.append(inner[:, m] + both[..., :DV])
-        scaled.append(both[..., DV:])
-        reach_map, reach_add = compose((reach_map, reach_add), (carry_mat[:, m], write_mat[:, m]))
-    return (jnp.stack(fixed, axis=1), jnp.stack(scaled, axis=1), reach_map, reach_add)
+        both = jnp.matmul(reach[:, m], total, precision=LOCAL_PRECISION)
+        scaled.append(both[..., :DK])
+        fixed.append(inner[:, m] + both[..., DK:])
+        total = compose_joined(total, reach_both[:, m])
+    return (jnp.stack(fixed, axis=1), jnp.stack(scaled, axis=1), total)
 
 
 def span_out(fixed, scaled, state_in):
@@ -170,13 +176,13 @@
     return jnp.matmul(got_carry, far_write, precision=FULL_PRECISION) + got_write
 
 
-def chain_states(block_carry, block_write):
+def chain_states(block_both):
     size = lax.axis_size("ctx")
     me = lax.axis_index("ctx")
     levels = 0
-    while size % 2 ** (levels + 1) == 0 and block_carry.shape[0] % 2 ** (levels + 1) == 0:
+    while size % 2 ** (levels + 1) == 0 and block_both.shape[0] % 2 ** (levels + 1) == 0:
         levels += 1
-    current = joined(block_carry, block_write)
+    current = block_both
     saved = []
     for level in range(levels):
         stride = 2**level
@@ -188,7 +194,7 @@
         earlier = jnp.where(upper, got, mine)
         later = jnp.where(upper, mine, got)
         saved.append((upper, earlier))
-        current = joined(*compose(split(earlier), split(later)))
+        current = compose_joined(earlier, later)
     state = exclusive_scan(*split(current), size, 2**levels)
     for level in reversed(range(levels)):
         stride = 2**level
@@ -267,8 +273,8 @@
     group_size = value_f.shape[0] // key_unit.shape[0]
     pieces = span_pass(key_unit, value_f, beta_gate, decay_log, group_size)
     query_unit = arrange_query(q_head)
-    fixed, scaled, total_carry, total_write = span_prep(query_unit, key_unit, group_size, pieces)
-    state_in = chain_states(total_carry, total_write)
+    fixed, scaled, total = span_prep(query_unit, key_unit, group_size, pieces)
+    state_in = chain_states(total)
     core_out = span_out(fixed, scaled, state_in)
     core_rows = head_outputs(to_rows(core_out).astype(jnp.bfloat16))
     return gated_norm(core_rows, output_gate, norm_gain)

time: 80.7 us -> 79.4 us (0.984)
  local copies, waits for them, and re-layouts: 6.55 us -> 5.32 us
    unnamed x17 -> x19, local copies, waits for them, and re-layouts: 2.12 us -> 0.95 us
where the time goes in v13:
time: 79.4 us; the launch traced here: 79.2 us
  waiting for transfers between devices  24.9 us (31%)
  starting transfers between devices  19.3 us (24%)
  matrix products  15 us (19%)
  other arithmetic  14 us (18%)
  local copies, waits for them, and re-layouts  5.32 us (7%)
    ppermute x6, waiting for transfers between devices, chain_states(): got = lax.ppermute(other, 'ctx', [(i, i ^ stride) for i in range(size)])  14.2 us
    ppermute x6, starting transfers between devices, chain_states(): got = lax.ppermute(other, 'ctx', [(i, i ^ stride) for i in range(size)])  7.75 us
    ppermute x1, waiting for transfers between devices, head_return(): got = lax.ppermute(sent, 'head', [(0, 1), (1, 0)])  6.51 us
    dot_general x5, matrix products, unit_lower_inverse(): jnp.matmul(jnp.concatenate([inverse, power], axis=-2), power, precision=L...  5.37 us
    ppermute x3, starting transfers between devices, head_swap(): got = lax.ppermute(sent, 'head', [(0, 1), (1, 0)])  5.18 us
    ppermute x1, starting transfers between devices, exclusive_scan(): return lax.ppermute(write, 'ctx', near)  4.74 us
    ppermute x3, waiting for transfers between devices, head_swap(): got = lax.ppermute(sent, 'head', [(0, 1), (1, 0)])  3.19 us
    select_n x3, other arithmetic, head_swap(): own = jnp.where(first, rows[..., :width], rows[..., width:])  3.15 us
  transfers between devices with their start and end apart: 11, of which 9 were waited for; matrix products, arithmetic and copies ran while one was open for 16% of the time, Pallas kernels for 0%

profile of v13, /device:TPU:0, one launch (start us, length us, event | category | flops | bytes accessed | tf_op | source)
XLA Modules:
  0.0 79.2 jit_solution(7133963817126343176)
XLA Ops:
  0.0 1.3 %broadcast_select_fusion.5 = (bf16[2,128,512]{2,1,0:T(8,128)(2,1)S(1)}, bf16[2,128,512]{2,1,0:T(8,128)(2,1)S(1)}) fusion(pred[]{:T(512)S(6)} %eq.29, bf16[1,128,1024]{2,1,0:T(8,128)(2,1)} %bitcast.116, bf16[1,128,1024]{2,1,0:T(8,128)(2,1)} %bitcast.117), kind=kLoop, calls=%fused_computation.121 | loop fusion | flops 1835008 | bytes 1048577 | tf_op jit(solution)/shard_map/jit(_where)/select_n | solution.py:226
  1.3 3.0 %collective-permute-start = (bf16[2,128,512]{2,1,0:T(8,128)(2,1)S(1)}, bf16[2,128,512]{2,1,0:T(8,128)(2,1)S(1)}, u32[]{:S(2)}, u32[]{:S(2)}) collective-permute-start(bf16[2,128,512]{2,1,0:T(8,128)(2,1)S(1)} %get-tuple-element.34), channel_id=1, source_target_pairs={{0,1},{1,0},{2,3},{3,2},{4,5},{5,4},{6,7},{7,6},{8,9},{9,8},{10,11... | collective-permute-start | bytes 786440 | tf_op jit(solution)/shard_map/ppermute | solution.py:228
  4.4 0.8 broadcast_select_fusion.18
  5.2 1.1 %broadcast_select_fusion.3 = (bf16[128,1024]{1,0:T(8,128)(2,1)S(1)}, bf16[128,1024]{1,0:T(8,128)(2,1)S(1)}) fusion(pred[]{:T(512)S(6)} %eq.29, bf16[128,2048]{1,0:T(8,128)(2,1)} %param.9), kind=kLoop, calls=%fused_computation.119 | loop fusion | flops 262144 | bytes 1048577 | tf_op jit(solution)/shard_map/jit(_where)/select_n | solution.py:226
  6.3 2.1 %collective-permute-start.2 = (bf16[128,1024]{1,0:T(8,128)(2,1)S(1)}, bf16[128,1024]{1,0:T(8,128)(2,1)S(1)}, u32[]{:S(2)}, u32[]{:S(2)}) collective-permute-start(bf16[128,1024]{1,0:T(8,128)(2,1)S(1)} %get-tuple-element.32), channel_id=1, source_target_pairs={{0,1},{1,0},{2,3},{3,2},{4,5},{5,4},{6,7},{7,6},{8,9},{9,8},{10,11... | collective-permute-start | bytes 786440 | tf_op jit(solution)/shard_map/ppermute | solution.py:228
  8.4 3.2 %collective-permute-done.1 = bf16[2,128,8]{1,2,0:T(8,128)(2,1)S(1)} collective-permute-done((bf16[2,128,8]{1,2,0:T(8,128)(2,1)S(1)}, bf16[2,128,8]{1,2,0:T(8,128)(2,1)S(1)}, u32[]{:S(2)}, u32[]{:S(2)}) %collective-permute-start.1) | collective-permute-done | bytes 4128 | tf_op jit(solution)/shard_map/ppermute | solution.py:228
  12.8 0.9 %slice_convert_fusion.1 = (f32[1,256,512]{2,1,0:T(8,128)}, f32[1,256,512]{2,1,0:T(8,128)S(1)}) fusion(bf16[2,256,512]{2,1,0:T(8,128)(2,1)S(1)} %maximum_select_fusion), kind=kLoop, calls=%fused_computation.111 | loop fusion | flops 262144 | bytes 1572864 | tf_op jit(solution)/shard_map/convert_element_type | solution.py:55
  16.9 1.1 %fusion = f32[8,2,256,128]{3,2,1,0:T(8,128)S(1)} fusion(f32[8,2,128,128]{3,2,1,0:T(8,128)S(1)} %fusion.89, f32[8,2,128,128]{3,2,1,0:T(8,128)S(1)} %get-tuple-element.21), kind=kOutput, calls=%fused_computation | convolution fusion | flops 403177472 | bytes 4194304 | tf_op jit(solution)/shard_map/dot_general | solution.py:65
  18.0 1.0 %slice_add_fusion.5 = (f32[8,2,128,128]{3,2,1,0:T(8,128)S(1)}, f32[8,2,128,128]{3,2,1,0:T(8,128)S(1)}, f32[8,2,128,128]{3,2,1,0:T(8,128)S(1)}) fusion(f32[8,2,256,128]{3,2,1,0:T(8,128)S(1)} %fusion, f32[4,2,128,128]{3,2,1,0:T(8,128)S(1)} %fusion.85, f32[8,2,128]{2,1,0:T(2,128)S(1)} %copy.43, pred[128,128]{1,0:T(8,128)(4,1)S(1)} %get-tuple-element.47, ...), kind=kLoop, calls=%fused_computation.68 | loop fusion | flops 1835008 | bytes 6922240 | tf_op jit(solution)/shard_map/add | solution.py:68
  19.0 1.1 %fusion.4 = f32[8,2,256,128]{3,2,1,0:T(8,128)S(1)} fusion(f32[8,2,128,128]{3,2,1,0:T(8,128)S(1)} %get-tuple-element.14, f32[8,2,128,128]{3,2,1,0:T(8,128)S(1)} %get-tuple-element.13), kind=kOutput, calls=%fused_computation.4 | convolution fusion | flops 403177472 | bytes 4194304 | tf_op jit(solution)/shard_map/dot_general | solution.py:65
  20.3 1.1 %fusion.8 = f32[8,2,256,128]{3,2,1,0:T(8,128)S(1)} fusion(f32[8,2,128,128]{3,2,1,0:T(8,128)S(1)} %get-tuple-element.12, f32[8,2,128,128]{3,2,1,0:T(8,128)S(1)} %get-tuple-element.11), kind=kOutput, calls=%fused_computation.8 | convolution fusion | flops 403177472 | bytes 4194304 | tf_op jit(solution)/shard_map/dot_general | solution.py:65
  21.6 1.1 %fusion.12 = f32[8,2,256,128]{3,2,1,0:T(8,128)S(1)} fusion(f32[8,2,128,128]{3,2,1,0:T(8,128)S(1)} %get-tuple-element.10, f32[8,2,128,128]{3,2,1,0:T(8,128)S(1)} %get-tuple-element.9), kind=kOutput, calls=%fused_computation.12 | convolution fusion | flops 403177472 | bytes 4194304 | tf_op jit(solution)/shard_map/dot_general | solution.py:65
  23.0 1.1 %fusion.16 = f32[8,2,256,128]{3,2,1,0:T(8,128)S(1)} fusion(f32[8,2,128,128]{3,2,1,0:T(8,128)S(1)} %get-tuple-element.8, f32[8,2,128,128]{3,2,1,0:T(8,128)S(1)} %get-tuple-element.7), kind=kOutput, calls=%fused_computation.16 | convolution fusion | flops 403177472 | bytes 4194304 | tf_op jit(solution)/shard_map/dot_general | solution.py:65
  25.4 1.2 %fusion.20 = f32[8,2,128,256]{3,2,1,0:T(8,128)S(1)} fusion(f32[8,2,128,128]{3,2,1,0:T(8,128)S(1)} %convolution_add_fusion, f32[8,2,128,128]{3,2,1,0:T(8,128)S(1)} %get-tuple-element.28, f32[8,2,128,128]{3,2,1,0:T(8,128)S(1)} %get-tuple-element.44), kind=kOutput, calls=%fused_computation.20 | convolution fusion | flops 403177472 | bytes 5242880 | tf_op jit(solution)/shard_map/dot_general | solution.py:93
  26.7 1.1 %fusion.90 = f32[8,2,128,256]{3,2,1,0:T(8,128)S(1)} fusion(f32[8,2,128,128]{3,2,1,0:T(8,128)S(1)} %get-tuple-element.27, f32[8,2,128,256]{3,2,1,0:T(8,128)S(1)} %fusion.20), kind=kOutput, calls=%fused_computation.187 | convolution fusion | flops 402653184 | bytes 5242880 | tf_op jit(solution)/shard_map/hmck,hmcj->hmkj/dot_general | solution.py:98
  29.0 1.0 %slice_select_fusion = f32[4,128,256]{2,1,0:T(8,128)} fusion(f32[8,128,256]{2,1,0:T(8,128)S(1)} %convolution_add_fusion.2, pred[]{:T(512)S(6)} %eq.31), kind=kLoop, calls=%fused_computation.105 | loop fusion | flops 131072 | bytes 1572865 | tf_op jit(solution)/shard_map/jit(_where)/select_n | solution.py:192
  30.2 2.0 %reshape.111 = f32[2,128,4,128]{3,2,1,0:T(4,128)} reshape(f32[1,256,512]{2,1,0:T(8,128)} %get-tuple-element.29) | data formatting | bytes 1048576 | tf_op jit(solution)/shard_map/convert_element_type | solution.py:55
  32.4 1.5 %broadcast_select_fusion.1 = (f32[4,128,256]{2,1,0:T(8,128)S(1)}, f32[4,128,256]{2,1,0:T(8,128)S(1)}) fusion(f32[4,128,256]{2,1,0:T(8,128)} %collective-permute-done.3, pred[]{:T(512)S(6)} %eq.31, f32[8,128,256]{2,1,0:T(8,128)} %copy-done.2), kind=kLoop, calls=%fused_computation.116 | loop fusion | flops 393216 | bytes 2621441 | tf_op jit(solution)/shard_map/jit(_where)/select_n | solution.py:195
  34.4 2.1 %collective-permute-start.4 = (f32[2,128,256]{2,1,0:T(8,128)S(1)}, f32[2,128,256]{2,1,0:T(8,128)S(1)}, u32[]{:S(2)}, u32[]{:S(2)}) collective-permute-start(f32[2,128,256]{2,1,0:T(8,128)S(1)} %slice_select_fusion.2), channel_id=1, source_target_pairs={{0,4},{2,6},{4,0},{6,2},{8,12},{10,14},{12,8},{14,10},{16,20},{18,... | collective-permute-start | bytes 786440 | tf_op jit(solution)/shard_map/ppermute | solution.py:193
  36.9 6.4 %collective-permute-done.4 = f32[2,128,256]{2,1,0:T(8,128)S(1)} collective-permute-done((f32[2,128,256]{2,1,0:T(8,128)S(1)}, f32[2,128,256]{2,1,0:T(8,128)S(1)}, u32[]{:S(2)}, u32[]{:S(2)}) %collective-permute-start.4) | collective-permute-done | bytes 262176 | tf_op jit(solution)/shard_map/ppermute | solution.py:193
  43.6 1.9 %collective-permute-start.5 = (f32[1,128,256]{2,1,0:T(8,128)S(1)}, f32[1,128,256]{2,1,0:T(8,128)S(1)}, u32[]{:S(2)}, u32[]{:S(2)}) collective-permute-start(f32[1,128,256]{2,1,0:T(8,128)S(1)} %slice_select_fusion.4), channel_id=1, source_target_pairs={{0,8},{2,10},{4,12},{6,14},{8,0},{10,2},{12,4},{14,6},{16,24},{18,... | collective-permute-start | bytes 393224 | tf_op jit(solution)/shard_map/ppermute | solution.py:193
  45.9 3.0 %collective-permute-done.5 = f32[1,128,256]{2,1,0:T(8,128)S(1)} collective-permute-done((f32[1,128,256]{2,1,0:T(8,128)S(1)}, f32[1,128,256]{2,1,0:T(8,128)S(1)}, u32[]{:S(2)}, u32[]{:S(2)}) %collective-permute-start.5) | collective-permute-done | bytes 131104 | tf_op jit(solution)/shard_map/ppermute | solution.py:193
  49.2 4.7 %collective-permute-start.6 = (f32[1,128,128]{2,1,0:T(8,128)S(1)}, f32[1,128,128]{2,1,0:T(8,128)S(1)}, u32[]{:S(2)}, u32[]{:S(2)}) collective-permute-start(f32[1,128,128]{2,1,0:T(8,128)S(1)} %slice_add_fusion.7), channel_id=1, source_target_pairs={{0,16},{2,18},{4,20},{6,22},{8,24},{10,26},{12,28},{14,30},{1,17},... | collective-permute-start | bytes 196616 | tf_op jit(solution)/shard_map/ppermute | solution.py:171
  54.6 1.0 %collective-permute-done.6 = f32[1,128,128]{2,1,0:T(8,128)S(1)} collective-permute-done((f32[1,128,128]{2,1,0:T(8,128)S(1)}, f32[1,128,128]{2,1,0:T(8,128)S(1)}, u32[]{:S(2)}, u32[]{:S(2)}) %collective-permute-start.6) | collective-permute-done | bytes 65568 | tf_op jit(solution)/shard_map/ppermute | solution.py:171
  55.7 2.1 %collective-permute-start.7 = (f32[1,128,128]{2,1,0:T(8,128)S(1)}, f32[1,128,128]{2,1,0:T(8,128)S(1)}, u32[]{:S(2)}, u32[]{:S(2)}) collective-permute-start(f32[1,128,128]{2,1,0:T(8,128)S(1)} %get-tuple-element.39), channel_id=1, source_target_pairs={{0,8},{2,10},{4,12},{6,14},{8,0},{10,2},{12,4},{14,6},{16,24},{18,... | collective-permute-start | bytes 196616 | tf_op jit(solution)/shard_map/ppermute | solution.py:206
  58.0 1.2 %fusion.34 = f32[8,2,128,256]{3,2,1,0:T(8,128)S(1)} fusion(f32[8,2,128,256]{3,2,1,0:T(8,128)S(1)} %fusion.20, f32[8,2,128,128]{3,2,1,0:T(8,128)S(1)} %bitcast.112, f32[8,2,128]{2,1,0:T(2,128)S(1)} %copy.43, pred[128,128]{1,0:T(8,128)(4,1)S(1)} %iota_compare_fusion.2), kind=kOutput, calls=%fused_computation.53 | convolution fusion | flops 403439616 | bytes 5267456 | tf_op jit(solution)/shard_map/hmij,hmjv->hmiv/dot_general | solution.py:118
  60.3 1.6 %collective-permute-start.8 = (f32[2,128,128]{2,1,0:T(8,128)S(1)}, f32[2,128,128]{2,1,0:T(8,128)S(1)}, u32[]{:S(2)}, u32[]{:S(2)}) collective-permute-start(f32[2,128,128]{2,1,0:T(8,128)S(1)} %get-tuple-element.37), channel_id=1, source_target_pairs={{0,4},{2,6},{4,0},{6,2},{8,12},{10,14},{12,8},{14,10},{16,20},{18,... | collective-permute-start | bytes 393224 | tf_op jit(solution)/shard_map/ppermute | solution.py:206
  62.5 2.8 %collective-permute-done.8 = f32[2,128,128]{2,1,0:T(8,128)S(1)} collective-permute-done((f32[2,128,128]{2,1,0:T(8,128)S(1)}, f32[2,128,128]{2,1,0:T(8,128)S(1)}, u32[]{:S(2)}, u32[]{:S(2)}) %collective-permute-start.8) | collective-permute-done | bytes 131104 | tf_op jit(solution)/shard_map/ppermute | solution.py:206
  65.9 1.3 %collective-permute-done.9 = f32[4,128,128]{2,1,0:T(8,128)S(1)} collective-permute-done((f32[4,128,128]{2,1,0:T(8,128)S(1)}, f32[4,128,128]{2,1,0:T(8,128)S(1)}, u32[]{:S(2)}, u32[]{:S(2)}) %collective-permute-start.9) | collective-permute-done | bytes 262176 | tf_op jit(solution)/shard_map/ppermute | solution.py:206
  68.1 1.6 %collective-permute-start.10 = (bf16[128,1024]{0,1:T(8,128)(2,1)S(1)}, bf16[128,1024]{0,1:T(8,128)(2,1)S(1)}, u32[]{:S(2)}, u32[]{:S(2)}) collective-permute-start(bf16[128,1024]{0,1:T(8,128)(2,1)S(1)} %bitcast.114), channel_id=1, source_target_pairs={{0,1},{1,0},{2,3},{3,2},{4,5},{5,4},{6,7},{7,6},{8,9},{9,8},{10,11... | collective-permute-start | bytes 786440 | tf_op jit(solution)/shard_map/ppermute | solution.py:240
  70.0 6.5 %collective-permute-done.10 = bf16[128,1024]{0,1:T(8,128)(2,1)S(1)} collective-permute-done((bf16[128,1024]{0,1:T(8,128)(2,1)S(1)}, bf16[128,1024]{0,1:T(8,128)(2,1)S(1)}, u32[]{:S(2)}, u32[]{:S(2)}) %collective-permute-start.10) | collective-permute-done | bytes 262176 | tf_op jit(solution)/shard_map/ppermute | solution.py:240
  78.2 1.0 %copy.64 = bf16[128,2048]{1,0:T(8,128)(2,1)} copy(bf16[128,2048]{0,1:T(8,128)(2,1)S(1)} %fusion.44) | data formatting | bytes 1048576 | tf_op jit(solution)/shard_map/convert_element_type | solution.py:220
  (93 shorter events, 15.7 us)
Async XLA Ops:
  1.3 11.2 %collective-permute-start = (bf16[2,128,512]{2,1,0:T(8,128)(2,1)S(1)}, bf16[2,128,512]{2,1,0:T(8,128)(2,1)S(1)}, u32[]{:S(2)}, u32[]{:S(2)}) collective-permute-start(bf16[2,128,512]{2,1,0:T(8,128)(2,1)S(1)} %get-tuple-element.34), channel_id=1, source_target_pairs={{0,1},{1,0},{2,3},{3,2},{4,5},{5,4},{6,7},{7,6},{8,9},{9,8},{10,11... | collective-permute-start | bytes 786440 | tf_op jit(solution)/shard_map/ppermute | solution.py:228
  5.1 6.5 %collective-permute-start.1 = (bf16[2,128,8]{1,2,0:T(8,128)(2,1)S(1)}, bf16[2,128,8]{1,2,0:T(8,128)(2,1)S(1)}, u32[]{:S(2)}, u32[]{:S(2)}) collective-permute-start(bf16[2,128,8]{1,2,0:T(8,128)(2,1)S(1)} %get-tuple-element.46), channel_id=1, source_target_pairs={{0,1},{1,0},{2,3},{3,2},{4,5},{5,4},{6,7},{7,6},{8,9},{9,8},{10,11... | collective-permute-start | bytes 12296 | tf_op jit(solution)/shard_map/ppermute | solution.py:228
  6.3 10.3 %collective-permute-start.2 = (bf16[128,1024]{1,0:T(8,128)(2,1)S(1)}, bf16[128,1024]{1,0:T(8,128)(2,1)S(1)}, u32[]{:S(2)}, u32[]{:S(2)}) collective-permute-start(bf16[128,1024]{1,0:T(8,128)(2,1)S(1)} %get-tuple-element.32), channel_id=1, source_target_pairs={{0,1},{1,0},{2,3},{3,2},{4,5},{5,4},{6,7},{7,6},{8,9},{9,8},{10,11... | collective-permute-start | bytes 786440 | tf_op jit(solution)/shard_map/ppermute | solution.py:228
  14.6 1.3 %copy-start.3 = (f32[4,2,128,128]{3,0,2,1:T(4,128)}, f32[4,2,128,128]{3,0,2,1:T(4,128)S(1)}, u32[]{:S(2)}) copy-start(f32[4,2,128,128]{3,0,2,1:T(4,128)S(1)} %multiply_bitcast_fusion) | copy-start | bytes 1572868
  28.0 1.0 %copy-start = (f32[8,2,128,128]{3,2,1,0:T(8,128)}, f32[8,2,128,128]{3,2,1,0:T(8,128)S(1)}, u32[]{:S(2)}) copy-start(f32[8,2,128,128]{3,2,1,0:T(8,128)S(1)} %get-tuple-element.6) | copy-start | bytes 3145732
  29.0 1.1 %copy-start.2 = (f32[8,128,256]{2,1,0:T(8,128)}, f32[8,128,256]{2,1,0:T(8,128)S(1)}, u32[]{:S(2)}) copy-start(f32[8,128,256]{2,1,0:T(8,128)S(1)} %convolution_add_fusion.2) | copy-start | bytes 3145732
  30.2 2.3 %collective-permute-start.3 = (f32[4,128,256]{2,1,0:T(8,128)}, f32[4,128,256]{2,1,0:T(8,128)}, u32[]{:S(2)}, u32[]{:S(2)}) collective-permute-start(f32[4,128,256]{2,1,0:T(8,128)} %slice_select_fusion), channel_id=1, source_target_pairs={{0,2},{2,0},{4,6},{6,4},{8,10},{10,8},{12,14},{14,12},{16,18},{18,... | collective-permute-start | bytes 1572872 | tf_op jit(solution)/shard_map/ppermute | solution.py:193
  32.2 4.2 %copy-start.5 = (f32[2,128,4,128]{3,2,1,0:T(4,128)S(1)}, f32[2,128,4,128]{3,2,1,0:T(4,128)}, u32[]{:S(2)}) copy-start(f32[2,128,4,128]{3,2,1,0:T(4,128)} %reshape.111) | copy-start | bytes 1572868
  34.4 8.9 %collective-permute-start.4 = (f32[2,128,256]{2,1,0:T(8,128)S(1)}, f32[2,128,256]{2,1,0:T(8,128)S(1)}, u32[]{:S(2)}, u32[]{:S(2)}) collective-permute-start(f32[2,128,256]{2,1,0:T(8,128)S(1)} %slice_select_fusion.2), channel_id=1, source_target_pairs={{0,4},{2,6},{4,0},{6,2},{8,12},{10,14},{12,8},{14,10},{16,20},{18,... | collective-permute-start | bytes 786440 | tf_op jit(solution)/shard_map/ppermute | solution.py:193
  36.8 17.1 %copy-start.4 = (f32[4,2,128,128]{3,0,2,1:T(4,128)S(1)}, f32[4,2,128,128]{3,0,2,1:T(4,128)}, u32[]{:S(2)}) copy-start(f32[4,2,128,128]{3,0,2,1:T(4,128)} %copy-done.3) | copy-start | bytes 1572868
  43.6 5.3 %collective-permute-start.5 = (f32[1,128,256]{2,1,0:T(8,128)S(1)}, f32[1,128,256]{2,1,0:T(8,128)S(1)}, u32[]{:S(2)}, u32[]{:S(2)}) collective-permute-start(f32[1,128,256]{2,1,0:T(8,128)S(1)} %slice_select_fusion.4), channel_id=1, source_target_pairs={{0,8},{2,10},{4,12},{6,14},{8,0},{10,2},{12,4},{14,6},{16,24},{18,... | collective-permute-start | bytes 393224 | tf_op jit(solution)/shard_map/ppermute | solution.py:193
  49.2 6.4 %collective-permute-start.6 = (f32[1,128,128]{2,1,0:T(8,128)S(1)}, f32[1,128,128]{2,1,0:T(8,128)S(1)}, u32[]{:S(2)}, u32[]{:S(2)}) collective-permute-start(f32[1,128,128]{2,1,0:T(8,128)S(1)} %slice_add_fusion.7), channel_id=1, source_target_pairs={{0,16},{2,18},{4,20},{6,22},{8,24},{10,26},{12,28},{14,30},{1,17},... | collective-permute-start | bytes 196616 | tf_op jit(solution)/shard_map/ppermute | solution.py:171
  55.7 4.4 %collective-permute-start.7 = (f32[1,128,128]{2,1,0:T(8,128)S(1)}, f32[1,128,128]{2,1,0:T(8,128)S(1)}, u32[]{:S(2)}, u32[]{:S(2)}) collective-permute-start(f32[1,128,128]{2,1,0:T(8,128)S(1)} %get-tuple-element.39), channel_id=1, source_target_pairs={{0,8},{2,10},{4,12},{6,14},{8,0},{10,2},{12,4},{14,6},{16,24},{18,... | collective-permute-start | bytes 196616 | tf_op jit(solution)/shard_map/ppermute | solution.py:206
  59.2 2.7 %copy-start.1 = (f32[8,2,128,128]{3,2,1,0:T(8,128)S(1)}, f32[8,2,128,128]{3,2,1,0:T(8,128)}, u32[]{:S(2)}) copy-start(f32[8,2,128,128]{3,2,1,0:T(8,128)} %copy-done) | copy-start | bytes 3145732
  60.3 5.0 %collective-permute-start.8 = (f32[2,128,128]{2,1,0:T(8,128)S(1)}, f32[2,128,128]{2,1,0:T(8,128)S(1)}, u32[]{:S(2)}, u32[]{:S(2)}) collective-permute-start(f32[2,128,128]{2,1,0:T(8,128)S(1)} %get-tuple-element.37), channel_id=1, source_target_pairs={{0,4},{2,6},{4,0},{6,2},{8,12},{10,14},{12,8},{14,10},{16,20},{18,... | collective-permute-start | bytes 393224 | tf_op jit(solution)/shard_map/ppermute | solution.py:206
  65.7 1.6 %collective-permute-start.9 = (f32[4,128,128]{2,1,0:T(8,128)S(1)}, f32[4,128,128]{2,1,0:T(8,128)S(1)}, u32[]{:S(2)}, u32[]{:S(2)}) collective-permute-start(f32[4,128,128]{2,1,0:T(8,128)S(1)} %get-tuple-element.25), channel_id=1, source_target_pairs={{0,2},{2,0},{4,6},{6,4},{8,10},{10,8},{12,14},{14,12},{16,18},{18,... | collective-permute-start | bytes 786440 | tf_op jit(solution)/shard_map/ppermute | solution.py:206
  67.3 2.5 %copy-start.6 = (bf16[128,2048]{1,0:T(8,128)(2,1)S(1)}, bf16[128,2048]{1,0:T(8,128)(2,1)}, u32[]{:S(2)}) copy-start(bf16[128,2048]{1,0:T(8,128)(2,1)} %param.10) | copy-start | bytes 1572868
  67.9 2.1 %copy-start.7 = (bf16[128]{0:T(256)(128)(2,1)S(1)}, bf16[128]{0:T(256)(128)(2,1)}, u32[]{:S(2)}) copy-start(bf16[128]{0:T(256)(128)(2,1)} %param.13) | copy-start | bytes 772
  68.1 8.4 %collective-permute-start.10 = (bf16[128,1024]{0,1:T(8,128)(2,1)S(1)}, bf16[128,1024]{0,1:T(8,128)(2,1)S(1)}, u32[]{:S(2)}, u32[]{:S(2)}) collective-permute-start(bf16[128,1024]{0,1:T(8,128)(2,1)S(1)} %bitcast.114), channel_id=1, source_target_pairs={{0,1},{1,0},{2,3},{3,2},{4,5},{5,4},{6,7},{7,6},{8,9},{9,8},{10,11... | collective-permute-start | bytes 786440 | tf_op jit(solution)/shard_map/ppermute | solution.py:240

commit v14 on v13

--- a/solution.py
+++ b/solution.py
@@ -28,6 +28,12 @@
     return jnp.matmul(
         later[..., : later.shape[-2]], earlier, precision=FULL_PRECISION
     ) + jnp.where(lane >= later.shape[-2], later, 0.0)
+
+
+def by_head(rows, width):
+    count = rows.shape[1] // width
+    parts = [rows[:, g * width : (g + 1) * width] for g in range(count)]
+    return jnp.stack(parts).reshape(count, rows.shape[0] // SPAN, SPAN, width)
 
 
 def arrange(key_part, value_part, beta_part, decay_part):
@@ -52,8 +58,8 @@
 def arrange_query(query_part):
     blocks = query_part.shape[0] // SPAN
     key_heads = query_part.shape[1] // DK
-    query_f = query_part.astype(jnp.float32).reshape(blocks, SPAN, key_heads, DK)
-    return (unit_rows(query_f) * DK ** (-0.5)).transpose(2, 0, 1, 3)
+    query_f = by_head(query_part, DK).astype(jnp.float32)
+    return unit_rows(query_f) * DK ** (-0.5)
 
 
 def unit_lower_inverse(strictly_lower):

time: 79.4 us -> 78.8 us (level)
  waiting for transfers between devices: 24.9 us -> 27.7 us
  local copies, waits for them, and re-layouts: 5.32 us -> 3.33 us
  other arithmetic: 14 us -> 12.8 us
    ppermute x6, waiting for transfers between devices: 14.2 us -> 16.9 us  [chain_states(): got = lax.ppermute(other, 'ctx', [(i, i ^ stride) for i in range(size)])]
    convert_element_type x1 -> x0, local copies, waits for them, and re-layouts: 2.01 us -> none  [arrange_query(): query_part.astype(jnp.float32).reshape(blocks, SPAN, key_heads, DK)]
    convert_element_type x1 -> x0, other arithmetic: 0.93 us -> none  [arrange_query(): query_part.astype(jnp.float32).reshape(blocks, SPAN, key_heads, DK)]
  transfers between devices with their start and end apart: 11 -> 11, of which waited for: 9 -> 10; matrix products, arithmetic and copies ran while one was open for 16% -> 12% of each run, Pallas kernels for 0% -> 0%
where the time goes in v14:
time: 78.8 us; the launch traced here: 78.6 us
  waiting for transfers between devices  27.7 us (35%)
  starting transfers between devices  19 us (24%)
  matrix products  15 us (19%)
  other arithmetic  12.8 us (16%)
  local copies, waits for them, and re-layouts  3.33 us (4%)
    ppermute x6, waiting for transfers between devices, chain_states(): got = lax.ppermute(other, 'ctx', [(i, i ^ stride) for i in range(size)])  16.9 us
    ppermute x6, starting transfers between devices, chain_states(): got = lax.ppermute(other, 'ctx', [(i, i ^ stride) for i in range(size)])  7.31 us
    ppermute x1, waiting for transfers between devices, head_return(): got = lax.ppermute(sent, 'head', [(0, 1), (1, 0)])  6.52 us
    dot_general x5, matrix products, unit_lower_inverse(): jnp.matmul(jnp.concatenate([inverse, power], axis=-2), power, precision=L...  5.37 us
    ppermute x3, starting transfers between devices, head_swap(): got = lax.ppermute(sent, 'head', [(0, 1), (1, 0)])  5.18 us
    ppermute x1, starting transfers between devices, exclusive_scan(): return lax.ppermute(write, 'ctx', near)  4.94 us
    ppermute x3, waiting for transfers between devices, head_swap(): got = lax.ppermute(sent, 'head', [(0, 1), (1, 0)])  3.87 us
    select_n x3, other arithmetic, head_swap(): own = jnp.where(first, rows[..., :width], rows[..., width:])  3.15 us
  transfers between devices with their start and end apart: 11, of which 10 were waited for; matrix products, arithmetic and copies ran while one was open for 12% of the time, Pallas kernels for 0%

profile of v14, /device:TPU:0, one launch (start us, length us, event | category | flops | bytes accessed | tf_op | source)
XLA Modules:
  0.0 78.6 jit_solution(3018245827092493736)
XLA Ops:
  0.0 1.3 %broadcast_select_fusion.5 = (bf16[2,128,512]{2,1,0:T(8,128)(2,1)S(1)}, bf16[2,128,512]{2,1,0:T(8,128)(2,1)S(1)}) fusion(pred[]{:T(512)S(6)} %eq.29, bf16[1,128,1024]{2,1,0:T(8,128)(2,1)} %bitcast.132, bf16[1,128,1024]{2,1,0:T(8,128)(2,1)} %bitcast.133), kind=kLoop, calls=%fused_computation.124 | loop fusion | flops 1835008 | bytes 1048577 | tf_op jit(solution)/shard_map/jit(_where)/select_n | solution.py:232
  1.3 3.0 %collective-permute-start = (bf16[2,128,512]{2,1,0:T(8,128)(2,1)S(1)}, bf16[2,128,512]{2,1,0:T(8,128)(2,1)S(1)}, u32[]{:S(2)}, u32[]{:S(2)}) collective-permute-start(bf16[2,128,512]{2,1,0:T(8,128)(2,1)S(1)} %get-tuple-element.34), channel_id=1, source_target_pairs={{0,1},{1,0},{2,3},{3,2},{4,5},{5,4},{6,7},{7,6},{8,9},{9,8},{10,11... | collective-permute-start | bytes 786440 | tf_op jit(solution)/shard_map/ppermute | solution.py:234
  4.4 0.8 broadcast_select_fusion.18
  5.2 1.1 %broadcast_select_fusion.3 = (bf16[128,1024]{1,0:T(8,128)(2,1)S(1)}, bf16[128,1024]{1,0:T(8,128)(2,1)S(1)}) fusion(pred[]{:T(512)S(6)} %eq.29, bf16[128,2048]{1,0:T(8,128)(2,1)} %param.9), kind=kLoop, calls=%fused_computation.122 | loop fusion | flops 262144 | bytes 1048577 | tf_op jit(solution)/shard_map/jit(_where)/select_n | solution.py:232
  6.3 2.1 %collective-permute-start.2 = (bf16[128,1024]{1,0:T(8,128)(2,1)S(1)}, bf16[128,1024]{1,0:T(8,128)(2,1)S(1)}, u32[]{:S(2)}, u32[]{:S(2)}) collective-permute-start(bf16[128,1024]{1,0:T(8,128)(2,1)S(1)} %get-tuple-element.32), channel_id=1, source_target_pairs={{0,1},{1,0},{2,3},{3,2},{4,5},{5,4},{6,7},{7,6},{8,9},{9,8},{10,11... | collective-permute-start | bytes 786440 | tf_op jit(solution)/shard_map/ppermute | solution.py:234
  8.4 3.2 %collective-permute-done.1 = bf16[2,128,8]{1,2,0:T(8,128)(2,1)S(1)} collective-permute-done((bf16[2,128,8]{1,2,0:T(8,128)(2,1)S(1)}, bf16[2,128,8]{1,2,0:T(8,128)(2,1)S(1)}, u32[]{:S(2)}, u32[]{:S(2)}) %collective-permute-start.1) | collective-permute-done | bytes 4128 | tf_op jit(solution)/shard_map/ppermute | solution.py:234
  16.7 1.1 %fusion = f32[8,2,256,128]{3,2,1,0:T(8,128)S(1)} fusion(f32[8,2,128,128]{3,2,1,0:T(8,128)S(1)} %fusion.93, f32[8,2,128,128]{3,2,1,0:T(8,128)S(1)} %get-tuple-element.21), kind=kOutput, calls=%fused_computation | convolution fusion | flops 403177472 | bytes 4194304 | tf_op jit(solution)/shard_map/dot_general | solution.py:71
  17.8 1.0 %slice_add_fusion.5 = (f32[8,2,128,128]{3,2,1,0:T(8,128)S(1)}, f32[8,2,128,128]{3,2,1,0:T(8,128)S(1)}, f32[8,2,128,128]{3,2,1,0:T(8,128)S(1)}) fusion(f32[8,2,256,128]{3,2,1,0:T(8,128)S(1)} %fusion, f32[4,2,128,128]{3,2,1,0:T(8,128)S(1)} %fusion.88, f32[8,2,128]{2,1,0:T(2,128)S(1)} %copy.40, pred[128,128]{1,0:T(8,128)(4,1)S(1)} %get-tuple-element.51, ...), kind=kLoop, calls=%fused_computation.68 | loop fusion | flops 1835008 | bytes 6922240 | tf_op jit(solution)/shard_map/add | solution.py:74
  18.8 1.1 %fusion.4 = f32[8,2,256,128]{3,2,1,0:T(8,128)S(1)} fusion(f32[8,2,128,128]{3,2,1,0:T(8,128)S(1)} %get-tuple-element.14, f32[8,2,128,128]{3,2,1,0:T(8,128)S(1)} %get-tuple-element.13), kind=kOutput, calls=%fused_computation.4 | convolution fusion | flops 403177472 | bytes 4194304 | tf_op jit(solution)/shard_map/dot_general | solution.py:71
  20.1 1.1 %fusion.8 = f32[8,2,256,128]{3,2,1,0:T(8,128)S(1)} fusion(f32[8,2,128,128]{3,2,1,0:T(8,128)S(1)} %get-tuple-element.12, f32[8,2,128,128]{3,2,1,0:T(8,128)S(1)} %get-tuple-element.11), kind=kOutput, calls=%fused_computation.8 | convolution fusion | flops 403177472 | bytes 4194304 | tf_op jit(solution)/shard_map/dot_general | solution.py:71
  21.5 1.1 %fusion.12 = f32[8,2,256,128]{3,2,1,0:T(8,128)S(1)} fusion(f32[8,2,128,128]{3,2,1,0:T(8,128)S(1)} %get-tuple-element.10, f32[8,2,128,128]{3,2,1,0:T(8,128)S(1)} %get-tuple-element.9), kind=kOutput, calls=%fused_computation.12 | convolution fusion | flops 403177472 | bytes 4194304 | tf_op jit(solution)/shard_map/dot_general | solution.py:71
  22.8 1.1 %fusion.16 = f32[8,2,256,128]{3,2,1,0:T(8,128)S(1)} fusion(f32[8,2,128,128]{3,2,1,0:T(8,128)S(1)} %get-tuple-element.8, f32[8,2,128,128]{3,2,1,0:T(8,128)S(1)} %get-tuple-element.7), kind=kOutput, calls=%fused_computation.16 | convolution fusion | flops 403177472 | bytes 4194304 | tf_op jit(solution)/shard_map/dot_general | solution.py:71
  23.9 0.7 convolution_add_fusion
  25.3 1.2 %fusion.20 = f32[8,2,128,256]{3,2,1,0:T(8,128)S(1)} fusion(f32[8,2,128,128]{3,2,1,0:T(8,128)S(1)} %convolution_add_fusion, f32[8,2,128,128]{3,2,1,0:T(8,128)S(1)} %get-tuple-element.28, f32[8,2,128,128]{3,2,1,0:T(8,128)S(1)} %get-tuple-element.48), kind=kOutput, calls=%fused_computation.20 | convolution fusion | flops 403177472 | bytes 5242880 | tf_op jit(solution)/shard_map/dot_general | solution.py:99
  26.5 1.1 %fusion.94 = f32[8,2,128,256]{3,2,1,0:T(8,128)S(1)} fusion(f32[8,2,128,128]{3,2,1,0:T(8,128)S(1)} %get-tuple-element.27, f32[8,2,128,256]{3,2,1,0:T(8,128)S(1)} %fusion.20), kind=kOutput, calls=%fused_computation.191 | convolution fusion | flops 402653184 | bytes 5242880 | tf_op jit(solution)/shard_map/hmck,hmcj->hmkj/dot_general | solution.py:104
  28.9 1.0 %slice_select_fusion = f32[4,128,256]{2,1,0:T(8,128)} fusion(f32[8,128,256]{2,1,0:T(8,128)S(1)} %convolution_add_fusion.2, pred[]{:T(512)S(6)} %eq.31), kind=kLoop, calls=%fused_computation.107 | loop fusion | flops 131072 | bytes 1572865 | tf_op jit(solution)/shard_map/jit(_where)/select_n | solution.py:198
  30.1 2.2 %collective-permute-done.3 = f32[4,128,256]{2,1,0:T(8,128)} collective-permute-done((f32[4,128,256]{2,1,0:T(8,128)}, f32[4,128,256]{2,1,0:T(8,128)}, u32[]{:S(2)}, u32[]{:S(2)}) %collective-permute-start.3) | collective-permute-done | bytes 524320 | tf_op jit(solution)/shard_map/ppermute | solution.py:199
  32.3 1.5 %broadcast_select_fusion.1 = (f32[4,128,256]{2,1,0:T(8,128)S(1)}, f32[4,128,256]{2,1,0:T(8,128)S(1)}) fusion(f32[4,128,256]{2,1,0:T(8,128)} %collective-permute-done.3, pred[]{:T(512)S(6)} %eq.31, f32[8,128,256]{2,1,0:T(8,128)} %copy-done.2), kind=kLoop, calls=%fused_computation.119 | loop fusion | flops 393216 | bytes 2621441 | tf_op jit(solution)/shard_map/jit(_where)/select_n | solution.py:201
  34.2 1.8 %collective-permute-start.4 = (f32[2,128,256]{2,1,0:T(8,128)S(1)}, f32[2,128,256]{2,1,0:T(8,128)S(1)}, u32[]{:S(2)}, u32[]{:S(2)}) collective-permute-start(f32[2,128,256]{2,1,0:T(8,128)S(1)} %slice_select_fusion.2), channel_id=1, source_target_pairs={{0,4},{2,6},{4,0},{6,2},{8,12},{10,14},{12,8},{14,10},{16,20},{18,... | collective-permute-start | bytes 786440 | tf_op jit(solution)/shard_map/ppermute | solution.py:199
  36.3 6.3 %collective-permute-done.4 = f32[2,128,256]{2,1,0:T(8,128)S(1)} collective-permute-done((f32[2,128,256]{2,1,0:T(8,128)S(1)}, f32[2,128,256]{2,1,0:T(8,128)S(1)}, u32[]{:S(2)}, u32[]{:S(2)}) %collective-permute-start.4) | collective-permute-done | bytes 262176 | tf_op jit(solution)/shard_map/ppermute | solution.py:199
  43.0 1.9 %collective-permute-start.5 = (f32[1,128,256]{2,1,0:T(8,128)S(1)}, f32[1,128,256]{2,1,0:T(8,128)S(1)}, u32[]{:S(2)}, u32[]{:S(2)}) collective-permute-start(f32[1,128,256]{2,1,0:T(8,128)S(1)} %slice_select_fusion.4), channel_id=1, source_target_pairs={{0,8},{2,10},{4,12},{6,14},{8,0},{10,2},{12,4},{14,6},{16,24},{18,... | collective-permute-start | bytes 393224 | tf_op jit(solution)/shard_map/ppermute | solution.py:199
  45.5 2.5 %collective-permute-done.5 = f32[1,128,256]{2,1,0:T(8,128)S(1)} collective-permute-done((f32[1,128,256]{2,1,0:T(8,128)S(1)}, f32[1,128,256]{2,1,0:T(8,128)S(1)}, u32[]{:S(2)}, u32[]{:S(2)}) %collective-permute-start.5) | collective-permute-done | bytes 131104 | tf_op jit(solution)/shard_map/ppermute | solution.py:199
  48.3 4.9 %collective-permute-start.6 = (f32[1,128,128]{2,1,0:T(8,128)S(1)}, f32[1,128,128]{2,1,0:T(8,128)S(1)}, u32[]{:S(2)}, u32[]{:S(2)}) collective-permute-start(f32[1,128,128]{2,1,0:T(8,128)S(1)} %slice_add_fusion.7), channel_id=1, source_target_pairs={{0,16},{2,18},{4,20},{6,22},{8,24},{10,26},{12,28},{14,30},{1,17},... | collective-permute-start | bytes 196616 | tf_op jit(solution)/shard_map/ppermute | solution.py:177
  53.3 1.2 %fusion.34 = f32[8,2,128,256]{3,2,1,0:T(8,128)S(1)} fusion(f32[8,2,128,256]{3,2,1,0:T(8,128)S(1)} %fusion.20, f32[8,2,128,128]{3,2,1,0:T(8,128)S(1)} %bitcast.116, f32[8,2,128]{2,1,0:T(2,128)S(1)} %copy.40, pred[128,128]{1,0:T(8,128)(4,1)S(1)} %iota_compare_fusion.2), kind=kOutput, calls=%fused_computation.53 | convolution fusion | flops 403439616 | bytes 5267456 | tf_op jit(solution)/shard_map/hmij,hmjv->hmiv/dot_general | solution.py:124
  55.2 2.0 %collective-permute-start.7 = (f32[1,128,128]{2,1,0:T(8,128)S(1)}, f32[1,128,128]{2,1,0:T(8,128)S(1)}, u32[]{:S(2)}, u32[]{:S(2)}) collective-permute-start(f32[1,128,128]{2,1,0:T(8,128)S(1)} %get-tuple-element.43), channel_id=1, source_target_pairs={{0,8},{2,10},{4,12},{6,14},{8,0},{10,2},{12,4},{14,6},{16,24},{18,... | collective-permute-start | bytes 196616 | tf_op jit(solution)/shard_map/ppermute | solution.py:212
  57.8 1.7 %collective-permute-done.7 = f32[1,128,128]{2,1,0:T(8,128)S(1)} collective-permute-done((f32[1,128,128]{2,1,0:T(8,128)S(1)}, f32[1,128,128]{2,1,0:T(8,128)S(1)}, u32[]{:S(2)}, u32[]{:S(2)}) %collective-permute-start.7) | collective-permute-done | bytes 65568 | tf_op jit(solution)/shard_map/ppermute | solution.py:212
  59.7 1.6 %collective-permute-start.8 = (f32[2,128,128]{2,1,0:T(8,128)S(1)}, f32[2,128,128]{2,1,0:T(8,128)S(1)}, u32[]{:S(2)}, u32[]{:S(2)}) collective-permute-start(f32[2,128,128]{2,1,0:T(8,128)S(1)} %get-tuple-element.37), channel_id=1, source_target_pairs={{0,4},{2,6},{4,0},{6,2},{8,12},{10,14},{12,8},{14,10},{16,20},{18,... | collective-permute-start | bytes 393224 | tf_op jit(solution)/shard_map/ppermute | solution.py:212
  61.9 2.8 %collective-permute-done.8 = f32[2,128,128]{2,1,0:T(8,128)S(1)} collective-permute-done((f32[2,128,128]{2,1,0:T(8,128)S(1)}, f32[2,128,128]{2,1,0:T(8,128)S(1)}, u32[]{:S(2)}, u32[]{:S(2)}) %collective-permute-start.8) | collective-permute-done | bytes 131104 | tf_op jit(solution)/shard_map/ppermute | solution.py:212
  65.3 1.3 %collective-permute-done.9 = f32[4,128,128]{2,1,0:T(8,128)S(1)} collective-permute-done((f32[4,128,128]{2,1,0:T(8,128)S(1)}, f32[4,128,128]{2,1,0:T(8,128)S(1)}, u32[]{:S(2)}, u32[]{:S(2)}) %collective-permute-start.9) | collective-permute-done | bytes 262176 | tf_op jit(solution)/shard_map/ppermute | solution.py:212
  67.5 1.6 %collective-permute-start.10 = (bf16[128,1024]{0,1:T(8,128)(2,1)S(1)}, bf16[128,1024]{0,1:T(8,128)(2,1)S(1)}, u32[]{:S(2)}, u32[]{:S(2)}) collective-permute-start(bf16[128,1024]{0,1:T(8,128)(2,1)S(1)} %bitcast.130), channel_id=1, source_target_pairs={{0,1},{1,0},{2,3},{3,2},{4,5},{5,4},{6,7},{7,6},{8,9},{9,8},{10,11... | collective-permute-start | bytes 786440 | tf_op jit(solution)/shard_map/ppermute | solution.py:246
  69.4 6.5 %collective-permute-done.10 = bf16[128,1024]{0,1:T(8,128)(2,1)S(1)} collective-permute-done((bf16[128,1024]{0,1:T(8,128)(2,1)S(1)}, bf16[128,1024]{0,1:T(8,128)(2,1)S(1)}, u32[]{:S(2)}, u32[]{:S(2)}) %collective-permute-start.10) | collective-permute-done | bytes 262176 | tf_op jit(solution)/shard_map/ppermute | solution.py:246
  77.6 1.0 %copy.60 = bf16[128,2048]{1,0:T(8,128)(2,1)} copy(bf16[128,2048]{0,1:T(8,128)(2,1)S(1)} %fusion.44) | data formatting | bytes 1048576 | tf_op jit(solution)/shard_map/convert_element_type | solution.py:226
  (90 shorter events, 15.2 us)
Async XLA Ops:
  1.3 11.2 %collective-permute-start = (bf16[2,128,512]{2,1,0:T(8,128)(2,1)S(1)}, bf16[2,128,512]{2,1,0:T(8,128)(2,1)S(1)}, u32[]{:S(2)}, u32[]{:S(2)}) collective-permute-start(bf16[2,128,512]{2,1,0:T(8,128)(2,1)S(1)} %get-tuple-element.34), channel_id=1, source_target_pairs={{0,1},{1,0},{2,3},{3,2},{4,5},{5,4},{6,7},{7,6},{8,9},{9,8},{10,11... | collective-permute-start | bytes 786440 | tf_op jit(solution)/shard_map/ppermute | solution.py:234
  5.1 6.5 %collective-permute-start.1 = (bf16[2,128,8]{1,2,0:T(8,128)(2,1)S(1)}, bf16[2,128,8]{1,2,0:T(8,128)(2,1)S(1)}, u32[]{:S(2)}, u32[]{:S(2)}) collective-permute-start(bf16[2,128,8]{1,2,0:T(8,128)(2,1)S(1)} %get-tuple-element.50), channel_id=1, source_target_pairs={{0,1},{1,0},{2,3},{3,2},{4,5},{5,4},{6,7},{7,6},{8,9},{9,8},{10,11... | collective-permute-start | bytes 12296 | tf_op jit(solution)/shard_map/ppermute | solution.py:234
  6.3 10.1 %collective-permute-start.2 = (bf16[128,1024]{1,0:T(8,128)(2,1)S(1)}, bf16[128,1024]{1,0:T(8,128)(2,1)S(1)}, u32[]{:S(2)}, u32[]{:S(2)}) collective-permute-start(bf16[128,1024]{1,0:T(8,128)(2,1)S(1)} %get-tuple-element.32), channel_id=1, source_target_pairs={{0,1},{1,0},{2,3},{3,2},{4,5},{5,4},{6,7},{7,6},{8,9},{9,8},{10,11... | collective-permute-start | bytes 786440 | tf_op jit(solution)/shard_map/ppermute | solution.py:234
  13.8 1.3 %copy-start.3 = (f32[4,2,128,128]{3,0,2,1:T(4,128)}, f32[4,2,128,128]{3,0,2,1:T(4,128)S(1)}, u32[]{:S(2)}) copy-start(f32[4,2,128,128]{3,0,2,1:T(4,128)S(1)} %multiply_bitcast_fusion) | copy-start | bytes 1572868
  27.9 1.0 %copy-start = (f32[8,2,128,128]{3,2,1,0:T(8,128)}, f32[8,2,128,128]{3,2,1,0:T(8,128)S(1)}, u32[]{:S(2)}) copy-start(f32[8,2,128,128]{3,2,1,0:T(8,128)S(1)} %get-tuple-element.6) | copy-start | bytes 3145732
  28.9 1.1 %copy-start.2 = (f32[8,128,256]{2,1,0:T(8,128)}, f32[8,128,256]{2,1,0:T(8,128)S(1)}, u32[]{:S(2)}) copy-start(f32[8,128,256]{2,1,0:T(8,128)S(1)} %convolution_add_fusion.2) | copy-start | bytes 3145732
  30.0 2.3 %collective-permute-start.3 = (f32[4,128,256]{2,1,0:T(8,128)}, f32[4,128,256]{2,1,0:T(8,128)}, u32[]{:S(2)}, u32[]{:S(2)}) collective-permute-start(f32[4,128,256]{2,1,0:T(8,128)} %slice_select_fusion), channel_id=1, source_target_pairs={{0,2},{2,0},{4,6},{6,4},{8,10},{10,8},{12,14},{14,12},{16,18},{18,... | collective-permute-start | bytes 1572872 | tf_op jit(solution)/shard_map/ppermute | solution.py:199
  34.2 10.7 %copy-start.4 = (f32[4,2,128,128]{3,0,2,1:T(4,128)S(1)}, f32[4,2,128,128]{3,0,2,1:T(4,128)}, u32[]{:S(2)}) copy-start(f32[4,2,128,128]{3,0,2,1:T(4,128)} %copy-done.3) | copy-start | bytes 1572868
  34.2 8.4 %collective-permute-start.4 = (f32[2,128,256]{2,1,0:T(8,128)S(1)}, f32[2,128,256]{2,1,0:T(8,128)S(1)}, u32[]{:S(2)}, u32[]{:S(2)}) collective-permute-start(f32[2,128,256]{2,1,0:T(8,128)S(1)} %slice_select_fusion.2), channel_id=1, source_target_pairs={{0,4},{2,6},{4,0},{6,2},{8,12},{10,14},{12,8},{14,10},{16,20},{18,... | collective-permute-start | bytes 786440 | tf_op jit(solution)/shard_map/ppermute | solution.py:199
  43.0 5.0 %collective-permute-start.5 = (f32[1,128,256]{2,1,0:T(8,128)S(1)}, f32[1,128,256]{2,1,0:T(8,128)S(1)}, u32[]{:S(2)}, u32[]{:S(2)}) collective-permute-start(f32[1,128,256]{2,1,0:T(8,128)S(1)} %slice_select_fusion.4), channel_id=1, source_target_pairs={{0,8},{2,10},{4,12},{6,14},{8,0},{10,2},{12,4},{14,6},{16,24},{18,... | collective-permute-start | bytes 393224 | tf_op jit(solution)/shard_map/ppermute | solution.py:199
  48.3 6.7 %collective-permute-start.6 = (f32[1,128,128]{2,1,0:T(8,128)S(1)}, f32[1,128,128]{2,1,0:T(8,128)S(1)}, u32[]{:S(2)}, u32[]{:S(2)}) collective-permute-start(f32[1,128,128]{2,1,0:T(8,128)S(1)} %slice_add_fusion.7), channel_id=1, source_target_pairs={{0,16},{2,18},{4,20},{6,22},{8,24},{10,26},{12,28},{14,30},{1,17},... | collective-permute-start | bytes 196616 | tf_op jit(solution)/shard_map/ppermute | solution.py:177
  55.2 6.1 %copy-start.1 = (f32[8,2,128,128]{3,2,1,0:T(8,128)S(1)}, f32[8,2,128,128]{3,2,1,0:T(8,128)}, u32[]{:S(2)}) copy-start(f32[8,2,128,128]{3,2,1,0:T(8,128)} %copy-done) | copy-start | bytes 3145732
  55.2 4.3 %collective-permute-start.7 = (f32[1,128,128]{2,1,0:T(8,128)S(1)}, f32[1,128,128]{2,1,0:T(8,128)S(1)}, u32[]{:S(2)}, u32[]{:S(2)}) collective-permute-start(f32[1,128,128]{2,1,0:T(8,128)S(1)} %get-tuple-element.43), channel_id=1, source_target_pairs={{0,8},{2,10},{4,12},{6,14},{8,0},{10,2},{12,4},{14,6},{16,24},{18,... | collective-permute-start | bytes 196616 | tf_op jit(solution)/shard_map/ppermute | solution.py:212
  59.7 5.0 %collective-permute-start.8 = (f32[2,128,128]{2,1,0:T(8,128)S(1)}, f32[2,128,128]{2,1,0:T(8,128)S(1)}, u32[]{:S(2)}, u32[]{:S(2)}) collective-permute-start(f32[2,128,128]{2,1,0:T(8,128)S(1)} %get-tuple-element.37), channel_id=1, source_target_pairs={{0,4},{2,6},{4,0},{6,2},{8,12},{10,14},{12,8},{14,10},{16,20},{18,... | collective-permute-start | bytes 393224 | tf_op jit(solution)/shard_map/ppermute | solution.py:212
  65.1 1.6 %collective-permute-start.9 = (f32[4,128,128]{2,1,0:T(8,128)S(1)}, f32[4,128,128]{2,1,0:T(8,128)S(1)}, u32[]{:S(2)}, u32[]{:S(2)}) collective-permute-start(f32[4,128,128]{2,1,0:T(8,128)S(1)} %get-tuple-element.25), channel_id=1, source_target_pairs={{0,2},{2,0},{4,6},{6,4},{8,10},{10,8},{12,14},{14,12},{16,18},{18,... | collective-permute-start | bytes 786440 | tf_op jit(solution)/shard_map/ppermute | solution.py:212
  66.7 2.5 %copy-start.5 = (bf16[128,2048]{1,0:T(8,128)(2,1)S(1)}, bf16[128,2048]{1,0:T(8,128)(2,1)}, u32[]{:S(2)}) copy-start(bf16[128,2048]{1,0:T(8,128)(2,1)} %param.10) | copy-start | bytes 1572868
  67.3 2.1 %copy-start.6 = (bf16[128]{0:T(256)(128)(2,1)S(1)}, bf16[128]{0:T(256)(128)(2,1)}, u32[]{:S(2)}) copy-start(bf16[128]{0:T(256)(128)(2,1)} %param.13) | copy-start | bytes 772
  67.5 8.4 %collective-permute-start.10 = (bf16[128,1024]{0,1:T(8,128)(2,1)S(1)}, bf16[128,1024]{0,1:T(8,128)(2,1)S(1)}, u32[]{:S(2)}, u32[]{:S(2)}) collective-permute-start(bf16[128,1024]{0,1:T(8,128)(2,1)S(1)} %bitcast.130), channel_id=1, source_target_pairs={{0,1},{1,0},{2,3},{3,2},{4,5},{5,4},{6,7},{7,6},{8,9},{9,8},{10,11... | collective-permute-start | bytes 786440 | tf_op jit(solution)/shard_map/ppermute | solution.py:246

commit v15 on v14

--- a/solution.py
+++ b/solution.py
@@ -40,12 +40,8 @@
     blocks = key_part.shape[0] // SPAN
     key_heads = key_part.shape[1] // DK
     value_heads = value_part.shape[1] // DV
-    key_unit = unit_rows(
-        key_part.astype(jnp.float32).reshape(blocks, SPAN, key_heads, DK)
-    ).transpose(2, 0, 1, 3)
-    value_f = (
-        value_part.astype(jnp.float32).reshape(blocks, SPAN, value_heads, DV).transpose(2, 0, 1, 3)
-    )
+    key_unit = unit_rows(by_head(key_part, DK).astype(jnp.float32))
+    value_f = by_head(value_part, DV).astype(jnp.float32)
     beta_gate = (
         jax.nn.sigmoid(beta_part.astype(jnp.float32))
         .reshape(blocks, SPAN, value_heads)

time: 78.8 us -> 88 us (1.12)
  local copies, waits for them, and re-layouts: 3.33 us -> 6.13 us
  waiting for transfers between devices: 27.7 us -> 30.2 us
  matrix products: 15 us -> 17 us
  other arithmetic: 12.8 us -> 14.7 us
    ppermute x3, waiting for transfers between devices: 3.87 us -> 7.97 us  [head_swap(): got = lax.ppermute(sent, 'head', [(0, 1), (1, 0)])]
    ppermute x6, waiting for transfers between devices: 16.9 us -> 15.3 us  [chain_states(): got = lax.ppermute(other, 'ctx', [(i, i ^ stride) for i in range(size)])]
    dot_general x4, matrix products: 1.52 us -> 2.85 us  [compose_joined(): jnp.matmul(later[..., :later.shape[-2]], earlier, precision=FULL_PRECISION)]
    slice x1, local copies, waits for them, and re-layouts: 0.01 us -> 1.14 us  [split(): return (both[..., :DK], both[..., DK:])]
    select_n x3, other arithmetic: 1.57 us -> 2.68 us  [chain_states(): later = jnp.where(upper, mine, got)]
    unnamed x17 -> x53, local copies, waits for them, and re-layouts: 0.96 us -> 2.05 us
  transfers between devices with their start and end apart: 11 -> 11, of which waited for: 10 -> 9; matrix products, arithmetic and copies ran while one was open for 12% -> 13% of each run, Pallas kernels for 0% -> 0%
where the time goes in v15:
time: 88 us; the launch traced here: 87.7 us
  waiting for transfers between devices  30.2 us (34%)
  starting transfers between devices  18.9 us (21%)
  matrix products  17 us (19%)
  other arithmetic  14.7 us (17%)
  local copies, waits for them, and re-layouts  6.13 us (7%)
    ppermute x6, waiting for transfers between devices, chain_states(): got = lax.ppermute(other, 'ctx', [(i, i ^ stride) for i in range(size)])  15.3 us
    ppermute x3, waiting for transfers between devices, head_swap(): got = lax.ppermute(sent, 'head', [(0, 1), (1, 0)])  7.97 us
    ppermute x6, starting transfers between devices, chain_states(): got = lax.ppermute(other, 'ctx', [(i, i ^ stride) for i in range(size)])  7.23 us
    ppermute x1, waiting for transfers between devices, head_return(): got = lax.ppermute(sent, 'head', [(0, 1), (1, 0)])  6.52 us
    dot_general x5, matrix products, unit_lower_inverse(): jnp.matmul(jnp.concatenate([inverse, power], axis=-2), power, precision=L...  5.37 us
    ppermute x3, starting transfers between devices, head_swap(): got = lax.ppermute(sent, 'head', [(0, 1), (1, 0)])  5.17 us
    ppermute x1, starting transfers between devices, exclusive_scan(): return lax.ppermute(write, 'ctx', near)  4.93 us
    dot_general x4, matrix products, compose_joined(): jnp.matmul(later[..., :later.shape[-2]], earlier, precision=FULL_PRECISION)  2.85 us
  transfers between devices with their start and end apart: 11, of which 9 were waited for; matrix products, arithmetic and copies ran while one was open for 13% of the time, Pallas kernels for 0%

profile of v15, /device:TPU:0, one launch (start us, length us, event | category | flops | bytes accessed | tf_op | source)
XLA Modules:
  0.0 87.7 jit_solution(701993963255577742)
XLA Ops:
  0.0 1.1 %broadcast_select_fusion.3 = (bf16[128,1024]{1,0:T(8,128)(2,1)S(1)}, bf16[128,1024]{1,0:T(8,128)(2,1)S(1)}) fusion(pred[]{:T(512)S(6)} %eq.29, bf16[128,2048]{1,0:T(8,128)(2,1)} %param.9), kind=kLoop, calls=%fused_computation.123 | loop fusion | flops 262144 | bytes 1048577 | tf_op jit(solution)/shard_map/jit(_where)/select_n | solution.py:228
  1.1 3.0 %collective-permute-start.2 = (bf16[128,1024]{1,0:T(8,128)(2,1)S(1)}, bf16[128,1024]{1,0:T(8,128)(2,1)S(1)}, u32[]{:S(2)}, u32[]{:S(2)}) collective-permute-start(bf16[128,1024]{1,0:T(8,128)(2,1)S(1)} %get-tuple-element.40), channel_id=1, source_target_pairs={{0,1},{1,0},{2,3},{3,2},{4,5},{5,4},{6,7},{7,6},{8,9},{9,8},{10,11... | collective-permute-start | bytes 786440 | tf_op jit(solution)/shard_map/ppermute | solution.py:230
  4.1 1.3 %broadcast_select_fusion.5 = (bf16[2,128,512]{2,1,0:T(8,128)(2,1)S(1)}, bf16[2,128,512]{2,1,0:T(8,128)(2,1)S(1)}) fusion(pred[]{:T(512)S(6)} %eq.29, bf16[1,128,1024]{2,1,0:T(8,128)(2,1)} %bitcast.161, bf16[1,128,1024]{2,1,0:T(8,128)(2,1)} %bitcast.162), kind=kLoop, calls=%fused_computation.125 | loop fusion | flops 1835008 | bytes 1048577 | tf_op jit(solution)/shard_map/jit(_where)/select_n | solution.py:228
  5.6 2.1 %collective-permute-start.1 = (bf16[2,128,8]{1,2,0:T(8,128)(2,1)S(1)}, bf16[2,128,8]{1,2,0:T(8,128)(2,1)S(1)}, u32[]{:S(2)}, u32[]{:S(2)}) collective-permute-start(bf16[2,128,8]{1,2,0:T(8,128)(2,1)S(1)} %get-tuple-element.62), channel_id=1, source_target_pairs={{0,1},{1,0},{2,3},{3,2},{4,5},{5,4},{6,7},{7,6},{8,9},{9,8},{10,11... | collective-permute-start | bytes 12296 | tf_op jit(solution)/shard_map/ppermute | solution.py:230
  8.2 8.0 %collective-permute-done.1 = bf16[2,128,8]{1,2,0:T(8,128)(2,1)S(1)} collective-permute-done((bf16[2,128,8]{1,2,0:T(8,128)(2,1)S(1)}, bf16[2,128,8]{1,2,0:T(8,128)(2,1)S(1)}, u32[]{:S(2)}, u32[]{:S(2)}) %collective-permute-start.1) | collective-permute-done | bytes 4128 | tf_op jit(solution)/shard_map/ppermute | solution.py:230
  21.2 1.1 %fusion = f32[8,2,256,128]{3,2,1,0:T(8,128)S(1)} fusion(f32[8,2,128,128]{3,2,1,0:T(8,128)S(1)} %fusion.94, f32[8,2,128,128]{3,2,1,0:T(8,128)S(1)} %get-tuple-element.21), kind=kOutput, calls=%fused_computation | convolution fusion | flops 403177472 | bytes 4194304 | tf_op jit(solution)/shard_map/dot_general | solution.py:67
  22.3 1.0 %slice_add_fusion.5 = (f32[8,2,128,128]{3,2,1,0:T(8,128)S(1)}, f32[8,2,128,128]{3,2,1,0:T(8,128)S(1)}, f32[8,2,128,128]{3,2,1,0:T(8,128)S(1)}) fusion(f32[8,2,256,128]{3,2,1,0:T(8,128)S(1)} %fusion, f32[4,2,128,128]{3,2,1,0:T(8,128)S(1)} %fusion.66, f32[8,2,128]{2,1,0:T(2,128)S(1)} %copy.19, pred[128,128]{1,0:T(8,128)(4,1)S(1)} %get-tuple-element.67, ...), kind=kLoop, calls=%fused_computation.68 | loop fusion | flops 2097152 | bytes 6397952 | tf_op jit(solution)/shard_map/add | solution.py:70
  23.3 1.1 %fusion.4 = f32[8,2,256,128]{3,2,1,0:T(8,128)S(1)} fusion(f32[8,2,128,128]{3,2,1,0:T(8,128)S(1)} %get-tuple-element.14, f32[8,2,128,128]{3,2,1,0:T(8,128)S(1)} %get-tuple-element.13), kind=kOutput, calls=%fused_computation.4 | convolution fusion | flops 403177472 | bytes 4194304 | tf_op jit(solution)/shard_map/dot_general | solution.py:67
  24.6 1.1 %fusion.8 = f32[8,2,256,128]{3,2,1,0:T(8,128)S(1)} fusion(f32[8,2,128,128]{3,2,1,0:T(8,128)S(1)} %get-tuple-element.12, f32[8,2,128,128]{3,2,1,0:T(8,128)S(1)} %get-tuple-element.11), kind=kOutput, calls=%fused_computation.8 | convolution fusion | flops 403177472 | bytes 4194304 | tf_op jit(solution)/shard_map/dot_general | solution.py:67
  26.0 1.1 %fusion.12 = f32[8,2,256,128]{3,2,1,0:T(8,128)S(1)} fusion(f32[8,2,128,128]{3,2,1,0:T(8,128)S(1)} %get-tuple-element.10, f32[8,2,128,128]{3,2,1,0:T(8,128)S(1)} %get-tuple-element.9), kind=kOutput, calls=%fused_computation.12 | convolution fusion | flops 403177472 | bytes 4194304 | tf_op jit(solution)/shard_map/dot_general | solution.py:67
  27.3 1.1 %fusion.16 = f32[8,2,256,128]{3,2,1,0:T(8,128)S(1)} fusion(f32[8,2,128,128]{3,2,1,0:T(8,128)S(1)} %get-tuple-element.8, f32[8,2,128,128]{3,2,1,0:T(8,128)S(1)} %get-tuple-element.7), kind=kOutput, calls=%fused_computation.16 | convolution fusion | flops 403177472 | bytes 4194304 | tf_op jit(solution)/shard_map/dot_general | solution.py:67
  29.8 1.2 %fusion.20 = f32[8,2,128,256]{3,2,1,0:T(8,128)S(1)} fusion(f32[8,2,128,128]{3,2,1,0:T(8,128)S(1)} %convolution_add_fusion, f32[8,2,128,128]{3,2,1,0:T(8,128)S(1)} %get-tuple-element.28, f32[8,2,128,128]{3,2,1,0:T(8,128)S(1)} %get-tuple-element.60), kind=kOutput, calls=%fused_computation.20 | convolution fusion | flops 403177472 | bytes 5242880 | tf_op jit(solution)/shard_map/dot_general | solution.py:95
  31.0 1.1 %fusion.95 = f32[8,2,128,256]{3,2,1,0:T(8,128)S(1)} fusion(f32[8,2,128,128]{3,2,1,0:T(8,128)S(1)} %get-tuple-element.27, f32[8,2,128,256]{3,2,1,0:T(8,128)S(1)} %fusion.20), kind=kOutput, calls=%fused_computation.200 | convolution fusion | flops 402653184 | bytes 5242880 | tf_op jit(solution)/shard_map/hmck,hmcj->hmkj/dot_general | solution.py:100
  34.9 2.2 %collective-permute-done.3 = f32[4,128,256]{2,1,0:T(8,128)} collective-permute-done((f32[4,128,256]{2,1,0:T(8,128)}, f32[4,128,256]{2,1,0:T(8,128)}, u32[]{:S(2)}, u32[]{:S(2)}) %collective-permute-start.3) | collective-permute-done | bytes 524320 | tf_op jit(solution)/shard_map/ppermute | solution.py:195
  37.2 1.5 %broadcast_select_fusion.1 = (f32[4,128,256]{2,1,0:T(8,128)S(1)}, f32[4,128,256]{2,1,0:T(8,128)S(1)}) fusion(f32[4,128,256]{2,1,0:T(8,128)} %collective-permute-done.3, pred[]{:T(512)S(6)} %eq.31, f32[8,128,256]{2,1,0:T(8,128)} %copy-done.2), kind=kLoop, calls=%fused_computation.120 | loop fusion | flops 393216 | bytes 2621441 | tf_op jit(solution)/shard_map/jit(_where)/select_n | solution.py:197
  38.7 1.1 %convolution_add_fusion.3 = f32[4,128,256]{2,1,0:T(8,128)S(1)} fusion(f32[4,128,256]{2,1,0:T(8,128)S(1)} %get-tuple-element.16, f32[4,128,256]{2,1,0:T(8,128)S(1)} %get-tuple-element.15, pred[256]{0:T(512)(128)(4,1)} %iota_compare_fusion.3), kind=kOutput, calls=%fused_computation.39 | convolution fusion | flops 100925440 | bytes 1835264 | tf_op jit(solution)/shard_map/dot_general | solution.py:28
  41.3 1.7 %collective-permute-start.4 = (f32[2,128,256]{2,1,0:T(8,128)}, f32[2,128,256]{2,1,0:T(8,128)}, u32[]{:S(2)}, u32[]{:S(2)}) collective-permute-start(f32[2,128,256]{2,1,0:T(8,128)} %slice_select_fusion.2), channel_id=1, source_target_pairs={{0,4},{2,6},{4,0},{6,2},{8,12},{10,14},{12,8},{14,10},{16,20},{18,... | collective-permute-start | bytes 786440 | tf_op jit(solution)/shard_map/ppermute | solution.py:195
  43.7 1.1 %slice.347 = pred[128]{0:T(512)(128)(4,1)} slice(pred[256]{0:T(512)(128)(4,1)} %iota_compare_fusion.3), slice={[128:256]} | slice | bytes 256 | tf_op jit(solution)/shard_map/slice | solution.py:154
  45.1 4.9 %collective-permute-done.4 = f32[2,128,256]{2,1,0:T(8,128)} collective-permute-done((f32[2,128,256]{2,1,0:T(8,128)}, f32[2,128,256]{2,1,0:T(8,128)}, u32[]{:S(2)}, u32[]{:S(2)}) %collective-permute-start.4) | collective-permute-done | bytes 262176 | tf_op jit(solution)/shard_map/ppermute | solution.py:195
  50.0 1.2 %broadcast_select_fusion.8 = (f32[2,128,256]{2,1,0:T(8,128)S(1)}, f32[2,128,256]{2,1,0:T(8,128)S(1)}) fusion(f32[2,128,256]{2,1,0:T(8,128)} %collective-permute-done.4, pred[]{:T(512)S(6)} %eq.32, f32[4,128,256]{2,1,0:T(8,128)} %copy-done.3), kind=kLoop, calls=%fused_computation.136 | loop fusion | flops 196608 | bytes 1310721 | tf_op jit(solution)/shard_map/jit(_where)/select_n | solution.py:197
  52.1 1.9 %collective-permute-start.5 = (f32[1,128,256]{2,1,0:T(8,128)S(1)}, f32[1,128,256]{2,1,0:T(8,128)S(1)}, u32[]{:S(2)}, u32[]{:S(2)}) collective-permute-start(f32[1,128,256]{2,1,0:T(8,128)S(1)} %slice_select_fusion.4), channel_id=1, source_target_pairs={{0,8},{2,10},{4,12},{6,14},{8,0},{10,2},{12,4},{14,6},{16,24},{18,... | collective-permute-start | bytes 393224 | tf_op jit(solution)/shard_map/ppermute | solution.py:195
  55.0 2.2 %collective-permute-done.5 = f32[1,128,256]{2,1,0:T(8,128)S(1)} collective-permute-done((f32[1,128,256]{2,1,0:T(8,128)S(1)}, f32[1,128,256]{2,1,0:T(8,128)S(1)}, u32[]{:S(2)}, u32[]{:S(2)}) %collective-permute-start.5) | collective-permute-done | bytes 131104 | tf_op jit(solution)/shard_map/ppermute | solution.py:195
  57.4 4.9 %collective-permute-start.6 = (f32[1,128,128]{2,1,0:T(8,128)S(1)}, f32[1,128,128]{2,1,0:T(8,128)S(1)}, u32[]{:S(2)}, u32[]{:S(2)}) collective-permute-start(f32[1,128,128]{2,1,0:T(8,128)S(1)} %slice_add_fusion.7), channel_id=1, source_target_pairs={{0,16},{2,18},{4,20},{6,22},{8,24},{10,26},{12,28},{14,30},{1,17},... | collective-permute-start | bytes 196616 | tf_op jit(solution)/shard_map/ppermute | solution.py:173
  62.5 1.2 %fusion.34 = f32[8,2,128,256]{3,2,1,0:T(8,128)S(1)} fusion(f32[8,2,128,256]{3,2,1,0:T(8,128)S(1)} %fusion.20, f32[8,2,128,128]{3,2,1,0:T(8,128)S(1)} %bitcast.122, f32[8,2,128]{2,1,0:T(2,128)S(1)} %copy.19, pred[128,128]{1,0:T(8,128)(4,1)S(1)} %copy-done.13), kind=kOutput, calls=%fused_computation.53 | convolution fusion | flops 403439616 | bytes 5267456 | tf_op jit(solution)/shard_map/hmij,hmjv->hmiv/dot_general | solution.py:120
  64.3 2.0 %collective-permute-start.7 = (f32[1,128,128]{2,1,0:T(8,128)S(1)}, f32[1,128,128]{2,1,0:T(8,128)S(1)}, u32[]{:S(2)}, u32[]{:S(2)}) collective-permute-start(f32[1,128,128]{2,1,0:T(8,128)S(1)} %get-tuple-element.55), channel_id=1, source_target_pairs={{0,8},{2,10},{4,12},{6,14},{8,0},{10,2},{12,4},{14,6},{16,24},{18,... | collective-permute-start | bytes 196616 | tf_op jit(solution)/shard_map/ppermute | solution.py:208
  66.9 1.7 %collective-permute-done.7 = f32[1,128,128]{2,1,0:T(8,128)S(1)} collective-permute-done((f32[1,128,128]{2,1,0:T(8,128)S(1)}, f32[1,128,128]{2,1,0:T(8,128)S(1)}, u32[]{:S(2)}, u32[]{:S(2)}) %collective-permute-start.7) | collective-permute-done | bytes 65568 | tf_op jit(solution)/shard_map/ppermute | solution.py:208
  68.9 1.6 %collective-permute-start.8 = (f32[2,128,128]{2,1,0:T(8,128)S(1)}, f32[2,128,128]{2,1,0:T(8,128)S(1)}, u32[]{:S(2)}, u32[]{:S(2)}) collective-permute-start(f32[2,128,128]{2,1,0:T(8,128)S(1)} %get-tuple-element.45), channel_id=1, source_target_pairs={{0,4},{2,6},{4,0},{6,2},{8,12},{10,14},{12,8},{14,10},{16,20},{18,... | collective-permute-start | bytes 393224 | tf_op jit(solution)/shard_map/ppermute | solution.py:208
  71.1 2.8 %collective-permute-done.8 = f32[2,128,128]{2,1,0:T(8,128)S(1)} collective-permute-done((f32[2,128,128]{2,1,0:T(8,128)S(1)}, f32[2,128,128]{2,1,0:T(8,128)S(1)}, u32[]{:S(2)}, u32[]{:S(2)}) %collective-permute-start.8) | collective-permute-done | bytes 131104 | tf_op jit(solution)/shard_map/ppermute | solution.py:208
  74.5 1.3 %collective-permute-done.9 = f32[4,128,128]{2,1,0:T(8,128)S(1)} collective-permute-done((f32[4,128,128]{2,1,0:T(8,128)S(1)}, f32[4,128,128]{2,1,0:T(8,128)S(1)}, u32[]{:S(2)}, u32[]{:S(2)}) %collective-permute-start.9) | collective-permute-done | bytes 262176 | tf_op jit(solution)/shard_map/ppermute | solution.py:208
  76.7 1.6 %collective-permute-start.10 = (bf16[128,1024]{0,1:T(8,128)(2,1)S(1)}, bf16[128,1024]{0,1:T(8,128)(2,1)S(1)}, u32[]{:S(2)}, u32[]{:S(2)}) collective-permute-start(bf16[128,1024]{0,1:T(8,128)(2,1)S(1)} %bitcast.159), channel_id=1, source_target_pairs={{0,1},{1,0},{2,3},{3,2},{4,5},{5,4},{6,7},{7,6},{8,9},{9,8},{10,11... | collective-permute-start | bytes 786440 | tf_op jit(solution)/shard_map/ppermute | solution.py:242
  78.6 6.5 %collective-permute-done.10 = bf16[128,1024]{0,1:T(8,128)(2,1)S(1)} collective-permute-done((bf16[128,1024]{0,1:T(8,128)(2,1)S(1)}, bf16[128,1024]{0,1:T(8,128)(2,1)S(1)}, u32[]{:S(2)}, u32[]{:S(2)}) %collective-permute-start.10) | collective-permute-done | bytes 262176 | tf_op jit(solution)/shard_map/ppermute | solution.py:242
  86.7 1.0 %copy.35 = bf16[128,2048]{1,0:T(8,128)(2,1)} copy(bf16[128,2048]{0,1:T(8,128)(2,1)S(1)} %fusion.44) | data formatting | bytes 1048576 | tf_op jit(solution)/shard_map/convert_element_type | solution.py:222
  (126 shorter events, 20.2 us)
Async XLA Ops:
  0.0 5.5 %copy-start.19 = (bf16[128,16]{0,1:T(8,128)(2,1)S(1)}, bf16[128,16]{0,1:T(8,128)(2,1)}, u32[]{:S(2)}) copy-start(bf16[128,16]{0,1:T(8,128)(2,1)} %param.11) | copy-start | bytes 12292
  0.0 5.5 %copy-start.18 = (bf16[128,16]{0,1:T(8,128)(2,1)S(1)}, bf16[128,16]{0,1:T(8,128)(2,1)}, u32[]{:S(2)}) copy-start(bf16[128,16]{0,1:T(8,128)(2,1)} %param.12) | copy-start | bytes 12292
  1.1 18.4 %collective-permute-start.2 = (bf16[128,1024]{1,0:T(8,128)(2,1)S(1)}, bf16[128,1024]{1,0:T(8,128)(2,1)S(1)}, u32[]{:S(2)}, u32[]{:S(2)}) collective-permute-start(bf16[128,1024]{1,0:T(8,128)(2,1)S(1)} %get-tuple-element.40), channel_id=1, source_target_pairs={{0,1},{1,0},{2,3},{3,2},{4,5},{5,4},{6,7},{7,6},{8,9},{9,8},{10,11... | collective-permute-start | bytes 786440 | tf_op jit(solution)/shard_map/ppermute | solution.py:230
  5.5 12.3 %collective-permute-start = (bf16[2,128,512]{2,1,0:T(8,128)(2,1)S(1)}, bf16[2,128,512]{2,1,0:T(8,128)(2,1)S(1)}, u32[]{:S(2)}, u32[]{:S(2)}) collective-permute-start(bf16[2,128,512]{2,1,0:T(8,128)(2,1)S(1)} %get-tuple-element.42), channel_id=1, source_target_pairs={{0,1},{1,0},{2,3},{3,2},{4,5},{5,4},{6,7},{7,6},{8,9},{9,8},{10,11... | collective-permute-start | bytes 786440 | tf_op jit(solution)/shard_map/ppermute | solution.py:230
  5.6 10.6 %collective-permute-start.1 = (bf16[2,128,8]{1,2,0:T(8,128)(2,1)S(1)}, bf16[2,128,8]{1,2,0:T(8,128)(2,1)S(1)}, u32[]{:S(2)}, u32[]{:S(2)}) collective-permute-start(bf16[2,128,8]{1,2,0:T(8,128)(2,1)S(1)} %get-tuple-element.62), channel_id=1, source_target_pairs={{0,1},{1,0},{2,3},{3,2},{4,5},{5,4},{6,7},{7,6},{8,9},{9,8},{10,11... | collective-permute-start | bytes 12296 | tf_op jit(solution)/shard_map/ppermute | solution.py:230
  18.1 1.7 %copy-start.6 = (bf16[256,128]{1,0:T(8,128)(2,1)}, bf16[256,128]{1,0:T(8,128)(2,1)S(1)}, u32[]{:S(2)}) copy-start(bf16[256,128]{1,0:T(8,128)(2,1)S(1)} %get-tuple-element.64) | copy-start | bytes 196612
  18.1 1.7 %copy-start.8 = (bf16[256,128]{1,0:T(8,128)(2,1)}, bf16[256,128]{1,0:T(8,128)(2,1)S(1)}, u32[]{:S(2)}) copy-start(bf16[256,128]{1,0:T(8,128)(2,1)S(1)} %get-tuple-element.65) | copy-start | bytes 196612
  18.1 1.7 %copy-start.10 = (bf16[256,128]{1,0:T(8,128)(2,1)}, bf16[256,128]{1,0:T(8,128)(2,1)S(1)}, u32[]{:S(2)}) copy-start(bf16[256,128]{1,0:T(8,128)(2,1)S(1)} %get-tuple-element.66) | copy-start | bytes 196612
  18.3 2.1 %copy-start.15 = (f32[4,2,128]{2,1,0:T(2,128)}, f32[4,2,128]{2,1,0:T(2,128)S(1)}, u32[]{:S(2)}) copy-start(f32[4,2,128]{2,1,0:T(2,128)S(1)} %add_rsqrt_fusion.1) | copy-start | bytes 12292
  31.0 1.1 %copy-start.14 = (f32[8,2]{1,0:T(8,128)S(1)}, f32[8,2]{1,0:T(8,128)}, u32[]{:S(2)}) copy-start(f32[8,2]{1,0:T(8,128)} %copy.25) | copy-start | bytes 196
  32.4 1.3 %copy-start = (f32[8,2,128,128]{3,2,1,0:T(8,128)}, f32[8,2,128,128]{3,2,1,0:T(8,128)S(1)}, u32[]{:S(2)}) copy-start(f32[8,2,128,128]{3,2,1,0:T(8,128)S(1)} %get-tuple-element.6) | copy-start | bytes 3145732
  33.7 1.2 %copy-start.2 = (f32[8,128,256]{2,1,0:T(8,128)}, f32[8,128,256]{2,1,0:T(8,128)S(1)}, u32[]{:S(2)}) copy-start(f32[8,128,256]{2,1,0:T(8,128)S(1)} %convolution_add_fusion.2) | copy-start | bytes 3145732
  34.9 2.3 %collective-permute-start.3 = (f32[4,128,256]{2,1,0:T(8,128)}, f32[4,128,256]{2,1,0:T(8,128)}, u32[]{:S(2)}, u32[]{:S(2)}) collective-permute-start(f32[4,128,256]{2,1,0:T(8,128)} %slice_select_fusion), channel_id=1, source_target_pairs={{0,2},{2,0},{4,6},{6,4},{8,10},{10,8},{12,14},{14,12},{16,18},{18,... | collective-permute-start | bytes 1572872 | tf_op jit(solution)/shard_map/ppermute | solution.py:195
  38.7 2.7 %copy-start.4 = (f32[4,128,256]{2,1,0:T(8,128)}, f32[4,128,256]{2,1,0:T(8,128)S(1)}, u32[]{:S(2)}) copy-start(f32[4,128,256]{2,1,0:T(8,128)S(1)} %get-tuple-element.16) | copy-start | bytes 1572868
  38.7 15.3 %copy-start.7 = (bf16[256,128]{1,0:T(8,128)(2,1)S(1)}, bf16[256,128]{1,0:T(8,128)(2,1)}, u32[]{:S(2)}) copy-start(bf16[256,128]{1,0:T(8,128)(2,1)} %copy-done.6) | copy-start | bytes 196612
  39.8 0.8 copy-start.3
  41.3 8.7 %collective-permute-start.4 = (f32[2,128,256]{2,1,0:T(8,128)}, f32[2,128,256]{2,1,0:T(8,128)}, u32[]{:S(2)}, u32[]{:S(2)}) collective-permute-start(f32[2,128,256]{2,1,0:T(8,128)} %slice_select_fusion.2), channel_id=1, source_target_pairs={{0,4},{2,6},{4,0},{6,2},{8,12},{10,14},{12,8},{14,10},{16,20},{18,... | collective-permute-start | bytes 786440 | tf_op jit(solution)/shard_map/ppermute | solution.py:195
  44.8 9.2 %copy-start.9 = (bf16[256,128]{1,0:T(8,128)(2,1)S(1)}, bf16[256,128]{1,0:T(8,128)(2,1)}, u32[]{:S(2)}) copy-start(bf16[256,128]{1,0:T(8,128)(2,1)} %copy-done.8) | copy-start | bytes 196612
  44.8 9.2 %copy-start.11 = (bf16[256,128]{1,0:T(8,128)(2,1)S(1)}, bf16[256,128]{1,0:T(8,128)(2,1)}, u32[]{:S(2)}) copy-start(bf16[256,128]{1,0:T(8,128)(2,1)} %copy-done.10) | copy-start | bytes 196612
  44.8 9.2 %copy-start.16 = (f32[4,2,128]{2,1,0:T(2,128)S(1)}, f32[4,2,128]{2,1,0:T(2,128)}, u32[]{:S(2)}) copy-start(f32[4,2,128]{2,1,0:T(2,128)} %copy-done.15) | copy-start | bytes 12292
  51.2 6.2 %copy-start.20 = (pred[128]{0:T(512)(128)(4,1)S(1)}, pred[128]{0:T(512)(128)(4,1)}, u32[]{:S(2)}) copy-start(pred[128]{0:T(512)(128)(4,1)} %slice.347) | copy-start | bytes 388
  52.1 10.4 %copy-start.13 = (pred[128,128]{1,0:T(8,128)(4,1)S(1)}, pred[128,128]{1,0:T(8,128)(4,1)}, u32[]{:S(2)}) copy-start(pred[128,128]{1,0:T(8,128)(4,1)} %iota_compare_fusion.2) | copy-start | bytes 49156
  52.1 5.0 %collective-permute-start.5 = (f32[1,128,256]{2,1,0:T(8,128)S(1)}, f32[1,128,256]{2,1,0:T(8,128)S(1)}, u32[]{:S(2)}, u32[]{:S(2)}) collective-permute-start(f32[1,128,256]{2,1,0:T(8,128)S(1)} %slice_select_fusion.4), channel_id=1, source_target_pairs={{0,8},{2,10},{4,12},{6,14},{8,0},{10,2},{12,4},{14,6},{16,24},{18,... | collective-permute-start | bytes 393224 | tf_op jit(solution)/shard_map/ppermute | solution.py:195
  57.4 6.7 %collective-permute-start.6 = (f32[1,128,128]{2,1,0:T(8,128)S(1)}, f32[1,128,128]{2,1,0:T(8,128)S(1)}, u32[]{:S(2)}, u32[]{:S(2)}) collective-permute-start(f32[1,128,128]{2,1,0:T(8,128)S(1)} %slice_add_fusion.7), channel_id=1, source_target_pairs={{0,16},{2,18},{4,20},{6,22},{8,24},{10,26},{12,28},{14,30},{1,17},... | collective-permute-start | bytes 196616 | tf_op jit(solution)/shard_map/ppermute | solution.py:173
  64.3 6.1 %copy-start.1 = (f32[8,2,128,128]{3,2,1,0:T(8,128)S(1)}, f32[8,2,128,128]{3,2,1,0:T(8,128)}, u32[]{:S(2)}) copy-start(f32[8,2,128,128]{3,2,1,0:T(8,128)} %copy-done) | copy-start | bytes 3145732
  64.3 4.3 %collective-permute-start.7 = (f32[1,128,128]{2,1,0:T(8,128)S(1)}, f32[1,128,128]{2,1,0:T(8,128)S(1)}, u32[]{:S(2)}, u32[]{:S(2)}) collective-permute-start(f32[1,128,128]{2,1,0:T(8,128)S(1)} %get-tuple-element.55), channel_id=1, source_target_pairs={{0,8},{2,10},{4,12},{6,14},{8,0},{10,2},{12,4},{14,6},{16,24},{18,... | collective-permute-start | bytes 196616 | tf_op jit(solution)/shard_map/ppermute | solution.py:208
  68.6 5.3 %copy-start.5 = (f32[4,128,256]{2,1,0:T(8,128)S(1)}, f32[4,128,256]{2,1,0:T(8,128)}, u32[]{:S(2)}) copy-start(f32[4,128,256]{2,1,0:T(8,128)} %copy-done.4) | copy-start | bytes 1572868
  68.9 5.0 %collective-permute-start.8 = (f32[2,128,128]{2,1,0:T(8,128)S(1)}, f32[2,128,128]{2,1,0:T(8,128)S(1)}, u32[]{:S(2)}, u32[]{:S(2)}) collective-permute-start(f32[2,128,128]{2,1,0:T(8,128)S(1)} %get-tuple-element.45), channel_id=1, source_target_pairs={{0,4},{2,6},{4,0},{6,2},{8,12},{10,14},{12,8},{14,10},{16,20},{18,... | collective-permute-start | bytes 393224 | tf_op jit(solution)/shard_map/ppermute | solution.py:208
  74.2 1.6 %collective-permute-start.9 = (f32[4,128,128]{2,1,0:T(8,128)S(1)}, f32[4,128,128]{2,1,0:T(8,128)S(1)}, u32[]{:S(2)}, u32[]{:S(2)}) collective-permute-start(f32[4,128,128]{2,1,0:T(8,128)S(1)} %get-tuple-element.25), channel_id=1, source_target_pairs={{0,2},{2,0},{4,6},{6,4},{8,10},{10,8},{12,14},{14,12},{16,18},{18,... | collective-permute-start | bytes 786440 | tf_op jit(solution)/shard_map/ppermute | solution.py:208
  75.8 2.5 %copy-start.12 = (bf16[128,2048]{1,0:T(8,128)(2,1)S(1)}, bf16[128,2048]{1,0:T(8,128)(2,1)}, u32[]{:S(2)}) copy-start(bf16[128,2048]{1,0:T(8,128)(2,1)} %param.10) | copy-start | bytes 1572868
  76.4 2.1 %copy-start.21 = (bf16[128]{0:T(256)(128)(2,1)S(1)}, bf16[128]{0:T(256)(128)(2,1)}, u32[]{:S(2)}) copy-start(bf16[128]{0:T(256)(128)(2,1)} %param.13) | copy-start | bytes 772
  76.7 8.4 %collective-permute-start.10 = (bf16[128,1024]{0,1:T(8,128)(2,1)S(1)}, bf16[128,1024]{0,1:T(8,128)(2,1)S(1)}, u32[]{:S(2)}, u32[]{:S(2)}) collective-permute-start(bf16[128,1024]{0,1:T(8,128)(2,1)S(1)} %bitcast.159), channel_id=1, source_target_pairs={{0,1},{1,0},{2,3},{3,2},{4,5},{5,4},{6,7},{7,6},{8,9},{9,8},{10,11... | collective-permute-start | bytes 786440 | tf_op jit(solution)/shard_map/ppermute | solution.py:242
  (1 other events, 0.6 us)

commit v16 on v15

--- a/solution.py
+++ b/solution.py
@@ -41,7 +41,9 @@
     key_heads = key_part.shape[1] // DK
     value_heads = value_part.shape[1] // DV
     key_unit = unit_rows(by_head(key_part, DK).astype(jnp.float32))
-    value_f = by_head(value_part, DV).astype(jnp.float32)
+    value_f = (
+        value_part.astype(jnp.float32).reshape(blocks, SPAN, value_heads, DV).transpose(2, 0, 1, 3)
+    )
     beta_gate = (
         jax.nn.sigmoid(beta_part.astype(jnp.float32))
         .reshape(blocks, SPAN, value_heads)

time: 88 us -> 83.1 us (0.944)
  waiting for transfers between devices: 30.2 us -> 24.9 us
    ppermute x3, waiting for transfers between devices: 7.97 us -> 2.82 us  [head_swap(): got = lax.ppermute(sent, 'head', [(0, 1), (1, 0)])]
    unnamed x53 -> x43, local copies, waits for them, and re-layouts: 2.05 us -> 2.1 us
  transfers between devices with their start and end apart: 11 -> 11, of which waited for: 9 -> 10; matrix products, arithmetic and copies ran while one was open for 13% -> 15% of each run, Pallas kernels for 0% -> 0%
where the time goes in v16:
time: 83.1 us; the launch traced here: 82.8 us
  waiting for transfers between devices  24.9 us (30%)
  starting transfers between devices  19.2 us (23%)
  matrix products  16.6 us (20%)
  other arithmetic  15.2 us (18%)
  local copies, waits for them, and re-layouts  6.14 us (7%)
    ppermute x6, waiting for transfers between devices, chain_states(): got = lax.ppermute(other, 'ctx', [(i, i ^ stride) for i in range(size)])  15.2 us
    ppermute x6, starting transfers between devices, chain_states(): got = lax.ppermute(other, 'ctx', [(i, i ^ stride) for i in range(size)])  7.47 us
    ppermute x1, waiting for transfers between devices, head_return(): got = lax.ppermute(sent, 'head', [(0, 1), (1, 0)])  6.52 us
    ppermute x3, starting transfers between devices, head_swap(): got = lax.ppermute(sent, 'head', [(0, 1), (1, 0)])  5.18 us
    dot_general x5, matrix products, unit_lower_inverse(): jnp.matmul(jnp.concatenate([inverse, power], axis=-2), power, precision=L...  4.97 us
    ppermute x1, starting transfers between devices, exclusive_scan(): return lax.ppermute(write, 'ctx', near)  4.96 us
    select_n x3, other arithmetic, head_swap(): own = jnp.where(first, rows[..., :width], rows[..., width:])  3.15 us
    dot_general x4, matrix products, compose_joined(): jnp.matmul(later[..., :later.shape[-2]], earlier, precision=FULL_PRECISION)  2.87 us
  transfers between devices with their start and end apart: 11, of which 10 were waited for; matrix products, arithmetic and copies ran while one was open for 15% of the time, Pallas kernels for 0%

profile of v16, /device:TPU:0, one launch (start us, length us, event | category | flops | bytes accessed | tf_op | source)
XLA Modules:
  0.0 82.8 jit_solution(4852378879795992775)
XLA Ops:
  0.0 1.3 %broadcast_select_fusion.5 = (bf16[2,128,512]{2,1,0:T(8,128)(2,1)S(1)}, bf16[2,128,512]{2,1,0:T(8,128)(2,1)S(1)}) fusion(pred[]{:T(512)S(6)} %eq.29, bf16[1,128,1024]{2,1,0:T(8,128)(2,1)} %bitcast.152, bf16[1,128,1024]{2,1,0:T(8,128)(2,1)} %bitcast.153), kind=kLoop, calls=%fused_computation.126 | loop fusion | flops 1835008 | bytes 1048577 | tf_op jit(solution)/shard_map/jit(_where)/select_n | solution.py:230
  1.3 3.0 %collective-permute-start = (bf16[2,128,512]{2,1,0:T(8,128)(2,1)S(1)}, bf16[2,128,512]{2,1,0:T(8,128)(2,1)S(1)}, u32[]{:S(2)}, u32[]{:S(2)}) collective-permute-start(bf16[2,128,512]{2,1,0:T(8,128)(2,1)S(1)} %get-tuple-element.34), channel_id=1, source_target_pairs={{0,1},{1,0},{2,3},{3,2},{4,5},{5,4},{6,7},{7,6},{8,9},{9,8},{10,11... | collective-permute-start | bytes 786440 | tf_op jit(solution)/shard_map/ppermute | solution.py:232
  5.2 1.1 %broadcast_select_fusion.3 = (bf16[128,1024]{1,0:T(8,128)(2,1)S(1)}, bf16[128,1024]{1,0:T(8,128)(2,1)S(1)}) fusion(pred[]{:T(512)S(6)} %eq.29, bf16[128,2048]{1,0:T(8,128)(2,1)} %param.9), kind=kLoop, calls=%fused_computation.124 | loop fusion | flops 262144 | bytes 1048577 | tf_op jit(solution)/shard_map/jit(_where)/select_n | solution.py:230
  6.3 2.1 %collective-permute-start.2 = (bf16[128,1024]{1,0:T(8,128)(2,1)S(1)}, bf16[128,1024]{1,0:T(8,128)(2,1)S(1)}, u32[]{:S(2)}, u32[]{:S(2)}) collective-permute-start(bf16[128,1024]{1,0:T(8,128)(2,1)S(1)} %get-tuple-element.32), channel_id=1, source_target_pairs={{0,1},{1,0},{2,3},{3,2},{4,5},{5,4},{6,7},{7,6},{8,9},{9,8},{10,11... | collective-permute-start | bytes 786440 | tf_op jit(solution)/shard_map/ppermute | solution.py:232
  8.9 2.7 %collective-permute-done.1 = bf16[2,128,8]{1,2,0:T(8,128)(2,1)S(1)} collective-permute-done((bf16[2,128,8]{1,2,0:T(8,128)(2,1)S(1)}, bf16[2,128,8]{1,2,0:T(8,128)(2,1)S(1)}, u32[]{:S(2)}, u32[]{:S(2)}) %collective-permute-start.1) | collective-permute-done | bytes 4128 | tf_op jit(solution)/shard_map/ppermute | solution.py:232
  16.7 1.0 %fusion = f32[8,2,256,128]{3,2,1,0:T(8,128)S(1)} fusion(f32[8,2,128,128]{3,2,1,0:T(8,128)S(1)} %fusion.93, f32[8,2,128,128]{3,2,1,0:T(8,128)S(1)} %get-tuple-element.21), kind=kOutput, calls=%fused_computation | convolution fusion | flops 403177472 | bytes 4194304 | tf_op jit(solution)/shard_map/dot_general | solution.py:69
  18.7 1.0 %fusion.4 = f32[8,2,256,128]{3,2,1,0:T(8,128)S(1)} fusion(f32[8,2,128,128]{3,2,1,0:T(8,128)S(1)} %get-tuple-element.14, f32[8,2,128,128]{3,2,1,0:T(8,128)S(1)} %get-tuple-element.13), kind=kOutput, calls=%fused_computation.4 | convolution fusion | flops 403177472 | bytes 4194304 | tf_op jit(solution)/shard_map/dot_general | solution.py:69
  19.9 1.0 %fusion.8 = f32[8,2,256,128]{3,2,1,0:T(8,128)S(1)} fusion(f32[8,2,128,128]{3,2,1,0:T(8,128)S(1)} %get-tuple-element.12, f32[8,2,128,128]{3,2,1,0:T(8,128)S(1)} %get-tuple-element.11), kind=kOutput, calls=%fused_computation.8 | convolution fusion | flops 403177472 | bytes 4194304 | tf_op jit(solution)/shard_map/dot_general | solution.py:69
  21.1 1.0 %fusion.12 = f32[8,2,256,128]{3,2,1,0:T(8,128)S(1)} fusion(f32[8,2,128,128]{3,2,1,0:T(8,128)S(1)} %get-tuple-element.10, f32[8,2,128,128]{3,2,1,0:T(8,128)S(1)} %get-tuple-element.9), kind=kOutput, calls=%fused_computation.12 | convolution fusion | flops 403177472 | bytes 4194304 | tf_op jit(solution)/shard_map/dot_general | solution.py:69
  22.3 1.0 %fusion.16 = f32[8,2,256,128]{3,2,1,0:T(8,128)S(1)} fusion(f32[8,2,128,128]{3,2,1,0:T(8,128)S(1)} %get-tuple-element.8, f32[8,2,128,128]{3,2,1,0:T(8,128)S(1)} %get-tuple-element.7), kind=kOutput, calls=%fused_computation.16 | convolution fusion | flops 403177472 | bytes 4194304 | tf_op jit(solution)/shard_map/dot_general | solution.py:69
  24.6 1.2 %fusion.20 = f32[8,2,128,256]{3,2,1,0:T(8,128)S(1)} fusion(f32[8,2,128,128]{3,2,1,0:T(8,128)S(1)} %convolution_add_fusion, f32[8,2,128,128]{3,2,1,0:T(8,128)S(1)} %get-tuple-element.28, f32[8,2,128,128]{3,2,1,0:T(8,128)S(1)} %get-tuple-element.52), kind=kOutput, calls=%fused_computation.20 | convolution fusion | flops 403177472 | bytes 5242880 | tf_op jit(solution)/shard_map/dot_general | solution.py:97
  25.8 1.1 %fusion.94 = f32[8,2,128,256]{3,2,1,0:T(8,128)S(1)} fusion(f32[8,2,128,128]{3,2,1,0:T(8,128)S(1)} %get-tuple-element.27, f32[8,2,128,256]{3,2,1,0:T(8,128)S(1)} %fusion.20), kind=kOutput, calls=%fused_computation.192 | convolution fusion | flops 402653184 | bytes 5242880 | tf_op jit(solution)/shard_map/hmck,hmcj->hmkj/dot_general | solution.py:102
  29.7 2.2 %collective-permute-done.3 = f32[4,128,256]{2,1,0:T(8,128)} collective-permute-done((f32[4,128,256]{2,1,0:T(8,128)}, f32[4,128,256]{2,1,0:T(8,128)}, u32[]{:S(2)}, u32[]{:S(2)}) %collective-permute-start.3) | collective-permute-done | bytes 524320 | tf_op jit(solution)/shard_map/ppermute | solution.py:197
  32.0 1.5 %broadcast_select_fusion.1 = (f32[4,128,256]{2,1,0:T(8,128)S(1)}, f32[4,128,256]{2,1,0:T(8,128)S(1)}) fusion(f32[4,128,256]{2,1,0:T(8,128)} %collective-permute-done.3, pred[]{:T(512)S(6)} %eq.31, f32[8,128,256]{2,1,0:T(8,128)} %copy-done.2), kind=kLoop, calls=%fused_computation.121 | loop fusion | flops 393216 | bytes 2621441 | tf_op jit(solution)/shard_map/jit(_where)/select_n | solution.py:199
  33.5 1.1 %convolution_add_fusion.3 = f32[4,128,256]{2,1,0:T(8,128)S(1)} fusion(f32[4,128,256]{2,1,0:T(8,128)S(1)} %get-tuple-element.16, f32[4,128,256]{2,1,0:T(8,128)S(1)} %get-tuple-element.15, pred[256]{0:T(512)(128)(4,1)} %iota_compare_fusion.3), kind=kOutput, calls=%fused_computation.39 | convolution fusion | flops 100925440 | bytes 1835264 | tf_op jit(solution)/shard_map/dot_general | solution.py:28
  36.1 1.9 %collective-permute-start.4 = (f32[2,128,256]{2,1,0:T(8,128)}, f32[2,128,256]{2,1,0:T(8,128)}, u32[]{:S(2)}, u32[]{:S(2)}) collective-permute-start(f32[2,128,256]{2,1,0:T(8,128)} %slice_select_fusion.2), channel_id=1, source_target_pairs={{0,4},{2,6},{4,0},{6,2},{8,12},{10,14},{12,8},{14,10},{16,20},{18,... | collective-permute-start | bytes 786440 | tf_op jit(solution)/shard_map/ppermute | solution.py:197
  38.7 1.2 %slice.307 = pred[128]{0:T(512)(128)(4,1)} slice(pred[256]{0:T(512)(128)(4,1)} %iota_compare_fusion.3), slice={[128:256]} | slice | bytes 256 | tf_op jit(solution)/shard_map/slice | solution.py:156
  40.1 4.9 %collective-permute-done.4 = f32[2,128,256]{2,1,0:T(8,128)} collective-permute-done((f32[2,128,256]{2,1,0:T(8,128)}, f32[2,128,256]{2,1,0:T(8,128)}, u32[]{:S(2)}, u32[]{:S(2)}) %collective-permute-start.4) | collective-permute-done | bytes 262176 | tf_op jit(solution)/shard_map/ppermute | solution.py:197
  45.0 1.2 %broadcast_select_fusion.8 = (f32[2,128,256]{2,1,0:T(8,128)S(1)}, f32[2,128,256]{2,1,0:T(8,128)S(1)}) fusion(f32[2,128,256]{2,1,0:T(8,128)} %collective-permute-done.4, pred[]{:T(512)S(6)} %eq.32, f32[4,128,256]{2,1,0:T(8,128)} %copy-done.3), kind=kLoop, calls=%fused_computation.137 | loop fusion | flops 196608 | bytes 1310721 | tf_op jit(solution)/shard_map/jit(_where)/select_n | solution.py:199
  47.1 1.9 %collective-permute-start.5 = (f32[1,128,256]{2,1,0:T(8,128)S(1)}, f32[1,128,256]{2,1,0:T(8,128)S(1)}, u32[]{:S(2)}, u32[]{:S(2)}) collective-permute-start(f32[1,128,256]{2,1,0:T(8,128)S(1)} %slice_select_fusion.4), channel_id=1, source_target_pairs={{0,8},{2,10},{4,12},{6,14},{8,0},{10,2},{12,4},{14,6},{16,24},{18,... | collective-permute-start | bytes 393224 | tf_op jit(solution)/shard_map/ppermute | solution.py:197
  49.0 1.0 %fusion.67 = f32[4,2,128,128]{3,2,1,0:T(8,128)S(1)} fusion(f32[4,2,128]{2,1,0:T(2,128)S(1)} %copy-done.16, f32[4,2,128]{2,1,0:T(2,128)S(1)} %add_rsqrt_fusion.2, bf16[1,2,128,128]{3,2,1,0:T(8,128)(2,1)S(1)} %bitcast.126, bf16[1,2,128,128]{3,2,1,0:T(8,128)(2,1)S(1)} %bitcast.129, bf16[1,2,128,128]{3,2,1,0:T(8,128)(2,1)S(1)} %bitcast.132, ...), kind=kOutput, calls=%fused_computation.131 | convolution fusion | flops 102105088 | bytes 1056768 | tf_op jit(solution)/shard_map/hmik,hmjk->hmij/dot_general | solution.py:115
  49.9 2.2 %collective-permute-done.5 = f32[1,128,256]{2,1,0:T(8,128)S(1)} collective-permute-done((f32[1,128,256]{2,1,0:T(8,128)S(1)}, f32[1,128,256]{2,1,0:T(8,128)S(1)}, u32[]{:S(2)}, u32[]{:S(2)}) %collective-permute-start.5) | collective-permute-done | bytes 131104 | tf_op jit(solution)/shard_map/ppermute | solution.py:197
  52.4 5.0 %collective-permute-start.6 = (f32[1,128,128]{2,1,0:T(8,128)S(1)}, f32[1,128,128]{2,1,0:T(8,128)S(1)}, u32[]{:S(2)}, u32[]{:S(2)}) collective-permute-start(f32[1,128,128]{2,1,0:T(8,128)S(1)} %slice_add_fusion.7), channel_id=1, source_target_pairs={{0,16},{2,18},{4,20},{6,22},{8,24},{10,26},{12,28},{14,30},{1,17},... | collective-permute-start | bytes 196616 | tf_op jit(solution)/shard_map/ppermute | solution.py:175
  57.5 1.2 %fusion.34 = f32[8,2,128,256]{3,2,1,0:T(8,128)S(1)} fusion(f32[8,2,128,256]{3,2,1,0:T(8,128)S(1)} %fusion.20, f32[8,2,128,128]{3,2,1,0:T(8,128)S(1)} %bitcast.120, f32[8,2,128]{2,1,0:T(2,128)S(1)} %copy.19, pred[128,128]{1,0:T(8,128)(4,1)S(1)} %copy-done.13), kind=kOutput, calls=%fused_computation.53 | convolution fusion | flops 403439616 | bytes 5267456 | tf_op jit(solution)/shard_map/hmij,hmjv->hmiv/dot_general | solution.py:122
  59.3 2.0 %collective-permute-start.7 = (f32[1,128,128]{2,1,0:T(8,128)S(1)}, f32[1,128,128]{2,1,0:T(8,128)S(1)}, u32[]{:S(2)}, u32[]{:S(2)}) collective-permute-start(f32[1,128,128]{2,1,0:T(8,128)S(1)} %get-tuple-element.47), channel_id=1, source_target_pairs={{0,8},{2,10},{4,12},{6,14},{8,0},{10,2},{12,4},{14,6},{16,24},{18,... | collective-permute-start | bytes 196616 | tf_op jit(solution)/shard_map/ppermute | solution.py:210
  61.9 1.7 %collective-permute-done.7 = f32[1,128,128]{2,1,0:T(8,128)S(1)} collective-permute-done((f32[1,128,128]{2,1,0:T(8,128)S(1)}, f32[1,128,128]{2,1,0:T(8,128)S(1)}, u32[]{:S(2)}, u32[]{:S(2)}) %collective-permute-start.7) | collective-permute-done | bytes 65568 | tf_op jit(solution)/shard_map/ppermute | solution.py:210
  63.8 1.5 %collective-permute-start.8 = (f32[2,128,128]{2,1,0:T(8,128)S(1)}, f32[2,128,128]{2,1,0:T(8,128)S(1)}, u32[]{:S(2)}, u32[]{:S(2)}) collective-permute-start(f32[2,128,128]{2,1,0:T(8,128)S(1)} %get-tuple-element.37), channel_id=1, source_target_pairs={{0,4},{2,6},{4,0},{6,2},{8,12},{10,14},{12,8},{14,10},{16,20},{18,... | collective-permute-start | bytes 393224 | tf_op jit(solution)/shard_map/ppermute | solution.py:210
  66.0 2.8 %collective-permute-done.8 = f32[2,128,128]{2,1,0:T(8,128)S(1)} collective-permute-done((f32[2,128,128]{2,1,0:T(8,128)S(1)}, f32[2,128,128]{2,1,0:T(8,128)S(1)}, u32[]{:S(2)}, u32[]{:S(2)}) %collective-permute-start.8) | collective-permute-done | bytes 131104 | tf_op jit(solution)/shard_map/ppermute | solution.py:210
  69.5 1.3 %collective-permute-done.9 = f32[4,128,128]{2,1,0:T(8,128)S(1)} collective-permute-done((f32[4,128,128]{2,1,0:T(8,128)S(1)}, f32[4,128,128]{2,1,0:T(8,128)S(1)}, u32[]{:S(2)}, u32[]{:S(2)}) %collective-permute-start.9) | collective-permute-done | bytes 262176 | tf_op jit(solution)/shard_map/ppermute | solution.py:210
  71.7 1.6 %collective-permute-start.10 = (bf16[128,1024]{0,1:T(8,128)(2,1)S(1)}, bf16[128,1024]{0,1:T(8,128)(2,1)S(1)}, u32[]{:S(2)}, u32[]{:S(2)}) collective-permute-start(bf16[128,1024]{0,1:T(8,128)(2,1)S(1)} %bitcast.150), channel_id=1, source_target_pairs={{0,1},{1,0},{2,3},{3,2},{4,5},{5,4},{6,7},{7,6},{8,9},{9,8},{10,11... | collective-permute-start | bytes 786440 | tf_op jit(solution)/shard_map/ppermute | solution.py:244
  73.6 6.5 %collective-permute-done.10 = bf16[128,1024]{0,1:T(8,128)(2,1)S(1)} collective-permute-done((bf16[128,1024]{0,1:T(8,128)(2,1)S(1)}, bf16[128,1024]{0,1:T(8,128)(2,1)S(1)}, u32[]{:S(2)}, u32[]{:S(2)}) %collective-permute-start.10) | collective-permute-done | bytes 262176 | tf_op jit(solution)/shard_map/ppermute | solution.py:244
  81.7 1.0 %copy.36 = bf16[128,2048]{1,0:T(8,128)(2,1)} copy(bf16[128,2048]{0,1:T(8,128)(2,1)S(1)} %fusion.44) | data formatting | bytes 1048576 | tf_op jit(solution)/shard_map/convert_element_type | solution.py:224
  (114 shorter events, 20.8 us)
Async XLA Ops:
  1.3 11.8 %collective-permute-start = (bf16[2,128,512]{2,1,0:T(8,128)(2,1)S(1)}, bf16[2,128,512]{2,1,0:T(8,128)(2,1)S(1)}, u32[]{:S(2)}, u32[]{:S(2)}) collective-permute-start(bf16[2,128,512]{2,1,0:T(8,128)(2,1)S(1)} %get-tuple-element.34), channel_id=1, source_target_pairs={{0,1},{1,0},{2,3},{3,2},{4,5},{5,4},{6,7},{7,6},{8,9},{9,8},{10,11... | collective-permute-start | bytes 786440 | tf_op jit(solution)/shard_map/ppermute | solution.py:232
  5.1 6.5 %collective-permute-start.1 = (bf16[2,128,8]{1,2,0:T(8,128)(2,1)S(1)}, bf16[2,128,8]{1,2,0:T(8,128)(2,1)S(1)}, u32[]{:S(2)}, u32[]{:S(2)}) collective-permute-start(bf16[2,128,8]{1,2,0:T(8,128)(2,1)S(1)} %get-tuple-element.54), channel_id=1, source_target_pairs={{0,1},{1,0},{2,3},{3,2},{4,5},{5,4},{6,7},{7,6},{8,9},{9,8},{10,11... | collective-permute-start | bytes 12296 | tf_op jit(solution)/shard_map/ppermute | solution.py:232
  6.3 10.1 %collective-permute-start.2 = (bf16[128,1024]{1,0:T(8,128)(2,1)S(1)}, bf16[128,1024]{1,0:T(8,128)(2,1)S(1)}, u32[]{:S(2)}, u32[]{:S(2)}) collective-permute-start(bf16[128,1024]{1,0:T(8,128)(2,1)S(1)} %get-tuple-element.32), channel_id=1, source_target_pairs={{0,1},{1,0},{2,3},{3,2},{4,5},{5,4},{6,7},{7,6},{8,9},{9,8},{10,11... | collective-permute-start | bytes 786440 | tf_op jit(solution)/shard_map/ppermute | solution.py:232
  13.5 2.5 %copy-start.6 = (bf16[256,128]{1,0:T(8,128)(2,1)}, bf16[256,128]{1,0:T(8,128)(2,1)S(1)}, u32[]{:S(2)}) copy-start(bf16[256,128]{1,0:T(8,128)(2,1)S(1)} %get-tuple-element.56) | copy-start | bytes 196612
  13.5 2.5 %copy-start.8 = (bf16[256,128]{1,0:T(8,128)(2,1)}, bf16[256,128]{1,0:T(8,128)(2,1)S(1)}, u32[]{:S(2)}) copy-start(bf16[256,128]{1,0:T(8,128)(2,1)S(1)} %get-tuple-element.57) | copy-start | bytes 196612
  13.5 2.5 %copy-start.10 = (bf16[256,128]{1,0:T(8,128)(2,1)}, bf16[256,128]{1,0:T(8,128)(2,1)S(1)}, u32[]{:S(2)}) copy-start(bf16[256,128]{1,0:T(8,128)(2,1)S(1)} %get-tuple-element.58) | copy-start | bytes 196612
  13.8 2.2 %copy-start.15 = (f32[4,2,128]{2,1,0:T(2,128)}, f32[4,2,128]{2,1,0:T(2,128)S(1)}, u32[]{:S(2)}) copy-start(f32[4,2,128]{2,1,0:T(2,128)S(1)} %add_rsqrt_fusion.1) | copy-start | bytes 12292
  25.8 1.2 %copy-start.14 = (f32[8,2]{1,0:T(8,128)S(1)}, f32[8,2]{1,0:T(8,128)}, u32[]{:S(2)}) copy-start(f32[8,2]{1,0:T(8,128)} %copy.26) | copy-start | bytes 196
  27.2 1.3 %copy-start = (f32[8,2,128,128]{3,2,1,0:T(8,128)}, f32[8,2,128,128]{3,2,1,0:T(8,128)S(1)}, u32[]{:S(2)}) copy-start(f32[8,2,128,128]{3,2,1,0:T(8,128)S(1)} %get-tuple-element.6) | copy-start | bytes 3145732
  27.3 0.6 copy-start.17
  28.6 1.2 %copy-start.2 = (f32[8,128,256]{2,1,0:T(8,128)}, f32[8,128,256]{2,1,0:T(8,128)S(1)}, u32[]{:S(2)}) copy-start(f32[8,128,256]{2,1,0:T(8,128)S(1)} %convolution_add_fusion.2) | copy-start | bytes 3145732
  29.7 2.3 %collective-permute-start.3 = (f32[4,128,256]{2,1,0:T(8,128)}, f32[4,128,256]{2,1,0:T(8,128)}, u32[]{:S(2)}, u32[]{:S(2)}) collective-permute-start(f32[4,128,256]{2,1,0:T(8,128)} %slice_select_fusion), channel_id=1, source_target_pairs={{0,2},{2,0},{4,6},{6,4},{8,10},{10,8},{12,14},{14,12},{16,18},{18,... | collective-permute-start | bytes 1572872 | tf_op jit(solution)/shard_map/ppermute | solution.py:197
  33.5 2.7 %copy-start.4 = (f32[4,128,256]{2,1,0:T(8,128)}, f32[4,128,256]{2,1,0:T(8,128)S(1)}, u32[]{:S(2)}) copy-start(f32[4,128,256]{2,1,0:T(8,128)S(1)} %get-tuple-element.16) | copy-start | bytes 1572868
  33.5 15.5 %copy-start.7 = (bf16[256,128]{1,0:T(8,128)(2,1)S(1)}, bf16[256,128]{1,0:T(8,128)(2,1)}, u32[]{:S(2)}) copy-start(bf16[256,128]{1,0:T(8,128)(2,1)} %copy-done.6) | copy-start | bytes 196612
  34.6 0.8 copy-start.3
  36.1 8.8 %collective-permute-start.4 = (f32[2,128,256]{2,1,0:T(8,128)}, f32[2,128,256]{2,1,0:T(8,128)}, u32[]{:S(2)}, u32[]{:S(2)}) collective-permute-start(f32[2,128,256]{2,1,0:T(8,128)} %slice_select_fusion.2), channel_id=1, source_target_pairs={{0,4},{2,6},{4,0},{6,2},{8,12},{10,14},{12,8},{14,10},{16,20},{18,... | collective-permute-start | bytes 786440 | tf_op jit(solution)/shard_map/ppermute | solution.py:197
  39.8 9.1 %copy-start.9 = (bf16[256,128]{1,0:T(8,128)(2,1)S(1)}, bf16[256,128]{1,0:T(8,128)(2,1)}, u32[]{:S(2)}) copy-start(bf16[256,128]{1,0:T(8,128)(2,1)} %copy-done.8) | copy-start | bytes 196612
  39.9 9.1 %copy-start.11 = (bf16[256,128]{1,0:T(8,128)(2,1)S(1)}, bf16[256,128]{1,0:T(8,128)(2,1)}, u32[]{:S(2)}) copy-start(bf16[256,128]{1,0:T(8,128)(2,1)} %copy-done.10) | copy-start | bytes 196612
  39.9 9.1 %copy-start.16 = (f32[4,2,128]{2,1,0:T(2,128)S(1)}, f32[4,2,128]{2,1,0:T(2,128)}, u32[]{:S(2)}) copy-start(f32[4,2,128]{2,1,0:T(2,128)} %copy-done.15) | copy-start | bytes 12292
  46.1 6.2 %copy-start.18 = (pred[128]{0:T(512)(128)(4,1)S(1)}, pred[128]{0:T(512)(128)(4,1)}, u32[]{:S(2)}) copy-start(pred[128]{0:T(512)(128)(4,1)} %slice.307) | copy-start | bytes 388
  47.1 10.4 %copy-start.13 = (pred[128,128]{1,0:T(8,128)(4,1)S(1)}, pred[128,128]{1,0:T(8,128)(4,1)}, u32[]{:S(2)}) copy-start(pred[128,128]{1,0:T(8,128)(4,1)} %iota_compare_fusion.2) | copy-start | bytes 49156
  47.1 5.0 %collective-permute-start.5 = (f32[1,128,256]{2,1,0:T(8,128)S(1)}, f32[1,128,256]{2,1,0:T(8,128)S(1)}, u32[]{:S(2)}, u32[]{:S(2)}) collective-permute-start(f32[1,128,256]{2,1,0:T(8,128)S(1)} %slice_select_fusion.4), channel_id=1, source_target_pairs={{0,8},{2,10},{4,12},{6,14},{8,0},{10,2},{12,4},{14,6},{16,24},{18,... | collective-permute-start | bytes 393224 | tf_op jit(solution)/shard_map/ppermute | solution.py:197
  52.4 6.7 %collective-permute-start.6 = (f32[1,128,128]{2,1,0:T(8,128)S(1)}, f32[1,128,128]{2,1,0:T(8,128)S(1)}, u32[]{:S(2)}, u32[]{:S(2)}) collective-permute-start(f32[1,128,128]{2,1,0:T(8,128)S(1)} %slice_add_fusion.7), channel_id=1, source_target_pairs={{0,16},{2,18},{4,20},{6,22},{8,24},{10,26},{12,28},{14,30},{1,17},... | collective-permute-start | bytes 196616 | tf_op jit(solution)/shard_map/ppermute | solution.py:175
  59.3 6.1 %copy-start.1 = (f32[8,2,128,128]{3,2,1,0:T(8,128)S(1)}, f32[8,2,128,128]{3,2,1,0:T(8,128)}, u32[]{:S(2)}) copy-start(f32[8,2,128,128]{3,2,1,0:T(8,128)} %copy-done) | copy-start | bytes 3145732
  59.3 4.3 %collective-permute-start.7 = (f32[1,128,128]{2,1,0:T(8,128)S(1)}, f32[1,128,128]{2,1,0:T(8,128)S(1)}, u32[]{:S(2)}, u32[]{:S(2)}) collective-permute-start(f32[1,128,128]{2,1,0:T(8,128)S(1)} %get-tuple-element.47), channel_id=1, source_target_pairs={{0,8},{2,10},{4,12},{6,14},{8,0},{10,2},{12,4},{14,6},{16,24},{18,... | collective-permute-start | bytes 196616 | tf_op jit(solution)/shard_map/ppermute | solution.py:210
  63.6 5.3 %copy-start.5 = (f32[4,128,256]{2,1,0:T(8,128)S(1)}, f32[4,128,256]{2,1,0:T(8,128)}, u32[]{:S(2)}) copy-start(f32[4,128,256]{2,1,0:T(8,128)} %copy-done.4) | copy-start | bytes 1572868
  63.8 5.0 %collective-permute-start.8 = (f32[2,128,128]{2,1,0:T(8,128)S(1)}, f32[2,128,128]{2,1,0:T(8,128)S(1)}, u32[]{:S(2)}, u32[]{:S(2)}) collective-permute-start(f32[2,128,128]{2,1,0:T(8,128)S(1)} %get-tuple-element.37), channel_id=1, source_target_pairs={{0,4},{2,6},{4,0},{6,2},{8,12},{10,14},{12,8},{14,10},{16,20},{18,... | collective-permute-start | bytes 393224 | tf_op jit(solution)/shard_map/ppermute | solution.py:210
  69.2 1.6 %collective-permute-start.9 = (f32[4,128,128]{2,1,0:T(8,128)S(1)}, f32[4,128,128]{2,1,0:T(8,128)S(1)}, u32[]{:S(2)}, u32[]{:S(2)}) collective-permute-start(f32[4,128,128]{2,1,0:T(8,128)S(1)} %get-tuple-element.25), channel_id=1, source_target_pairs={{0,2},{2,0},{4,6},{6,4},{8,10},{10,8},{12,14},{14,12},{16,18},{18,... | collective-permute-start | bytes 786440 | tf_op jit(solution)/shard_map/ppermute | solution.py:210
  70.8 2.5 %copy-start.12 = (bf16[128,2048]{1,0:T(8,128)(2,1)S(1)}, bf16[128,2048]{1,0:T(8,128)(2,1)}, u32[]{:S(2)}) copy-start(bf16[128,2048]{1,0:T(8,128)(2,1)} %param.10) | copy-start | bytes 1572868
  71.4 2.1 %copy-start.19 = (bf16[128]{0:T(256)(128)(2,1)S(1)}, bf16[128]{0:T(256)(128)(2,1)}, u32[]{:S(2)}) copy-start(bf16[128]{0:T(256)(128)(2,1)} %param.13) | copy-start | bytes 772
  71.7 8.4 %collective-permute-start.10 = (bf16[128,1024]{0,1:T(8,128)(2,1)S(1)}, bf16[128,1024]{0,1:T(8,128)(2,1)S(1)}, u32[]{:S(2)}, u32[]{:S(2)}) collective-permute-start(bf16[128,1024]{0,1:T(8,128)(2,1)S(1)} %bitcast.150), channel_id=1, source_target_pairs={{0,1},{1,0},{2,3},{3,2},{4,5},{5,4},{6,7},{7,6},{8,9},{9,8},{10,11... | collective-permute-start | bytes 786440 | tf_op jit(solution)/shard_map/ppermute | solution.py:244

commit v17 on v14

--- a/solution.py
+++ b/solution.py
@@ -241,8 +241,9 @@
 def head_return(rows):
     tokens = rows.shape[0] // 2
     first = lax.axis_index("head") == 0
-    own = jnp.where(first, rows[:tokens], rows[tokens:])
-    sent = jnp.where(first, rows[tokens:], rows[:tokens])
+    half = lax.axis_index("head")
+    own = lax.dynamic_slice_in_dim(rows, half * tokens, tokens, 0)
+    sent = lax.dynamic_slice_in_dim(rows, (1 - half) * tokens, tokens, 0)
     got = lax.ppermute(sent, "head", [(0, 1), (1, 0)])
     return jnp.where(first, jnp.concatenate([own, got], 1), jnp.concatenate([got, own], 1))
 

time: 78.8 us -> 78.7 us (level)
  local copies, waits for them, and re-layouts: 3.33 us -> 2.11 us
  other arithmetic: 12.8 us -> 13.7 us
    convert_element_type x1, other arithmetic: 0.36 us -> 1.33 us  [gated_norm(): return gated_rows.reshape(token_count, head_count * DV).astype(jnp.bfloat16)]
where the time goes in v17:
time: 78.7 us; the launch traced here: 78.5 us
  waiting for transfers between devices  28 us (36%)
  starting transfers between devices  19 us (24%)
  matrix products  15 us (19%)
  other arithmetic  13.7 us (17%)
  local copies, waits for them, and re-layouts  2.11 us (3%)
    ppermute x6, waiting for transfers between devices, chain_states(): got = lax.ppermute(other, 'ctx', [(i, i ^ stride) for i in range(size)])  16.9 us
    ppermute x6, starting transfers between devices, chain_states(): got = lax.ppermute(other, 'ctx', [(i, i ^ stride) for i in range(size)])  7.31 us
    ppermute x1, waiting for transfers between devices, head_return(): got = lax.ppermute(sent, 'head', [(0, 1), (1, 0)])  6.77 us
    dot_general x5, matrix products, unit_lower_inverse(): jnp.matmul(jnp.concatenate([inverse, power], axis=-2), power, precision=L...  5.37 us
    ppermute x3, starting transfers between devices, head_swap(): got = lax.ppermute(sent, 'head', [(0, 1), (1, 0)])  5.18 us
    ppermute x1, starting transfers between devices, exclusive_scan(): return lax.ppermute(write, 'ctx', near)  4.94 us
    ppermute x3, waiting for transfers between devices, head_swap(): got = lax.ppermute(sent, 'head', [(0, 1), (1, 0)])  3.87 us
    select_n x3, other arithmetic, head_swap(): own = jnp.where(first, rows[..., :width], rows[..., width:])  3.15 us
  transfers between devices with their start and end apart: 11, of which 10 were waited for; matrix products, arithmetic and copies ran while one was open for 12% of the time, Pallas kernels for 0%

profile of v17, /device:TPU:0, one launch (start us, length us, event | category | flops | bytes accessed | tf_op | source)
XLA Modules:
  0.0 78.5 jit_solution(13159240087730953689)
XLA Ops:
  0.0 1.3 %broadcast_select_fusion.5 = (bf16[2,128,512]{2,1,0:T(8,128)(2,1)S(1)}, bf16[2,128,512]{2,1,0:T(8,128)(2,1)S(1)}) fusion(pred[]{:T(512)S(6)} %eq.29, bf16[1,128,1024]{2,1,0:T(8,128)(2,1)} %bitcast.145, bf16[1,128,1024]{2,1,0:T(8,128)(2,1)} %bitcast.146), kind=kLoop, calls=%fused_computation.125 | loop fusion | flops 1835008 | bytes 1048577 | tf_op jit(solution)/shard_map/jit(_where)/select_n | solution.py:232
  1.3 3.0 %collective-permute-start = (bf16[2,128,512]{2,1,0:T(8,128)(2,1)S(1)}, bf16[2,128,512]{2,1,0:T(8,128)(2,1)S(1)}, u32[]{:S(2)}, u32[]{:S(2)}) collective-permute-start(bf16[2,128,512]{2,1,0:T(8,128)(2,1)S(1)} %get-tuple-element.34), channel_id=1, source_target_pairs={{0,1},{1,0},{2,3},{3,2},{4,5},{5,4},{6,7},{7,6},{8,9},{9,8},{10,11... | collective-permute-start | bytes 786440 | tf_op jit(solution)/shard_map/ppermute | solution.py:234
  4.4 0.8 broadcast_select_fusion.17
  5.2 1.1 %broadcast_select_fusion.3 = (bf16[128,1024]{1,0:T(8,128)(2,1)S(1)}, bf16[128,1024]{1,0:T(8,128)(2,1)S(1)}) fusion(pred[]{:T(512)S(6)} %eq.29, bf16[128,2048]{1,0:T(8,128)(2,1)} %param.9), kind=kLoop, calls=%fused_computation.123 | loop fusion | flops 262144 | bytes 1048577 | tf_op jit(solution)/shard_map/jit(_where)/select_n | solution.py:232
  6.3 2.1 %collective-permute-start.2 = (bf16[128,1024]{1,0:T(8,128)(2,1)S(1)}, bf16[128,1024]{1,0:T(8,128)(2,1)S(1)}, u32[]{:S(2)}, u32[]{:S(2)}) collective-permute-start(bf16[128,1024]{1,0:T(8,128)(2,1)S(1)} %get-tuple-element.32), channel_id=1, source_target_pairs={{0,1},{1,0},{2,3},{3,2},{4,5},{5,4},{6,7},{7,6},{8,9},{9,8},{10,11... | collective-permute-start | bytes 786440 | tf_op jit(solution)/shard_map/ppermute | solution.py:234
  8.4 3.2 %collective-permute-done.1 = bf16[2,128,8]{1,2,0:T(8,128)(2,1)S(1)} collective-permute-done((bf16[2,128,8]{1,2,0:T(8,128)(2,1)S(1)}, bf16[2,128,8]{1,2,0:T(8,128)(2,1)S(1)}, u32[]{:S(2)}, u32[]{:S(2)}) %collective-permute-start.1) | collective-permute-done | bytes 4128 | tf_op jit(solution)/shard_map/ppermute | solution.py:234
  16.7 1.1 %fusion = f32[8,2,256,128]{3,2,1,0:T(8,128)S(1)} fusion(f32[8,2,128,128]{3,2,1,0:T(8,128)S(1)} %fusion.93, f32[8,2,128,128]{3,2,1,0:T(8,128)S(1)} %get-tuple-element.21), kind=kOutput, calls=%fused_computation | convolution fusion | flops 403177472 | bytes 4194304 | tf_op jit(solution)/shard_map/dot_general | solution.py:71
  17.8 1.0 %slice_add_fusion.5 = (f32[8,2,128,128]{3,2,1,0:T(8,128)S(1)}, f32[8,2,128,128]{3,2,1,0:T(8,128)S(1)}, f32[8,2,128,128]{3,2,1,0:T(8,128)S(1)}) fusion(f32[8,2,256,128]{3,2,1,0:T(8,128)S(1)} %fusion, f32[4,2,128,128]{3,2,1,0:T(8,128)S(1)} %fusion.88, f32[8,2,128]{2,1,0:T(2,128)S(1)} %copy.66, pred[128,128]{1,0:T(8,128)(4,1)S(1)} %get-tuple-element.51, ...), kind=kLoop, calls=%fused_computation.69 | loop fusion | flops 1835008 | bytes 6922240 | tf_op jit(solution)/shard_map/add | solution.py:74
  18.8 1.1 %fusion.4 = f32[8,2,256,128]{3,2,1,0:T(8,128)S(1)} fusion(f32[8,2,128,128]{3,2,1,0:T(8,128)S(1)} %get-tuple-element.14, f32[8,2,128,128]{3,2,1,0:T(8,128)S(1)} %get-tuple-element.13), kind=kOutput, calls=%fused_computation.4 | convolution fusion | flops 403177472 | bytes 4194304 | tf_op jit(solution)/shard_map/dot_general | solution.py:71
  20.1 1.1 %fusion.8 = f32[8,2,256,128]{3,2,1,0:T(8,128)S(1)} fusion(f32[8,2,128,128]{3,2,1,0:T(8,128)S(1)} %get-tuple-element.12, f32[8,2,128,128]{3,2,1,0:T(8,128)S(1)} %get-tuple-element.11), kind=kOutput, calls=%fused_computation.8 | convolution fusion | flops 403177472 | bytes 4194304 | tf_op jit(solution)/shard_map/dot_general | solution.py:71
  21.5 1.1 %fusion.12 = f32[8,2,256,128]{3,2,1,0:T(8,128)S(1)} fusion(f32[8,2,128,128]{3,2,1,0:T(8,128)S(1)} %get-tuple-element.10, f32[8,2,128,128]{3,2,1,0:T(8,128)S(1)} %get-tuple-element.9), kind=kOutput, calls=%fused_computation.12 | convolution fusion | flops 403177472 | bytes 4194304 | tf_op jit(solution)/shard_map/dot_general | solution.py:71
  22.8 1.1 %fusion.16 = f32[8,2,256,128]{3,2,1,0:T(8,128)S(1)} fusion(f32[8,2,128,128]{3,2,1,0:T(8,128)S(1)} %get-tuple-element.8, f32[8,2,128,128]{3,2,1,0:T(8,128)S(1)} %get-tuple-element.7), kind=kOutput, calls=%fused_computation.16 | convolution fusion | flops 403177472 | bytes 4194304 | tf_op jit(solution)/shard_map/dot_general | solution.py:71
  23.9 0.7 convolution_add_fusion
  25.3 1.2 %fusion.20 = f32[8,2,128,256]{3,2,1,0:T(8,128)S(1)} fusion(f32[8,2,128,128]{3,2,1,0:T(8,128)S(1)} %convolution_add_fusion, f32[8,2,128,128]{3,2,1,0:T(8,128)S(1)} %get-tuple-element.28, f32[8,2,128,128]{3,2,1,0:T(8,128)S(1)} %get-tuple-element.48), kind=kOutput, calls=%fused_computation.20 | convolution fusion | flops 403177472 | bytes 5242880 | tf_op jit(solution)/shard_map/dot_general | solution.py:99
  26.5 1.1 %fusion.94 = f32[8,2,128,256]{3,2,1,0:T(8,128)S(1)} fusion(f32[8,2,128,128]{3,2,1,0:T(8,128)S(1)} %get-tuple-element.27, f32[8,2,128,256]{3,2,1,0:T(8,128)S(1)} %fusion.20), kind=kOutput, calls=%fused_computation.192 | convolution fusion | flops 402653184 | bytes 5242880 | tf_op jit(solution)/shard_map/hmck,hmcj->hmkj/dot_general | solution.py:104
  28.9 1.0 %slice_select_fusion = f32[4,128,256]{2,1,0:T(8,128)} fusion(f32[8,128,256]{2,1,0:T(8,128)S(1)} %convolution_add_fusion.2, pred[]{:T(512)S(6)} %eq.31), kind=kLoop, calls=%fused_computation.108 | loop fusion | flops 131072 | bytes 1572865 | tf_op jit(solution)/shard_map/jit(_where)/select_n | solution.py:198
  30.1 2.2 %collective-permute-done.3 = f32[4,128,256]{2,1,0:T(8,128)} collective-permute-done((f32[4,128,256]{2,1,0:T(8,128)}, f32[4,128,256]{2,1,0:T(8,128)}, u32[]{:S(2)}, u32[]{:S(2)}) %collective-permute-start.3) | collective-permute-done | bytes 524320 | tf_op jit(solution)/shard_map/ppermute | solution.py:199
  32.3 1.5 %broadcast_select_fusion.1 = (f32[4,128,256]{2,1,0:T(8,128)S(1)}, f32[4,128,256]{2,1,0:T(8,128)S(1)}) fusion(f32[4,128,256]{2,1,0:T(8,128)} %collective-permute-done.3, pred[]{:T(512)S(6)} %eq.31, f32[8,128,256]{2,1,0:T(8,128)} %copy-done.2), kind=kLoop, calls=%fused_computation.120 | loop fusion | flops 393216 | bytes 2621441 | tf_op jit(solution)/shard_map/jit(_where)/select_n | solution.py:201
  34.2 1.8 %collective-permute-start.4 = (f32[2,128,256]{2,1,0:T(8,128)S(1)}, f32[2,128,256]{2,1,0:T(8,128)S(1)}, u32[]{:S(2)}, u32[]{:S(2)}) collective-permute-start(f32[2,128,256]{2,1,0:T(8,128)S(1)} %slice_select_fusion.2), channel_id=1, source_target_pairs={{0,4},{2,6},{4,0},{6,2},{8,12},{10,14},{12,8},{14,10},{16,20},{18,... | collective-permute-start | bytes 786440 | tf_op jit(solution)/shard_map/ppermute | solution.py:199
  36.3 6.3 %collective-permute-done.4 = f32[2,128,256]{2,1,0:T(8,128)S(1)} collective-permute-done((f32[2,128,256]{2,1,0:T(8,128)S(1)}, f32[2,128,256]{2,1,0:T(8,128)S(1)}, u32[]{:S(2)}, u32[]{:S(2)}) %collective-permute-start.4) | collective-permute-done | bytes 262176 | tf_op jit(solution)/shard_map/ppermute | solution.py:199
  43.0 1.9 %collective-permute-start.5 = (f32[1,128,256]{2,1,0:T(8,128)S(1)}, f32[1,128,256]{2,1,0:T(8,128)S(1)}, u32[]{:S(2)}, u32[]{:S(2)}) collective-permute-start(f32[1,128,256]{2,1,0:T(8,128)S(1)} %slice_select_fusion.4), channel_id=1, source_target_pairs={{0,8},{2,10},{4,12},{6,14},{8,0},{10,2},{12,4},{14,6},{16,24},{18,... | collective-permute-start | bytes 393224 | tf_op jit(solution)/shard_map/ppermute | solution.py:199
  45.5 2.5 %collective-permute-done.5 = f32[1,128,256]{2,1,0:T(8,128)S(1)} collective-permute-done((f32[1,128,256]{2,1,0:T(8,128)S(1)}, f32[1,128,256]{2,1,0:T(8,128)S(1)}, u32[]{:S(2)}, u32[]{:S(2)}) %collective-permute-start.5) | collective-permute-done | bytes 131104 | tf_op jit(solution)/shard_map/ppermute | solution.py:199
  48.3 4.9 %collective-permute-start.6 = (f32[1,128,128]{2,1,0:T(8,128)S(1)}, f32[1,128,128]{2,1,0:T(8,128)S(1)}, u32[]{:S(2)}, u32[]{:S(2)}) collective-permute-start(f32[1,128,128]{2,1,0:T(8,128)S(1)} %slice_add_fusion.7), channel_id=1, source_target_pairs={{0,16},{2,18},{4,20},{6,22},{8,24},{10,26},{12,28},{14,30},{1,17},... | collective-permute-start | bytes 196616 | tf_op jit(solution)/shard_map/ppermute | solution.py:177
  53.3 1.2 %fusion.34 = f32[8,2,128,256]{3,2,1,0:T(8,128)S(1)} fusion(f32[8,2,128,256]{3,2,1,0:T(8,128)S(1)} %fusion.20, f32[8,2,128,128]{3,2,1,0:T(8,128)S(1)} %bitcast.123, f32[8,2,128]{2,1,0:T(2,128)S(1)} %copy.66, pred[128,128]{1,0:T(8,128)(4,1)S(1)} %iota_compare_fusion.2), kind=kOutput, calls=%fused_computation.53 | convolution fusion | flops 403439616 | bytes 5267456 | tf_op jit(solution)/shard_map/hmij,hmjv->hmiv/dot_general | solution.py:124
  55.2 2.0 %collective-permute-start.7 = (f32[1,128,128]{2,1,0:T(8,128)S(1)}, f32[1,128,128]{2,1,0:T(8,128)S(1)}, u32[]{:S(2)}, u32[]{:S(2)}) collective-permute-start(f32[1,128,128]{2,1,0:T(8,128)S(1)} %get-tuple-element.43), channel_id=1, source_target_pairs={{0,8},{2,10},{4,12},{6,14},{8,0},{10,2},{12,4},{14,6},{16,24},{18,... | collective-permute-start | bytes 196616 | tf_op jit(solution)/shard_map/ppermute | solution.py:212
  57.8 1.7 %collective-permute-done.7 = f32[1,128,128]{2,1,0:T(8,128)S(1)} collective-permute-done((f32[1,128,128]{2,1,0:T(8,128)S(1)}, f32[1,128,128]{2,1,0:T(8,128)S(1)}, u32[]{:S(2)}, u32[]{:S(2)}) %collective-permute-start.7) | collective-permute-done | bytes 65568 | tf_op jit(solution)/shard_map/ppermute | solution.py:212
  59.7 1.6 %collective-permute-start.8 = (f32[2,128,128]{2,1,0:T(8,128)S(1)}, f32[2,128,128]{2,1,0:T(8,128)S(1)}, u32[]{:S(2)}, u32[]{:S(2)}) collective-permute-start(f32[2,128,128]{2,1,0:T(8,128)S(1)} %get-tuple-element.37), channel_id=1, source_target_pairs={{0,4},{2,6},{4,0},{6,2},{8,12},{10,14},{12,8},{14,10},{16,20},{18,... | collective-permute-start | bytes 393224 | tf_op jit(solution)/shard_map/ppermute | solution.py:212
  61.9 2.8 %collective-permute-done.8 = f32[2,128,128]{2,1,0:T(8,128)S(1)} collective-permute-done((f32[2,128,128]{2,1,0:T(8,128)S(1)}, f32[2,128,128]{2,1,0:T(8,128)S(1)}, u32[]{:S(2)}, u32[]{:S(2)}) %collective-permute-start.8) | collective-permute-done | bytes 131104 | tf_op jit(solution)/shard_map/ppermute | solution.py:212
  65.3 1.3 %collective-permute-done.9 = f32[4,128,128]{2,1,0:T(8,128)S(1)} collective-permute-done((f32[4,128,128]{2,1,0:T(8,128)S(1)}, f32[4,128,128]{2,1,0:T(8,128)S(1)}, u32[]{:S(2)}, u32[]{:S(2)}) %collective-permute-start.9) | collective-permute-done | bytes 262176 | tf_op jit(solution)/shard_map/ppermute | solution.py:212
  67.8 1.6 %collective-permute-start.10 = (bf16[128,1024]{1,0:T(8,128)(2,1)S(1)}, bf16[128,1024]{1,0:T(8,128)(2,1)S(1)}, u32[]{:S(2)}, u32[]{:S(2)}) collective-permute-start(bf16[128,1024]{1,0:T(8,128)(2,1)S(1)} %get-tuple-element.23), channel_id=1, source_target_pairs={{0,1},{1,0},{2,3},{3,2},{4,5},{5,4},{6,7},{7,6},{8,9},{9,8},{10,11... | collective-permute-start | bytes 786440 | tf_op jit(solution)/shard_map/ppermute | solution.py:247
  69.5 6.8 %collective-permute-done.10 = bf16[128,1024]{1,0:T(8,128)(2,1)S(1)} collective-permute-done((bf16[128,1024]{1,0:T(8,128)(2,1)S(1)}, bf16[128,1024]{1,0:T(8,128)(2,1)S(1)}, u32[]{:S(2)}, u32[]{:S(2)}) %collective-permute-start.10) | collective-permute-done | bytes 262176 | tf_op jit(solution)/shard_map/ppermute | solution.py:247
  77.2 1.3 %fusion.44 = bf16[128,2048]{1,0:T(8,128)(2,1)} fusion(bf16[128,2048]{1,0:T(8,128)(2,1)S(1)} %copy-done.5, f32[16,8,16,128]{3,2,1,0:T(8,128)S(1)} %bitcast.124, f32[2048]{0:T(1024)S(1)} %broadcast_bitcast_fusion), kind=kLoop, calls=%fused_computation.75 | loop fusion | flops 2097152 | bytes 2105344 | tf_op jit(solution)/shard_map/convert_element_type | solution.py:226
  (91 shorter events, 14.6 us)
Async XLA Ops:
  1.3 11.2 %collective-permute-start = (bf16[2,128,512]{2,1,0:T(8,128)(2,1)S(1)}, bf16[2,128,512]{2,1,0:T(8,128)(2,1)S(1)}, u32[]{:S(2)}, u32[]{:S(2)}) collective-permute-start(bf16[2,128,512]{2,1,0:T(8,128)(2,1)S(1)} %get-tuple-element.34), channel_id=1, source_target_pairs={{0,1},{1,0},{2,3},{3,2},{4,5},{5,4},{6,7},{7,6},{8,9},{9,8},{10,11... | collective-permute-start | bytes 786440 | tf_op jit(solution)/shard_map/ppermute | solution.py:234
  5.1 6.5 %collective-permute-start.1 = (bf16[2,128,8]{1,2,0:T(8,128)(2,1)S(1)}, bf16[2,128,8]{1,2,0:T(8,128)(2,1)S(1)}, u32[]{:S(2)}, u32[]{:S(2)}) collective-permute-start(bf16[2,128,8]{1,2,0:T(8,128)(2,1)S(1)} %get-tuple-element.50), channel_id=1, source_target_pairs={{0,1},{1,0},{2,3},{3,2},{4,5},{5,4},{6,7},{7,6},{8,9},{9,8},{10,11... | collective-permute-start | bytes 12296 | tf_op jit(solution)/shard_map/ppermute | solution.py:234
  6.3 10.1 %collective-permute-start.2 = (bf16[128,1024]{1,0:T(8,128)(2,1)S(1)}, bf16[128,1024]{1,0:T(8,128)(2,1)S(1)}, u32[]{:S(2)}, u32[]{:S(2)}) collective-permute-start(bf16[128,1024]{1,0:T(8,128)(2,1)S(1)} %get-tuple-element.32), channel_id=1, source_target_pairs={{0,1},{1,0},{2,3},{3,2},{4,5},{5,4},{6,7},{7,6},{8,9},{9,8},{10,11... | collective-permute-start | bytes 786440 | tf_op jit(solution)/shard_map/ppermute | solution.py:234
  13.8 1.3 %copy-start.3 = (f32[4,2,128,128]{3,0,2,1:T(4,128)}, f32[4,2,128,128]{3,0,2,1:T(4,128)S(1)}, u32[]{:S(2)}) copy-start(f32[4,2,128,128]{3,0,2,1:T(4,128)S(1)} %multiply_bitcast_fusion) | copy-start | bytes 1572868
  27.9 1.0 %copy-start = (f32[8,2,128,128]{3,2,1,0:T(8,128)}, f32[8,2,128,128]{3,2,1,0:T(8,128)S(1)}, u32[]{:S(2)}) copy-start(f32[8,2,128,128]{3,2,1,0:T(8,128)S(1)} %get-tuple-element.6) | copy-start | bytes 3145732
  28.9 1.1 %copy-start.2 = (f32[8,128,256]{2,1,0:T(8,128)}, f32[8,128,256]{2,1,0:T(8,128)S(1)}, u32[]{:S(2)}) copy-start(f32[8,128,256]{2,1,0:T(8,128)S(1)} %convolution_add_fusion.2) | copy-start | bytes 3145732
  30.0 2.3 %collective-permute-start.3 = (f32[4,128,256]{2,1,0:T(8,128)}, f32[4,128,256]{2,1,0:T(8,128)}, u32[]{:S(2)}, u32[]{:S(2)}) collective-permute-start(f32[4,128,256]{2,1,0:T(8,128)} %slice_select_fusion), channel_id=1, source_target_pairs={{0,2},{2,0},{4,6},{6,4},{8,10},{10,8},{12,14},{14,12},{16,18},{18,... | collective-permute-start | bytes 1572872 | tf_op jit(solution)/shard_map/ppermute | solution.py:199
  34.2 10.7 %copy-start.4 = (f32[4,2,128,128]{3,0,2,1:T(4,128)S(1)}, f32[4,2,128,128]{3,0,2,1:T(4,128)}, u32[]{:S(2)}) copy-start(f32[4,2,128,128]{3,0,2,1:T(4,128)} %copy-done.3) | copy-start | bytes 1572868
  34.2 8.4 %collective-permute-start.4 = (f32[2,128,256]{2,1,0:T(8,128)S(1)}, f32[2,128,256]{2,1,0:T(8,128)S(1)}, u32[]{:S(2)}, u32[]{:S(2)}) collective-permute-start(f32[2,128,256]{2,1,0:T(8,128)S(1)} %slice_select_fusion.2), channel_id=1, source_target_pairs={{0,4},{2,6},{4,0},{6,2},{8,12},{10,14},{12,8},{14,10},{16,20},{18,... | collective-permute-start | bytes 786440 | tf_op jit(solution)/shard_map/ppermute | solution.py:199
  43.0 5.0 %collective-permute-start.5 = (f32[1,128,256]{2,1,0:T(8,128)S(1)}, f32[1,128,256]{2,1,0:T(8,128)S(1)}, u32[]{:S(2)}, u32[]{:S(2)}) collective-permute-start(f32[1,128,256]{2,1,0:T(8,128)S(1)} %slice_select_fusion.4), channel_id=1, source_target_pairs={{0,8},{2,10},{4,12},{6,14},{8,0},{10,2},{12,4},{14,6},{16,24},{18,... | collective-permute-start | bytes 393224 | tf_op jit(solution)/shard_map/ppermute | solution.py:199
  48.3 6.7 %collective-permute-start.6 = (f32[1,128,128]{2,1,0:T(8,128)S(1)}, f32[1,128,128]{2,1,0:T(8,128)S(1)}, u32[]{:S(2)}, u32[]{:S(2)}) collective-permute-start(f32[1,128,128]{2,1,0:T(8,128)S(1)} %slice_add_fusion.7), channel_id=1, source_target_pairs={{0,16},{2,18},{4,20},{6,22},{8,24},{10,26},{12,28},{14,30},{1,17},... | collective-permute-start | bytes 196616 | tf_op jit(solution)/shard_map/ppermute | solution.py:177
  55.2 6.1 %copy-start.1 = (f32[8,2,128,128]{3,2,1,0:T(8,128)S(1)}, f32[8,2,128,128]{3,2,1,0:T(8,128)}, u32[]{:S(2)}) copy-start(f32[8,2,128,128]{3,2,1,0:T(8,128)} %copy-done) | copy-start | bytes 3145732
  55.2 4.3 %collective-permute-start.7 = (f32[1,128,128]{2,1,0:T(8,128)S(1)}, f32[1,128,128]{2,1,0:T(8,128)S(1)}, u32[]{:S(2)}, u32[]{:S(2)}) collective-permute-start(f32[1,128,128]{2,1,0:T(8,128)S(1)} %get-tuple-element.43), channel_id=1, source_target_pairs={{0,8},{2,10},{4,12},{6,14},{8,0},{10,2},{12,4},{14,6},{16,24},{18,... | collective-permute-start | bytes 196616 | tf_op jit(solution)/shard_map/ppermute | solution.py:212
  59.7 5.0 %collective-permute-start.8 = (f32[2,128,128]{2,1,0:T(8,128)S(1)}, f32[2,128,128]{2,1,0:T(8,128)S(1)}, u32[]{:S(2)}, u32[]{:S(2)}) collective-permute-start(f32[2,128,128]{2,1,0:T(8,128)S(1)} %get-tuple-element.37), channel_id=1, source_target_pairs={{0,4},{2,6},{4,0},{6,2},{8,12},{10,14},{12,8},{14,10},{16,20},{18,... | collective-permute-start | bytes 393224 | tf_op jit(solution)/shard_map/ppermute | solution.py:212
  65.1 1.6 %collective-permute-start.9 = (f32[4,128,128]{2,1,0:T(8,128)S(1)}, f32[4,128,128]{2,1,0:T(8,128)S(1)}, u32[]{:S(2)}, u32[]{:S(2)}) collective-permute-start(f32[4,128,128]{2,1,0:T(8,128)S(1)} %get-tuple-element.25), channel_id=1, source_target_pairs={{0,2},{2,0},{4,6},{6,4},{8,10},{10,8},{12,14},{14,12},{16,18},{18,... | collective-permute-start | bytes 786440 | tf_op jit(solution)/shard_map/ppermute | solution.py:212
  67.3 2.1 %copy-start.6 = (bf16[128]{0:T(256)(128)(2,1)S(1)}, bf16[128]{0:T(256)(128)(2,1)}, u32[]{:S(2)}) copy-start(bf16[128]{0:T(256)(128)(2,1)} %param.13) | copy-start | bytes 772
  67.8 9.4 %copy-start.5 = (bf16[128,2048]{1,0:T(8,128)(2,1)S(1)}, bf16[128,2048]{1,0:T(8,128)(2,1)}, u32[]{:S(2)}) copy-start(bf16[128,2048]{1,0:T(8,128)(2,1)} %param.10) | copy-start | bytes 1572868
  67.8 8.4 %collective-permute-start.10 = (bf16[128,1024]{1,0:T(8,128)(2,1)S(1)}, bf16[128,1024]{1,0:T(8,128)(2,1)S(1)}, u32[]{:S(2)}, u32[]{:S(2)}) collective-permute-start(bf16[128,1024]{1,0:T(8,128)(2,1)S(1)} %get-tuple-element.23), channel_id=1, source_target_pairs={{0,1},{1,0},{2,3},{3,2},{4,5},{5,4},{6,7},{7,6},{8,9},{9,8},{10,11... | collective-permute-start | bytes 786440 | tf_op jit(solution)/shard_map/ppermute | solution.py:247

commit v18 on v17

--- a/solution.py
+++ b/solution.py
@@ -194,8 +194,9 @@
         stride = 2**level
         upper = (me // stride) % 2 == 1
         half = current.shape[0] // 2
-        mine = jnp.where(upper, current[half:], current[:half])
-        other = jnp.where(upper, current[:half], current[half:])
+        bit = (me // stride) % 2
+        mine = lax.dynamic_slice_in_dim(current, bit * half, half, 0)
+        other = lax.dynamic_slice_in_dim(current, (1 - bit) * half, half, 0)
         got = lax.ppermute(other, "ctx", [(i, i ^ stride) for i in range(size)])
         earlier = jnp.where(upper, got, mine)
         later = jnp.where(upper, mine, got)

time: 78.7 us -> 78.5 us (level)
  other arithmetic: 13.7 us -> 12.5 us
  local copies, waits for them, and re-layouts: 2.11 us -> 3.1 us
    select_n x3 -> x0, other arithmetic: 1.01 us -> none  [chain_states(): other = jnp.where(upper, current[:half], current[half:])]
    dynamic_slice x0 -> x3, local copies, waits for them, and re-layouts: none -> 0.92 us  [chain_states(): other = lax.dynamic_slice_in_dim(current, (1 - bit) * half, half, 0)]
where the time goes in v18:
time: 78.5 us; the launch traced here: 78.3 us
  waiting for transfers between devices  28 us (36%)
  starting transfers between devices  19 us (24%)
  matrix products  15 us (19%)
  other arithmetic  12.5 us (16%)
  local copies, waits for them, and re-layouts  3.1 us (4%)
    ppermute x6, waiting for transfers between devices, chain_states(): got = lax.ppermute(other, 'ctx', [(i, i ^ stride) for i in range(size)])  16.9 us
    ppermute x6, starting transfers between devices, chain_states(): got = lax.ppermute(other, 'ctx', [(i, i ^ stride) for i in range(size)])  7.3 us
    ppermute x1, waiting for transfers between devices, head_return(): got = lax.ppermute(sent, 'head', [(0, 1), (1, 0)])  6.77 us
    dot_general x5, matrix products, unit_lower_inverse(): jnp.matmul(jnp.concatenate([inverse, power], axis=-2), power, precision=L...  5.37 us
    ppermute x3, starting transfers between devices, head_swap(): got = lax.ppermute(sent, 'head', [(0, 1), (1, 0)])  5.18 us
    ppermute x1, starting transfers between devices, exclusive_scan(): return lax.ppermute(write, 'ctx', near)  4.93 us
    ppermute x3, waiting for transfers between devices, head_swap(): got = lax.ppermute(sent, 'head', [(0, 1), (1, 0)])  3.86 us
    select_n x3, other arithmetic, head_swap(): own = jnp.where(first, rows[..., :width], rows[..., width:])  3.15 us
  transfers between devices with their start and end apart: 11, of which 10 were waited for; matrix products, arithmetic and copies ran while one was open for 12% of the time, Pallas kernels for 0%

profile of v18, /device:TPU:0, one launch (start us, length us, event | category | flops | bytes accessed | tf_op | source)
XLA Modules:
  0.0 78.3 jit_solution(6187069223972604741)
XLA Ops:
  0.0 1.3 %broadcast_select_fusion.3 = (bf16[2,128,512]{2,1,0:T(8,128)(2,1)S(1)}, bf16[2,128,512]{2,1,0:T(8,128)(2,1)S(1)}) fusion(pred[]{:T(512)S(6)} %eq.32, bf16[1,128,1024]{2,1,0:T(8,128)(2,1)} %bitcast.145, bf16[1,128,1024]{2,1,0:T(8,128)(2,1)} %bitcast.146), kind=kLoop, calls=%fused_computation.123 | loop fusion | flops 1835008 | bytes 1048577 | tf_op jit(solution)/shard_map/jit(_where)/select_n | solution.py:233
  1.3 3.0 %collective-permute-start = (bf16[2,128,512]{2,1,0:T(8,128)(2,1)S(1)}, bf16[2,128,512]{2,1,0:T(8,128)(2,1)S(1)}, u32[]{:S(2)}, u32[]{:S(2)}) collective-permute-start(bf16[2,128,512]{2,1,0:T(8,128)(2,1)S(1)} %get-tuple-element.34), channel_id=1, source_target_pairs={{0,1},{1,0},{2,3},{3,2},{4,5},{5,4},{6,7},{7,6},{8,9},{9,8},{10,11... | collective-permute-start | bytes 786440 | tf_op jit(solution)/shard_map/ppermute | solution.py:235
  4.4 0.8 broadcast_select_fusion.11
  5.2 1.1 %broadcast_select_fusion.1 = (bf16[128,1024]{1,0:T(8,128)(2,1)S(1)}, bf16[128,1024]{1,0:T(8,128)(2,1)S(1)}) fusion(pred[]{:T(512)S(6)} %eq.32, bf16[128,2048]{1,0:T(8,128)(2,1)} %param.9), kind=kLoop, calls=%fused_computation.121 | loop fusion | flops 262144 | bytes 1048577 | tf_op jit(solution)/shard_map/jit(_where)/select_n | solution.py:233
  6.3 2.1 %collective-permute-start.2 = (bf16[128,1024]{1,0:T(8,128)(2,1)S(1)}, bf16[128,1024]{1,0:T(8,128)(2,1)S(1)}, u32[]{:S(2)}, u32[]{:S(2)}) collective-permute-start(bf16[128,1024]{1,0:T(8,128)(2,1)S(1)} %get-tuple-element.32), channel_id=1, source_target_pairs={{0,1},{1,0},{2,3},{3,2},{4,5},{5,4},{6,7},{7,6},{8,9},{9,8},{10,11... | collective-permute-start | bytes 786440 | tf_op jit(solution)/shard_map/ppermute | solution.py:235
  8.4 3.2 %collective-permute-done.1 = bf16[2,128,8]{1,2,0:T(8,128)(2,1)S(1)} collective-permute-done((bf16[2,128,8]{1,2,0:T(8,128)(2,1)S(1)}, bf16[2,128,8]{1,2,0:T(8,128)(2,1)S(1)}, u32[]{:S(2)}, u32[]{:S(2)}) %collective-permute-start.1) | collective-permute-done | bytes 4128 | tf_op jit(solution)/shard_map/ppermute | solution.py:235
  16.7 1.1 %fusion = f32[8,2,256,128]{3,2,1,0:T(8,128)S(1)} fusion(f32[8,2,128,128]{3,2,1,0:T(8,128)S(1)} %fusion.93, f32[8,2,128,128]{3,2,1,0:T(8,128)S(1)} %get-tuple-element.21), kind=kOutput, calls=%fused_computation | convolution fusion | flops 403177472 | bytes 4194304 | tf_op jit(solution)/shard_map/dot_general | solution.py:71
  17.8 1.0 %slice_add_fusion.5 = (f32[8,2,128,128]{3,2,1,0:T(8,128)S(1)}, f32[8,2,128,128]{3,2,1,0:T(8,128)S(1)}, f32[8,2,128,128]{3,2,1,0:T(8,128)S(1)}) fusion(f32[8,2,256,128]{3,2,1,0:T(8,128)S(1)} %fusion, f32[4,2,128,128]{3,2,1,0:T(8,128)S(1)} %fusion.88, f32[8,2,128]{2,1,0:T(2,128)S(1)} %copy.66, pred[128,128]{1,0:T(8,128)(4,1)S(1)} %get-tuple-element.51, ...), kind=kLoop, calls=%fused_computation.69 | loop fusion | flops 1835008 | bytes 6922240 | tf_op jit(solution)/shard_map/add | solution.py:74
  18.8 1.1 %fusion.4 = f32[8,2,256,128]{3,2,1,0:T(8,128)S(1)} fusion(f32[8,2,128,128]{3,2,1,0:T(8,128)S(1)} %get-tuple-element.14, f32[8,2,128,128]{3,2,1,0:T(8,128)S(1)} %get-tuple-element.13), kind=kOutput, calls=%fused_computation.4 | convolution fusion | flops 403177472 | bytes 4194304 | tf_op jit(solution)/shard_map/dot_general | solution.py:71
  20.1 1.1 %fusion.8 = f32[8,2,256,128]{3,2,1,0:T(8,128)S(1)} fusion(f32[8,2,128,128]{3,2,1,0:T(8,128)S(1)} %get-tuple-element.12, f32[8,2,128,128]{3,2,1,0:T(8,128)S(1)} %get-tuple-element.11), kind=kOutput, calls=%fused_computation.8 | convolution fusion | flops 403177472 | bytes 4194304 | tf_op jit(solution)/shard_map/dot_general | solution.py:71
  21.5 1.1 %fusion.12 = f32[8,2,256,128]{3,2,1,0:T(8,128)S(1)} fusion(f32[8,2,128,128]{3,2,1,0:T(8,128)S(1)} %get-tuple-element.10, f32[8,2,128,128]{3,2,1,0:T(8,128)S(1)} %get-tuple-element.9), kind=kOutput, calls=%fused_computation.12 | convolution fusion | flops 403177472 | bytes 4194304 | tf_op jit(solution)/shard_map/dot_general | solution.py:71
  22.8 1.1 %fusion.16 = f32[8,2,256,128]{3,2,1,0:T(8,128)S(1)} fusion(f32[8,2,128,128]{3,2,1,0:T(8,128)S(1)} %get-tuple-element.8, f32[8,2,128,128]{3,2,1,0:T(8,128)S(1)} %get-tuple-element.7), kind=kOutput, calls=%fused_computation.16 | convolution fusion | flops 403177472 | bytes 4194304 | tf_op jit(solution)/shard_map/dot_general | solution.py:71
  23.9 0.7 convolution_add_fusion
  25.2 1.2 %fusion.20 = f32[8,2,128,256]{3,2,1,0:T(8,128)S(1)} fusion(f32[8,2,128,128]{3,2,1,0:T(8,128)S(1)} %convolution_add_fusion, f32[8,2,128,128]{3,2,1,0:T(8,128)S(1)} %get-tuple-element.28, f32[8,2,128,128]{3,2,1,0:T(8,128)S(1)} %get-tuple-element.48), kind=kOutput, calls=%fused_computation.20 | convolution fusion | flops 403177472 | bytes 5242880 | tf_op jit(solution)/shard_map/dot_general | solution.py:99
  26.5 1.1 %fusion.94 = f32[8,2,128,256]{3,2,1,0:T(8,128)S(1)} fusion(f32[8,2,128,128]{3,2,1,0:T(8,128)S(1)} %get-tuple-element.27, f32[8,2,128,256]{3,2,1,0:T(8,128)S(1)} %fusion.20), kind=kOutput, calls=%fused_computation.189 | convolution fusion | flops 402653184 | bytes 5242880 | tf_op jit(solution)/shard_map/hmck,hmcj->hmkj/dot_general | solution.py:104
  28.9 0.9 %constant_dynamic-slice_fusion.3 = f32[4,128,256]{2,1,0:T(8,128)} fusion(f32[8,128,256]{2,1,0:T(8,128)S(1)} %convolution_add_fusion.2, s32[]{:T(128)S(6)} %select_n.278), kind=kLoop, calls=%fused_computation.167 | loop fusion | bytes 1048580 | tf_op jit(solution)/shard_map/dynamic_slice | solution.py:199
  30.1 2.2 %collective-permute-done.3 = f32[4,128,256]{2,1,0:T(8,128)} collective-permute-done((f32[4,128,256]{2,1,0:T(8,128)}, f32[4,128,256]{2,1,0:T(8,128)}, u32[]{:S(2)}, u32[]{:S(2)}) %collective-permute-start.3) | collective-permute-done | bytes 524320 | tf_op jit(solution)/shard_map/ppermute | solution.py:200
  32.2 1.3 %dynamic-slice_select_fusion.1 = (f32[4,128,256]{2,1,0:T(8,128)S(1)}, f32[4,128,256]{2,1,0:T(8,128)S(1)}) fusion(f32[4,128,256]{2,1,0:T(8,128)} %collective-permute-done.3, f32[8,128,256]{2,1,0:T(8,128)} %copy-done.4, s32[]{:T(128)S(6)} %select_n.277, pred[]{:T(512)S(6)} %eq.34), kind=kLoop, calls=%fused_computation.109 | loop fusion | flops 262144 | bytes 2097157 | tf_op jit(solution)/shard_map/jit(_where)/select_n | solution.py:202
  34.0 1.8 %collective-permute-start.4 = (f32[2,128,256]{2,1,0:T(8,128)S(1)}, f32[2,128,256]{2,1,0:T(8,128)S(1)}, u32[]{:S(2)}, u32[]{:S(2)}) collective-permute-start(f32[2,128,256]{2,1,0:T(8,128)S(1)} %constant_dynamic-slice_fusion.2), channel_id=1, source_target_pairs={{0,4},{2,6},{4,0},{6,2},{8,12},{10,14},{12,8},{14,10},{16,20},{18,... | collective-permute-start | bytes 786440 | tf_op jit(solution)/shard_map/ppermute | solution.py:200
  36.1 6.4 %collective-permute-done.4 = f32[2,128,256]{2,1,0:T(8,128)S(1)} collective-permute-done((f32[2,128,256]{2,1,0:T(8,128)S(1)}, f32[2,128,256]{2,1,0:T(8,128)S(1)}, u32[]{:S(2)}, u32[]{:S(2)}) %collective-permute-start.4) | collective-permute-done | bytes 262176 | tf_op jit(solution)/shard_map/ppermute | solution.py:200
  42.7 1.9 %collective-permute-start.5 = (f32[1,128,256]{2,1,0:T(8,128)S(1)}, f32[1,128,256]{2,1,0:T(8,128)S(1)}, u32[]{:S(2)}, u32[]{:S(2)}) collective-permute-start(f32[1,128,256]{2,1,0:T(8,128)S(1)} %constant_dynamic-slice_fusion.1), channel_id=1, source_target_pairs={{0,8},{2,10},{4,12},{6,14},{8,0},{10,2},{12,4},{14,6},{16,24},{18,... | collective-permute-start | bytes 393224 | tf_op jit(solution)/shard_map/ppermute | solution.py:200
  45.3 2.5 %collective-permute-done.5 = f32[1,128,256]{2,1,0:T(8,128)S(1)} collective-permute-done((f32[1,128,256]{2,1,0:T(8,128)S(1)}, f32[1,128,256]{2,1,0:T(8,128)S(1)}, u32[]{:S(2)}, u32[]{:S(2)}) %collective-permute-start.5) | collective-permute-done | bytes 131104 | tf_op jit(solution)/shard_map/ppermute | solution.py:200
  48.0 4.9 %collective-permute-start.6 = (f32[1,128,128]{2,1,0:T(8,128)S(1)}, f32[1,128,128]{2,1,0:T(8,128)S(1)}, u32[]{:S(2)}, u32[]{:S(2)}) collective-permute-start(f32[1,128,128]{2,1,0:T(8,128)S(1)} %slice_add_fusion.7), channel_id=1, source_target_pairs={{0,16},{2,18},{4,20},{6,22},{8,24},{10,26},{12,28},{14,30},{1,17},... | collective-permute-start | bytes 196616 | tf_op jit(solution)/shard_map/ppermute | solution.py:177
  53.1 1.2 %fusion.34 = f32[8,2,128,256]{3,2,1,0:T(8,128)S(1)} fusion(f32[8,2,128,256]{3,2,1,0:T(8,128)S(1)} %fusion.20, f32[8,2,128,128]{3,2,1,0:T(8,128)S(1)} %bitcast.123, f32[8,2,128]{2,1,0:T(2,128)S(1)} %copy.66, pred[128,128]{1,0:T(8,128)(4,1)S(1)} %iota_compare_fusion.2), kind=kOutput, calls=%fused_computation.53 | convolution fusion | flops 403439616 | bytes 5267456 | tf_op jit(solution)/shard_map/hmij,hmjv->hmiv/dot_general | solution.py:124
  54.9 2.0 %collective-permute-start.7 = (f32[1,128,128]{2,1,0:T(8,128)S(1)}, f32[1,128,128]{2,1,0:T(8,128)S(1)}, u32[]{:S(2)}, u32[]{:S(2)}) collective-permute-start(f32[1,128,128]{2,1,0:T(8,128)S(1)} %get-tuple-element.43), channel_id=1, source_target_pairs={{0,8},{2,10},{4,12},{6,14},{8,0},{10,2},{12,4},{14,6},{16,24},{18,... | collective-permute-start | bytes 196616 | tf_op jit(solution)/shard_map/ppermute | solution.py:213
  57.5 1.7 %collective-permute-done.7 = f32[1,128,128]{2,1,0:T(8,128)S(1)} collective-permute-done((f32[1,128,128]{2,1,0:T(8,128)S(1)}, f32[1,128,128]{2,1,0:T(8,128)S(1)}, u32[]{:S(2)}, u32[]{:S(2)}) %collective-permute-start.7) | collective-permute-done | bytes 65568 | tf_op jit(solution)/shard_map/ppermute | solution.py:213
  59.5 1.6 %collective-permute-start.8 = (f32[2,128,128]{2,1,0:T(8,128)S(1)}, f32[2,128,128]{2,1,0:T(8,128)S(1)}, u32[]{:S(2)}, u32[]{:S(2)}) collective-permute-start(f32[2,128,128]{2,1,0:T(8,128)S(1)} %get-tuple-element.37), channel_id=1, source_target_pairs={{0,4},{2,6},{4,0},{6,2},{8,12},{10,14},{12,8},{14,10},{16,20},{18,... | collective-permute-start | bytes 393224 | tf_op jit(solution)/shard_map/ppermute | solution.py:213
  61.7 2.8 %collective-permute-done.8 = f32[2,128,128]{2,1,0:T(8,128)S(1)} collective-permute-done((f32[2,128,128]{2,1,0:T(8,128)S(1)}, f32[2,128,128]{2,1,0:T(8,128)S(1)}, u32[]{:S(2)}, u32[]{:S(2)}) %collective-permute-start.8) | collective-permute-done | bytes 131104 | tf_op jit(solution)/shard_map/ppermute | solution.py:213
  65.1 1.3 %collective-permute-done.9 = f32[4,128,128]{2,1,0:T(8,128)S(1)} collective-permute-done((f32[4,128,128]{2,1,0:T(8,128)S(1)}, f32[4,128,128]{2,1,0:T(8,128)S(1)}, u32[]{:S(2)}, u32[]{:S(2)}) %collective-permute-start.9) | collective-permute-done | bytes 262176 | tf_op jit(solution)/shard_map/ppermute | solution.py:213
  67.6 1.6 %collective-permute-start.10 = (bf16[128,1024]{1,0:T(8,128)(2,1)S(1)}, bf16[128,1024]{1,0:T(8,128)(2,1)S(1)}, u32[]{:S(2)}, u32[]{:S(2)}) collective-permute-start(bf16[128,1024]{1,0:T(8,128)(2,1)S(1)} %get-tuple-element.23), channel_id=1, source_target_pairs={{0,1},{1,0},{2,3},{3,2},{4,5},{5,4},{6,7},{7,6},{8,9},{9,8},{10,11... | collective-permute-start | bytes 786440 | tf_op jit(solution)/shard_map/ppermute | solution.py:248
  69.2 6.8 %collective-permute-done.10 = bf16[128,1024]{1,0:T(8,128)(2,1)S(1)} collective-permute-done((bf16[128,1024]{1,0:T(8,128)(2,1)S(1)}, bf16[128,1024]{1,0:T(8,128)(2,1)S(1)}, u32[]{:S(2)}, u32[]{:S(2)}) %collective-permute-start.10) | collective-permute-done | bytes 262176 | tf_op jit(solution)/shard_map/ppermute | solution.py:248
  76.9 1.3 %fusion.44 = bf16[128,2048]{1,0:T(8,128)(2,1)} fusion(bf16[128,2048]{1,0:T(8,128)(2,1)S(1)} %copy-done.5, f32[16,8,16,128]{3,2,1,0:T(8,128)S(1)} %bitcast.124, f32[2048]{0:T(1024)S(1)} %broadcast_bitcast_fusion), kind=kLoop, calls=%fused_computation.75 | loop fusion | flops 2097152 | bytes 2105344 | tf_op jit(solution)/shard_map/convert_element_type | solution.py:227
  (91 shorter events, 14.6 us)
Async XLA Ops:
  1.3 11.2 %collective-permute-start = (bf16[2,128,512]{2,1,0:T(8,128)(2,1)S(1)}, bf16[2,128,512]{2,1,0:T(8,128)(2,1)S(1)}, u32[]{:S(2)}, u32[]{:S(2)}) collective-permute-start(bf16[2,128,512]{2,1,0:T(8,128)(2,1)S(1)} %get-tuple-element.34), channel_id=1, source_target_pairs={{0,1},{1,0},{2,3},{3,2},{4,5},{5,4},{6,7},{7,6},{8,9},{9,8},{10,11... | collective-permute-start | bytes 786440 | tf_op jit(solution)/shard_map/ppermute | solution.py:235
  5.1 6.5 %collective-permute-start.1 = (bf16[2,128,8]{1,2,0:T(8,128)(2,1)S(1)}, bf16[2,128,8]{1,2,0:T(8,128)(2,1)S(1)}, u32[]{:S(2)}, u32[]{:S(2)}) collective-permute-start(bf16[2,128,8]{1,2,0:T(8,128)(2,1)S(1)} %get-tuple-element.50), channel_id=1, source_target_pairs={{0,1},{1,0},{2,3},{3,2},{4,5},{5,4},{6,7},{7,6},{8,9},{9,8},{10,11... | collective-permute-start | bytes 12296 | tf_op jit(solution)/shard_map/ppermute | solution.py:235
  6.3 10.1 %collective-permute-start.2 = (bf16[128,1024]{1,0:T(8,128)(2,1)S(1)}, bf16[128,1024]{1,0:T(8,128)(2,1)S(1)}, u32[]{:S(2)}, u32[]{:S(2)}) collective-permute-start(bf16[128,1024]{1,0:T(8,128)(2,1)S(1)} %get-tuple-element.32), channel_id=1, source_target_pairs={{0,1},{1,0},{2,3},{3,2},{4,5},{5,4},{6,7},{7,6},{8,9},{9,8},{10,11... | collective-permute-start | bytes 786440 | tf_op jit(solution)/shard_map/ppermute | solution.py:235
  13.8 1.3 %copy-start.2 = (f32[4,2,128,128]{3,0,2,1:T(4,128)}, f32[4,2,128,128]{3,0,2,1:T(4,128)S(1)}, u32[]{:S(2)}) copy-start(f32[4,2,128,128]{3,0,2,1:T(4,128)S(1)} %multiply_bitcast_fusion) | copy-start | bytes 1572868
  27.8 1.0 %copy-start = (f32[8,2,128,128]{3,2,1,0:T(8,128)}, f32[8,2,128,128]{3,2,1,0:T(8,128)S(1)}, u32[]{:S(2)}) copy-start(f32[8,2,128,128]{3,2,1,0:T(8,128)S(1)} %get-tuple-element.6) | copy-start | bytes 3145732
  28.9 1.1 %copy-start.4 = (f32[8,128,256]{2,1,0:T(8,128)}, f32[8,128,256]{2,1,0:T(8,128)S(1)}, u32[]{:S(2)}) copy-start(f32[8,128,256]{2,1,0:T(8,128)S(1)} %convolution_add_fusion.2) | copy-start | bytes 3145732
  30.0 2.3 %collective-permute-start.3 = (f32[4,128,256]{2,1,0:T(8,128)}, f32[4,128,256]{2,1,0:T(8,128)}, u32[]{:S(2)}, u32[]{:S(2)}) collective-permute-start(f32[4,128,256]{2,1,0:T(8,128)} %constant_dynamic-slice_fusion.3), channel_id=1, source_target_pairs={{0,2},{2,0},{4,6},{6,4},{8,10},{10,8},{12,14},{14,12},{16,18},{18,... | collective-permute-start | bytes 1572872 | tf_op jit(solution)/shard_map/ppermute | solution.py:200
  33.5 11.1 %copy-start.3 = (f32[4,2,128,128]{3,0,2,1:T(4,128)S(1)}, f32[4,2,128,128]{3,0,2,1:T(4,128)}, u32[]{:S(2)}) copy-start(f32[4,2,128,128]{3,0,2,1:T(4,128)} %copy-done.2) | copy-start | bytes 1572868
  34.0 8.4 %collective-permute-start.4 = (f32[2,128,256]{2,1,0:T(8,128)S(1)}, f32[2,128,256]{2,1,0:T(8,128)S(1)}, u32[]{:S(2)}, u32[]{:S(2)}) collective-permute-start(f32[2,128,256]{2,1,0:T(8,128)S(1)} %constant_dynamic-slice_fusion.2), channel_id=1, source_target_pairs={{0,4},{2,6},{4,0},{6,2},{8,12},{10,14},{12,8},{14,10},{16,20},{18,... | collective-permute-start | bytes 786440 | tf_op jit(solution)/shard_map/ppermute | solution.py:200
  42.7 5.0 %collective-permute-start.5 = (f32[1,128,256]{2,1,0:T(8,128)S(1)}, f32[1,128,256]{2,1,0:T(8,128)S(1)}, u32[]{:S(2)}, u32[]{:S(2)}) collective-permute-start(f32[1,128,256]{2,1,0:T(8,128)S(1)} %constant_dynamic-slice_fusion.1), channel_id=1, source_target_pairs={{0,8},{2,10},{4,12},{6,14},{8,0},{10,2},{12,4},{14,6},{16,24},{18,... | collective-permute-start | bytes 393224 | tf_op jit(solution)/shard_map/ppermute | solution.py:200
  48.0 6.7 %collective-permute-start.6 = (f32[1,128,128]{2,1,0:T(8,128)S(1)}, f32[1,128,128]{2,1,0:T(8,128)S(1)}, u32[]{:S(2)}, u32[]{:S(2)}) collective-permute-start(f32[1,128,128]{2,1,0:T(8,128)S(1)} %slice_add_fusion.7), channel_id=1, source_target_pairs={{0,16},{2,18},{4,20},{6,22},{8,24},{10,26},{12,28},{14,30},{1,17},... | collective-permute-start | bytes 196616 | tf_op jit(solution)/shard_map/ppermute | solution.py:177
  54.9 6.1 %copy-start.1 = (f32[8,2,128,128]{3,2,1,0:T(8,128)S(1)}, f32[8,2,128,128]{3,2,1,0:T(8,128)}, u32[]{:S(2)}) copy-start(f32[8,2,128,128]{3,2,1,0:T(8,128)} %copy-done) | copy-start | bytes 3145732
  54.9 4.3 %collective-permute-start.7 = (f32[1,128,128]{2,1,0:T(8,128)S(1)}, f32[1,128,128]{2,1,0:T(8,128)S(1)}, u32[]{:S(2)}, u32[]{:S(2)}) collective-permute-start(f32[1,128,128]{2,1,0:T(8,128)S(1)} %get-tuple-element.43), channel_id=1, source_target_pairs={{0,8},{2,10},{4,12},{6,14},{8,0},{10,2},{12,4},{14,6},{16,24},{18,... | collective-permute-start | bytes 196616 | tf_op jit(solution)/shard_map/ppermute | solution.py:213
  59.5 5.0 %collective-permute-start.8 = (f32[2,128,128]{2,1,0:T(8,128)S(1)}, f32[2,128,128]{2,1,0:T(8,128)S(1)}, u32[]{:S(2)}, u32[]{:S(2)}) collective-permute-start(f32[2,128,128]{2,1,0:T(8,128)S(1)} %get-tuple-element.37), channel_id=1, source_target_pairs={{0,4},{2,6},{4,0},{6,2},{8,12},{10,14},{12,8},{14,10},{16,20},{18,... | collective-permute-start | bytes 393224 | tf_op jit(solution)/shard_map/ppermute | solution.py:213
  64.8 1.6 %collective-permute-start.9 = (f32[4,128,128]{2,1,0:T(8,128)S(1)}, f32[4,128,128]{2,1,0:T(8,128)S(1)}, u32[]{:S(2)}, u32[]{:S(2)}) collective-permute-start(f32[4,128,128]{2,1,0:T(8,128)S(1)} %get-tuple-element.25), channel_id=1, source_target_pairs={{0,2},{2,0},{4,6},{6,4},{8,10},{10,8},{12,14},{14,12},{16,18},{18,... | collective-permute-start | bytes 786440 | tf_op jit(solution)/shard_map/ppermute | solution.py:213
  67.1 2.1 %copy-start.6 = (bf16[128]{0:T(256)(128)(2,1)S(1)}, bf16[128]{0:T(256)(128)(2,1)}, u32[]{:S(2)}) copy-start(bf16[128]{0:T(256)(128)(2,1)} %param.13) | copy-start | bytes 772
  67.5 9.4 %copy-start.5 = (bf16[128,2048]{1,0:T(8,128)(2,1)S(1)}, bf16[128,2048]{1,0:T(8,128)(2,1)}, u32[]{:S(2)}) copy-start(bf16[128,2048]{1,0:T(8,128)(2,1)} %param.10) | copy-start | bytes 1572868
  67.6 8.4 %collective-permute-start.10 = (bf16[128,1024]{1,0:T(8,128)(2,1)S(1)}, bf16[128,1024]{1,0:T(8,128)(2,1)S(1)}, u32[]{:S(2)}, u32[]{:S(2)}) collective-permute-start(bf16[128,1024]{1,0:T(8,128)(2,1)S(1)} %get-tuple-element.23), channel_id=1, source_target_pairs={{0,1},{1,0},{2,3},{3,2},{4,5},{5,4},{6,7},{7,6},{8,9},{9,8},{10,11... | collective-permute-start | bytes 786440 | tf_op jit(solution)/shard_map/ppermute | solution.py:248

commit v19 on v18

--- a/solution.py
+++ b/solution.py
@@ -230,8 +230,9 @@
 def head_swap(rows):
     width = rows.shape[-1] // 2
     first = lax.axis_index("head") == 0
-    own = jnp.where(first, rows[..., :width], rows[..., width:])
-    sent = jnp.where(first, rows[..., width:], rows[..., :width])
+    half = lax.axis_index("head")
+    own = lax.dynamic_slice_in_dim(rows, half * width, width, rows.ndim - 1)
+    sent = lax.dynamic_slice_in_dim(rows, (1 - half) * width, width, rows.ndim - 1)
     got = lax.ppermute(sent, "head", [(0, 1), (1, 0)])
     axis = rows.ndim - 2
     return jnp.where(

time: 78.5 us -> 78.3 us (level)
  other arithmetic: 12.5 us -> 11.2 us
  local copies, waits for them, and re-layouts: 3.1 us -> 4.16 us
    select_n x3 -> x0, other arithmetic: 3.15 us -> none  [head_swap(): own = jnp.where(first, rows[..., :width], rows[..., width:])]
    another operation x0 -> x2, other arithmetic: none -> 1.86 us  [the longest x1 1.13 us: head_inputs(): query_key = head_swap(jnp.stack([query_rows, key_rows]))]
    dynamic_slice x0 -> x1, local copies, waits for them, and re-layouts: none -> 1.06 us  [head_swap(): own = lax.dynamic_slice_in_dim(rows, half * width, width, rows.ndim - 1)]
where the time goes in v19:
time: 78.3 us; the launch traced here: 78.1 us
  waiting for transfers between devices  28 us (36%)
  starting transfers between devices  19 us (24%)
  matrix products  15 us (19%)
  other arithmetic  11.2 us (14%)
  local copies, waits for them, and re-layouts  4.16 us (5%)
    ppermute x6, waiting for transfers between devices, chain_states(): got = lax.ppermute(other, 'ctx', [(i, i ^ stride) for i in range(size)])  16.9 us
    ppermute x6, starting transfers between devices, chain_states(): got = lax.ppermute(other, 'ctx', [(i, i ^ stride) for i in range(size)])  7.32 us
    ppermute x1, waiting for transfers between devices, head_return(): got = lax.ppermute(sent, 'head', [(0, 1), (1, 0)])  6.76 us
    dot_general x5, matrix products, unit_lower_inverse(): jnp.matmul(jnp.concatenate([inverse, power], axis=-2), power, precision=L...  5.36 us
    ppermute x3, starting transfers between devices, head_swap(): got = lax.ppermute(sent, 'head', [(0, 1), (1, 0)])  5.12 us
    ppermute x1, starting transfers between devices, exclusive_scan(): return lax.ppermute(write, 'ctx', near)  4.94 us
    ppermute x3, waiting for transfers between devices, head_swap(): got = lax.ppermute(sent, 'head', [(0, 1), (1, 0)])  3.96 us
    add x4, other arithmetic, unit_lower_inverse(): inverse = inverse + both[..., :SPAN, :]  1.76 us
  transfers between devices with their start and end apart: 11, of which 10 were waited for; matrix products, arithmetic and copies ran while one was open for 12% of the time, Pallas kernels for 0%

profile of v19, /device:TPU:0, one launch (start us, length us, event | category | flops | bytes accessed | tf_op | source)
XLA Modules:
  0.0 78.1 jit_solution(18222425787901487638)
XLA Ops:
  0.0 1.1 %fusion.62 = (bf16[2,128,512]{2,1,0:T(8,128)(2,1)S(1)}, bf16[2,128,512]{2,1,0:T(8,128)(2,1)S(1)}) fusion(s32[]{:T(128)S(6)} %select_n.228, bf16[1,128,1024]{2,1,0:T(8,128)(2,1)} %bitcast.144, bf16[1,128,1024]{2,1,0:T(8,128)(2,1)} %bitcast.145, s32[]{:T(128)S(6)} %select_n.229), kind=kLoop, calls=%fused_computation.113 | loop fusion | flops 1048576 | bytes 1048584 | tf_op jit(solution)/shard_map/stack | solution.py:257
  1.1 3.0 %collective-permute-start = (bf16[2,128,512]{2,1,0:T(8,128)(2,1)S(1)}, bf16[2,128,512]{2,1,0:T(8,128)(2,1)S(1)}, u32[]{:S(2)}, u32[]{:S(2)}) collective-permute-start(bf16[2,128,512]{2,1,0:T(8,128)(2,1)S(1)} %get-tuple-element.34), channel_id=1, source_target_pairs={{0,1},{1,0},{2,3},{3,2},{4,5},{5,4},{6,7},{7,6},{8,9},{9,8},{10,11... | collective-permute-start | bytes 786440 | tf_op jit(solution)/shard_map/ppermute | solution.py:236
  4.2 0.7 fusion.76
  4.9 1.1 %constant_dynamic-slice_fusion.5 = (bf16[128,1024]{1,0:T(8,128)(2,1)S(1)}, bf16[128,1024]{1,0:T(8,128)(2,1)S(1)}) fusion(bf16[128,2048]{1,0:T(8,128)(2,1)} %param.9, s32[]{:T(128)S(6)} %select_n.238, s32[]{:T(128)S(6)} %select_n.239), kind=kLoop, calls=%fused_computation.162 | loop fusion | bytes 1048584 | tf_op jit(solution)/shard_map/dynamic_slice | solution.py:234
  6.0 2.1 %collective-permute-start.2 = (bf16[128,1024]{1,0:T(8,128)(2,1)S(1)}, bf16[128,1024]{1,0:T(8,128)(2,1)S(1)}, u32[]{:S(2)}, u32[]{:S(2)}) collective-permute-start(bf16[128,1024]{1,0:T(8,128)(2,1)S(1)} %get-tuple-element.32), channel_id=1, source_target_pairs={{0,1},{1,0},{2,3},{3,2},{4,5},{5,4},{6,7},{7,6},{8,9},{9,8},{10,11... | collective-permute-start | bytes 786440 | tf_op jit(solution)/shard_map/ppermute | solution.py:236
  8.1 3.3 %collective-permute-done.1 = bf16[2,128,8]{1,2,0:T(8,128)(2,1)S(1)} collective-permute-done((bf16[2,128,8]{1,2,0:T(8,128)(2,1)S(1)}, bf16[2,128,8]{1,2,0:T(8,128)(2,1)S(1)}, u32[]{:S(2)}, u32[]{:S(2)}) %collective-permute-start.1) | collective-permute-done | bytes 4128 | tf_op jit(solution)/shard_map/ppermute | solution.py:236
  16.5 1.1 %fusion = f32[8,2,256,128]{3,2,1,0:T(8,128)S(1)} fusion(f32[8,2,128,128]{3,2,1,0:T(8,128)S(1)} %fusion.95, f32[8,2,128,128]{3,2,1,0:T(8,128)S(1)} %get-tuple-element.21), kind=kOutput, calls=%fused_computation | convolution fusion | flops 403177472 | bytes 4194304 | tf_op jit(solution)/shard_map/dot_general | solution.py:71
  17.6 1.0 %slice_add_fusion.5 = (f32[8,2,128,128]{3,2,1,0:T(8,128)S(1)}, f32[8,2,128,128]{3,2,1,0:T(8,128)S(1)}, f32[8,2,128,128]{3,2,1,0:T(8,128)S(1)}) fusion(f32[8,2,256,128]{3,2,1,0:T(8,128)S(1)} %fusion, f32[4,2,128,128]{3,2,1,0:T(8,128)S(1)} %fusion.90, f32[8,2,128]{2,1,0:T(2,128)S(1)} %copy.66, pred[128,128]{1,0:T(8,128)(4,1)S(1)} %get-tuple-element.51, ...), kind=kLoop, calls=%fused_computation.69 | loop fusion | flops 1835008 | bytes 6922240 | tf_op jit(solution)/shard_map/add | solution.py:74
  18.6 1.1 %fusion.4 = f32[8,2,256,128]{3,2,1,0:T(8,128)S(1)} fusion(f32[8,2,128,128]{3,2,1,0:T(8,128)S(1)} %get-tuple-element.14, f32[8,2,128,128]{3,2,1,0:T(8,128)S(1)} %get-tuple-element.13), kind=kOutput, calls=%fused_computation.4 | convolution fusion | flops 403177472 | bytes 4194304 | tf_op jit(solution)/shard_map/dot_general | solution.py:71
  19.9 1.1 %fusion.8 = f32[8,2,256,128]{3,2,1,0:T(8,128)S(1)} fusion(f32[8,2,128,128]{3,2,1,0:T(8,128)S(1)} %get-tuple-element.12, f32[8,2,128,128]{3,2,1,0:T(8,128)S(1)} %get-tuple-element.11), kind=kOutput, calls=%fused_computation.8 | convolution fusion | flops 403177472 | bytes 4194304 | tf_op jit(solution)/shard_map/dot_general | solution.py:71
  21.3 1.1 %fusion.12 = f32[8,2,256,128]{3,2,1,0:T(8,128)S(1)} fusion(f32[8,2,128,128]{3,2,1,0:T(8,128)S(1)} %get-tuple-element.10, f32[8,2,128,128]{3,2,1,0:T(8,128)S(1)} %get-tuple-element.9), kind=kOutput, calls=%fused_computation.12 | convolution fusion | flops 403177472 | bytes 4194304 | tf_op jit(solution)/shard_map/dot_general | solution.py:71
  22.6 1.1 %fusion.16 = f32[8,2,256,128]{3,2,1,0:T(8,128)S(1)} fusion(f32[8,2,128,128]{3,2,1,0:T(8,128)S(1)} %get-tuple-element.8, f32[8,2,128,128]{3,2,1,0:T(8,128)S(1)} %get-tuple-element.7), kind=kOutput, calls=%fused_computation.16 | convolution fusion | flops 403177472 | bytes 4194304 | tf_op jit(solution)/shard_map/dot_general | solution.py:71
  23.7 0.7 convolution_add_fusion
  25.1 1.2 %fusion.20 = f32[8,2,128,256]{3,2,1,0:T(8,128)S(1)} fusion(f32[8,2,128,128]{3,2,1,0:T(8,128)S(1)} %convolution_add_fusion, f32[8,2,128,128]{3,2,1,0:T(8,128)S(1)} %get-tuple-element.28, f32[8,2,128,128]{3,2,1,0:T(8,128)S(1)} %get-tuple-element.48), kind=kOutput, calls=%fused_computation.20 | convolution fusion | flops 403177472 | bytes 5242880 | tf_op jit(solution)/shard_map/dot_general | solution.py:99
  26.3 1.1 %fusion.96 = f32[8,2,128,256]{3,2,1,0:T(8,128)S(1)} fusion(f32[8,2,128,128]{3,2,1,0:T(8,128)S(1)} %get-tuple-element.27, f32[8,2,128,256]{3,2,1,0:T(8,128)S(1)} %fusion.20), kind=kOutput, calls=%fused_computation.189 | convolution fusion | flops 402653184 | bytes 5242880 | tf_op jit(solution)/shard_map/hmck,hmcj->hmkj/dot_general | solution.py:104
  28.7 0.9 %constant_dynamic-slice_fusion.3 = f32[4,128,256]{2,1,0:T(8,128)} fusion(f32[8,128,256]{2,1,0:T(8,128)S(1)} %convolution_add_fusion.2, s32[]{:T(128)S(6)} %select_n.257), kind=kLoop, calls=%fused_computation.160 | loop fusion | bytes 1048580 | tf_op jit(solution)/shard_map/dynamic_slice | solution.py:199
  29.9 2.2 %collective-permute-done.3 = f32[4,128,256]{2,1,0:T(8,128)} collective-permute-done((f32[4,128,256]{2,1,0:T(8,128)}, f32[4,128,256]{2,1,0:T(8,128)}, u32[]{:S(2)}, u32[]{:S(2)}) %collective-permute-start.3) | collective-permute-done | bytes 524320 | tf_op jit(solution)/shard_map/ppermute | solution.py:200
  32.0 1.3 %dynamic-slice_select_fusion.1 = (f32[4,128,256]{2,1,0:T(8,128)S(1)}, f32[4,128,256]{2,1,0:T(8,128)S(1)}) fusion(f32[4,128,256]{2,1,0:T(8,128)} %collective-permute-done.3, f32[8,128,256]{2,1,0:T(8,128)} %copy-done.4, s32[]{:T(128)S(6)} %select_n.256, pred[]{:T(512)S(6)} %eq.34), kind=kLoop, calls=%fused_computation.111 | loop fusion | flops 262144 | bytes 2097157 | tf_op jit(solution)/shard_map/jit(_where)/select_n | solution.py:202
  33.8 1.8 %collective-permute-start.4 = (f32[2,128,256]{2,1,0:T(8,128)S(1)}, f32[2,128,256]{2,1,0:T(8,128)S(1)}, u32[]{:S(2)}, u32[]{:S(2)}) collective-permute-start(f32[2,128,256]{2,1,0:T(8,128)S(1)} %constant_dynamic-slice_fusion.2), channel_id=1, source_target_pairs={{0,4},{2,6},{4,0},{6,2},{8,12},{10,14},{12,8},{14,10},{16,20},{18,... | collective-permute-start | bytes 786440 | tf_op jit(solution)/shard_map/ppermute | solution.py:200
  35.9 6.3 %collective-permute-done.4 = f32[2,128,256]{2,1,0:T(8,128)S(1)} collective-permute-done((f32[2,128,256]{2,1,0:T(8,128)S(1)}, f32[2,128,256]{2,1,0:T(8,128)S(1)}, u32[]{:S(2)}, u32[]{:S(2)}) %collective-permute-start.4) | collective-permute-done | bytes 262176 | tf_op jit(solution)/shard_map/ppermute | solution.py:200
  42.5 1.9 %collective-permute-start.5 = (f32[1,128,256]{2,1,0:T(8,128)S(1)}, f32[1,128,256]{2,1,0:T(8,128)S(1)}, u32[]{:S(2)}, u32[]{:S(2)}) collective-permute-start(f32[1,128,256]{2,1,0:T(8,128)S(1)} %constant_dynamic-slice_fusion.1), channel_id=1, source_target_pairs={{0,8},{2,10},{4,12},{6,14},{8,0},{10,2},{12,4},{14,6},{16,24},{18,... | collective-permute-start | bytes 393224 | tf_op jit(solution)/shard_map/ppermute | solution.py:200
  45.1 2.5 %collective-permute-done.5 = f32[1,128,256]{2,1,0:T(8,128)S(1)} collective-permute-done((f32[1,128,256]{2,1,0:T(8,128)S(1)}, f32[1,128,256]{2,1,0:T(8,128)S(1)}, u32[]{:S(2)}, u32[]{:S(2)}) %collective-permute-start.5) | collective-permute-done | bytes 131104 | tf_op jit(solution)/shard_map/ppermute | solution.py:200
  47.8 4.9 %collective-permute-start.6 = (f32[1,128,128]{2,1,0:T(8,128)S(1)}, f32[1,128,128]{2,1,0:T(8,128)S(1)}, u32[]{:S(2)}, u32[]{:S(2)}) collective-permute-start(f32[1,128,128]{2,1,0:T(8,128)S(1)} %slice_add_fusion.7), channel_id=1, source_target_pairs={{0,16},{2,18},{4,20},{6,22},{8,24},{10,26},{12,28},{14,30},{1,17},... | collective-permute-start | bytes 196616 | tf_op jit(solution)/shard_map/ppermute | solution.py:177
  52.9 1.2 %fusion.34 = f32[8,2,128,256]{3,2,1,0:T(8,128)S(1)} fusion(f32[8,2,128,256]{3,2,1,0:T(8,128)S(1)} %fusion.20, f32[8,2,128,128]{3,2,1,0:T(8,128)S(1)} %bitcast.123, f32[8,2,128]{2,1,0:T(2,128)S(1)} %copy.66, pred[128,128]{1,0:T(8,128)(4,1)S(1)} %iota_compare_fusion.2), kind=kOutput, calls=%fused_computation.53 | convolution fusion | flops 403439616 | bytes 5267456 | tf_op jit(solution)/shard_map/hmij,hmjv->hmiv/dot_general | solution.py:124
  54.7 2.0 %collective-permute-start.7 = (f32[1,128,128]{2,1,0:T(8,128)S(1)}, f32[1,128,128]{2,1,0:T(8,128)S(1)}, u32[]{:S(2)}, u32[]{:S(2)}) collective-permute-start(f32[1,128,128]{2,1,0:T(8,128)S(1)} %get-tuple-element.43), channel_id=1, source_target_pairs={{0,8},{2,10},{4,12},{6,14},{8,0},{10,2},{12,4},{14,6},{16,24},{18,... | collective-permute-start | bytes 196616 | tf_op jit(solution)/shard_map/ppermute | solution.py:213
  57.3 1.7 %collective-permute-done.7 = f32[1,128,128]{2,1,0:T(8,128)S(1)} collective-permute-done((f32[1,128,128]{2,1,0:T(8,128)S(1)}, f32[1,128,128]{2,1,0:T(8,128)S(1)}, u32[]{:S(2)}, u32[]{:S(2)}) %collective-permute-start.7) | collective-permute-done | bytes 65568 | tf_op jit(solution)/shard_map/ppermute | solution.py:213
  59.3 1.6 %collective-permute-start.8 = (f32[2,128,128]{2,1,0:T(8,128)S(1)}, f32[2,128,128]{2,1,0:T(8,128)S(1)}, u32[]{:S(2)}, u32[]{:S(2)}) collective-permute-start(f32[2,128,128]{2,1,0:T(8,128)S(1)} %get-tuple-element.37), channel_id=1, source_target_pairs={{0,4},{2,6},{4,0},{6,2},{8,12},{10,14},{12,8},{14,10},{16,20},{18,... | collective-permute-start | bytes 393224 | tf_op jit(solution)/shard_map/ppermute | solution.py:213
  61.5 2.8 %collective-permute-done.8 = f32[2,128,128]{2,1,0:T(8,128)S(1)} collective-permute-done((f32[2,128,128]{2,1,0:T(8,128)S(1)}, f32[2,128,128]{2,1,0:T(8,128)S(1)}, u32[]{:S(2)}, u32[]{:S(2)}) %collective-permute-start.8) | collective-permute-done | bytes 131104 | tf_op jit(solution)/shard_map/ppermute | solution.py:213
  64.9 1.3 %collective-permute-done.9 = f32[4,128,128]{2,1,0:T(8,128)S(1)} collective-permute-done((f32[4,128,128]{2,1,0:T(8,128)S(1)}, f32[4,128,128]{2,1,0:T(8,128)S(1)}, u32[]{:S(2)}, u32[]{:S(2)}) %collective-permute-start.9) | collective-permute-done | bytes 262176 | tf_op jit(solution)/shard_map/ppermute | solution.py:213
  67.4 1.6 %collective-permute-start.10 = (bf16[128,1024]{1,0:T(8,128)(2,1)S(1)}, bf16[128,1024]{1,0:T(8,128)(2,1)S(1)}, u32[]{:S(2)}, u32[]{:S(2)}) collective-permute-start(bf16[128,1024]{1,0:T(8,128)(2,1)S(1)} %get-tuple-element.23), channel_id=1, source_target_pairs={{0,1},{1,0},{2,3},{3,2},{4,5},{5,4},{6,7},{7,6},{8,9},{9,8},{10,11... | collective-permute-start | bytes 786440 | tf_op jit(solution)/shard_map/ppermute | solution.py:249
  69.0 6.8 %collective-permute-done.10 = bf16[128,1024]{1,0:T(8,128)(2,1)S(1)} collective-permute-done((bf16[128,1024]{1,0:T(8,128)(2,1)S(1)}, bf16[128,1024]{1,0:T(8,128)(2,1)S(1)}, u32[]{:S(2)}, u32[]{:S(2)}) %collective-permute-start.10) | collective-permute-done | bytes 262176 | tf_op jit(solution)/shard_map/ppermute | solution.py:249
  76.7 1.3 %fusion.44 = bf16[128,2048]{1,0:T(8,128)(2,1)} fusion(bf16[128,2048]{1,0:T(8,128)(2,1)S(1)} %copy-done.5, f32[16,8,16,128]{3,2,1,0:T(8,128)S(1)} %bitcast.124, f32[2048]{0:T(1024)S(1)} %broadcast_bitcast_fusion), kind=kLoop, calls=%fused_computation.75 | loop fusion | flops 2097152 | bytes 2105344 | tf_op jit(solution)/shard_map/convert_element_type | solution.py:227
  (91 shorter events, 14.6 us)
Async XLA Ops:
  1.1 11.2 %collective-permute-start = (bf16[2,128,512]{2,1,0:T(8,128)(2,1)S(1)}, bf16[2,128,512]{2,1,0:T(8,128)(2,1)S(1)}, u32[]{:S(2)}, u32[]{:S(2)}) collective-permute-start(bf16[2,128,512]{2,1,0:T(8,128)(2,1)S(1)} %get-tuple-element.34), channel_id=1, source_target_pairs={{0,1},{1,0},{2,3},{3,2},{4,5},{5,4},{6,7},{7,6},{8,9},{9,8},{10,11... | collective-permute-start | bytes 786440 | tf_op jit(solution)/shard_map/ppermute | solution.py:236
  4.9 6.5 %collective-permute-start.1 = (bf16[2,128,8]{1,2,0:T(8,128)(2,1)S(1)}, bf16[2,128,8]{1,2,0:T(8,128)(2,1)S(1)}, u32[]{:S(2)}, u32[]{:S(2)}) collective-permute-start(bf16[2,128,8]{1,2,0:T(8,128)(2,1)S(1)} %get-tuple-element.50), channel_id=1, source_target_pairs={{0,1},{1,0},{2,3},{3,2},{4,5},{5,4},{6,7},{7,6},{8,9},{9,8},{10,11... | collective-permute-start | bytes 12296 | tf_op jit(solution)/shard_map/ppermute | solution.py:236
  6.0 10.2 %collective-permute-start.2 = (bf16[128,1024]{1,0:T(8,128)(2,1)S(1)}, bf16[128,1024]{1,0:T(8,128)(2,1)S(1)}, u32[]{:S(2)}, u32[]{:S(2)}) collective-permute-start(bf16[128,1024]{1,0:T(8,128)(2,1)S(1)} %get-tuple-element.32), channel_id=1, source_target_pairs={{0,1},{1,0},{2,3},{3,2},{4,5},{5,4},{6,7},{7,6},{8,9},{9,8},{10,11... | collective-permute-start | bytes 786440 | tf_op jit(solution)/shard_map/ppermute | solution.py:236
  13.6 1.3 %copy-start.2 = (f32[4,2,128,128]{3,0,2,1:T(4,128)}, f32[4,2,128,128]{3,0,2,1:T(4,128)S(1)}, u32[]{:S(2)}) copy-start(f32[4,2,128,128]{3,0,2,1:T(4,128)S(1)} %multiply_bitcast_fusion) | copy-start | bytes 1572868
  27.6 1.0 %copy-start = (f32[8,2,128,128]{3,2,1,0:T(8,128)}, f32[8,2,128,128]{3,2,1,0:T(8,128)S(1)}, u32[]{:S(2)}) copy-start(f32[8,2,128,128]{3,2,1,0:T(8,128)S(1)} %get-tuple-element.6) | copy-start | bytes 3145732
  28.7 1.1 %copy-start.4 = (f32[8,128,256]{2,1,0:T(8,128)}, f32[8,128,256]{2,1,0:T(8,128)S(1)}, u32[]{:S(2)}) copy-start(f32[8,128,256]{2,1,0:T(8,128)S(1)} %convolution_add_fusion.2) | copy-start | bytes 3145732
  29.8 2.3 %collective-permute-start.3 = (f32[4,128,256]{2,1,0:T(8,128)}, f32[4,128,256]{2,1,0:T(8,128)}, u32[]{:S(2)}, u32[]{:S(2)}) collective-permute-start(f32[4,128,256]{2,1,0:T(8,128)} %constant_dynamic-slice_fusion.3), channel_id=1, source_target_pairs={{0,2},{2,0},{4,6},{6,4},{8,10},{10,8},{12,14},{14,12},{16,18},{18,... | collective-permute-start | bytes 1572872 | tf_op jit(solution)/shard_map/ppermute | solution.py:200
  33.3 11.1 %copy-start.3 = (f32[4,2,128,128]{3,0,2,1:T(4,128)S(1)}, f32[4,2,128,128]{3,0,2,1:T(4,128)}, u32[]{:S(2)}) copy-start(f32[4,2,128,128]{3,0,2,1:T(4,128)} %copy-done.2) | copy-start | bytes 1572868
  33.8 8.4 %collective-permute-start.4 = (f32[2,128,256]{2,1,0:T(8,128)S(1)}, f32[2,128,256]{2,1,0:T(8,128)S(1)}, u32[]{:S(2)}, u32[]{:S(2)}) collective-permute-start(f32[2,128,256]{2,1,0:T(8,128)S(1)} %constant_dynamic-slice_fusion.2), channel_id=1, source_target_pairs={{0,4},{2,6},{4,0},{6,2},{8,12},{10,14},{12,8},{14,10},{16,20},{18,... | collective-permute-start | bytes 786440 | tf_op jit(solution)/shard_map/ppermute | solution.py:200
  42.5 5.0 %collective-permute-start.5 = (f32[1,128,256]{2,1,0:T(8,128)S(1)}, f32[1,128,256]{2,1,0:T(8,128)S(1)}, u32[]{:S(2)}, u32[]{:S(2)}) collective-permute-start(f32[1,128,256]{2,1,0:T(8,128)S(1)} %constant_dynamic-slice_fusion.1), channel_id=1, source_target_pairs={{0,8},{2,10},{4,12},{6,14},{8,0},{10,2},{12,4},{14,6},{16,24},{18,... | collective-permute-start | bytes 393224 | tf_op jit(solution)/shard_map/ppermute | solution.py:200
  47.8 6.7 %collective-permute-start.6 = (f32[1,128,128]{2,1,0:T(8,128)S(1)}, f32[1,128,128]{2,1,0:T(8,128)S(1)}, u32[]{:S(2)}, u32[]{:S(2)}) collective-permute-start(f32[1,128,128]{2,1,0:T(8,128)S(1)} %slice_add_fusion.7), channel_id=1, source_target_pairs={{0,16},{2,18},{4,20},{6,22},{8,24},{10,26},{12,28},{14,30},{1,17},... | collective-permute-start | bytes 196616 | tf_op jit(solution)/shard_map/ppermute | solution.py:177
  54.7 6.1 %copy-start.1 = (f32[8,2,128,128]{3,2,1,0:T(8,128)S(1)}, f32[8,2,128,128]{3,2,1,0:T(8,128)}, u32[]{:S(2)}) copy-start(f32[8,2,128,128]{3,2,1,0:T(8,128)} %copy-done) | copy-start | bytes 3145732
  54.7 4.3 %collective-permute-start.7 = (f32[1,128,128]{2,1,0:T(8,128)S(1)}, f32[1,128,128]{2,1,0:T(8,128)S(1)}, u32[]{:S(2)}, u32[]{:S(2)}) collective-permute-start(f32[1,128,128]{2,1,0:T(8,128)S(1)} %get-tuple-element.43), channel_id=1, source_target_pairs={{0,8},{2,10},{4,12},{6,14},{8,0},{10,2},{12,4},{14,6},{16,24},{18,... | collective-permute-start | bytes 196616 | tf_op jit(solution)/shard_map/ppermute | solution.py:213
  59.3 5.0 %collective-permute-start.8 = (f32[2,128,128]{2,1,0:T(8,128)S(1)}, f32[2,128,128]{2,1,0:T(8,128)S(1)}, u32[]{:S(2)}, u32[]{:S(2)}) collective-permute-start(f32[2,128,128]{2,1,0:T(8,128)S(1)} %get-tuple-element.37), channel_id=1, source_target_pairs={{0,4},{2,6},{4,0},{6,2},{8,12},{10,14},{12,8},{14,10},{16,20},{18,... | collective-permute-start | bytes 393224 | tf_op jit(solution)/shard_map/ppermute | solution.py:213
  64.6 1.6 %collective-permute-start.9 = (f32[4,128,128]{2,1,0:T(8,128)S(1)}, f32[4,128,128]{2,1,0:T(8,128)S(1)}, u32[]{:S(2)}, u32[]{:S(2)}) collective-permute-start(f32[4,128,128]{2,1,0:T(8,128)S(1)} %get-tuple-element.25), channel_id=1, source_target_pairs={{0,2},{2,0},{4,6},{6,4},{8,10},{10,8},{12,14},{14,12},{16,18},{18,... | collective-permute-start | bytes 786440 | tf_op jit(solution)/shard_map/ppermute | solution.py:213
  66.9 2.1 %copy-start.6 = (bf16[128]{0:T(256)(128)(2,1)S(1)}, bf16[128]{0:T(256)(128)(2,1)}, u32[]{:S(2)}) copy-start(bf16[128]{0:T(256)(128)(2,1)} %param.13) | copy-start | bytes 772
  67.3 9.4 %copy-start.5 = (bf16[128,2048]{1,0:T(8,128)(2,1)S(1)}, bf16[128,2048]{1,0:T(8,128)(2,1)}, u32[]{:S(2)}) copy-start(bf16[128,2048]{1,0:T(8,128)(2,1)} %param.10) | copy-start | bytes 1572868
  67.4 8.4 %collective-permute-start.10 = (bf16[128,1024]{1,0:T(8,128)(2,1)S(1)}, bf16[128,1024]{1,0:T(8,128)(2,1)S(1)}, u32[]{:S(2)}, u32[]{:S(2)}) collective-permute-start(bf16[128,1024]{1,0:T(8,128)(2,1)S(1)} %get-tuple-element.23), channel_id=1, source_target_pairs={{0,1},{1,0},{2,3},{3,2},{4,5},{5,4},{6,7},{7,6},{8,9},{9,8},{10,11... | collective-permute-start | bytes 786440 | tf_op jit(solution)/shard_map/ppermute | solution.py:249
